TPU v7x, 512 devices: a whole 4x4x16 slice. The times are simulated.
512 devices in a mesh: comp: 32 (over z, core), feat: 16 (over x, y).
Axes of the slice: x: 4, y: 4, z: 16, core: 2. Of those that a mesh axis runs over, the one named last changes fastest.
Arguments:
- block_values: bfloat16 [32, 16, 24, 128, 128], P('comp', 'feat'), may hold values from -0.0625 to 0.0625
- block_rows: int32 [32, 16, 24], P('comp', 'feat'), may hold values from 0 to 15, as said below
- block_cols: int32 [32, 16, 24], P('comp', 'feat'), may hold values from 0 to 13, as said below
- block_counts: int32 [32, 16], P('comp', 'feat'), may hold values from 8 to 24, as said below
- right_side: float32 [65536, 128], P(('comp', 'feat')), may hold values from -6 to 6
- ridge: float32 [128], replicated, may hold values from 0.1 to 2
Outputs:
- solution: float32 [28672, 128], P('feat')
- residual: float32 [65536, 128], P(('comp', 'feat'))
Inputs may be any that keep to these rules, and one draw needn't show every extreme that they name: Within one device the listed (block_rows, block_cols) pairs of all 24 slots are distinct; block rows are very uneven in how many blocks they hold. `block_cols`: see block_rows. `block_counts`: slots at or beyond a device's count are ignored; some device is full in every draw.
All inputs are finite; a program needn't handle non-finite values.
Results may differ from a plain program's by a relative error of at most 0.0029.
Values may be sent and summed in bfloat16 or wider, within the bound.
No kernel may reach another device: no remote copies, remote signals or barrier semaphores. Data moves between devices by JAX's collectives and lax.ppermute only.
A program may use at most 64 MiB of HBM per device.

v0:
```python
import jax
import jax.numpy as jnp
from jax import lax
from jax.sharding import PartitionSpec as P

RB_DEV = 16
CB_DEV = 14
ITERS = 2


def shards(block_values, block_rows, block_cols, block_counts, right_side, ridge):
    values = block_values[0, 0]
    slot_rows = block_rows[0, 0]
    slot_cols = block_cols[0, 0]
    count_of_slots = block_counts[0, 0]
    responses = right_side.shape[1]
    total_slot_number = values.shape[0]
    block_edge = values.shape[1]
    slot_live = (jnp.arange(total_slot_number) < count_of_slots).astype(jnp.float32)
    row_lookup_table = (jnp.arange(RB_DEV)[:, None] == slot_rows[None, :]).astype(
        jnp.float32
    ) * slot_live[None, :]
    col_table = (jnp.arange(CB_DEV)[:, None] == slot_cols[None, :]).astype(jnp.float32) * slot_live[
        None, :
    ]
    first_comp = (lax.axis_index("comp") == 0).astype(jnp.float32)

    def backward(low_slab):
        row_slabs = low_slab.reshape(RB_DEV, block_edge, responses)
        selected = jnp.take(row_slabs, slot_rows, axis=0)
        block_products = jnp.einsum(
            "sij,sik->sjk", values, selected, preferred_element_type=jnp.float32
        )
        summed = jnp.einsum(
            "qs,sjk->qjk", col_table, block_products, precision=lax.Precision.HIGHEST
        )
        return summed.reshape(CB_DEV * block_edge, responses)

    residual = right_side
    image_weight = 1.0

    def slab_of(current):
        return lax.all_gather(current.astype(jnp.bfloat16), "feat", axis=0, tiled=True)

    def reduce_grad(partial_contribution):
        return lax.psum(partial_contribution, "comp")

    def grad_total(gradient):
        return lax.psum(first_comp * jnp.sum(gradient * gradient, axis=0), ("comp", "feat"))

    gradient = reduce_grad(backward(slab_of(residual)))
    energy = grad_total(gradient)
    search_direction = gradient
    solution = jnp.zeros_like(gradient)
    for step_index in range(ITERS):
        col_panels = search_direction.astype(jnp.bfloat16).reshape(CB_DEV, block_edge, responses)
        forward_selected = jnp.take(col_panels, slot_cols, axis=0)
        forward_block_products = jnp.einsum(
            "sij,sjk->sik", values, forward_selected, preferred_element_type=jnp.float32
        )
        forward_summed = jnp.einsum(
            "rs,sik->rik", row_lookup_table, forward_block_products, precision=lax.Precision.HIGHEST
        )
        image_rows = lax.psum_scatter(
            forward_summed.reshape(RB_DEV * block_edge, responses),
            "feat",
            scatter_dimension=0,
            tiled=True,
        )
        image_energy, direction_energy = lax.psum(
            (
                image_weight * jnp.sum(image_rows * image_rows, axis=0),
                first_comp * jnp.sum(search_direction * search_direction, axis=0),
            ),
            ("comp", "feat"),
        )
        step_size = energy / (image_energy + ridge * direction_energy)
        solution = solution + step_size * search_direction
        residual = residual - step_size * image_rows
        if step_index + 1 < ITERS:
            gradient = reduce_grad(backward(slab_of(residual))) - ridge * solution
            next_energy = grad_total(gradient)
            search_direction = gradient + next_energy / energy * search_direction
            energy = next_energy
    return (solution, residual)


def solution(mesh):
    placed = (
        P("comp", "feat", None, None, None),
        P("comp", "feat", None),
        P("comp", "feat", None),
        P("comp", "feat"),
        P(("comp", "feat"), None),
        P(),
    )
    return jax.shard_map(
        shards,
        mesh=mesh,
        in_specs=placed,
        out_specs=(P("feat", None), P(("comp", "feat"), None)),
        check_vma=False,
    )
```

profile of v0, /device:TPU:1, one launch (start us, length us, event | category | flops | bytes accessed | tf_op | source)
XLA Modules:
  0.0 996.0 jit_solution(15830034595637753856)
XLA Ops:
  7.2 0.0 all-reduce.5.cloned.1.call-start
  7.2 0.7 compare_and_fusion.1
  8.0 0.7 compare_select_fusion.1
  9.3 0.8 convert_element_type.26
  10.1 20.0 %all_gather.6 = bf16[2048,128]{1,0:T(8,128)(2,1)S(1)} all-gather(bf16[128,128]{1,0:T(8,128)(2,1)S(1)} %convert_element_type.26), channel_id=1, replica_groups=mesh['comp'=32,'feat'=16] {'feat'}, dimensions={0}, use_global_device_ids=true | all-gather | bytes 557056 | tf_op jit(solution)/shard_map/all_gather | solution.py:43
  30.1 0.7 gather_fusion
  30.8 1.7 fusion.14
  32.5 2.0 copy.12
  34.5 1.0 fusion.6
  35.5 1.2 copy.8
  36.7 0.0 all-reduce.5.cloned.1.call-update
  36.7 0.0 reduce-scatter.3.cloned.1.call-start
  36.8 213.7 %all-reduce.5.cloned.1.call-done = f32[1792,128]{1,0:T(8,128)} async-done(((f32[1792,128]{1,0:T(8,128)}), f32[1792,128]{1,0:T(8,128)}) %all-reduce.5.cloned.1.call-update) | async-done | bytes 917520 | tf_op jit(solution)/shard_map/psum | solution.py:46
  250.5 1.7 multiply_reduce_fusion.2
  252.3 0.7 gather_fusion.1
  253.0 2.0 fusion.12
  255.0 2.0 copy.13
  257.0 1.0 fusion.4
  258.0 1.3 copy.9
  259.3 0.0 reduce-scatter.3.cloned.1.call-update
  259.3 0.0 all-reduce.7.cloned.1.call-start
  259.4 86.1 %reduce-scatter.3.cloned.1.call-done = f32[128,128]{1,0:T(8,128)} async-done(((f32[2048,128]{1,0:T(8,128)}), f32[128,128]{1,0:T(8,128)}) %reduce-scatter.3.cloned.1.call-update) | async-done | bytes 65552 | tf_op jit(solution)/shard_map/reduce_scatter | solution.py:64
  345.5 0.9 multiply_reduce_fusion.4
  346.3 105.3 %all-reduce.1 = (f32[128]{0:T(128)S(1)}, f32[128]{0:T(128)S(1)}) all-reduce(f32[128]{0:T(128)S(1)} %broadcast_multiply_fusion.2, f32[128]{0:T(128)S(1)} %multiply_reduce_fusion.4), channel_id=1, replica_groups=mesh['comp'=32,'feat'=16] {'comp','feat'}, use_global_device_ids=true, to_apply=%region_2.4 | all-reduce | flops 256 | bytes 2048 | tf_op jit(solution)/shard_map/psum | solution.py:49
  451.6 0.9 fusion.28
  452.5 16.0 %all_gather.7 = bf16[2048,128]{1,0:T(8,128)(2,1)S(1)} all-gather(bf16[128,128]{1,0:T(8,128)(2,1)S(1)} %fusion.28), channel_id=1, replica_groups=mesh['comp'=32,'feat'=16] {'feat'}, dimensions={0}, use_global_device_ids=true | all-gather | bytes 557056 | tf_op jit(solution)/shard_map/all_gather | solution.py:43
  468.5 0.7 gather_fusion.2
  469.2 1.7 fusion.10
  470.9 2.0 copy.14
  472.9 1.0 fusion.2
  473.9 1.2 copy.10
  475.1 0.0 all-reduce.7.cloned.1.call-update
  475.1 0.0 reduce-scatter.5.cloned.1.call-start
  475.2 208.0 %all-reduce.7.cloned.1.call-done = f32[1792,128]{1,0:T(8,128)} async-done(((f32[1792,128]{1,0:T(8,128)}), f32[1792,128]{1,0:T(8,128)}) %all-reduce.7.cloned.1.call-update) | async-done | bytes 917520 | tf_op jit(solution)/shard_map/psum | solution.py:46
  683.2 1.5 multiply_reduce_fusion.1
  684.7 105.2 %psum.56 = f32[128]{0:T(128)S(1)} all-reduce(f32[128]{0:T(128)S(1)} %broadcast_multiply_fusion.1), channel_id=1, replica_groups=mesh['comp'=32,'feat'=16] {'comp','feat'}, use_global_device_ids=true, to_apply=%region_8.11 | all-reduce | flops 128 | bytes 1024 | tf_op jit(solution)/shard_map/psum | solution.py:49
  789.9 0.3 multiply_reduce_fusion
  790.2 1.6 gather_fusion.3
  791.7 3.1 fusion.8
  794.8 3.0 copy.15
  797.9 2.4 fusion
  800.3 1.3 copy.11
  801.6 0.0 reduce-scatter.5.cloned.1.call-update
  801.6 79.8 %reduce-scatter.5.cloned.1.call-done = f32[128,128]{1,0:T(8,128)} async-done(((f32[2048,128]{1,0:T(8,128)}), f32[128,128]{1,0:T(8,128)}) %reduce-scatter.5.cloned.1.call-update) | async-done | bytes 65552 | tf_op jit(solution)/shard_map/reduce_scatter | solution.py:64
  881.5 0.9 multiply_reduce_fusion.3
  882.4 105.3 %all-reduce = (f32[128]{0:T(128)S(1)}, f32[128]{0:T(128)S(1)}) all-reduce(f32[128]{0:T(128)S(1)} %multiply_reduce_fusion.3, f32[128]{0:T(128)S(1)} %broadcast_multiply_fusion), channel_id=1, replica_groups=mesh['comp'=32,'feat'=16] {'comp','feat'}, use_global_device_ids=true, to_apply=%region_11.14 | all-reduce | flops 256 | bytes 2048 | tf_op jit(solution)/shard_map/psum | solution.py:70
  987.7 1.1 multiply_add_fusion
  988.8 0.6 multiply_subtract_fusion.1
  (29 shorter events, 0.1 us)
Async XLA Ops:
  7.2 23.6 %copy-start = (bf16[1,1,24,128,128]{4,3,2,1,0:T(8,128)(2,1)S(1)}, bf16[1,1,24,128,128]{4,3,2,1,0:T(8,128)(2,1)}, u32[]{:S(2)}) copy-start(bf16[1,1,24,128,128]{4,3,2,1,0:T(8,128)(2,1)} %param.10) | copy-start | bytes 2359300
  7.2 243.4 %all-reduce.5.cloned.1.call-start = ((), (), s32[]{:S(2)}) async-start(), calls=%async_computation.2 | async-start | bytes 1835008 | tf_op jit(solution)/shard_map/psum | solution.py:46
  32.5 2.0 copy-start.7
  36.7 308.8 %reduce-scatter.3.cloned.1.call-start = ((), (), s32[]{:S(2)}) async-start(), calls=%async_computation.3 | async-start | bytes 1114112 | tf_op jit(solution)/shard_map/reduce_scatter | solution.py:64
  255.0 2.0 copy-start.8
  258.0 193.6 %copy-start.6 = (f32[128]{0:T(128)S(1)}, f32[128]{0:T(128)}, u32[]{:S(2)}) copy-start(f32[128]{0:T(128)} %param.15) | copy-start | bytes 1540
  258.0 193.6 %copy-start.3 = (f32[128,128]{1,0:T(8,128)S(1)}, f32[128,128]{1,0:T(8,128)}, u32[]{:S(2)}) copy-start(f32[128,128]{1,0:T(8,128)} %param.14) | copy-start | bytes 196612
  259.3 423.9 %all-reduce.7.cloned.1.call-start = ((), (), s32[]{:S(2)}) async-start(), calls=%async_computation.4 | async-start | bytes 1835008 | tf_op jit(solution)/shard_map/psum | solution.py:46
  473.9 209.3 %copy-start.1 = (f32[1792,128]{1,0:T(8,128)S(1)}, f32[1792,128]{1,0:T(8,128)}, u32[]{:S(2)}) copy-start(f32[1792,128]{1,0:T(8,128)} %all-reduce.5.cloned.1.call-done) | copy-start | bytes 2752516
  475.1 406.3 %reduce-scatter.5.cloned.1.call-start = ((), (), s32[]{:S(2)}) async-start(), calls=%async_computation.5 | async-start | bytes 1114112 | tf_op jit(solution)/shard_map/reduce_scatter | solution.py:64
  683.2 106.7 %copy-start.2 = (f32[1792,128]{1,0:T(8,128)S(1)}, f32[1792,128]{1,0:T(8,128)}, u32[]{:S(2)}) copy-start(f32[1792,128]{1,0:T(8,128)} %all-reduce.7.cloned.1.call-done) | copy-start | bytes 2752516
  801.6 187.2 %copy-start.4 = (f32[128,128]{1,0:T(8,128)S(1)}, f32[128,128]{1,0:T(8,128)}, u32[]{:S(2)}) copy-start(f32[128,128]{1,0:T(8,128)} %reduce-scatter.3.cloned.1.call-done) | copy-start | bytes 196612
  881.4 107.4 %copy-start.5 = (f32[128,128]{1,0:T(8,128)S(1)}, f32[128,128]{1,0:T(8,128)}, u32[]{:S(2)}) copy-start(f32[128,128]{1,0:T(8,128)} %reduce-scatter.5.cloned.1.call-done) | copy-start | bytes 196612
Sparse Core Ops, SparseCore 0:
  36.8 213.6 all-reduce.4
  259.5 85.9 reduce-scatter.2
  475.3 207.9 all-reduce.6
  801.7 79.6 reduce-scatter.4
where the time goes:
time: 997 us; the launch traced here: 996 us
  waiting for transfers between devices  588 us (59%)
  blocking collectives  352 us (35%)
  local copies, waits for them, and re-layouts  17.6 us (2%)
  between operations  14.6 us (1%)
  matrix products  13.9 us (1%)
  other arithmetic  10.2 us (1%)
    psum x2, waiting for transfers between devices, reduce_grad(): return lax.psum(partial_contribution, 'comp')  422 us
    psum x2, blocking collectives, grad_total(): lax.psum(first_comp * jnp.sum(gradient * gradient, axis=0), ('comp', 'fea...  210 us
    reduce_scatter x2, waiting for transfers between devices, shards(): lax.psum_scatter(forward_summed.reshape(RB_DEV * block_edge, responses),...  166 us
    psum x1, blocking collectives, shards(): lax.psum((image_weight * jnp.sum(image_rows * image_rows, axis=0), first_...  105 us
    all_gather x2, blocking collectives, slab_of(): lax.all_gather(current.astype(jnp.bfloat16), 'feat', axis=0, tiled=True)  36 us
  transfers between devices with their start and end apart: 4, of which 4 were waited for; matrix products, arithmetic and copies ran while one was open for 0% of the time, Pallas kernels for 0%

commit v1 on v0

v1 whole, which is shorter than its diff:
```python
import jax
import jax.numpy as jnp
from jax import lax
from jax.sharding import PartitionSpec as P

RB_DEV = 16
CB_DEV = 14
ITERS = 2


def reduce_over(partial, axis, parts):
    rows = partial.shape[0] // parts
    pieces = partial.reshape(parts, rows, *partial.shape[1:])
    return lax.all_to_all(pieces, axis, 0, 0, tiled=True).sum(0)


def total_over_mesh(stacked, n_comp, n_feat):
    spread = jnp.broadcast_to(stacked[None], (n_feat,) + stacked.shape)
    by_feat = lax.all_to_all(spread, "feat", 0, 0, tiled=True).sum(0)
    spread = jnp.broadcast_to(by_feat[None], (n_comp,) + stacked.shape)
    return lax.all_to_all(spread, "comp", 0, 0, tiled=True).sum(0)


def shards(block_values, block_rows, block_cols, block_counts, right_side, ridge, n_comp, n_feat):
    values = block_values[0, 0]
    slot_rows = block_rows[0, 0]
    slot_cols = block_cols[0, 0]
    count_of_slots = block_counts[0, 0]
    responses = right_side.shape[1]
    total_slot_number = values.shape[0]
    block_edge = values.shape[1]
    feat_rows = CB_DEV * block_edge
    own_rows = feat_rows // n_comp
    comp_index = lax.axis_index("comp")
    slot_live = (jnp.arange(total_slot_number) < count_of_slots).astype(jnp.float32)
    row_lookup_table = (jnp.arange(RB_DEV)[:, None] == slot_rows[None, :]).astype(
        jnp.float32
    ) * slot_live[None, :]
    col_table = (jnp.arange(CB_DEV)[:, None] == slot_cols[None, :]).astype(jnp.float32) * slot_live[
        None, :
    ]

    def backward(low_slab):
        row_slabs = low_slab.reshape(RB_DEV, block_edge, responses)
        selected = jnp.take(row_slabs, slot_rows, axis=0)
        block_products = jnp.einsum(
            "sij,sik->sjk", values, selected, preferred_element_type=jnp.float32
        )
        summed = jnp.einsum(
            "qs,sjk->qjk", col_table, block_products, precision=lax.Precision.HIGHEST
        )
        return summed.reshape(feat_rows, responses)

    def forward(direction):
        col_panels = direction.astype(jnp.bfloat16).reshape(CB_DEV, block_edge, responses)
        forward_selected = jnp.take(col_panels, slot_cols, axis=0)
        forward_block_products = jnp.einsum(
            "sij,sjk->sik", values, forward_selected, preferred_element_type=jnp.float32
        )
        forward_summed = jnp.einsum(
            "rs,sik->rik", row_lookup_table, forward_block_products, precision=lax.Precision.HIGHEST
        )
        return reduce_over(forward_summed.reshape(RB_DEV * block_edge, responses), "feat", n_feat)

    def slab_of(current):
        return lax.all_gather(current.astype(jnp.bfloat16), "feat", axis=0, tiled=True)

    def gradient_rows(current):
        return reduce_over(backward(slab_of(current)), "comp", n_comp)

    def own_part(full):
        return lax.dynamic_slice_in_dim(full, comp_index * own_rows, own_rows, axis=0)

    def col_sq(x):
        return jnp.sum(x * x, axis=0)

    residual = right_side

    gradient_own = gradient_rows(residual)
    direction = lax.all_gather(gradient_own, "comp", axis=0, tiled=True)
    image_rows = forward(direction)
    energy, image_energy = total_over_mesh(
        jnp.stack([col_sq(gradient_own), col_sq(image_rows)]), n_comp, n_feat
    )
    step_size = energy / (image_energy + ridge * energy)
    solution = step_size * direction
    residual = residual - step_size * image_rows

    for _ in range(1, ITERS):
        gradient_own = gradient_rows(residual) - ridge * own_part(solution)
        gathered = lax.all_gather(
            jnp.concatenate([gradient_own, col_sq(gradient_own)[None]], axis=0),
            "comp",
            axis=0,
            tiled=False,
        )
        gradient = gathered[:, :own_rows].reshape(feat_rows, responses)
        comp_energy = jnp.sum(gathered[:, own_rows], axis=0)
        spread = jnp.broadcast_to(comp_energy[None, None], (n_feat, 1, responses))
        next_energy = lax.all_to_all(spread, "feat", 0, 0, tiled=True).sum(0)[0]
        direction = gradient + next_energy / energy * direction
        energy = next_energy
        image_rows = forward(direction)
        image_energy, direction_energy = total_over_mesh(
            jnp.stack([col_sq(image_rows), col_sq(own_part(direction))]), n_comp, n_feat
        )
        step_size = energy / (image_energy + ridge * direction_energy)
        solution = solution + step_size * direction
        residual = residual - step_size * image_rows
    return (solution, residual)


def solution(mesh):
    placed = (
        P("comp", "feat", None, None, None),
        P("comp", "feat", None),
        P("comp", "feat", None),
        P("comp", "feat"),
        P(("comp", "feat"), None),
        P(),
    )
    n_comp = mesh.shape["comp"]
    n_feat = mesh.shape["feat"]

    def body(*args):
        return shards(*args, n_comp=n_comp, n_feat=n_feat)

    return jax.shard_map(
        body,
        mesh=mesh,
        in_specs=placed,
        out_specs=(P("feat", None), P(("comp", "feat"), None)),
        check_vma=False,
    )
```

time: 997 us -> 378 us (0.38)
  waiting for transfers between devices: 588 us -> 135 us
  blocking collectives: 352 us -> 157 us
  starting transfers between devices: 0.16 us -> 43.7 us
  between operations: 14.6 us -> 1.55 us
    psum x2 -> x0, waiting for transfers between devices: 422 us -> none  [reduce_grad(): return lax.psum(partial_contribution, 'comp')]
    psum x3 -> x0, blocking collectives: 316 us -> none  [the longest x2 210 us: grad_total(): lax.psum(first_comp * jnp.sum(gradient * gradient, axis=0), ('comp', 'fea...]
    reduce_scatter x2 -> x0, waiting for transfers between devices: 166 us -> none  [shards(): lax.psum_scatter(forward_summed.reshape(RB_DEV * block_edge, responses),...]
    all_to_all x0 -> x5, waiting for transfers between devices: none -> 135 us  [the longest x4 130 us: reduce_over(): return lax.all_to_all(pieces, axis, 0, 0, tiled=True).sum(0)]
    all_gather x0 -> x2, blocking collectives: none -> 60.3 us  [the longest x1 30.6 us: shards(): lax.all_gather(jnp.concatenate([gradient_own, col_sq(gradient_own)[None]]...]
    all_to_all x0 -> x4, blocking collectives: none -> 60.2 us  [the longest x2 39.4 us: total_over_mesh(): return lax.all_to_all(spread, 'comp', 0, 0, tiled=True).sum(0)]
    all_to_all x0 -> x5, starting transfers between devices: none -> 43.7 us  [the longest x4 39.6 us: reduce_over(): return lax.all_to_all(pieces, axis, 0, 0, tiled=True).sum(0)]
  transfers between devices with their start and end apart: 4 -> 5, of which waited for: 4 -> 5; matrix products, arithmetic and copies ran while one was open for 0% -> 1% of each run, Pallas kernels for 0% -> 0%
where the time goes in v1:
time: 378 us; the launch traced here: 377 us
  blocking collectives  157 us (42%)
  waiting for transfers between devices  135 us (36%)
  starting transfers between devices  43.7 us (12%)
  local copies, waits for them, and re-layouts  17.3 us (5%)
  matrix products  11.4 us (3%)
  other arithmetic  10.5 us (3%)
    all_to_all x4, waiting for transfers between devices, reduce_over(): return lax.all_to_all(pieces, axis, 0, 0, tiled=True).sum(0)  130 us
    all_to_all x4, starting transfers between devices, reduce_over(): return lax.all_to_all(pieces, axis, 0, 0, tiled=True).sum(0)  39.6 us
    all_to_all x2, blocking collectives, total_over_mesh(): return lax.all_to_all(spread, 'comp', 0, 0, tiled=True).sum(0)  39.4 us
    all_gather x2, blocking collectives, slab_of(): lax.all_gather(current.astype(jnp.bfloat16), 'feat', axis=0, tiled=True)  36.6 us
    all_gather x1, blocking collectives, shards(): lax.all_gather(jnp.concatenate([gradient_own, col_sq(gradient_own)[None]]...  30.6 us
    all_gather x1, blocking collectives, shards(): direction = lax.all_gather(gradient_own, 'comp', axis=0, tiled=True)  29.7 us
    all_to_all x2, blocking collectives, total_over_mesh(): by_feat = lax.all_to_all(spread, 'feat', 0, 0, tiled=True).sum(0)  20.8 us
  transfers between devices with their start and end apart: 5, of which 5 were waited for; matrix products, arithmetic and copies ran while one was open for 1% of the time, Pallas kernels for 0%

profile of v1, /device:TPU:1, one launch (start us, length us, event | category | flops | bytes accessed | tf_op | source)
XLA Modules:
  0.0 376.8 jit_solution(10062302333413157449)
XLA Ops:
  0.6 0.7 compare_and_fusion.1
  1.4 0.7 compare_select_fusion.1
  2.7 0.8 convert_element_type.22
  3.6 20.0 %all_gather.15 = bf16[2048,128]{1,0:T(8,128)(2,1)S(1)} all-gather(bf16[128,128]{1,0:T(8,128)(2,1)S(1)} %convert_element_type.22), channel_id=1, replica_groups=mesh['comp'=32,'feat'=16] {'feat'}, dimensions={0}, use_global_device_ids=true | all-gather | bytes 557056 | tf_op jit(solution)/shard_map/all_gather | solution.py:66
  23.5 0.7 gather_fusion
  24.2 1.7 convolution_bitcast_fusion.3
  25.9 2.0 copy.43
  27.9 1.0 fusion.25
  28.9 1.2 copy.44
  30.1 21.0 %all-to-all-start = ((f32[32,56,128]{2,1,0:T(8,128)}), f32[32,56,128]{2,1,0:T(8,128)S(1)}, u32[]{:S(2)}, u32[]{:S(2)}) async-start(f32[32,56,128]{2,1,0:T(8,128)} %bitcast.7), calls=%async_computation | async-start | bytes 1835008 | tf_op jit(solution)/shard_map/all_to_all | solution.py:14
  51.2 50.2 %all-to-all-done = f32[32,56,128]{2,1,0:T(8,128)S(1)} async-done(((f32[32,56,128]{2,1,0:T(8,128)}), f32[32,56,128]{2,1,0:T(8,128)S(1)}, u32[]{:S(2)}, u32[]{:S(2)}) %all-to-all-start) | async-done | bytes 917536 | tf_op jit(solution)/shard_map/all_to_all | solution.py:14
  101.4 29.7 %all_gather.16 = f32[1792,128]{1,0:T(8,128)S(1)} all-gather(f32[56,128]{1,0:T(8,128)S(1)} %reduce_sum.137), channel_id=1, replica_groups=mesh['comp'=32,'feat'=16] {'comp'}, dimensions={0}, use_global_device_ids=true | all-gather | bytes 946176 | tf_op jit(solution)/shard_map/all_gather | solution.py:80
  131.2 0.7 gather_fusion.1
  131.9 2.0 convolution_bitcast_fusion.2
  133.9 2.0 copy.46
  135.9 1.0 fusion.19
  136.9 1.3 copy.47
  138.2 4.8 %all-to-all-start.1 = ((f32[16,128,128]{2,1,0:T(8,128)}), f32[16,128,128]{2,1,0:T(8,128)S(1)}, u32[]{:S(2)}, u32[]{:S(2)}) async-start(f32[16,128,128]{2,1,0:T(8,128)} %copy.47), calls=%async_computation.1 | async-start | bytes 2097152 | tf_op jit(solution)/shard_map/all_to_all | solution.py:14
  143.1 16.0 %all-to-all-done.1 = f32[16,128,128]{2,1,0:T(8,128)S(1)} async-done(((f32[16,128,128]{2,1,0:T(8,128)}), f32[16,128,128]{2,1,0:T(8,128)S(1)}, u32[]{:S(2)}, u32[]{:S(2)}) %all-to-all-start.1) | async-done | bytes 1048608 | tf_op jit(solution)/shard_map/all_to_all | solution.py:14
  159.2 10.6 %all_to_all.45 = f32[16,2,128]{2,1,0:T(2,128)S(1)} all-to-all(f32[16,2,128]{2,1,0:T(2,128)S(1)} %broadcast_in_dim.30), channel_id=1, replica_groups=mesh['comp'=32,'feat'=16] {'feat'}, dimensions={0} | all-to-all | bytes 32768 | tf_op jit(solution)/shard_map/all_to_all | solution.py:19
  169.9 19.7 %all_to_all.46 = f32[32,2,128]{2,1,0:T(2,128)S(1)} all-to-all(f32[32,2,128]{2,1,0:T(2,128)S(1)} %broadcast_in_dim.31), channel_id=1, replica_groups=mesh['comp'=32,'feat'=16] {'comp'}, dimensions={0} | all-to-all | bytes 65536 | tf_op jit(solution)/shard_map/all_to_all | solution.py:21
  189.6 16.7 %all_gather.17 = bf16[2048,128]{1,0:T(8,128)(2,1)S(1)} all-gather(bf16[128,128]{1,0:T(8,128)(2,1)S(1)} %fusion.16), channel_id=1, replica_groups=mesh['comp'=32,'feat'=16] {'feat'}, dimensions={0}, use_global_device_ids=true | all-gather | bytes 557056 | tf_op jit(solution)/shard_map/all_gather | solution.py:66
  206.3 0.7 gather_fusion.2
  207.0 1.7 convolution_bitcast_fusion.1
  208.7 2.0 copy.51
  210.6 1.0 fusion.23
  211.7 1.2 copy.52
  212.9 10.1 %all-to-all-start.4 = ((f32[32,56,128]{2,1,0:T(8,128)}), f32[32,56,128]{2,1,0:T(8,128)S(1)}, u32[]{:S(2)}, u32[]{:S(2)}) async-start(f32[32,56,128]{2,1,0:T(8,128)} %bitcast.17), calls=%async_computation.4 | async-start | bytes 1835008 | tf_op jit(solution)/shard_map/all_to_all | solution.py:14
  223.0 1.0 broadcast_multiply_fusion
  224.0 49.3 %all-to-all-done.4 = f32[32,56,128]{2,1,0:T(8,128)S(1)} async-done(((f32[32,56,128]{2,1,0:T(8,128)}), f32[32,56,128]{2,1,0:T(8,128)S(1)}, u32[]{:S(2)}, u32[]{:S(2)}) %all-to-all-start.4) | async-done | bytes 917536 | tf_op jit(solution)/shard_map/all_to_all | solution.py:14
  273.3 0.8 multiply_reduce_fusion.3
  274.1 30.6 %all-gather.1 = f32[32,57,128]{2,1,0:T(8,128)S(1)} all-gather(f32[1,57,128]{2,1,0:T(8,128)S(1)} %maximum_bitcast_fusion), channel_id=2, replica_groups=mesh['comp'=32,'feat'=16] {'comp'}, dimensions={0}, use_global_device_ids=true | all-gather | bytes 963072 | tf_op jit(solution)/shard_map/all_gather | solution.py:91
  305.4 4.0 %all-to-all-start.5 = ((f32[16,1,128]{2,1,0:T(1,128)}), f32[16,1,128]{2,1,0:T(1,128)S(1)}, u32[]{:S(2)}, u32[]{:S(2)}) async-start(f32[16,1,128]{2,1,0:T(1,128)} %broadcast_in_dim.33), calls=%async_computation.5 | async-start | bytes 16384 | tf_op jit(solution)/shard_map/all_to_all | solution.py:100
  309.4 1.0 slice.17
  310.4 5.3 %all-to-all-done.5 = f32[16,1,128]{2,1,0:T(1,128)S(1)} async-done(((f32[16,1,128]{2,1,0:T(1,128)}), f32[16,1,128]{2,1,0:T(1,128)S(1)}, u32[]{:S(2)}, u32[]{:S(2)}) %all-to-all-start.5) | async-done | bytes 8224 | tf_op jit(solution)/shard_map/all_to_all | solution.py:100
  315.8 2.2 fusion.53
  318.0 0.7 gather_fusion.3
  318.7 2.0 convolution_bitcast_fusion
  320.7 2.0 copy.55
  322.7 1.0 fusion.17
  323.7 1.3 copy.56
  325.0 3.7 all-to-all-start.6
  328.7 0.8 multiply_reduce_fusion.2
  329.4 14.4 %all-to-all-done.6 = f32[16,128,128]{2,1,0:T(8,128)S(1)} async-done(((f32[16,128,128]{2,1,0:T(8,128)}), f32[16,128,128]{2,1,0:T(8,128)S(1)}, u32[]{:S(2)}, u32[]{:S(2)}) %all-to-all-start.6) | async-done | bytes 1048608 | tf_op jit(solution)/shard_map/all_to_all | solution.py:14
  344.0 10.1 %all_to_all.47 = f32[16,2,128]{2,1,0:T(2,128)S(1)} all-to-all(f32[16,2,128]{2,1,0:T(2,128)S(1)} %broadcast_in_dim.34), channel_id=1, replica_groups=mesh['comp'=32,'feat'=16] {'feat'}, dimensions={0} | all-to-all | bytes 32768 | tf_op jit(solution)/shard_map/all_to_all | solution.py:19
  354.2 19.7 %all_to_all.48 = f32[32,2,128]{2,1,0:T(2,128)S(1)} all-to-all(f32[32,2,128]{2,1,0:T(2,128)S(1)} %broadcast_in_dim.35), channel_id=1, replica_groups=mesh['comp'=32,'feat'=16] {'comp'}, dimensions={0} | all-to-all | bytes 65536 | tf_op jit(solution)/shard_map/all_to_all | solution.py:21
  374.0 2.2 multiply_add_fusion
  376.2 0.6 multiply_subtract_fusion
  (41 shorter events, 1.4 us)
Async XLA Ops:
  0.6 23.6 %copy-start = (bf16[1,1,24,128,128]{4,3,2,1,0:T(8,128)(2,1)S(1)}, bf16[1,1,24,128,128]{4,3,2,1,0:T(8,128)(2,1)}, u32[]{:S(2)}) copy-start(bf16[1,1,24,128,128]{4,3,2,1,0:T(8,128)(2,1)} %param.10) | copy-start | bytes 2359300
  25.9 2.0 copy-start.3
  30.1 71.2 %all-to-all-start = ((f32[32,56,128]{2,1,0:T(8,128)}), f32[32,56,128]{2,1,0:T(8,128)S(1)}, u32[]{:S(2)}, u32[]{:S(2)}) async-start(f32[32,56,128]{2,1,0:T(8,128)} %bitcast.7), calls=%async_computation | async-start | bytes 1835008 | tf_op jit(solution)/shard_map/all_to_all | solution.py:14
  133.9 2.0 copy-start.4
  138.2 51.4 %copy-start.2 = (f32[128]{0:T(128)S(1)}, f32[128]{0:T(128)}, u32[]{:S(2)}) copy-start(f32[128]{0:T(128)} %param.15) | copy-start | bytes 1540
  138.2 51.4 %copy-start.1 = (f32[128,128]{1,0:T(8,128)S(1)}, f32[128,128]{1,0:T(8,128)}, u32[]{:S(2)}) copy-start(f32[128,128]{1,0:T(8,128)} %param.14) | copy-start | bytes 196612
  138.2 20.9 %all-to-all-start.1 = ((f32[16,128,128]{2,1,0:T(8,128)}), f32[16,128,128]{2,1,0:T(8,128)S(1)}, u32[]{:S(2)}, u32[]{:S(2)}) async-start(f32[16,128,128]{2,1,0:T(8,128)} %copy.47), calls=%async_computation.1 | async-start | bytes 2097152 | tf_op jit(solution)/shard_map/all_to_all | solution.py:14
  212.9 60.4 %all-to-all-start.4 = ((f32[32,56,128]{2,1,0:T(8,128)}), f32[32,56,128]{2,1,0:T(8,128)S(1)}, u32[]{:S(2)}, u32[]{:S(2)}) async-start(f32[32,56,128]{2,1,0:T(8,128)} %bitcast.17), calls=%async_computation.4 | async-start | bytes 1835008 | tf_op jit(solution)/shard_map/all_to_all | solution.py:14
  305.4 10.4 %all-to-all-start.5 = ((f32[16,1,128]{2,1,0:T(1,128)}), f32[16,1,128]{2,1,0:T(1,128)S(1)}, u32[]{:S(2)}, u32[]{:S(2)}) async-start(f32[16,1,128]{2,1,0:T(1,128)} %broadcast_in_dim.33), calls=%async_computation.5 | async-start | bytes 16384 | tf_op jit(solution)/shard_map/all_to_all | solution.py:100
  325.0 18.9 %all-to-all-start.6 = ((f32[16,128,128]{2,1,0:T(8,128)}), f32[16,128,128]{2,1,0:T(8,128)S(1)}, u32[]{:S(2)}, u32[]{:S(2)}) async-start(f32[16,128,128]{2,1,0:T(8,128)} %copy.56), calls=%async_computation.6 | async-start | bytes 2097152 | tf_op jit(solution)/shard_map/all_to_all | solution.py:14

commit v2 on v1

--- a/solution.py
+++ b/solution.py
@@ -65,11 +65,29 @@
     def slab_of(current):
         return lax.all_gather(current.astype(jnp.bfloat16), "feat", axis=0, tiled=True)
 
+    core = comp_index % 2
+    half_rows = feat_rows // 2
+    part_rows = half_rows // n_comp
+    siblings = [(i, i ^ 1) for i in range(n_comp)]
+
     def gradient_rows(current):
-        return reduce_over(backward(slab_of(current)), "comp", n_comp)
+        partial = backward(slab_of(current))
+        kept = lax.dynamic_slice_in_dim(partial, core * half_rows, half_rows, axis=0)
+        sent = lax.dynamic_slice_in_dim(partial, (1 - core) * half_rows, half_rows, axis=0)
+        chip_sum = kept + lax.ppermute(sent, "comp", siblings)
+        pieces = chip_sum.reshape(n_comp, part_rows, chip_sum.shape[1])
+        landed = lax.all_to_all(pieces, "comp", 0, 0, tiled=True)
+        halves = landed.reshape(n_comp // 2, 2, part_rows, chip_sum.shape[1]).sum(0)
+        return halves.reshape(own_rows, chip_sum.shape[1])
+
+    def whole_of(gathered):
+        split = gathered.reshape(n_comp, 2, part_rows, gathered.shape[-1])
+        return split.transpose(1, 0, 2, 3).reshape(feat_rows, gathered.shape[-1])
 
     def own_part(full):
-        return lax.dynamic_slice_in_dim(full, comp_index * own_rows, own_rows, axis=0)
+        split = full.reshape(2, n_comp, part_rows, full.shape[-1])
+        mine = lax.dynamic_slice_in_dim(split, comp_index, 1, axis=1)
+        return mine.reshape(own_rows, full.shape[-1])
 
     def col_sq(x):
         return jnp.sum(x * x, axis=0)
@@ -77,7 +95,7 @@
     residual = right_side
 
     gradient_own = gradient_rows(residual)
-    direction = lax.all_gather(gradient_own, "comp", axis=0, tiled=True)
+    direction = whole_of(lax.all_gather(gradient_own, "comp", axis=0, tiled=False))
     image_rows = forward(direction)
     energy, image_energy = total_over_mesh(
         jnp.stack([col_sq(gradient_own), col_sq(image_rows)]), n_comp, n_feat
@@ -94,7 +112,7 @@
             axis=0,
             tiled=False,
         )
-        gradient = gathered[:, :own_rows].reshape(feat_rows, responses)
+        gradient = whole_of(gathered[:, :own_rows])
         comp_energy = jnp.sum(gathered[:, own_rows], axis=0)
         spread = jnp.broadcast_to(comp_energy[None, None], (n_feat, 1, responses))
         next_energy = lax.all_to_all(spread, "feat", 0, 0, tiled=True).sum(0)[0]

time: 378 us -> 366 us (0.968)
  waiting for transfers between devices: 135 us -> 113 us
  blocking collectives: 157 us -> 137 us
  starting transfers between devices: 43.7 us -> 57.1 us
  local copies, waits for them, and re-layouts: 17.3 us -> 27.9 us
  matrix products: 11.4 us -> 17.1 us
    all_to_all x4 -> x2, waiting for transfers between devices: 130 us -> 30.2 us  [reduce_over(): return lax.all_to_all(pieces, axis, 0, 0, tiled=True).sum(0)]
    all_to_all x0 -> x3, waiting for transfers between devices: none -> 76.1 us  [the longest x2 66 us: gradient_rows(): landed = lax.all_to_all(pieces, 'comp', 0, 0, tiled=True)]
    all_to_all x4 -> x2, starting transfers between devices: 39.6 us -> 9.13 us  [reduce_over(): return lax.all_to_all(pieces, axis, 0, 0, tiled=True).sum(0)]
    all_to_all x0 -> x3, starting transfers between devices: none -> 25.5 us  [the longest x2 17.4 us: gradient_rows(): landed = lax.all_to_all(pieces, 'comp', 0, 0, tiled=True)]
    all_to_all x2 -> x1, blocking collectives: 39.4 us -> 19.7 us  [total_over_mesh(): return lax.all_to_all(spread, 'comp', 0, 0, tiled=True).sum(0)]
    ppermute x0 -> x2, starting transfers between devices: none -> 18.5 us  [gradient_rows(): chip_sum = kept + lax.ppermute(sent, 'comp', siblings)]
    reshape x0 -> x7, local copies, waits for them, and re-layouts: none -> 4.71 us  [the longest x4 3.05 us: whole_of(): return split.transpose(1, 0, 2, 3).reshape(feat_rows, gathered.shape[-1])]
  transfers between devices with their start and end apart: 5 -> 8, of which waited for: 5 -> 8; matrix products, arithmetic and copies ran while one was open for 1% -> 2% of each run, Pallas kernels for 0% -> 0%
where the time goes in v2:
time: 366 us; the launch traced here: 365 us
  blocking collectives  137 us (37%)
  waiting for transfers between devices  113 us (31%)
  starting transfers between devices  57.1 us (16%)
  local copies, waits for them, and re-layouts  27.9 us (8%)
  matrix products  17.1 us (5%)
  other arithmetic  10.9 us (3%)
    all_to_all x2, waiting for transfers between devices, gradient_rows(): landed = lax.all_to_all(pieces, 'comp', 0, 0, tiled=True)  66 us
    all_gather x2, blocking collectives, slab_of(): lax.all_gather(current.astype(jnp.bfloat16), 'feat', axis=0, tiled=True)  36.6 us
    all_gather x1, blocking collectives, shards(): lax.all_gather(jnp.concatenate([gradient_own, col_sq(gradient_own)[None]]...  30.4 us
    all_to_all x2, waiting for transfers between devices, reduce_over(): return lax.all_to_all(pieces, axis, 0, 0, tiled=True).sum(0)  30.2 us
    all_gather x1, blocking collectives, shards(): lax.all_gather(gradient_own, 'comp', axis=0, tiled=False)  29.8 us
    all_to_all x2, blocking collectives, total_over_mesh(): by_feat = lax.all_to_all(spread, 'feat', 0, 0, tiled=True).sum(0)  20.7 us
    all_to_all x1, blocking collectives, total_over_mesh(): return lax.all_to_all(spread, 'comp', 0, 0, tiled=True).sum(0)  19.7 us
    ppermute x2, starting transfers between devices, gradient_rows(): chip_sum = kept + lax.ppermute(sent, 'comp', siblings)  18.5 us
  transfers between devices with their start and end apart: 8, of which 8 were waited for; matrix products, arithmetic and copies ran while one was open for 2% of the time, Pallas kernels for 0%

profile of v2, /device:TPU:1, one launch (start us, length us, event | category | flops | bytes accessed | tf_op | source)
XLA Modules:
  0.0 364.6 jit_solution(9498467656124753706)
XLA Ops:
  3.6 20.0 %all_gather.15 = bf16[2048,128]{1,0:T(8,128)(2,1)S(1)} all-gather(bf16[128,128]{1,0:T(8,128)(2,1)S(1)} %convert_element_type.24), channel_id=1, replica_groups=mesh['comp'=32,'feat'=16] {'feat'}, dimensions={0}, use_global_device_ids=true | all-gather | bytes 557056 | tf_op jit(solution)/shard_map/all_gather | solution.py:66
  24.3 1.7 convolution_bitcast_fusion.3
  25.9 2.0 copy.91
  27.9 1.0 fusion.30
  29.3 9.8 %collective-permute-start = (f32[896,128]{1,0:T(8,128)S(1)}, f32[896,128]{1,0:T(8,128)S(1)}, u32[]{:S(2)}, u32[]{:S(2)}) collective-permute-start(f32[896,128]{1,0:T(8,128)S(1)} %constant_dynamic-slice_fusion.1), channel_id=1, source_target_pairs={{0,16},{16,0},{32,48},{48,32},{64,80},{80,64},{96,112},{112,96},{1... | collective-permute-start | bytes 1376264 | tf_op jit(solution)/shard_map/ppermute | solution.py:77
  39.2 1.4 collective-permute-done
  41.5 13.5 %all-to-all-start = ((f32[32,28,128]{2,1,0:T(8,128)}), f32[32,28,128]{2,1,0:T(8,128)S(1)}, u32[]{:S(2)}, u32[]{:S(2)}) async-start(f32[32,28,128]{2,1,0:T(8,128)} %reshape.111), calls=%async_computation | async-start | bytes 1048576 | tf_op jit(solution)/shard_map/all_to_all | solution.py:79
  55.0 33.5 %all-to-all-done = f32[32,28,128]{2,1,0:T(8,128)S(1)} async-done(((f32[32,28,128]{2,1,0:T(8,128)}), f32[32,28,128]{2,1,0:T(8,128)S(1)}, u32[]{:S(2)}, u32[]{:S(2)}) %all-to-all-start) | async-done | bytes 458784 | tf_op jit(solution)/shard_map/all_to_all | solution.py:79
  88.5 29.8 %all_gather.16 = f32[32,56,128]{2,1,0:T(8,128)S(1)} all-gather(f32[1,56,128]{2,1,0:T(8,128)S(1)} %all_gather_reshape.3), channel_id=1, replica_groups=mesh['comp'=32,'feat'=16] {'comp'}, dimensions={0}, use_global_device_ids=true | all-gather | bytes 946176 | tf_op jit(solution)/shard_map/all_gather | solution.py:98
  120.1 1.6 gather_fusion.1
  121.7 3.1 convolution_bitcast_fusion.2
  124.8 3.0 copy.96
  127.9 2.4 fusion.24
  130.3 1.3 copy.97
  131.6 4.8 %all-to-all-start.1 = ((f32[16,128,128]{2,1,0:T(8,128)}), f32[16,128,128]{2,1,0:T(8,128)S(1)}, u32[]{:S(2)}, u32[]{:S(2)}) async-start(f32[16,128,128]{2,1,0:T(8,128)} %copy.97), calls=%async_computation.1 | async-start | bytes 2097152 | tf_op jit(solution)/shard_map/all_to_all | solution.py:14
  136.4 16.1 %all-to-all-done.1 = f32[16,128,128]{2,1,0:T(8,128)S(1)} async-done(((f32[16,128,128]{2,1,0:T(8,128)}), f32[16,128,128]{2,1,0:T(8,128)S(1)}, u32[]{:S(2)}, u32[]{:S(2)}) %all-to-all-start.1) | async-done | bytes 1048608 | tf_op jit(solution)/shard_map/all_to_all | solution.py:14
  152.6 10.6 %all_to_all.45 = f32[16,2,128]{2,1,0:T(2,128)S(1)} all-to-all(f32[16,2,128]{2,1,0:T(2,128)S(1)} %broadcast_in_dim.30), channel_id=1, replica_groups=mesh['comp'=32,'feat'=16] {'feat'}, dimensions={0} | all-to-all | bytes 32768 | tf_op jit(solution)/shard_map/all_to_all | solution.py:19
  163.3 19.7 %all_to_all.46 = f32[32,2,128]{2,1,0:T(2,128)S(1)} all-to-all(f32[32,2,128]{2,1,0:T(2,128)S(1)} %broadcast_in_dim.31), channel_id=1, replica_groups=mesh['comp'=32,'feat'=16] {'comp'}, dimensions={0} | all-to-all | bytes 65536 | tf_op jit(solution)/shard_map/all_to_all | solution.py:21
  183.6 16.7 %all_gather.17 = bf16[2048,128]{1,0:T(8,128)(2,1)S(1)} all-gather(bf16[128,128]{1,0:T(8,128)(2,1)S(1)} %fusion.21), channel_id=1, replica_groups=mesh['comp'=32,'feat'=16] {'feat'}, dimensions={0}, use_global_device_ids=true | all-gather | bytes 557056 | tf_op jit(solution)/shard_map/all_gather | solution.py:66
  201.1 1.7 convolution_bitcast_fusion.1
  202.8 2.0 copy.102
  204.7 1.7 fusion.28
  206.7 8.6 %collective-permute-start.1 = (f32[896,128]{1,0:T(8,128)S(1)}, f32[896,128]{1,0:T(8,128)S(1)}, u32[]{:S(2)}, u32[]{:S(2)}) collective-permute-start(f32[896,128]{1,0:T(8,128)S(1)} %constant_dynamic-slice_fusion), channel_id=1, source_target_pairs={{0,16},{16,0},{32,48},{48,32},{64,80},{80,64},{96,112},{112,96},{1... | collective-permute-start | bytes 1376264 | tf_op jit(solution)/shard_map/ppermute | solution.py:77
  215.4 1.2 collective-permute-done.1
  217.5 3.9 %all-to-all-start.4 = ((f32[32,28,128]{2,1,0:T(8,128)}), f32[32,28,128]{2,1,0:T(8,128)S(1)}, u32[]{:S(2)}, u32[]{:S(2)}) async-start(f32[32,28,128]{2,1,0:T(8,128)} %reshape.118), calls=%async_computation.4 | async-start | bytes 1048576 | tf_op jit(solution)/shard_map/all_to_all | solution.py:79
  221.4 1.0 dynamic-slice_multiply_fusion
  222.4 32.5 %all-to-all-done.4 = f32[32,28,128]{2,1,0:T(8,128)S(1)} async-done(((f32[32,28,128]{2,1,0:T(8,128)}), f32[32,28,128]{2,1,0:T(8,128)S(1)}, u32[]{:S(2)}, u32[]{:S(2)}) %all-to-all-start.4) | async-done | bytes 458784 | tf_op jit(solution)/shard_map/all_to_all | solution.py:79
  255.1 30.4 %all-gather.1 = f32[32,57,128]{2,1,0:T(8,128)S(1)} all-gather(f32[1,57,128]{2,1,0:T(8,128)S(1)} %maximum_bitcast_fusion), channel_id=2, replica_groups=mesh['comp'=32,'feat'=16] {'comp'}, dimensions={0}, use_global_device_ids=true | all-gather | bytes 963072 | tf_op jit(solution)/shard_map/all_gather | solution.py:109
  286.2 4.0 %all-to-all-start.5 = ((f32[16,1,128]{2,1,0:T(1,128)}), f32[16,1,128]{2,1,0:T(1,128)S(1)}, u32[]{:S(2)}, u32[]{:S(2)}) async-start(f32[16,1,128]{2,1,0:T(1,128)} %broadcast_in_dim.33), calls=%async_computation.5 | async-start | bytes 16384 | tf_op jit(solution)/shard_map/all_to_all | solution.py:118
  290.5 0.9 copy-done.3
  292.0 1.0 reshape.124
  293.0 3.6 all-to-all-done.5
  296.6 1.6 add_convert_fusion
  298.2 1.6 gather_fusion.3
  299.7 3.1 convolution_bitcast_fusion
  302.9 3.0 copy.110
  305.9 2.4 fusion.22
  308.4 1.4 copy.111
  309.7 4.3 %all-to-all-start.6 = ((f32[16,128,128]{2,1,0:T(8,128)}), f32[16,128,128]{2,1,0:T(8,128)}, u32[]{:S(2)}, u32[]{:S(2)}) async-start(f32[16,128,128]{2,1,0:T(8,128)} %copy.111), calls=%async_computation.6 | async-start | bytes 2097152 | tf_op jit(solution)/shard_map/all_to_all | solution.py:14
  314.1 1.1 fusion.20
  315.2 14.1 %all-to-all-done.6 = f32[16,128,128]{2,1,0:T(8,128)} async-done(((f32[16,128,128]{2,1,0:T(8,128)}), f32[16,128,128]{2,1,0:T(8,128)}, u32[]{:S(2)}, u32[]{:S(2)}) %all-to-all-start.6) | async-done | bytes 1048608 | tf_op jit(solution)/shard_map/all_to_all | solution.py:14
  329.3 1.3 reduce_sum.148
  330.7 10.1 %all_to_all.47 = f32[16,2,128]{2,1,0:T(2,128)S(1)} all-to-all(f32[16,2,128]{2,1,0:T(2,128)S(1)} %broadcast_in_dim.34), channel_id=1, replica_groups=mesh['comp'=32,'feat'=16] {'feat'}, dimensions={0} | all-to-all | bytes 32768 | tf_op jit(solution)/shard_map/all_to_all | solution.py:19
  341.5 8.1 %all-to-all-start.8 = ((f32[32,2,128]{2,1,0:T(2,128)}), f32[32,2,128]{2,1,0:T(2,128)S(1)}, u32[]{:S(2)}, u32[]{:S(2)}) async-start(f32[32,2,128]{2,1,0:T(2,128)} %broadcast_in_dim.35), calls=%async_computation.8 | async-start | bytes 65536 | tf_op jit(solution)/shard_map/all_to_all | solution.py:21
  349.5 1.0 reshape.115
  350.5 1.0 reshape.125
  351.5 10.1 %all-to-all-done.8 = f32[32,2,128]{2,1,0:T(2,128)S(1)} async-done(((f32[32,2,128]{2,1,0:T(2,128)}), f32[32,2,128]{2,1,0:T(2,128)S(1)}, u32[]{:S(2)}, u32[]{:S(2)}) %all-to-all-start.8) | async-done | bytes 32800 | tf_op jit(solution)/shard_map/all_to_all | solution.py:21
  362.4 2.3 multiply_add_fusion
  (88 shorter events, 11.9 us)
Async XLA Ops:
  0.6 23.6 %copy-start = (bf16[1,1,24,128,128]{4,3,2,1,0:T(8,128)(2,1)S(1)}, bf16[1,1,24,128,128]{4,3,2,1,0:T(8,128)(2,1)}, u32[]{:S(2)}) copy-start(bf16[1,1,24,128,128]{4,3,2,1,0:T(8,128)(2,1)} %param.10) | copy-start | bytes 2359300
  1.4 24.5 %copy-start.15 = (pred[24]{0:T(512)(128)(4,1)}, pred[24]{0:T(512)(128)(4,1)S(1)}, u32[]{:S(2)}) copy-start(pred[24]{0:T(512)(128)(4,1)S(1)} %compare_and_fusion.1) | copy-start | bytes 76
  2.7 23.2 %copy-start.7 = (s32[1024]{0:T(1024)}, s32[1024]{0:T(1024)S(1)}, u32[]{:S(2)}) copy-start(s32[1024]{0:T(1024)S(1)} %pad_clamp_fusion.1) | copy-start | bytes 12292
  25.9 2.0 copy-start.10
  29.3 11.3 %collective-permute-start = (f32[896,128]{1,0:T(8,128)S(1)}, f32[896,128]{1,0:T(8,128)S(1)}, u32[]{:S(2)}, u32[]{:S(2)}) collective-permute-start(f32[896,128]{1,0:T(8,128)S(1)} %constant_dynamic-slice_fusion.1), channel_id=1, source_target_pairs={{0,16},{16,0},{32,48},{48,32},{64,80},{80,64},{96,112},{112,96},{1... | collective-permute-start | bytes 1376264 | tf_op jit(solution)/shard_map/ppermute | solution.py:77
  41.5 47.0 %all-to-all-start = ((f32[32,28,128]{2,1,0:T(8,128)}), f32[32,28,128]{2,1,0:T(8,128)S(1)}, u32[]{:S(2)}, u32[]{:S(2)}) async-start(f32[32,28,128]{2,1,0:T(8,128)} %reshape.111), calls=%async_computation | async-start | bytes 1048576 | tf_op jit(solution)/shard_map/all_to_all | solution.py:79
  55.0 66.7 %copy-start.13 = (pred[24]{0:T(512)(128)(4,1)}, pred[24]{0:T(512)(128)(4,1)S(1)}, u32[]{:S(2)}) copy-start(pred[24]{0:T(512)(128)(4,1)S(1)} %compare_and_fusion) | copy-start | bytes 76
  118.5 0.9 copy-start.2
  120.0 4.8 %copy-start.1 = (f32[14,128,128]{2,1,0:T(8,128)}, f32[14,128,128]{2,1,0:T(8,128)S(1)}, u32[]{:S(2)}) copy-start(f32[14,128,128]{2,1,0:T(8,128)S(1)} %reshape.114) | copy-start | bytes 2752516
  124.8 3.0 copy-start.11
  131.6 51.4 %copy-start.6 = (f32[128]{0:T(128)S(1)}, f32[128]{0:T(128)}, u32[]{:S(2)}) copy-start(f32[128]{0:T(128)} %param.15) | copy-start | bytes 1540
  131.6 52.0 %copy-start.5 = (f32[128,128]{1,0:T(8,128)S(1)}, f32[128,128]{1,0:T(8,128)}, u32[]{:S(2)}) copy-start(f32[128,128]{1,0:T(8,128)} %param.14) | copy-start | bytes 196612
  131.6 20.9 %all-to-all-start.1 = ((f32[16,128,128]{2,1,0:T(8,128)}), f32[16,128,128]{2,1,0:T(8,128)S(1)}, u32[]{:S(2)}, u32[]{:S(2)}) async-start(f32[16,128,128]{2,1,0:T(8,128)} %copy.97), calls=%async_computation.1 | async-start | bytes 2097152 | tf_op jit(solution)/shard_map/all_to_all | solution.py:14
  136.4 64.6 %copy-start.16 = (pred[24]{0:T(512)(128)(4,1)S(1)}, pred[24]{0:T(512)(128)(4,1)}, u32[]{:S(2)}) copy-start(pred[24]{0:T(512)(128)(4,1)} %copy-done.15) | copy-start | bytes 76
  183.0 0.6 copy-start.8
  206.7 9.9 %collective-permute-start.1 = (f32[896,128]{1,0:T(8,128)S(1)}, f32[896,128]{1,0:T(8,128)S(1)}, u32[]{:S(2)}, u32[]{:S(2)}) collective-permute-start(f32[896,128]{1,0:T(8,128)S(1)} %constant_dynamic-slice_fusion), channel_id=1, source_target_pairs={{0,16},{16,0},{32,48},{48,32},{64,80},{80,64},{96,112},{112,96},{1... | collective-permute-start | bytes 1376264 | tf_op jit(solution)/shard_map/ppermute | solution.py:77
  217.5 37.5 %all-to-all-start.4 = ((f32[32,28,128]{2,1,0:T(8,128)}), f32[32,28,128]{2,1,0:T(8,128)S(1)}, u32[]{:S(2)}, u32[]{:S(2)}) async-start(f32[32,28,128]{2,1,0:T(8,128)} %reshape.118), calls=%async_computation.4 | async-start | bytes 1048576 | tf_op jit(solution)/shard_map/all_to_all | solution.py:79
  286.2 10.4 %all-to-all-start.5 = ((f32[16,1,128]{2,1,0:T(1,128)}), f32[16,1,128]{2,1,0:T(1,128)S(1)}, u32[]{:S(2)}, u32[]{:S(2)}) async-start(f32[16,1,128]{2,1,0:T(1,128)} %broadcast_in_dim.33), calls=%async_computation.5 | async-start | bytes 16384 | tf_op jit(solution)/shard_map/all_to_all | solution.py:118
  290.5 0.9 copy-start.3
  291.4 5.2 %copy-start.9 = (f32[2,128]{1,0:T(2,128)S(1)}, f32[2,128]{1,0:T(2,128)}, u32[]{:S(2)}) copy-start(f32[2,128]{1,0:T(2,128)} %copy-done.8) | copy-start | bytes 3076
  296.6 3.2 copy-start.14
  302.9 3.0 copy-start.12
  309.7 19.6 %all-to-all-start.6 = ((f32[16,128,128]{2,1,0:T(8,128)}), f32[16,128,128]{2,1,0:T(8,128)}, u32[]{:S(2)}, u32[]{:S(2)}) async-start(f32[16,128,128]{2,1,0:T(8,128)} %copy.111), calls=%async_computation.6 | async-start | bytes 2097152 | tf_op jit(solution)/shard_map/all_to_all | solution.py:14
  341.5 20.2 %all-to-all-start.8 = ((f32[32,2,128]{2,1,0:T(2,128)}), f32[32,2,128]{2,1,0:T(2,128)S(1)}, u32[]{:S(2)}, u32[]{:S(2)}) async-start(f32[32,2,128]{2,1,0:T(2,128)} %broadcast_in_dim.35), calls=%async_computation.8 | async-start | bytes 65536 | tf_op jit(solution)/shard_map/all_to_all | solution.py:21
  350.5 11.8 %copy-start.4 = (f32[1792,128]{1,0:T(8,128)S(1)}, f32[1792,128]{1,0:T(8,128)}, u32[]{:S(2)}) copy-start(f32[1792,128]{1,0:T(8,128)} %reshape.115) | copy-start | bytes 2752516

commit v3 on v2

--- a/solution.py
+++ b/solution.py
@@ -1,11 +1,51 @@
+import functools
+
 import jax
 import jax.numpy as jnp
 from jax import lax
+from jax.experimental import pallas as pl
+from jax.experimental.pallas import tpu as pltpu
 from jax.sharding import PartitionSpec as P
 
 RB_DEV = 16
 CB_DEV = 14
 ITERS = 2
+
+
+def _block_kernel(transpose, count_ref, out_idx_ref, in_idx_ref, values_ref, x_ref, out_ref):
+    edge = values_ref.shape[1]
+    out_ref[...] = jnp.zeros_like(out_ref)
+
+    def body(s, carry):
+        @pl.when(s < count_ref[0])
+        def _():
+            src = pl.multiple_of(in_idx_ref[s] * edge, edge)
+            dst = pl.multiple_of(out_idx_ref[s] * edge, edge)
+            block = values_ref[s]
+            x = x_ref[pl.ds(src, edge), :]
+            if transpose:
+                prod = lax.dot_general(
+                    block, x, (((0,), (0,)), ((), ())), preferred_element_type=jnp.float32
+                )
+            else:
+                prod = jnp.dot(block, x, preferred_element_type=jnp.float32)
+            out_ref[pl.ds(dst, edge), :] += prod
+
+        return carry
+
+    lax.fori_loop(0, values_ref.shape[0], body, 0)
+
+
+def block_apply(values, count, out_idx, in_idx, x, out_blocks, transpose):
+    edge = values.shape[1]
+    smem = pl.BlockSpec(memory_space=pltpu.SMEM)
+    vmem = pl.BlockSpec(memory_space=pltpu.VMEM)
+    return pl.pallas_call(
+        functools.partial(_block_kernel, transpose),
+        out_shape=jax.ShapeDtypeStruct((out_blocks * edge, x.shape[1]), jnp.float32),
+        in_specs=[smem, smem, smem, vmem, vmem],
+        out_specs=vmem,
+    )(count.reshape(1), out_idx, in_idx, values, x)
 
 
 def reduce_over(partial, axis, parts):
@@ -27,40 +67,18 @@
     slot_cols = block_cols[0, 0]
     count_of_slots = block_counts[0, 0]
     responses = right_side.shape[1]
-    total_slot_number = values.shape[0]
     block_edge = values.shape[1]
     feat_rows = CB_DEV * block_edge
     own_rows = feat_rows // n_comp
     comp_index = lax.axis_index("comp")
-    slot_live = (jnp.arange(total_slot_number) < count_of_slots).astype(jnp.float32)
-    row_lookup_table = (jnp.arange(RB_DEV)[:, None] == slot_rows[None, :]).astype(
-        jnp.float32
-    ) * slot_live[None, :]
-    col_table = (jnp.arange(CB_DEV)[:, None] == slot_cols[None, :]).astype(jnp.float32) * slot_live[
-        None, :
-    ]
 
     def backward(low_slab):
-        row_slabs = low_slab.reshape(RB_DEV, block_edge, responses)
-        selected = jnp.take(row_slabs, slot_rows, axis=0)
-        block_products = jnp.einsum(
-            "sij,sik->sjk", values, selected, preferred_element_type=jnp.float32
-        )
-        summed = jnp.einsum(
-            "qs,sjk->qjk", col_table, block_products, precision=lax.Precision.HIGHEST
-        )
-        return summed.reshape(feat_rows, responses)
+        return block_apply(values, count_of_slots, slot_cols, slot_rows, low_slab, CB_DEV, True)
 
     def forward(direction):
-        col_panels = direction.astype(jnp.bfloat16).reshape(CB_DEV, block_edge, responses)
-        forward_selected = jnp.take(col_panels, slot_cols, axis=0)
-        forward_block_products = jnp.einsum(
-            "sij,sjk->sik", values, forward_selected, preferred_element_type=jnp.float32
-        )
-        forward_summed = jnp.einsum(
-            "rs,sik->rik", row_lookup_table, forward_block_products, precision=lax.Precision.HIGHEST
-        )
-        return reduce_over(forward_summed.reshape(RB_DEV * block_edge, responses), "feat", n_feat)
+        low = direction.astype(jnp.bfloat16)
+        summed = block_apply(values, count_of_slots, slot_rows, slot_cols, low, RB_DEV, False)
+        return reduce_over(summed, "feat", n_feat)
 
     def slab_of(current):
         return lax.all_gather(current.astype(jnp.bfloat16), "feat", axis=0, tiled=True)

time: 366 us -> 351 us (0.959)
  blocking collectives: 137 us -> 210 us
  waiting for transfers between devices: 113 us -> 70 us
  starting transfers between devices: 57.1 us -> 35.7 us
  local copies, waits for them, and re-layouts: 27.9 us -> 6.98 us
  Pallas kernels: 0 us -> 20 us
  matrix products: 17.1 us -> 0 us
  other arithmetic: 10.9 us -> 6.18 us
    all_to_all x0 -> x1, blocking collectives: none -> 47.2 us  [gradient_rows(): landed = lax.all_to_all(pieces, 'comp', 0, 0, tiled=True)]
    all_to_all x2 -> x1, waiting for transfers between devices: 66 us -> 33.4 us  [gradient_rows(): landed = lax.all_to_all(pieces, 'comp', 0, 0, tiled=True)]
    all_to_all x1 -> x2, blocking collectives: 19.7 us -> 41.6 us  [total_over_mesh(): return lax.all_to_all(spread, 'comp', 0, 0, tiled=True).sum(0)]
    pallas_call x0 -> x4, Pallas kernels: none -> 20 us  [block_apply(): pl.pallas_call(functools.partial(_block_kernel, transpose), out_shape=jax...]
    dot_general x8 -> x0, matrix products: 17.1 us -> none  [the longest x2 6.26 us: forward(): jnp.einsum('sij,sjk->sik', values, forward_selected, preferred_element_ty...]
    all_to_all x2 -> x1, starting transfers between devices: 17.4 us -> 4.03 us  [gradient_rows(): landed = lax.all_to_all(pieces, 'comp', 0, 0, tiled=True)]
    dot_general x8 -> x0, local copies, waits for them, and re-layouts: 13.3 us -> none  [the longest x2 6.08 us: forward(): jnp.einsum('sij,sjk->sik', values, forward_selected, preferred_element_ty...]
    all_to_all x1 -> x0, waiting for transfers between devices: 10.1 us -> none  [total_over_mesh(): return lax.all_to_all(spread, 'comp', 0, 0, tiled=True).sum(0)]
  transfers between devices with their start and end apart: 8 -> 6, of which waited for: 8 -> 6; matrix products, arithmetic and copies ran while one was open for 2% -> 1% of each run, Pallas kernels for 0% -> 0%
where the time goes in v3:
time: 351 us; the launch traced here: 350 us
  blocking collectives  210 us (60%)
  waiting for transfers between devices  70 us (20%)
  starting transfers between devices  35.7 us (10%)
  Pallas kernels  20 us (6%)
  local copies, waits for them, and re-layouts  6.98 us (2%)
  other arithmetic  6.18 us (2%)
    all_to_all x1, blocking collectives, gradient_rows(): landed = lax.all_to_all(pieces, 'comp', 0, 0, tiled=True)  47.2 us
    all_to_all x2, blocking collectives, total_over_mesh(): return lax.all_to_all(spread, 'comp', 0, 0, tiled=True).sum(0)  41.6 us
    all_gather x2, blocking collectives, slab_of(): lax.all_gather(current.astype(jnp.bfloat16), 'feat', axis=0, tiled=True)  40.4 us
    all_to_all x1, waiting for transfers between devices, gradient_rows(): landed = lax.all_to_all(pieces, 'comp', 0, 0, tiled=True)  33.4 us
    all_gather x1, blocking collectives, shards(): lax.all_gather(jnp.concatenate([gradient_own, col_sq(gradient_own)[None]]...  30.1 us
    all_gather x1, blocking collectives, shards(): lax.all_gather(gradient_own, 'comp', axis=0, tiled=False)  29.8 us
    all_to_all x2, waiting for transfers between devices, reduce_over(): return lax.all_to_all(pieces, axis, 0, 0, tiled=True).sum(0)  29.2 us
    all_to_all x2, blocking collectives, total_over_mesh(): by_feat = lax.all_to_all(spread, 'feat', 0, 0, tiled=True).sum(0)  21 us
  transfers between devices with their start and end apart: 6, of which 6 were waited for; matrix products, arithmetic and copies ran while one was open for 1% of the time, Pallas kernels for 0%

profile of v3, /device:TPU:1, one launch (start us, length us, event | category | flops | bytes accessed | tf_op | source)
XLA Modules:
  0.0 350.5 jit_solution(11893623879524887370)
XLA Ops:
  1.3 0.8 convert_element_type.12
  2.1 21.9 %all_gather.15.x_ref = bf16[2048,128]{1,0:T(8,128)(2,1)} all-gather(bf16[128,128]{1,0:T(8,128)(2,1)S(1)} %convert_element_type.12), channel_id=1, replica_groups=mesh['comp'=32,'feat'=16] {'feat'}, dimensions={0}, use_global_device_ids=true | all-gather | bytes 557056 | tf_op jit(solution)/shard_map/all_gather | solution.py:84
  24.0 5.4 %shard_map.77 = f32[1792,128]{1,0:T(8,128)} custom-call(s32[1]{0:T(128)} %bitcast.49.count_ref, s32[24]{0:T(128)} %bitcast.69, s32[24]{0:T(128)} %bitcast.73, bf16[24,128,128]{2,1,0:T(8,128)(2,1)} %bitcast.53, bf16[2048,128]{1,0:T(8,128)(2,1)} %all_gather.15.x_ref), custom_call_target="tpu_custom_call" | custom-call | tf_op jit(solution)/shard_map/pallas_call | solution.py:43
  29.4 1.1 constant_dynamic-slice_fusion.1
  30.6 10.0 %collective-permute-start = (f32[896,128]{1,0:T(8,128)S(1)}, f32[896,128]{1,0:T(8,128)S(1)}, u32[]{:S(2)}, u32[]{:S(2)}) collective-permute-start(f32[896,128]{1,0:T(8,128)S(1)} %constant_dynamic-slice_fusion.1), channel_id=1, source_target_pairs={{0,16},{16,0},{32,48},{48,32},{64,80},{80,64},{96,112},{112,96},{1... | collective-permute-start | bytes 1376264 | tf_op jit(solution)/shard_map/ppermute | solution.py:95
  40.6 1.4 collective-permute-done
  42.1 47.2 %all_to_all.45 = f32[32,28,128]{2,1,0:T(8,128)S(1)} all-to-all(f32[32,28,128]{2,1,0:T(8,128)S(1)} %reshape.72), channel_id=1, replica_groups=mesh['comp'=32,'feat'=16] {'comp'}, dimensions={0} | all-to-all | bytes 917504 | tf_op jit(solution)/shard_map/all_to_all | solution.py:97
  89.4 29.8 %all_gather.16 = f32[32,56,128]{2,1,0:T(8,128)S(1)} all-gather(f32[1,56,128]{2,1,0:T(8,128)S(1)} %all_gather_reshape.3), channel_id=1, replica_groups=mesh['comp'=32,'feat'=16] {'comp'}, dimensions={0}, use_global_device_ids=true | all-gather | bytes 946176 | tf_op jit(solution)/shard_map/all_gather | solution.py:116
  119.2 0.2 copy.30
  119.4 0.5 copy.31
  119.9 0.1 reshape.75
  120.0 0.8 convert_element_type.13.x_ref
  120.8 4.6 %shard_map.78 = f32[2048,128]{1,0:T(8,128)} custom-call(s32[1]{0:T(128)} %bitcast.50.count_ref, s32[24]{0:T(128)} %bitcast.74, s32[24]{0:T(128)} %bitcast.70, bf16[24,128,128]{2,1,0:T(8,128)(2,1)} %bitcast.54, bf16[1792,128]{1,0:T(8,128)(2,1)} %convert_element_type.13.x_ref), custom_call_target="tpu_custom_call" | custom-call | tf_op jit(solution)/shard_map/pallas_call | solution.py:43
  125.4 4.6 %all-to-all-start.1 = ((f32[16,128,128]{2,1,0:T(8,128)}), f32[16,128,128]{2,1,0:T(8,128)S(1)}, u32[]{:S(2)}, u32[]{:S(2)}) async-start(f32[16,128,128]{2,1,0:T(8,128)} %bitcast.58), calls=%async_computation.1 | async-start | bytes 2097152 | tf_op jit(solution)/shard_map/all_to_all | solution.py:54
  130.1 15.4 %all-to-all-done.1 = f32[16,128,128]{2,1,0:T(8,128)S(1)} async-done(((f32[16,128,128]{2,1,0:T(8,128)}), f32[16,128,128]{2,1,0:T(8,128)S(1)}, u32[]{:S(2)}, u32[]{:S(2)}) %all-to-all-start.1) | async-done | bytes 1048608 | tf_op jit(solution)/shard_map/all_to_all | solution.py:54
  145.4 0.1 reduce_sum.139
  145.6 10.5 %all_to_all.46 = f32[16,2,128]{2,1,0:T(2,128)S(1)} all-to-all(f32[16,2,128]{2,1,0:T(2,128)S(1)} %broadcast_in_dim.12), channel_id=1, replica_groups=mesh['comp'=32,'feat'=16] {'feat'}, dimensions={0} | all-to-all | bytes 32768 | tf_op jit(solution)/shard_map/all_to_all | solution.py:59
  156.1 20.8 %all_to_all.47 = f32[32,2,128]{2,1,0:T(2,128)S(1)} all-to-all(f32[32,2,128]{2,1,0:T(2,128)S(1)} %broadcast_in_dim.13), channel_id=1, replica_groups=mesh['comp'=32,'feat'=16] {'comp'}, dimensions={0} | all-to-all | bytes 65536 | tf_op jit(solution)/shard_map/all_to_all | solution.py:61
  176.9 0.6 copy-done.5
  177.6 18.5 %all_gather.17.x_ref = bf16[2048,128]{1,0:T(8,128)(2,1)} all-gather(bf16[128,128]{1,0:T(8,128)(2,1)S(1)} %fusion.6), channel_id=1, replica_groups=mesh['comp'=32,'feat'=16] {'feat'}, dimensions={0}, use_global_device_ids=true | all-gather | bytes 557056 | tf_op jit(solution)/shard_map/all_gather | solution.py:84
  196.0 5.4 %shard_map.79 = f32[1792,128]{1,0:T(8,128)} custom-call(s32[1]{0:T(128)} %bitcast.51.count_ref, s32[24]{0:T(128)} %bitcast.71, s32[24]{0:T(128)} %bitcast.75, bf16[24,128,128]{2,1,0:T(8,128)(2,1)} %bitcast.55, bf16[2048,128]{1,0:T(8,128)(2,1)} %all_gather.17.x_ref), custom_call_target="tpu_custom_call" | custom-call | tf_op jit(solution)/shard_map/pallas_call | solution.py:43
  201.5 1.1 constant_dynamic-slice_fusion
  202.6 8.3 %collective-permute-start.1 = (f32[896,128]{1,0:T(8,128)S(1)}, f32[896,128]{1,0:T(8,128)S(1)}, u32[]{:S(2)}, u32[]{:S(2)}) collective-permute-start(f32[896,128]{1,0:T(8,128)S(1)} %constant_dynamic-slice_fusion), channel_id=1, source_target_pairs={{0,16},{16,0},{32,48},{48,32},{64,80},{80,64},{96,112},{112,96},{1... | collective-permute-start | bytes 1376264 | tf_op jit(solution)/shard_map/ppermute | solution.py:95
  210.9 1.4 collective-permute-done.1
  212.4 0.8 reshape.77
  213.2 4.0 %all-to-all-start.4 = ((f32[32,28,128]{2,1,0:T(8,128)}), f32[32,28,128]{2,1,0:T(8,128)S(1)}, u32[]{:S(2)}, u32[]{:S(2)}) async-start(f32[32,28,128]{2,1,0:T(8,128)} %reshape.77), calls=%async_computation.4 | async-start | bytes 1048576 | tf_op jit(solution)/shard_map/all_to_all | solution.py:97
  217.3 33.4 %all-to-all-done.4 = f32[32,28,128]{2,1,0:T(8,128)S(1)} async-done(((f32[32,28,128]{2,1,0:T(8,128)}), f32[32,28,128]{2,1,0:T(8,128)S(1)}, u32[]{:S(2)}, u32[]{:S(2)}) %all-to-all-start.4) | async-done | bytes 458784 | tf_op jit(solution)/shard_map/all_to_all | solution.py:97
  250.8 30.1 %all-gather.1 = f32[32,57,128]{2,1,0:T(8,128)S(1)} all-gather(f32[1,57,128]{2,1,0:T(8,128)S(1)} %maximum_bitcast_fusion), channel_id=2, replica_groups=mesh['comp'=32,'feat'=16] {'comp'}, dimensions={0}, use_global_device_ids=true | all-gather | bytes 963072 | tf_op jit(solution)/shard_map/all_gather | solution.py:127
  281.0 0.1 slice_reduce_fusion
  281.0 0.6 broadcast_in_dim.15
  281.6 5.1 %all-to-all-start.5 = ((f32[16,1,128]{2,1,0:T(1,128)}), f32[16,1,128]{2,1,0:T(1,128)S(1)}, u32[]{:S(2)}, u32[]{:S(2)}) async-start(f32[16,1,128]{2,1,0:T(1,128)} %broadcast_in_dim.15), calls=%async_computation.5 | async-start | bytes 16384 | tf_op jit(solution)/shard_map/all_to_all | solution.py:136
  286.7 0.1 slice.9
  286.8 0.2 copy.47
  287.0 0.0 copy-start.1
  287.0 0.9 copy-done.1
  287.9 0.5 copy.38
  288.4 0.1 reshape.83
  288.5 4.5 %all-to-all-done.5 = f32[16,1,128]{2,1,0:T(1,128)S(1)} async-done(((f32[16,1,128]{2,1,0:T(1,128)}), f32[16,1,128]{2,1,0:T(1,128)S(1)}, u32[]{:S(2)}, u32[]{:S(2)}) %all-to-all-start.5) | async-done | bytes 8224 | tf_op jit(solution)/shard_map/all_to_all | solution.py:136
  293.1 0.9 fusion.x_ref
  294.0 4.6 %shard_map.80 = f32[2048,128]{1,0:T(8,128)} custom-call(s32[1]{0:T(128)} %bitcast.52.count_ref, s32[24]{0:T(128)} %bitcast.76, s32[24]{0:T(128)} %bitcast.72, bf16[24,128,128]{2,1,0:T(8,128)(2,1)} %bitcast.56, bf16[1792,128]{1,0:T(8,128)(2,1)} %fusion.x_ref), custom_call_target="tpu_custom_call" | custom-call | tf_op jit(solution)/shard_map/pallas_call | solution.py:43
  298.6 3.7 %all-to-all-start.6 = ((f32[16,128,128]{2,1,0:T(8,128)}), f32[16,128,128]{2,1,0:T(8,128)S(1)}, u32[]{:S(2)}, u32[]{:S(2)}) async-start(f32[16,128,128]{2,1,0:T(8,128)} %bitcast.57), calls=%async_computation.6 | async-start | bytes 2097152 | tf_op jit(solution)/shard_map/all_to_all | solution.py:54
  302.2 1.1 fusion.5
  303.4 13.8 %all-to-all-done.6 = f32[16,128,128]{2,1,0:T(8,128)S(1)} async-done(((f32[16,128,128]{2,1,0:T(8,128)}), f32[16,128,128]{2,1,0:T(8,128)S(1)}, u32[]{:S(2)}, u32[]{:S(2)}) %all-to-all-start.6) | async-done | bytes 1048608 | tf_op jit(solution)/shard_map/all_to_all | solution.py:54
  317.2 0.1 reduce_sum.148
  317.3 10.5 %all_to_all.48 = f32[16,2,128]{2,1,0:T(2,128)S(1)} all-to-all(f32[16,2,128]{2,1,0:T(2,128)S(1)} %broadcast_in_dim.16), channel_id=1, replica_groups=mesh['comp'=32,'feat'=16] {'feat'}, dimensions={0} | all-to-all | bytes 32768 | tf_op jit(solution)/shard_map/all_to_all | solution.py:59
  327.9 20.8 %all_to_all.49 = f32[32,2,128]{2,1,0:T(2,128)S(1)} all-to-all(f32[32,2,128]{2,1,0:T(2,128)S(1)} %broadcast_in_dim.17), channel_id=1, replica_groups=mesh['comp'=32,'feat'=16] {'comp'}, dimensions={0} | all-to-all | bytes 65536 | tf_op jit(solution)/shard_map/all_to_all | solution.py:61
  348.7 1.1 multiply_add_fusion
  349.8 0.6 multiply_subtract_fusion
  (39 shorter events, 0.7 us)
Async XLA Ops:
  29.4 12.6 %copy-start.2 = (f32[1792,128]{1,0:T(8,128)S(1)}, f32[1792,128]{1,0:T(8,128)}, u32[]{:S(2)}) copy-start(f32[1792,128]{1,0:T(8,128)} %shard_map.77) | copy-start | bytes 2752516
  30.6 11.5 %collective-permute-start = (f32[896,128]{1,0:T(8,128)S(1)}, f32[896,128]{1,0:T(8,128)S(1)}, u32[]{:S(2)}, u32[]{:S(2)}) collective-permute-start(f32[896,128]{1,0:T(8,128)S(1)} %constant_dynamic-slice_fusion.1), channel_id=1, source_target_pairs={{0,16},{16,0},{32,48},{48,32},{64,80},{80,64},{96,112},{112,96},{1... | collective-permute-start | bytes 1376264 | tf_op jit(solution)/shard_map/ppermute | solution.py:95
  119.4 97.9 %copy-start = (f32[32,56,128]{2,0,1:T(8,128)}, f32[32,56,128]{2,0,1:T(8,128)S(1)}, u32[]{:S(2)}) copy-start(f32[32,56,128]{2,0,1:T(8,128)S(1)} %copy.30) | copy-start | bytes 2752516
  125.4 20.1 %all-to-all-start.1 = ((f32[16,128,128]{2,1,0:T(8,128)}), f32[16,128,128]{2,1,0:T(8,128)S(1)}, u32[]{:S(2)}, u32[]{:S(2)}) async-start(f32[16,128,128]{2,1,0:T(8,128)} %bitcast.58), calls=%async_computation.1 | async-start | bytes 2097152 | tf_op jit(solution)/shard_map/all_to_all | solution.py:54
  156.1 21.5 %copy-start.4 = (f32[128,128]{1,0:T(8,128)S(1)}, f32[128,128]{1,0:T(8,128)}, u32[]{:S(2)}) copy-start(f32[128,128]{1,0:T(8,128)} %param.10) | copy-start | bytes 196612
  176.9 0.7 copy-start.5
  201.5 10.8 %copy-start.3 = (f32[1792,128]{1,0:T(8,128)S(1)}, f32[1792,128]{1,0:T(8,128)}, u32[]{:S(2)}) copy-start(f32[1792,128]{1,0:T(8,128)} %shard_map.79) | copy-start | bytes 2752516
  202.6 9.7 %collective-permute-start.1 = (f32[896,128]{1,0:T(8,128)S(1)}, f32[896,128]{1,0:T(8,128)S(1)}, u32[]{:S(2)}, u32[]{:S(2)}) collective-permute-start(f32[896,128]{1,0:T(8,128)S(1)} %constant_dynamic-slice_fusion), channel_id=1, source_target_pairs={{0,16},{16,0},{32,48},{48,32},{64,80},{80,64},{96,112},{112,96},{1... | collective-permute-start | bytes 1376264 | tf_op jit(solution)/shard_map/ppermute | solution.py:95
  213.2 37.5 %all-to-all-start.4 = ((f32[32,28,128]{2,1,0:T(8,128)}), f32[32,28,128]{2,1,0:T(8,128)S(1)}, u32[]{:S(2)}, u32[]{:S(2)}) async-start(f32[32,28,128]{2,1,0:T(8,128)} %reshape.77), calls=%async_computation.4 | async-start | bytes 1048576 | tf_op jit(solution)/shard_map/all_to_all | solution.py:97
  281.6 11.4 %all-to-all-start.5 = ((f32[16,1,128]{2,1,0:T(1,128)}), f32[16,1,128]{2,1,0:T(1,128)S(1)}, u32[]{:S(2)}, u32[]{:S(2)}) async-start(f32[16,1,128]{2,1,0:T(1,128)} %broadcast_in_dim.15), calls=%async_computation.5 | async-start | bytes 16384 | tf_op jit(solution)/shard_map/all_to_all | solution.py:136
  287.0 0.9 copy-start.1
  298.6 18.6 %all-to-all-start.6 = ((f32[16,128,128]{2,1,0:T(8,128)}), f32[16,128,128]{2,1,0:T(8,128)S(1)}, u32[]{:S(2)}, u32[]{:S(2)}) async-start(f32[16,128,128]{2,1,0:T(8,128)} %bitcast.57), calls=%async_computation.6 | async-start | bytes 2097152 | tf_op jit(solution)/shard_map/all_to_all | solution.py:54

commit v4 on v3

--- a/solution.py
+++ b/solution.py
@@ -80,16 +80,12 @@
         summed = block_apply(values, count_of_slots, slot_rows, slot_cols, low, RB_DEV, False)
         return reduce_over(summed, "feat", n_feat)
 
-    def slab_of(current):
-        return lax.all_gather(current.astype(jnp.bfloat16), "feat", axis=0, tiled=True)
-
     core = comp_index % 2
     half_rows = feat_rows // 2
     part_rows = half_rows // n_comp
     siblings = [(i, i ^ 1) for i in range(n_comp)]
 
-    def gradient_rows(current):
-        partial = backward(slab_of(current))
+    def reduce_gradient(partial):
         kept = lax.dynamic_slice_in_dim(partial, core * half_rows, half_rows, axis=0)
         sent = lax.dynamic_slice_in_dim(partial, (1 - core) * half_rows, half_rows, axis=0)
         chip_sum = kept + lax.ppermute(sent, "comp", siblings)
@@ -110,39 +106,72 @@
     def col_sq(x):
         return jnp.sum(x * x, axis=0)
 
-    residual = right_side
+    feat_index = lax.axis_index("feat")
 
-    gradient_own = gradient_rows(residual)
+    def gather_feat(own):
+        spread = jnp.broadcast_to(own[None], (n_feat,) + own.shape)
+        return lax.all_to_all(spread, "feat", 0, 0, tiled=True)
+
+    def comp_total(stacked):
+        spread = jnp.broadcast_to(stacked[None], (n_comp,) + stacked.shape)
+        return lax.all_to_all(spread, "comp", 0, 0, tiled=True).sum(0)
+
+    own_block = right_side.shape[0]
+    residual_slab = gather_feat(right_side).reshape(RB_DEV * own_block, responses)
+
+    def low_slab(slab):
+        return slab.astype(jnp.bfloat16)
+
+    gradient_own = reduce_gradient(backward(low_slab(residual_slab)))
+    energy_own = col_sq(gradient_own)
     direction = whole_of(lax.all_gather(gradient_own, "comp", axis=0, tiled=False))
-    image_rows = forward(direction)
-    energy, image_energy = total_over_mesh(
-        jnp.stack([col_sq(gradient_own), col_sq(image_rows)]), n_comp, n_feat
-    )
-    step_size = energy / (image_energy + ridge * energy)
-    solution = step_size * direction
-    residual = residual - step_size * image_rows
-
-    for _ in range(1, ITERS):
-        gradient_own = gradient_rows(residual) - ridge * own_part(solution)
-        gathered = lax.all_gather(
-            jnp.concatenate([gradient_own, col_sq(gradient_own)[None]], axis=0),
-            "comp",
-            axis=0,
-            tiled=False,
-        )
-        gradient = whole_of(gathered[:, :own_rows])
-        comp_energy = jnp.sum(gathered[:, own_rows], axis=0)
-        spread = jnp.broadcast_to(comp_energy[None, None], (n_feat, 1, responses))
-        next_energy = lax.all_to_all(spread, "feat", 0, 0, tiled=True).sum(0)[0]
-        direction = gradient + next_energy / energy * direction
-        energy = next_energy
+    energy = None
+    solution = None
+    for step_index in range(ITERS):
+        last = step_index + 1 == ITERS
+        if step_index > 0:
+            gradient_own = reduce_gradient(backward(low_slab(residual_slab))) - ridge * own_part(
+                solution
+            )
+            gathered = lax.all_gather(
+                jnp.concatenate([gradient_own, col_sq(gradient_own)[None]], axis=0),
+                "comp",
+                axis=0,
+                tiled=False,
+            )
+            gradient = whole_of(gathered[:, :own_rows])
+            comp_energy = jnp.sum(gathered[:, own_rows], axis=0)
+            spread = jnp.broadcast_to(comp_energy[None, None], (n_feat, 1, responses))
+            next_energy = lax.all_to_all(spread, "feat", 0, 0, tiled=True).sum(0)[0]
+            direction = gradient + next_energy / energy * direction
+            energy = next_energy
         image_rows = forward(direction)
-        image_energy, direction_energy = total_over_mesh(
-            jnp.stack([col_sq(image_rows), col_sq(own_part(direction))]), n_comp, n_feat
-        )
+        if last:
+            sums = [col_sq(image_rows), col_sq(own_part(direction))]
+            if energy is None:
+                sums.append(energy_own)
+            totals = total_over_mesh(jnp.stack(sums), n_comp, n_feat)
+            if energy is None:
+                energy = totals[2]
+            image_energy, direction_energy = totals[0], totals[1]
+        else:
+            parts = [image_rows, col_sq(own_part(direction))[None]]
+            if energy is None:
+                parts.append(energy_own[None])
+            gathered = gather_feat(jnp.concatenate(parts, axis=0))
+            image_slab = gathered[:, :own_block].reshape(RB_DEV * own_block, responses)
+            feat_sums = jnp.sum(gathered[:, own_block:], axis=0)
+            totals = comp_total(jnp.concatenate([col_sq(image_slab)[None], feat_sums], axis=0))
+            if energy is None:
+                energy = totals[2]
+            image_energy, direction_energy = totals[0], totals[1]
         step_size = energy / (image_energy + ridge * direction_energy)
-        solution = solution + step_size * direction
-        residual = residual - step_size * image_rows
+        solution = step_size * direction if solution is None else solution + step_size * direction
+        if last:
+            own_residual = lax.dynamic_slice_in_dim(residual_slab, feat_index * own_block, own_block)
+            residual = own_residual - step_size * image_rows
+        else:
+            residual_slab = residual_slab - step_size * image_slab
     return (solution, residual)
 
 

time: 351 us -> 341 us (0.972)
  blocking collectives: 210 us -> 163 us
  waiting for transfers between devices: 70 us -> 92.9 us
  starting transfers between devices: 35.7 us -> 45.6 us
  other arithmetic: 6.18 us -> 10.5 us
    all_gather x2 -> x0, blocking collectives: 40.4 us -> none  [slab_of(): lax.all_gather(current.astype(jnp.bfloat16), 'feat', axis=0, tiled=True)]
    all_to_all x1 -> x3, waiting for transfers between devices: 33.4 us -> 58.2 us  [the longest x1 32.5 us: reduce_gradient(): landed = lax.all_to_all(pieces, 'comp', 0, 0, tiled=True)]
    all_to_all x1 -> x3, starting transfers between devices: 4.03 us -> 20.1 us  [the longest x1 8.57 us: total_over_mesh(): return lax.all_to_all(spread, 'comp', 0, 0, tiled=True).sum(0)]
    all_to_all x2 -> x1, blocking collectives: 21 us -> 11.2 us  [total_over_mesh(): by_feat = lax.all_to_all(spread, 'feat', 0, 0, tiled=True).sum(0)]
    ppermute x2, starting transfers between devices: 18.3 us -> 14.2 us  [reduce_gradient(): chip_sum = kept + lax.ppermute(sent, 'comp', siblings)]
    pallas_call x4, Pallas kernels: 20 us -> 16.5 us  [block_apply(): pl.pallas_call(functools.partial(_block_kernel, transpose), out_shape=jax...]
  transfers between devices with their start and end apart: 6 -> 8, of which waited for: 6 -> 8; matrix products, arithmetic and copies ran while one was open for 1% -> 1% of each run, Pallas kernels for 0% -> 0%
where the time goes in v4:
time: 341 us; the launch traced here: 340 us
  blocking collectives  163 us (48%)
  waiting for transfers between devices  92.9 us (27%)
  starting transfers between devices  45.6 us (13%)
  Pallas kernels  16.5 us (5%)
  other arithmetic  10.5 us (3%)
  local copies, waits for them, and re-layouts  9.92 us (3%)
    all_to_all x1, blocking collectives, reduce_gradient(): landed = lax.all_to_all(pieces, 'comp', 0, 0, tiled=True)  49 us
    all_to_all x1, waiting for transfers between devices, reduce_gradient(): landed = lax.all_to_all(pieces, 'comp', 0, 0, tiled=True)  32.5 us
    all_gather x1, blocking collectives, shards(): lax.all_gather(jnp.concatenate([gradient_own, col_sq(gradient_own)[None]]...  30.4 us
    all_gather x1, blocking collectives, shards(): lax.all_gather(gradient_own, 'comp', axis=0, tiled=False)  29.8 us
    all_to_all x2, waiting for transfers between devices, reduce_over(): return lax.all_to_all(pieces, axis, 0, 0, tiled=True).sum(0)  27.3 us
    all_to_all x1, blocking collectives, comp_total(): return lax.all_to_all(spread, 'comp', 0, 0, tiled=True).sum(0)  23.5 us
    all_to_all x1, blocking collectives, gather_feat(): return lax.all_to_all(spread, 'feat', 0, 0, tiled=True)  19.4 us
    pallas_call x4, Pallas kernels, block_apply(): pl.pallas_call(functools.partial(_block_kernel, transpose), out_shape=jax...  16.5 us
  transfers between devices with their start and end apart: 8, of which 8 were waited for; matrix products, arithmetic and copies ran while one was open for 1% of the time, Pallas kernels for 0%

profile of v4, /device:TPU:1, one launch (start us, length us, event | category | flops | bytes accessed | tf_op | source)
XLA Modules:
  0.0 340.2 jit_solution(6607294940555198767)
XLA Ops:
  0.6 1.9 broadcast_in_dim.20
  2.6 7.6 %all-to-all-start = ((f32[16,128,128]{2,1,0:T(8,128)}), f32[16,128,128]{2,1,0:T(8,128)S(1)}, u32[]{:S(2)}, u32[]{:S(2)}) async-start(f32[16,128,128]{2,1,0:T(8,128)} %broadcast_in_dim.20), calls=%async_computation | async-start | bytes 2097152 | tf_op jit(solution)/shard_map/all_to_all | solution.py:113
  10.8 13.6 %all-to-all-done = f32[16,128,128]{2,1,0:T(8,128)S(1)} async-done(((f32[16,128,128]{2,1,0:T(8,128)}), f32[16,128,128]{2,1,0:T(8,128)S(1)}, u32[]{:S(2)}, u32[]{:S(2)}) %all-to-all-start) | async-done | bytes 1048608 | tf_op jit(solution)/shard_map/all_to_all | solution.py:113
  24.4 0.8 bitcast_convert_fusion.x_ref
  25.2 4.4 %shard_map.77 = f32[1792,128]{1,0:T(8,128)} custom-call(s32[1]{0:T(128)} %bitcast.60.count_ref, s32[24]{0:T(128)} %bitcast.81, s32[24]{0:T(128)} %bitcast.85, bf16[24,128,128]{2,1,0:T(8,128)(2,1)} %bitcast.64, bf16[2048,128]{1,0:T(8,128)(2,1)} %bitcast_convert_fusion.x_ref), custom_call_target="tpu_custom_call" | custom-call | tf_op jit(solution)/shard_map/pallas_call | solution.py:43
  29.6 1.1 constant_dynamic-slice_fusion.1
  30.7 8.2 %collective-permute-start = (f32[896,128]{1,0:T(8,128)S(1)}, f32[896,128]{1,0:T(8,128)S(1)}, u32[]{:S(2)}, u32[]{:S(2)}) collective-permute-start(f32[896,128]{1,0:T(8,128)S(1)} %constant_dynamic-slice_fusion.1), channel_id=1, source_target_pairs={{0,16},{16,0},{32,48},{48,32},{64,80},{80,64},{96,112},{112,96},{1... | collective-permute-start | bytes 1376264 | tf_op jit(solution)/shard_map/ppermute | solution.py:91
  39.0 1.4 collective-permute-done
  40.5 49.0 %all_to_all.50 = f32[32,28,128]{2,1,0:T(8,128)S(1)} all-to-all(f32[32,28,128]{2,1,0:T(8,128)S(1)} %reshape.92), channel_id=1, replica_groups=mesh['comp'=32,'feat'=16] {'comp'}, dimensions={0} | all-to-all | bytes 917504 | tf_op jit(solution)/shard_map/all_to_all | solution.py:93
  89.5 29.8 %all_gather.9 = f32[32,56,128]{2,1,0:T(8,128)S(1)} all-gather(f32[1,56,128]{2,1,0:T(8,128)S(1)} %all_gather_reshape.3), channel_id=1, replica_groups=mesh['comp'=32,'feat'=16] {'comp'}, dimensions={0}, use_global_device_ids=true | all-gather | bytes 946176 | tf_op jit(solution)/shard_map/all_gather | solution.py:127
  119.3 0.2 copy.30
  119.5 0.9 copy-done
  120.4 0.5 copy.31
  121.0 0.8 convert_element_type.13.x_ref
  121.9 3.8 %shard_map.78 = f32[2048,128]{1,0:T(8,128)} custom-call(s32[1]{0:T(128)} %bitcast.61.count_ref, s32[24]{0:T(128)} %bitcast.86, s32[24]{0:T(128)} %bitcast.82, bf16[24,128,128]{2,1,0:T(8,128)(2,1)} %bitcast.65, bf16[1792,128]{1,0:T(8,128)(2,1)} %convert_element_type.13.x_ref), custom_call_target="tpu_custom_call" | custom-call | tf_op jit(solution)/shard_map/pallas_call | solution.py:43
  125.7 3.7 %all-to-all-start.2 = ((f32[16,128,128]{2,1,0:T(8,128)}), f32[16,128,128]{2,1,0:T(8,128)S(1)}, u32[]{:S(2)}, u32[]{:S(2)}) async-start(f32[16,128,128]{2,1,0:T(8,128)} %bitcast.68), calls=%async_computation.2 | async-start | bytes 2097152 | tf_op jit(solution)/shard_map/all_to_all | solution.py:54
  129.4 1.0 multiply_reduce_fusion.3
  130.5 13.9 %all-to-all-done.2 = f32[16,128,128]{2,1,0:T(8,128)S(1)} async-done(((f32[16,128,128]{2,1,0:T(8,128)}), f32[16,128,128]{2,1,0:T(8,128)S(1)}, u32[]{:S(2)}, u32[]{:S(2)}) %all-to-all-start.2) | async-done | bytes 1048608 | tf_op jit(solution)/shard_map/all_to_all | solution.py:54
  144.5 19.4 %all_to_all.51 = f32[16,130,128]{2,1,0:T(8,128)S(1)} all-to-all(f32[16,130,128]{2,1,0:T(8,128)S(1)} %broadcast_in_dim.23), channel_id=1, replica_groups=mesh['comp'=32,'feat'=16] {'feat'}, dimensions={0} | all-to-all | bytes 2129920 | tf_op jit(solution)/shard_map/all_to_all | solution.py:113
  163.9 0.3 multiply_reduce_fusion
  164.2 23.5 %all_to_all.52 = f32[32,3,128]{2,1,0:T(4,128)S(1)} all-to-all(f32[32,3,128]{2,1,0:T(4,128)S(1)} %broadcast_in_dim.25), channel_id=1, replica_groups=mesh['comp'=32,'feat'=16] {'comp'}, dimensions={0} | all-to-all | bytes 98304 | tf_op jit(solution)/shard_map/all_to_all | solution.py:117
  187.8 1.3 fusion.12
  189.1 4.4 %shard_map.79 = f32[1792,128]{1,0:T(8,128)} custom-call(s32[1]{0:T(128)} %bitcast.62.count_ref, s32[24]{0:T(128)} %bitcast.83, s32[24]{0:T(128)} %bitcast.87, bf16[24,128,128]{2,1,0:T(8,128)(2,1)} %bitcast.66, bf16[2048,128]{1,0:T(8,128)(2,1)} %get-tuple-element.2.x_ref), custom_call_target="tpu_custom_call" | custom-call | tf_op jit(solution)/shard_map/pallas_call | solution.py:43
  193.5 1.1 constant_dynamic-slice_fusion
  194.6 6.0 %collective-permute-start.1 = (f32[896,128]{1,0:T(8,128)S(1)}, f32[896,128]{1,0:T(8,128)S(1)}, u32[]{:S(2)}, u32[]{:S(2)}) collective-permute-start(f32[896,128]{1,0:T(8,128)S(1)} %constant_dynamic-slice_fusion), channel_id=1, source_target_pairs={{0,16},{16,0},{32,48},{48,32},{64,80},{80,64},{96,112},{112,96},{1... | collective-permute-start | bytes 1376264 | tf_op jit(solution)/shard_map/ppermute | solution.py:91
  200.6 1.4 collective-permute-done.1
  202.1 0.9 reshape.98
  202.9 3.9 %all-to-all-start.5 = ((f32[32,28,128]{2,1,0:T(8,128)}), f32[32,28,128]{2,1,0:T(8,128)S(1)}, u32[]{:S(2)}, u32[]{:S(2)}) async-start(f32[32,28,128]{2,1,0:T(8,128)} %reshape.98), calls=%async_computation.5 | async-start | bytes 1048576 | tf_op jit(solution)/shard_map/all_to_all | solution.py:93
  206.8 1.0 dynamic-slice_multiply_fusion
  207.8 32.5 %all-to-all-done.5 = f32[32,28,128]{2,1,0:T(8,128)S(1)} async-done(((f32[32,28,128]{2,1,0:T(8,128)}), f32[32,28,128]{2,1,0:T(8,128)S(1)}, u32[]{:S(2)}, u32[]{:S(2)}) %all-to-all-start.5) | async-done | bytes 458784 | tf_op jit(solution)/shard_map/all_to_all | solution.py:93
  240.5 30.4 %all-gather.1 = f32[32,57,128]{2,1,0:T(8,128)S(1)} all-gather(f32[1,57,128]{2,1,0:T(8,128)S(1)} %maximum_bitcast_fusion), channel_id=2, replica_groups=mesh['comp'=32,'feat'=16] {'comp'}, dimensions={0}, use_global_device_ids=true | all-gather | bytes 963072 | tf_op jit(solution)/shard_map/all_gather | solution.py:136
  271.0 0.6 broadcast_in_dim.27
  271.6 3.5 %all-to-all-start.6 = ((f32[16,1,128]{2,1,0:T(1,128)}), f32[16,1,128]{2,1,0:T(1,128)S(1)}, u32[]{:S(2)}, u32[]{:S(2)}) async-start(f32[16,1,128]{2,1,0:T(1,128)} %broadcast_in_dim.27), calls=%async_computation.6 | async-start | bytes 16384 | tf_op jit(solution)/shard_map/all_to_all | solution.py:145
  275.1 0.2 copy.46
  275.3 0.9 copy-done.1
  276.2 0.5 copy.37
  276.9 4.5 %all-to-all-done.6 = f32[16,1,128]{2,1,0:T(1,128)S(1)} async-done(((f32[16,1,128]{2,1,0:T(1,128)}), f32[16,1,128]{2,1,0:T(1,128)S(1)}, u32[]{:S(2)}, u32[]{:S(2)}) %all-to-all-start.6) | async-done | bytes 8224 | tf_op jit(solution)/shard_map/all_to_all | solution.py:145
  281.4 0.9 fusion.1.x_ref
  282.2 3.9 %shard_map.80 = f32[2048,128]{1,0:T(8,128)} custom-call(s32[1]{0:T(128)} %bitcast.63.count_ref, s32[24]{0:T(128)} %bitcast.88, s32[24]{0:T(128)} %bitcast.84, bf16[24,128,128]{2,1,0:T(8,128)(2,1)} %bitcast.67, bf16[1792,128]{1,0:T(8,128)(2,1)} %fusion.1.x_ref), custom_call_target="tpu_custom_call" | custom-call | tf_op jit(solution)/shard_map/pallas_call | solution.py:43
  286.1 4.2 %all-to-all-start.7 = ((f32[16,128,128]{2,1,0:T(8,128)}), f32[16,128,128]{2,1,0:T(8,128)S(1)}, u32[]{:S(2)}, u32[]{:S(2)}) async-start(f32[16,128,128]{2,1,0:T(8,128)} %bitcast.69), calls=%async_computation.7 | async-start | bytes 2097152 | tf_op jit(solution)/shard_map/all_to_all | solution.py:54
  290.3 1.1 fusion.6
  291.4 13.4 %all-to-all-done.7 = f32[16,128,128]{2,1,0:T(8,128)S(1)} async-done(((f32[16,128,128]{2,1,0:T(8,128)}), f32[16,128,128]{2,1,0:T(8,128)S(1)}, u32[]{:S(2)}, u32[]{:S(2)}) %all-to-all-start.7) | async-done | bytes 1048608 | tf_op jit(solution)/shard_map/all_to_all | solution.py:54
  305.0 11.2 %all_to_all.53 = f32[16,2,128]{2,1,0:T(2,128)S(1)} all-to-all(f32[16,2,128]{2,1,0:T(2,128)S(1)} %broadcast_in_dim.28), channel_id=1, replica_groups=mesh['comp'=32,'feat'=16] {'feat'}, dimensions={0} | all-to-all | bytes 32768 | tf_op jit(solution)/shard_map/all_to_all | solution.py:59
  316.2 0.6 broadcast_in_dim.29
  316.9 8.6 %all-to-all-start.9 = ((f32[32,2,128]{2,1,0:T(2,128)}), f32[32,2,128]{2,1,0:T(2,128)S(1)}, u32[]{:S(2)}, u32[]{:S(2)}) async-start(f32[32,2,128]{2,1,0:T(2,128)} %broadcast_in_dim.29), calls=%async_computation.9 | async-start | bytes 65536 | tf_op jit(solution)/shard_map/all_to_all | solution.py:61
  325.4 12.1 %all-to-all-done.9 = f32[32,2,128]{2,1,0:T(2,128)S(1)} async-done(((f32[32,2,128]{2,1,0:T(2,128)}), f32[32,2,128]{2,1,0:T(2,128)S(1)}, u32[]{:S(2)}, u32[]{:S(2)}) %all-to-all-start.9) | async-done | bytes 32800 | tf_op jit(solution)/shard_map/all_to_all | solution.py:61
  337.6 1.1 multiply_add_fusion
  338.7 1.5 multiply_subtract_fusion
  (41 shorter events, 1.0 us)
Async XLA Ops:
  2.6 21.8 %all-to-all-start = ((f32[16,128,128]{2,1,0:T(8,128)}), f32[16,128,128]{2,1,0:T(8,128)S(1)}, u32[]{:S(2)}, u32[]{:S(2)}) async-start(f32[16,128,128]{2,1,0:T(8,128)} %broadcast_in_dim.20), calls=%async_computation | async-start | bytes 2097152 | tf_op jit(solution)/shard_map/all_to_all | solution.py:113
  29.6 10.8 %copy-start.2 = (f32[1792,128]{1,0:T(8,128)S(1)}, f32[1792,128]{1,0:T(8,128)}, u32[]{:S(2)}) copy-start(f32[1792,128]{1,0:T(8,128)} %shard_map.77) | copy-start | bytes 2752516
  30.7 9.6 %collective-permute-start = (f32[896,128]{1,0:T(8,128)S(1)}, f32[896,128]{1,0:T(8,128)S(1)}, u32[]{:S(2)}, u32[]{:S(2)}) collective-permute-start(f32[896,128]{1,0:T(8,128)S(1)} %constant_dynamic-slice_fusion.1), channel_id=1, source_target_pairs={{0,16},{16,0},{32,48},{48,32},{64,80},{80,64},{96,112},{112,96},{1... | collective-permute-start | bytes 1376264 | tf_op jit(solution)/shard_map/ppermute | solution.py:91
  119.5 0.9 copy-start
  125.7 18.7 %all-to-all-start.2 = ((f32[16,128,128]{2,1,0:T(8,128)}), f32[16,128,128]{2,1,0:T(8,128)S(1)}, u32[]{:S(2)}, u32[]{:S(2)}) async-start(f32[16,128,128]{2,1,0:T(8,128)} %bitcast.68), calls=%async_computation.2 | async-start | bytes 2097152 | tf_op jit(solution)/shard_map/all_to_all | solution.py:54
  163.9 23.9 %copy-start.4 = (f32[128]{0:T(128)S(1)}, f32[128]{0:T(128)}, u32[]{:S(2)}) copy-start(f32[128]{0:T(128)} %param.11) | copy-start | bytes 1540
  193.5 8.5 %copy-start.3 = (f32[1792,128]{1,0:T(8,128)S(1)}, f32[1792,128]{1,0:T(8,128)}, u32[]{:S(2)}) copy-start(f32[1792,128]{1,0:T(8,128)} %shard_map.79) | copy-start | bytes 2752516
  194.6 7.4 %collective-permute-start.1 = (f32[896,128]{1,0:T(8,128)S(1)}, f32[896,128]{1,0:T(8,128)S(1)}, u32[]{:S(2)}, u32[]{:S(2)}) collective-permute-start(f32[896,128]{1,0:T(8,128)S(1)} %constant_dynamic-slice_fusion), channel_id=1, source_target_pairs={{0,16},{16,0},{32,48},{48,32},{64,80},{80,64},{96,112},{112,96},{1... | collective-permute-start | bytes 1376264 | tf_op jit(solution)/shard_map/ppermute | solution.py:91
  202.9 37.5 %all-to-all-start.5 = ((f32[32,28,128]{2,1,0:T(8,128)}), f32[32,28,128]{2,1,0:T(8,128)S(1)}, u32[]{:S(2)}, u32[]{:S(2)}) async-start(f32[32,28,128]{2,1,0:T(8,128)} %reshape.98), calls=%async_computation.5 | async-start | bytes 1048576 | tf_op jit(solution)/shard_map/all_to_all | solution.py:93
  271.6 9.8 %all-to-all-start.6 = ((f32[16,1,128]{2,1,0:T(1,128)}), f32[16,1,128]{2,1,0:T(1,128)S(1)}, u32[]{:S(2)}, u32[]{:S(2)}) async-start(f32[16,1,128]{2,1,0:T(1,128)} %broadcast_in_dim.27), calls=%async_computation.6 | async-start | bytes 16384 | tf_op jit(solution)/shard_map/all_to_all | solution.py:145
  275.3 0.9 copy-start.1
  286.1 18.8 %all-to-all-start.7 = ((f32[16,128,128]{2,1,0:T(8,128)}), f32[16,128,128]{2,1,0:T(8,128)S(1)}, u32[]{:S(2)}, u32[]{:S(2)}) async-start(f32[16,128,128]{2,1,0:T(8,128)} %bitcast.69), calls=%async_computation.7 | async-start | bytes 2097152 | tf_op jit(solution)/shard_map/all_to_all | solution.py:54
  316.9 20.7 %all-to-all-start.9 = ((f32[32,2,128]{2,1,0:T(2,128)}), f32[32,2,128]{2,1,0:T(2,128)S(1)}, u32[]{:S(2)}, u32[]{:S(2)}) async-start(f32[32,2,128]{2,1,0:T(2,128)} %broadcast_in_dim.29), calls=%async_computation.9 | async-start | bytes 65536 | tf_op jit(solution)/shard_map/all_to_all | solution.py:61

commit v5 on v4

--- a/solution.py
+++ b/solution.py
@@ -54,13 +54,6 @@
     return lax.all_to_all(pieces, axis, 0, 0, tiled=True).sum(0)
 
 
-def total_over_mesh(stacked, n_comp, n_feat):
-    spread = jnp.broadcast_to(stacked[None], (n_feat,) + stacked.shape)
-    by_feat = lax.all_to_all(spread, "feat", 0, 0, tiled=True).sum(0)
-    spread = jnp.broadcast_to(by_feat[None], (n_comp,) + stacked.shape)
-    return lax.all_to_all(spread, "comp", 0, 0, tiled=True).sum(0)
-
-
 def shards(block_values, block_rows, block_cols, block_counts, right_side, ridge, n_comp, n_feat):
     values = block_values[0, 0]
     slot_rows = block_rows[0, 0]
@@ -81,27 +74,34 @@
         return reduce_over(summed, "feat", n_feat)
 
     core = comp_index % 2
+    chip = comp_index // 2
+    n_chips = n_comp // 2
     half_rows = feat_rows // 2
-    part_rows = half_rows // n_comp
     siblings = [(i, i ^ 1) for i in range(n_comp)]
+    same_core = [[i for i in range(n_comp) if i % 2 == p] for p in range(2)]
+
+    def swap_with_sibling(x):
+        return lax.ppermute(x, "comp", siblings)
 
     def reduce_gradient(partial):
         kept = lax.dynamic_slice_in_dim(partial, core * half_rows, half_rows, axis=0)
         sent = lax.dynamic_slice_in_dim(partial, (1 - core) * half_rows, half_rows, axis=0)
-        chip_sum = kept + lax.ppermute(sent, "comp", siblings)
-        pieces = chip_sum.reshape(n_comp, part_rows, chip_sum.shape[1])
-        landed = lax.all_to_all(pieces, "comp", 0, 0, tiled=True)
-        halves = landed.reshape(n_comp // 2, 2, part_rows, chip_sum.shape[1]).sum(0)
-        return halves.reshape(own_rows, chip_sum.shape[1])
+        chip_sum = kept + swap_with_sibling(sent)
+        pieces = chip_sum.reshape(n_chips, own_rows, chip_sum.shape[1])
+        landed = lax.all_to_all(pieces, "comp", 0, 0, tiled=True, axis_index_groups=same_core)
+        return landed.sum(0)
 
-    def whole_of(gathered):
-        split = gathered.reshape(n_comp, 2, part_rows, gathered.shape[-1])
-        return split.transpose(1, 0, 2, 3).reshape(feat_rows, gathered.shape[-1])
+    def gather_gradient(own):
+        got = lax.all_gather(own, "comp", axis=0, tiled=False, axis_index_groups=same_core)
+        half = got[:, :own_rows].reshape(half_rows, own.shape[1])
+        sums = jnp.sum(got[:, own_rows:], axis=0)
+        other_half, other_sums = swap_with_sibling((half, sums))
+        first = jnp.where(core == 0, half, other_half)
+        second = jnp.where(core == 0, other_half, half)
+        return jnp.concatenate([first, second], axis=0), sums + other_sums
 
     def own_part(full):
-        split = full.reshape(2, n_comp, part_rows, full.shape[-1])
-        mine = lax.dynamic_slice_in_dim(split, comp_index, 1, axis=1)
-        return mine.reshape(own_rows, full.shape[-1])
+        return lax.dynamic_slice_in_dim(full, core * half_rows + chip * own_rows, own_rows, axis=0)
 
     def col_sq(x):
         return jnp.sum(x * x, axis=0)
@@ -113,8 +113,10 @@
         return lax.all_to_all(spread, "feat", 0, 0, tiled=True)
 
     def comp_total(stacked):
-        spread = jnp.broadcast_to(stacked[None], (n_comp,) + stacked.shape)
-        return lax.all_to_all(spread, "comp", 0, 0, tiled=True).sum(0)
+        spread = jnp.broadcast_to(stacked[None], (n_chips,) + stacked.shape)
+        by_chip = lax.all_to_all(spread, "comp", 0, 0, tiled=True, axis_index_groups=same_core)
+        mine = by_chip.sum(0)
+        return mine + swap_with_sibling(mine)
 
     own_block = right_side.shape[0]
     residual_slab = gather_feat(right_side).reshape(RB_DEV * own_block, responses)
@@ -124,7 +126,7 @@
 
     gradient_own = reduce_gradient(backward(low_slab(residual_slab)))
     energy_own = col_sq(gradient_own)
-    direction = whole_of(lax.all_gather(gradient_own, "comp", axis=0, tiled=False))
+    direction, _ = gather_gradient(gradient_own)
     energy = None
     solution = None
     for step_index in range(ITERS):
@@ -133,14 +135,10 @@
             gradient_own = reduce_gradient(backward(low_slab(residual_slab))) - ridge * own_part(
                 solution
             )
-            gathered = lax.all_gather(
-                jnp.concatenate([gradient_own, col_sq(gradient_own)[None]], axis=0),
-                "comp",
-                axis=0,
-                tiled=False,
+            gradient, comp_energy = gather_gradient(
+                jnp.concatenate([gradient_own, col_sq(gradient_own)[None]], axis=0)
             )
-            gradient = whole_of(gathered[:, :own_rows])
-            comp_energy = jnp.sum(gathered[:, own_rows], axis=0)
+            comp_energy = comp_energy[0]
             spread = jnp.broadcast_to(comp_energy[None, None], (n_feat, 1, responses))
             next_energy = lax.all_to_all(spread, "feat", 0, 0, tiled=True).sum(0)[0]
             direction = gradient + next_energy / energy * direction
@@ -150,7 +148,8 @@
             sums = [col_sq(image_rows), col_sq(own_part(direction))]
             if energy is None:
                 sums.append(energy_own)
-            totals = total_over_mesh(jnp.stack(sums), n_comp, n_feat)
+            spread = jnp.broadcast_to(jnp.stack(sums)[None], (n_feat, len(sums), responses))
+            totals = comp_total(lax.all_to_all(spread, "feat", 0, 0, tiled=True).sum(0))
             if energy is None:
                 energy = totals[2]
             image_energy, direction_energy = totals[0], totals[1]

time: 341 us -> 340 us (level)
  starting transfers between devices: 45.6 us -> 66.9 us
  waiting for transfers between devices: 92.9 us -> 72 us
  local copies, waits for them, and re-layouts: 9.92 us -> 4.35 us
    ppermute x2 -> x7, starting transfers between devices: 14.2 us -> 48.2 us  [swap_with_sibling(): return lax.ppermute(x, 'comp', siblings)]
    all_to_all x3 -> x1, waiting for transfers between devices: 49.1 us -> 20.6 us  [reduce_gradient(): lax.all_to_all(pieces, 'comp', 0, 0, tiled=True, axis_index_groups=same_c...]
    all_to_all x3 -> x1, starting transfers between devices: 16 us -> 3.67 us  [reduce_gradient(): lax.all_to_all(pieces, 'comp', 0, 0, tiled=True, axis_index_groups=same_c...]
    all_to_all x3 -> x5, blocking collectives: 83.7 us -> 91.1 us  [the longest x1 37.3 us: reduce_gradient(): lax.all_to_all(pieces, 'comp', 0, 0, tiled=True, axis_index_groups=same_c...]
    ppermute x2 -> x7, waiting for transfers between devices: 2.83 us -> 7.29 us  [swap_with_sibling(): return lax.ppermute(x, 'comp', siblings)]
    all_gather x2, blocking collectives: 60.2 us -> 56.1 us  [gather_gradient(): lax.all_gather(own, 'comp', axis=0, tiled=False, axis_index_groups=same_c...]
  transfers between devices with their start and end apart: 8 -> 11, of which waited for: 8 -> 10; matrix products, arithmetic and copies ran while one was open for 1% -> 0% of each run, Pallas kernels for 0% -> 0%
where the time goes in v5:
time: 340 us; the launch traced here: 339 us
  blocking collectives  166 us (49%)
  waiting for transfers between devices  72 us (21%)
  starting transfers between devices  66.9 us (20%)
  Pallas kernels  19.4 us (6%)
  other arithmetic  8.58 us (3%)
  local copies, waits for them, and re-layouts  4.35 us (1%)
    all_gather x2, blocking collectives, gather_gradient(): lax.all_gather(own, 'comp', axis=0, tiled=False, axis_index_groups=same_c...  56.1 us
    ppermute x7, starting transfers between devices, swap_with_sibling(): return lax.ppermute(x, 'comp', siblings)  48.2 us
    all_to_all x1, blocking collectives, reduce_gradient(): lax.all_to_all(pieces, 'comp', 0, 0, tiled=True, axis_index_groups=same_c...  37.3 us
    all_to_all x2, blocking collectives, comp_total(): lax.all_to_all(spread, 'comp', 0, 0, tiled=True, axis_index_groups=same_c...  33.7 us
    all_to_all x2, waiting for transfers between devices, reduce_over(): return lax.all_to_all(pieces, axis, 0, 0, tiled=True).sum(0)  30.6 us
    all_to_all x1, waiting for transfers between devices, reduce_gradient(): lax.all_to_all(pieces, 'comp', 0, 0, tiled=True, axis_index_groups=same_c...  20.6 us
    pallas_call x4, Pallas kernels, block_apply(): pl.pallas_call(functools.partial(_block_kernel, transpose), out_shape=jax...  19.4 us
    all_to_all x1, blocking collectives, gather_feat(): return lax.all_to_all(spread, 'feat', 0, 0, tiled=True)  19 us
  transfers between devices with their start and end apart: 11, of which 10 were waited for; matrix products, arithmetic and copies ran while one was open for 0% of the time, Pallas kernels for 0%

profile of v5, /device:TPU:1, one launch (start us, length us, event | category | flops | bytes accessed | tf_op | source)
XLA Modules:
  0.0 339.0 jit_solution(17294067931729383040)
XLA Ops:
  0.6 1.9 broadcast_in_dim.22
  2.6 7.6 %all-to-all-start = ((f32[16,128,128]{2,1,0:T(8,128)}), f32[16,128,128]{2,1,0:T(8,128)S(1)}, u32[]{:S(2)}, u32[]{:S(2)}) async-start(f32[16,128,128]{2,1,0:T(8,128)} %broadcast_in_dim.22), calls=%async_computation | async-start | bytes 2097152 | tf_op jit(solution)/shard_map/all_to_all | solution.py:113
  10.8 13.6 %all-to-all-done = f32[16,128,128]{2,1,0:T(8,128)S(1)} async-done(((f32[16,128,128]{2,1,0:T(8,128)}), f32[16,128,128]{2,1,0:T(8,128)S(1)}, u32[]{:S(2)}, u32[]{:S(2)}) %all-to-all-start) | async-done | bytes 1048608 | tf_op jit(solution)/shard_map/all_to_all | solution.py:113
  24.4 0.8 bitcast_convert_fusion.x_ref
  25.2 5.3 %shard_map.77 = f32[1792,128]{1,0:T(8,128)} custom-call(s32[1]{0:T(128)} %bitcast.57.count_ref, s32[24]{0:T(128)} %bitcast.70, s32[24]{0:T(128)} %bitcast.74, bf16[24,128,128]{2,1,0:T(8,128)(2,1)} %bitcast.61, bf16[2048,128]{1,0:T(8,128)(2,1)} %bitcast_convert_fusion.x_ref), custom_call_target="tpu_custom_call" | custom-call | tf_op jit(solution)/shard_map/pallas_call | solution.py:43
  30.5 1.1 constant_dynamic-slice_fusion.1
  31.6 4.7 %collective-permute-start = (f32[896,128]{1,0:T(8,128)S(1)}, f32[896,128]{1,0:T(8,128)S(1)}, u32[]{:S(2)}, u32[]{:S(2)}) collective-permute-start(f32[896,128]{1,0:T(8,128)S(1)} %constant_dynamic-slice_fusion.1), channel_id=1, source_target_pairs={{0,16},{16,0},{32,48},{48,32},{64,80},{80,64},{96,112},{112,96},{1... | collective-permute-start | bytes 1376264 | tf_op jit(solution)/shard_map/ppermute | solution.py:84
  36.3 1.4 collective-permute-done
  37.8 37.3 %all_to_all.50 = f32[16,56,128]{2,1,0:T(8,128)S(1)} all-to-all(f32[16,56,128]{2,1,0:T(8,128)S(1)} %bitcast.67), channel_id=1, replica_groups={{0,32,64,96,128,160,192,224,256,288,320,352,384,416,448,480},{16,48,80,..., dimensions={0} | all-to-all | bytes 917504 | tf_op jit(solution)/shard_map/all_to_all | solution.py:91
  75.1 28.0 %all-gather = f32[896,128]{1,0:T(8,128)S(1)} all-gather(f32[56,128]{1,0:T(8,128)S(1)} %reduce_sum.148), channel_id=2, replica_groups={{0,32,64,96,128,160,192,224,256,288,320,352,384,416,448,480},{16,48,80,..., dimensions={0}, use_global_device_ids=true | all-gather | bytes 487424 | tf_op jit(solution)/shard_map/all_gather | solution.py:95
  103.1 13.6 %collective-permute-start.1 = (f32[896,128]{1,0:T(8,128)S(1)}, f32[896,128]{1,0:T(8,128)S(1)}, u32[]{:S(2)}, u32[]{:S(2)}) collective-permute-start(f32[896,128]{1,0:T(8,128)S(1)} %all-gather), channel_id=1, source_target_pairs={{0,16},{16,0},{32,48},{48,32},{64,80},{80,64},{96,112},{112,96},{1... | collective-permute-start | bytes 1376264 | tf_op jit(solution)/shard_map/ppermute | solution.py:84
  116.7 1.4 collective-permute-done.1
  118.1 0.1 broadcast_select_fusion.3
  118.2 0.8 fusion.2.x_ref
  119.0 4.4 %shard_map.78 = f32[2048,128]{1,0:T(8,128)} custom-call(s32[1]{0:T(128)} %bitcast.58.count_ref, s32[24]{0:T(128)} %bitcast.75, s32[24]{0:T(128)} %bitcast.71, bf16[24,128,128]{2,1,0:T(8,128)(2,1)} %bitcast.62, bf16[1792,128]{1,0:T(8,128)(2,1)} %fusion.2.x_ref), custom_call_target="tpu_custom_call" | custom-call | tf_op jit(solution)/shard_map/pallas_call | solution.py:43
  123.5 3.7 %all-to-all-start.2 = ((f32[16,128,128]{2,1,0:T(8,128)}), f32[16,128,128]{2,1,0:T(8,128)S(1)}, u32[]{:S(2)}, u32[]{:S(2)}) async-start(f32[16,128,128]{2,1,0:T(8,128)} %bitcast.65), calls=%async_computation.2 | async-start | bytes 2097152 | tf_op jit(solution)/shard_map/all_to_all | solution.py:54
  127.2 15.4 %all-to-all-done.2 = f32[16,128,128]{2,1,0:T(8,128)S(1)} async-done(((f32[16,128,128]{2,1,0:T(8,128)}), f32[16,128,128]{2,1,0:T(8,128)S(1)}, u32[]{:S(2)}, u32[]{:S(2)}) %all-to-all-start.2) | async-done | bytes 1048608 | tf_op jit(solution)/shard_map/all_to_all | solution.py:54
  142.7 0.1 broadcast_in_dim.25
  142.8 19.0 %all_to_all.51 = f32[16,130,128]{2,1,0:T(8,128)S(1)} all-to-all(f32[16,130,128]{2,1,0:T(8,128)S(1)} %broadcast_in_dim.25), channel_id=1, replica_groups=mesh['comp'=32,'feat'=16] {'feat'}, dimensions={0} | all-to-all | bytes 2129920 | tf_op jit(solution)/shard_map/all_to_all | solution.py:113
  161.9 0.3 fusion.12
  162.2 18.5 %all_to_all.52 = f32[16,3,128]{2,1,0:T(4,128)S(1)} all-to-all(f32[16,3,128]{2,1,0:T(4,128)S(1)} %broadcast_in_dim.27), channel_id=1, replica_groups={{0,32,64,96,128,160,192,224,256,288,320,352,384,416,448,480},{16,48,80,..., dimensions={0} | all-to-all | bytes 49152 | tf_op jit(solution)/shard_map/all_to_all | solution.py:117
  180.7 5.5 %collective-permute-start.2 = (f32[3,128]{1,0:T(4,128)S(1)}, f32[3,128]{1,0:T(4,128)S(1)}, u32[]{:S(2)}, u32[]{:S(2)}) collective-permute-start(f32[3,128]{1,0:T(4,128)S(1)} %reduce_sum.154), channel_id=1, source_target_pairs={{0,16},{16,0},{32,48},{48,32},{64,80},{80,64},{96,112},{112,96},{1... | collective-permute-start | bytes 4616 | tf_op jit(solution)/shard_map/ppermute | solution.py:84
  186.2 0.8 collective-permute-done.2
  187.0 1.3 fusion.10
  188.3 5.3 %shard_map.79 = f32[1792,128]{1,0:T(8,128)} custom-call(s32[1]{0:T(128)} %bitcast.59.count_ref, s32[24]{0:T(128)} %bitcast.72, s32[24]{0:T(128)} %bitcast.76, bf16[24,128,128]{2,1,0:T(8,128)(2,1)} %bitcast.63, bf16[2048,128]{1,0:T(8,128)(2,1)} %get-tuple-element.6.x_ref), custom_call_target="tpu_custom_call" | custom-call | tf_op jit(solution)/shard_map/pallas_call | solution.py:43
  193.6 1.1 constant_dynamic-slice_fusion
  194.7 1.9 collective-permute-start.3
  196.6 1.8 collective-permute-done.3
  198.4 0.8 dynamic-slice_add_fusion
  199.2 3.7 %all-to-all-start.5 = ((f32[16,56,128]{2,1,0:T(8,128)}), f32[16,56,128]{2,1,0:T(8,128)S(1)}, u32[]{:S(2)}, u32[]{:S(2)}) async-start(f32[16,56,128]{2,1,0:T(8,128)} %bitcast.14), calls=%async_computation.5 | async-start | bytes 917504 | tf_op jit(solution)/shard_map/all_to_all | solution.py:91
  202.9 0.1 fusion.1
  203.0 20.6 %all-to-all-done.5 = f32[16,56,128]{2,1,0:T(8,128)S(1)} async-done(((f32[16,56,128]{2,1,0:T(8,128)}), f32[16,56,128]{2,1,0:T(8,128)S(1)}, u32[]{:S(2)}, u32[]{:S(2)}) %all-to-all-start.5) | async-done | bytes 458784 | tf_op jit(solution)/shard_map/all_to_all | solution.py:91
  223.6 28.2 %all-gather.2 = f32[16,57,128]{2,1,0:T(8,128)S(1)} all-gather(f32[1,57,128]{2,1,0:T(8,128)S(1)} %maximum_bitcast_fusion), channel_id=3, replica_groups={{0,32,64,96,128,160,192,224,256,288,320,352,384,416,448,480},{16,48,80,..., dimensions={0}, use_global_device_ids=true | all-gather | bytes 496128 | tf_op jit(solution)/shard_map/all_gather | solution.py:95
  251.8 13.7 %collective-permute-start.5 = (f32[896,128]{1,0:T(8,128)S(1)}, f32[896,128]{1,0:T(8,128)S(1)}, u32[]{:S(2)}, u32[]{:S(2)}) collective-permute-start(f32[896,128]{1,0:T(8,128)S(1)} %bitcast.68), channel_id=1, source_target_pairs={{0,16},{16,0},{32,48},{48,32},{64,80},{80,64},{96,112},{112,96},{1... | collective-permute-start | bytes 1376264 | tf_op jit(solution)/shard_map/ppermute | solution.py:84
  265.6 1.9 collective-permute-start.4
  267.5 1.1 collective-permute-done.4
  268.6 9.9 %all_to_all.53 = f32[16,1,128]{2,1,0:T(1,128)S(1)} all-to-all(f32[16,1,128]{2,1,0:T(1,128)S(1)} %broadcast_in_dim.30), channel_id=1, replica_groups=mesh['comp'=32,'feat'=16] {'feat'}, dimensions={0} | all-to-all | bytes 16384 | tf_op jit(solution)/shard_map/all_to_all | solution.py:143
  278.5 0.1 broadcast_select_fusion.1
  278.6 1.2 fusion.9
  279.8 4.5 %shard_map.80 = f32[2048,128]{1,0:T(8,128)} custom-call(s32[1]{0:T(128)} %bitcast.60.count_ref, s32[24]{0:T(128)} %bitcast.77, s32[24]{0:T(128)} %bitcast.73, bf16[24,128,128]{2,1,0:T(8,128)(2,1)} %bitcast.64, bf16[1792,128]{1,0:T(8,128)(2,1)} %get-tuple-element.2.x_ref), custom_call_target="tpu_custom_call" | custom-call | tf_op jit(solution)/shard_map/pallas_call | solution.py:43
  284.3 3.8 %all-to-all-start.7 = ((f32[16,128,128]{2,1,0:T(8,128)}), f32[16,128,128]{2,1,0:T(8,128)S(1)}, u32[]{:S(2)}, u32[]{:S(2)}) async-start(f32[16,128,128]{2,1,0:T(8,128)} %bitcast.66), calls=%async_computation.7 | async-start | bytes 2097152 | tf_op jit(solution)/shard_map/all_to_all | solution.py:54
  288.1 15.2 %all-to-all-done.7 = f32[16,128,128]{2,1,0:T(8,128)S(1)} async-done(((f32[16,128,128]{2,1,0:T(8,128)}), f32[16,128,128]{2,1,0:T(8,128)S(1)}, u32[]{:S(2)}, u32[]{:S(2)}) %all-to-all-start.7) | async-done | bytes 1048608 | tf_op jit(solution)/shard_map/all_to_all | solution.py:54
  303.4 10.2 %all_to_all.54 = f32[16,2,128]{2,1,0:T(2,128)S(1)} all-to-all(f32[16,2,128]{2,1,0:T(2,128)S(1)} %broadcast_in_dim.31), channel_id=1, replica_groups=mesh['comp'=32,'feat'=16] {'feat'}, dimensions={0} | all-to-all | bytes 32768 | tf_op jit(solution)/shard_map/all_to_all | solution.py:152
  313.6 15.2 %all_to_all.55 = f32[16,2,128]{2,1,0:T(2,128)S(1)} all-to-all(f32[16,2,128]{2,1,0:T(2,128)S(1)} %broadcast_in_dim.32), channel_id=1, replica_groups={{0,32,64,96,128,160,192,224,256,288,320,352,384,416,448,480},{16,48,80,..., dimensions={0} | all-to-all | bytes 32768 | tf_op jit(solution)/shard_map/all_to_all | solution.py:117
  328.9 6.9 %collective-permute-start.6 = (f32[2,128]{1,0:T(2,128)S(1)}, f32[2,128]{1,0:T(2,128)S(1)}, u32[]{:S(2)}, u32[]{:S(2)}) collective-permute-start(f32[2,128]{1,0:T(2,128)S(1)} %reduce_sum.165), channel_id=1, source_target_pairs={{0,16},{16,0},{32,48},{48,32},{64,80},{80,64},{96,112},{112,96},{1... | collective-permute-start | bytes 3080 | tf_op jit(solution)/shard_map/ppermute | solution.py:84
  335.7 0.8 collective-permute-done.6
  336.5 1.0 multiply_add_fusion
  337.6 1.5 multiply_subtract_fusion
  (40 shorter events, 0.7 us)
Async XLA Ops:
  2.6 21.8 %all-to-all-start = ((f32[16,128,128]{2,1,0:T(8,128)}), f32[16,128,128]{2,1,0:T(8,128)S(1)}, u32[]{:S(2)}, u32[]{:S(2)}) async-start(f32[16,128,128]{2,1,0:T(8,128)} %broadcast_in_dim.22), calls=%async_computation | async-start | bytes 2097152 | tf_op jit(solution)/shard_map/all_to_all | solution.py:113
  30.5 7.2 %copy-start.1 = (f32[1792,128]{1,0:T(8,128)S(1)}, f32[1792,128]{1,0:T(8,128)}, u32[]{:S(2)}) copy-start(f32[1792,128]{1,0:T(8,128)} %shard_map.77) | copy-start | bytes 2752516
  31.6 6.1 %collective-permute-start = (f32[896,128]{1,0:T(8,128)S(1)}, f32[896,128]{1,0:T(8,128)S(1)}, u32[]{:S(2)}, u32[]{:S(2)}) collective-permute-start(f32[896,128]{1,0:T(8,128)S(1)} %constant_dynamic-slice_fusion.1), channel_id=1, source_target_pairs={{0,16},{16,0},{32,48},{48,32},{64,80},{80,64},{96,112},{112,96},{1... | collective-permute-start | bytes 1376264 | tf_op jit(solution)/shard_map/ppermute | solution.py:84
  103.1 15.0 %collective-permute-start.1 = (f32[896,128]{1,0:T(8,128)S(1)}, f32[896,128]{1,0:T(8,128)S(1)}, u32[]{:S(2)}, u32[]{:S(2)}) collective-permute-start(f32[896,128]{1,0:T(8,128)S(1)} %all-gather), channel_id=1, source_target_pairs={{0,16},{16,0},{32,48},{48,32},{64,80},{80,64},{96,112},{112,96},{1... | collective-permute-start | bytes 1376264 | tf_op jit(solution)/shard_map/ppermute | solution.py:84
  123.5 19.2 %all-to-all-start.2 = ((f32[16,128,128]{2,1,0:T(8,128)}), f32[16,128,128]{2,1,0:T(8,128)S(1)}, u32[]{:S(2)}, u32[]{:S(2)}) async-start(f32[16,128,128]{2,1,0:T(8,128)} %bitcast.65), calls=%async_computation.2 | async-start | bytes 2097152 | tf_op jit(solution)/shard_map/all_to_all | solution.py:54
  161.8 25.2 %copy-start.3 = (f32[128]{0:T(128)S(1)}, f32[128]{0:T(128)}, u32[]{:S(2)}) copy-start(f32[128]{0:T(128)} %param.11) | copy-start | bytes 1540
  180.7 6.3 %collective-permute-start.2 = (f32[3,128]{1,0:T(4,128)S(1)}, f32[3,128]{1,0:T(4,128)S(1)}, u32[]{:S(2)}, u32[]{:S(2)}) collective-permute-start(f32[3,128]{1,0:T(4,128)S(1)} %reduce_sum.154), channel_id=1, source_target_pairs={{0,16},{16,0},{32,48},{48,32},{64,80},{80,64},{96,112},{112,96},{1... | collective-permute-start | bytes 4616 | tf_op jit(solution)/shard_map/ppermute | solution.py:84
  193.6 4.8 %copy-start.2 = (f32[1792,128]{1,0:T(8,128)S(1)}, f32[1792,128]{1,0:T(8,128)}, u32[]{:S(2)}) copy-start(f32[1792,128]{1,0:T(8,128)} %shard_map.79) | copy-start | bytes 2752516
  194.7 3.7 %collective-permute-start.3 = (f32[896,128]{1,0:T(8,128)S(1)}, f32[896,128]{1,0:T(8,128)S(1)}, u32[]{:S(2)}, u32[]{:S(2)}) collective-permute-start(f32[896,128]{1,0:T(8,128)S(1)} %constant_dynamic-slice_fusion), channel_id=1, source_target_pairs={{0,16},{16,0},{32,48},{48,32},{64,80},{80,64},{96,112},{112,96},{1... | collective-permute-start | bytes 1376264 | tf_op jit(solution)/shard_map/ppermute | solution.py:84
  199.2 24.3 %all-to-all-start.5 = ((f32[16,56,128]{2,1,0:T(8,128)}), f32[16,56,128]{2,1,0:T(8,128)S(1)}, u32[]{:S(2)}, u32[]{:S(2)}) async-start(f32[16,56,128]{2,1,0:T(8,128)} %bitcast.14), calls=%async_computation.5 | async-start | bytes 917504 | tf_op jit(solution)/shard_map/all_to_all | solution.py:91
  251.8 26.7 %collective-permute-start.5 = (f32[896,128]{1,0:T(8,128)S(1)}, f32[896,128]{1,0:T(8,128)S(1)}, u32[]{:S(2)}, u32[]{:S(2)}) collective-permute-start(f32[896,128]{1,0:T(8,128)S(1)} %bitcast.68), channel_id=1, source_target_pairs={{0,16},{16,0},{32,48},{48,32},{64,80},{80,64},{96,112},{112,96},{1... | collective-permute-start | bytes 1376264 | tf_op jit(solution)/shard_map/ppermute | solution.py:84
  265.6 3.0 collective-permute-start.4
  284.3 3.8 %copy-start = (f32[1792,128]{1,0:T(8,128)S(1)}, f32[1792,128]{1,0:T(8,128)}, u32[]{:S(2)}) copy-start(f32[1792,128]{1,0:T(8,128)} %get-tuple-element.3) | copy-start | bytes 2752516
  284.3 19.0 %all-to-all-start.7 = ((f32[16,128,128]{2,1,0:T(8,128)}), f32[16,128,128]{2,1,0:T(8,128)S(1)}, u32[]{:S(2)}, u32[]{:S(2)}) async-start(f32[16,128,128]{2,1,0:T(8,128)} %bitcast.66), calls=%async_computation.7 | async-start | bytes 2097152 | tf_op jit(solution)/shard_map/all_to_all | solution.py:54
  328.9 7.7 %collective-permute-start.6 = (f32[2,128]{1,0:T(2,128)S(1)}, f32[2,128]{1,0:T(2,128)S(1)}, u32[]{:S(2)}, u32[]{:S(2)}) collective-permute-start(f32[2,128]{1,0:T(2,128)S(1)} %reduce_sum.165), channel_id=1, source_target_pairs={{0,16},{16,0},{32,48},{48,32},{64,80},{80,64},{96,112},{112,96},{1... | collective-permute-start | bytes 3080 | tf_op jit(solution)/shard_map/ppermute | solution.py:84

commit v6 on v5

--- a/solution.py
+++ b/solution.py
@@ -92,13 +92,10 @@
         return landed.sum(0)
 
     def gather_gradient(own):
-        got = lax.all_gather(own, "comp", axis=0, tiled=False, axis_index_groups=same_core)
-        half = got[:, :own_rows].reshape(half_rows, own.shape[1])
-        sums = jnp.sum(got[:, own_rows:], axis=0)
-        other_half, other_sums = swap_with_sibling((half, sums))
-        first = jnp.where(core == 0, half, other_half)
-        second = jnp.where(core == 0, other_half, half)
-        return jnp.concatenate([first, second], axis=0), sums + other_sums
+        got = lax.all_gather(own, "comp", axis=0, tiled=False)
+        by_chip = got[:, :own_rows].reshape(n_chips, 2, own_rows, own.shape[1])
+        rows = by_chip.transpose(1, 0, 2, 3).reshape(feat_rows, own.shape[1])
+        return rows, jnp.sum(got[:, own_rows:], axis=0)
 
     def own_part(full):
         return lax.dynamic_slice_in_dim(full, core * half_rows + chip * own_rows, own_rows, axis=0)
@@ -113,10 +110,8 @@
         return lax.all_to_all(spread, "feat", 0, 0, tiled=True)
 
     def comp_total(stacked):
-        spread = jnp.broadcast_to(stacked[None], (n_chips,) + stacked.shape)
-        by_chip = lax.all_to_all(spread, "comp", 0, 0, tiled=True, axis_index_groups=same_core)
-        mine = by_chip.sum(0)
-        return mine + swap_with_sibling(mine)
+        spread = jnp.broadcast_to(stacked[None], (n_comp,) + stacked.shape)
+        return lax.all_to_all(spread, "comp", 0, 0, tiled=True).sum(0)
 
     own_block = right_side.shape[0]
     residual_slab = gather_feat(right_side).reshape(RB_DEV * own_block, responses)

time: 340 us -> 332 us (0.976)
  starting transfers between devices: 66.9 us -> 38.9 us
  waiting for transfers between devices: 72 us -> 88 us
    ppermute x7 -> x2, starting transfers between devices: 48.2 us -> 8.52 us  [swap_with_sibling(): return lax.ppermute(x, 'comp', siblings)]
    all_gather x2, blocking collectives: 56.1 us -> 80.3 us  [gather_gradient(): got = lax.all_gather(own, 'comp', axis=0, tiled=False)]
    all_to_all x3 -> x1, blocking collectives: 43.6 us -> 20.6 us  [comp_total(): return lax.all_to_all(spread, 'comp', 0, 0, tiled=True).sum(0)]
    all_to_all x0 -> x2, waiting for transfers between devices: none -> 18.3 us  [the longest x1 12.1 us: comp_total(): return lax.all_to_all(spread, 'comp', 0, 0, tiled=True).sum(0)]
    all_to_all x0 -> x2, starting transfers between devices: none -> 11.9 us  [the longest x1 7.89 us: comp_total(): return lax.all_to_all(spread, 'comp', 0, 0, tiled=True).sum(0)]
    ppermute x7 -> x2, waiting for transfers between devices: 7.29 us -> 2.83 us  [swap_with_sibling(): return lax.ppermute(x, 'comp', siblings)]
  transfers between devices with their start and end apart: 11 -> 8, of which waited for: 10 -> 8; matrix products, arithmetic and copies ran while one was open for 0% -> 0% of each run, Pallas kernels for 0% -> 0%
where the time goes in v6:
time: 332 us; the launch traced here: 331 us
  blocking collectives  166 us (50%)
  waiting for transfers between devices  88 us (27%)
  starting transfers between devices  38.9 us (12%)
  Pallas kernels  22.6 us (7%)
  other arithmetic  8.18 us (2%)
  local copies, waits for them, and re-layouts  5.72 us (2%)
    all_gather x2, blocking collectives, gather_gradient(): got = lax.all_gather(own, 'comp', axis=0, tiled=False)  80.3 us
    all_to_all x1, blocking collectives, reduce_gradient(): lax.all_to_all(pieces, 'comp', 0, 0, tiled=True, axis_index_groups=same_c...  35.8 us
    all_to_all x2, waiting for transfers between devices, reduce_over(): return lax.all_to_all(pieces, axis, 0, 0, tiled=True).sum(0)  32.4 us
    pallas_call x4, Pallas kernels, block_apply(): pl.pallas_call(functools.partial(_block_kernel, transpose), out_shape=jax...  22.6 us
    all_to_all x1, waiting for transfers between devices, reduce_gradient(): lax.all_to_all(pieces, 'comp', 0, 0, tiled=True, axis_index_groups=same_c...  20.8 us
    all_to_all x1, blocking collectives, comp_total(): return lax.all_to_all(spread, 'comp', 0, 0, tiled=True).sum(0)  20.6 us
    all_to_all x1, blocking collectives, gather_feat(): return lax.all_to_all(spread, 'feat', 0, 0, tiled=True)  19.2 us
    all_to_all x1, waiting for transfers between devices, gather_feat(): return lax.all_to_all(spread, 'feat', 0, 0, tiled=True)  13.6 us
  transfers between devices with their start and end apart: 8, of which 8 were waited for; matrix products, arithmetic and copies ran while one was open for 0% of the time, Pallas kernels for 0%

profile of v6, /device:TPU:1, one launch (start us, length us, event | category | flops | bytes accessed | tf_op | source)
XLA Modules:
  0.0 331.0 jit_solution(17348309619106754785)
XLA Ops:
  0.6 1.9 broadcast_in_dim.20
  2.6 7.6 %all-to-all-start = ((f32[16,128,128]{2,1,0:T(8,128)}), f32[16,128,128]{2,1,0:T(8,128)S(1)}, u32[]{:S(2)}, u32[]{:S(2)}) async-start(f32[16,128,128]{2,1,0:T(8,128)} %broadcast_in_dim.20), calls=%async_computation | async-start | bytes 2097152 | tf_op jit(solution)/shard_map/all_to_all | solution.py:110
  10.8 13.6 %all-to-all-done = f32[16,128,128]{2,1,0:T(8,128)S(1)} async-done(((f32[16,128,128]{2,1,0:T(8,128)}), f32[16,128,128]{2,1,0:T(8,128)S(1)}, u32[]{:S(2)}, u32[]{:S(2)}) %all-to-all-start) | async-done | bytes 1048608 | tf_op jit(solution)/shard_map/all_to_all | solution.py:110
  24.4 0.8 bitcast_convert_fusion.x_ref
  25.2 6.1 %shard_map.77 = f32[1792,128]{1,0:T(8,128)} custom-call(s32[1]{0:T(128)} %bitcast.66.count_ref, s32[24]{0:T(128)} %bitcast.81, s32[24]{0:T(128)} %bitcast.85, bf16[24,128,128]{2,1,0:T(8,128)(2,1)} %bitcast.71, bf16[2048,128]{1,0:T(8,128)(2,1)} %bitcast_convert_fusion.x_ref), custom_call_target="tpu_custom_call" | custom-call | tf_op jit(solution)/shard_map/pallas_call | solution.py:43
  31.4 1.1 constant_dynamic-slice_fusion.1
  32.5 5.4 %collective-permute-start = (f32[896,128]{1,0:T(8,128)S(1)}, f32[896,128]{1,0:T(8,128)S(1)}, u32[]{:S(2)}, u32[]{:S(2)}) collective-permute-start(f32[896,128]{1,0:T(8,128)S(1)} %constant_dynamic-slice_fusion.1), channel_id=1, source_target_pairs={{0,16},{16,0},{32,48},{48,32},{64,80},{80,64},{96,112},{112,96},{1... | collective-permute-start | bytes 1376264 | tf_op jit(solution)/shard_map/ppermute | solution.py:84
  37.9 1.4 collective-permute-done
  39.4 35.8 %all_to_all.50 = f32[16,56,128]{2,1,0:T(8,128)S(1)} all-to-all(f32[16,56,128]{2,1,0:T(8,128)S(1)} %bitcast.79), channel_id=1, replica_groups={{0,32,64,96,128,160,192,224,256,288,320,352,384,416,448,480},{16,48,80,..., dimensions={0} | all-to-all | bytes 917504 | tf_op jit(solution)/shard_map/all_to_all | solution.py:91
  75.2 40.1 %all-gather = f32[1792,128]{1,0:T(8,128)S(1)} all-gather(f32[56,128]{1,0:T(8,128)S(1)} %reduce_sum.146), channel_id=2, replica_groups=mesh['comp'=32,'feat'=16] {'comp'}, dimensions={0}, use_global_device_ids=true | all-gather | bytes 946176 | tf_op jit(solution)/shard_map/all_gather | solution.py:95
  115.3 0.1 copy.15
  115.4 0.8 bitcast_convert_fusion.1.x_ref
  116.2 5.1 %shard_map.78 = f32[2048,128]{1,0:T(8,128)} custom-call(s32[1]{0:T(128)} %bitcast.67.count_ref, s32[24]{0:T(128)} %bitcast.86, s32[24]{0:T(128)} %bitcast.82, bf16[24,128,128]{2,1,0:T(8,128)(2,1)} %bitcast.72, bf16[1792,128]{1,0:T(8,128)(2,1)} %bitcast_convert_fusion.1.x_ref), custom_call_target="tpu_custom_call" | custom-call | tf_op jit(solution)/shard_map/pallas_call | solution.py:43
  121.4 3.7 %all-to-all-start.2 = ((f32[16,128,128]{2,1,0:T(8,128)}), f32[16,128,128]{2,1,0:T(8,128)S(1)}, u32[]{:S(2)}, u32[]{:S(2)}) async-start(f32[16,128,128]{2,1,0:T(8,128)} %bitcast.75), calls=%async_computation.2 | async-start | bytes 2097152 | tf_op jit(solution)/shard_map/all_to_all | solution.py:54
  125.1 17.4 %all-to-all-done.2 = f32[16,128,128]{2,1,0:T(8,128)S(1)} async-done(((f32[16,128,128]{2,1,0:T(8,128)}), f32[16,128,128]{2,1,0:T(8,128)S(1)}, u32[]{:S(2)}, u32[]{:S(2)}) %all-to-all-start.2) | async-done | bytes 1048608 | tf_op jit(solution)/shard_map/all_to_all | solution.py:54
  142.5 0.1 reduce_sum.147
  142.5 0.1 broadcast_in_dim.23
  142.6 19.2 %all_to_all.51 = f32[16,130,128]{2,1,0:T(8,128)S(1)} all-to-all(f32[16,130,128]{2,1,0:T(8,128)S(1)} %broadcast_in_dim.23), channel_id=1, replica_groups=mesh['comp'=32,'feat'=16] {'feat'}, dimensions={0} | all-to-all | bytes 2129920 | tf_op jit(solution)/shard_map/all_to_all | solution.py:110
  161.8 0.3 fusion.9
  162.1 20.6 %all_to_all.52 = f32[32,3,128]{2,1,0:T(4,128)S(1)} all-to-all(f32[32,3,128]{2,1,0:T(4,128)S(1)} %broadcast_in_dim.25), channel_id=1, replica_groups=mesh['comp'=32,'feat'=16] {'comp'}, dimensions={0} | all-to-all | bytes 98304 | tf_op jit(solution)/shard_map/all_to_all | solution.py:114
  182.8 1.3 fusion.7
  184.1 6.1 %shard_map.79 = f32[1792,128]{1,0:T(8,128)} custom-call(s32[1]{0:T(128)} %bitcast.68.count_ref, s32[24]{0:T(128)} %bitcast.83, s32[24]{0:T(128)} %bitcast.87, bf16[24,128,128]{2,1,0:T(8,128)(2,1)} %bitcast.73, bf16[2048,128]{1,0:T(8,128)(2,1)} %get-tuple-element.6.x_ref), custom_call_target="tpu_custom_call" | custom-call | tf_op jit(solution)/shard_map/pallas_call | solution.py:43
  190.2 1.1 constant_dynamic-slice_fusion
  191.4 3.1 collective-permute-start.1
  194.5 1.4 collective-permute-done.1
  195.9 0.0 copy-done.1
  195.9 0.8 dynamic-slice_add_fusion
  196.7 3.6 %all-to-all-start.5 = ((f32[16,56,128]{2,1,0:T(8,128)}), f32[16,56,128]{2,1,0:T(8,128)S(1)}, u32[]{:S(2)}, u32[]{:S(2)}) async-start(f32[16,56,128]{2,1,0:T(8,128)} %bitcast.17), calls=%async_computation.5 | async-start | bytes 917504 | tf_op jit(solution)/shard_map/all_to_all | solution.py:91
  200.3 0.1 broadcast_multiply_fusion
  200.4 20.8 %all-to-all-done.5 = f32[16,56,128]{2,1,0:T(8,128)S(1)} async-done(((f32[16,56,128]{2,1,0:T(8,128)}), f32[16,56,128]{2,1,0:T(8,128)S(1)}, u32[]{:S(2)}, u32[]{:S(2)}) %all-to-all-start.5) | async-done | bytes 458784 | tf_op jit(solution)/shard_map/all_to_all | solution.py:91
  221.3 40.2 %all-gather.2 = f32[32,57,128]{2,1,0:T(8,128)S(1)} all-gather(f32[1,57,128]{2,1,0:T(8,128)S(1)} %maximum_bitcast_fusion), channel_id=3, replica_groups=mesh['comp'=32,'feat'=16] {'comp'}, dimensions={0}, use_global_device_ids=true | all-gather | bytes 963072 | tf_op jit(solution)/shard_map/all_gather | solution.py:95
  261.5 0.1 slice_reduce_fusion
  261.6 0.6 broadcast_in_dim.27
  262.2 4.0 %all-to-all-start.6 = ((f32[16,1,128]{2,1,0:T(1,128)}), f32[16,1,128]{2,1,0:T(1,128)S(1)}, u32[]{:S(2)}, u32[]{:S(2)}) async-start(f32[16,1,128]{2,1,0:T(1,128)} %broadcast_in_dim.27), calls=%async_computation.6 | async-start | bytes 16384 | tf_op jit(solution)/shard_map/all_to_all | solution.py:138
  266.2 0.1 slice.39
  266.3 0.1 copy.18
  266.4 6.2 %all-to-all-done.6 = f32[16,1,128]{2,1,0:T(1,128)S(1)} async-done(((f32[16,1,128]{2,1,0:T(1,128)}), f32[16,1,128]{2,1,0:T(1,128)S(1)}, u32[]{:S(2)}, u32[]{:S(2)}) %all-to-all-start.6) | async-done | bytes 8224 | tf_op jit(solution)/shard_map/all_to_all | solution.py:138
  272.6 0.9 fusion.6
  273.5 5.2 %shard_map.80 = f32[2048,128]{1,0:T(8,128)} custom-call(s32[1]{0:T(128)} %bitcast.69.count_ref, s32[24]{0:T(128)} %bitcast.88, s32[24]{0:T(128)} %bitcast.84, bf16[24,128,128]{2,1,0:T(8,128)(2,1)} %bitcast.74, bf16[1792,128]{1,0:T(8,128)(2,1)} %get-tuple-element.2.x_ref), custom_call_target="tpu_custom_call" | custom-call | tf_op jit(solution)/shard_map/pallas_call | solution.py:43
  278.7 3.7 %all-to-all-start.7 = ((f32[16,128,128]{2,1,0:T(8,128)}), f32[16,128,128]{2,1,0:T(8,128)S(1)}, u32[]{:S(2)}, u32[]{:S(2)}) async-start(f32[16,128,128]{2,1,0:T(8,128)} %bitcast.76), calls=%async_computation.7 | async-start | bytes 2097152 | tf_op jit(solution)/shard_map/all_to_all | solution.py:54
  282.4 15.1 %all-to-all-done.7 = f32[16,128,128]{2,1,0:T(8,128)S(1)} async-done(((f32[16,128,128]{2,1,0:T(8,128)}), f32[16,128,128]{2,1,0:T(8,128)S(1)}, u32[]{:S(2)}, u32[]{:S(2)}) %all-to-all-start.7) | async-done | bytes 1048608 | tf_op jit(solution)/shard_map/all_to_all | solution.py:54
  297.4 0.1 reduce_sum.158
  297.5 10.3 %all_to_all.53 = f32[16,2,128]{2,1,0:T(2,128)S(1)} all-to-all(f32[16,2,128]{2,1,0:T(2,128)S(1)} %broadcast_in_dim.28), channel_id=1, replica_groups=mesh['comp'=32,'feat'=16] {'feat'}, dimensions={0} | all-to-all | bytes 32768 | tf_op jit(solution)/shard_map/all_to_all | solution.py:147
  307.8 0.6 broadcast_in_dim.29
  308.5 7.9 %all-to-all-start.9 = ((f32[32,2,128]{2,1,0:T(2,128)}), f32[32,2,128]{2,1,0:T(2,128)S(1)}, u32[]{:S(2)}, u32[]{:S(2)}) async-start(f32[32,2,128]{2,1,0:T(2,128)} %broadcast_in_dim.29), calls=%async_computation.9 | async-start | bytes 65536 | tf_op jit(solution)/shard_map/all_to_all | solution.py:114
  316.4 12.1 %all-to-all-done.9 = f32[32,2,128]{2,1,0:T(2,128)S(1)} async-done(((f32[32,2,128]{2,1,0:T(2,128)}), f32[32,2,128]{2,1,0:T(2,128)S(1)}, u32[]{:S(2)}, u32[]{:S(2)}) %all-to-all-start.9) | async-done | bytes 32800 | tf_op jit(solution)/shard_map/all_to_all | solution.py:114
  328.5 1.0 multiply_add_fusion
  329.6 1.5 multiply_subtract_fusion
  (27 shorter events, 0.5 us)
Async XLA Ops:
  2.6 21.8 %all-to-all-start = ((f32[16,128,128]{2,1,0:T(8,128)}), f32[16,128,128]{2,1,0:T(8,128)S(1)}, u32[]{:S(2)}, u32[]{:S(2)}) async-start(f32[16,128,128]{2,1,0:T(8,128)} %broadcast_in_dim.20), calls=%async_computation | async-start | bytes 2097152 | tf_op jit(solution)/shard_map/all_to_all | solution.py:110
  31.4 8.0 %copy-start = (f32[1792,128]{1,0:T(8,128)S(1)}, f32[1792,128]{1,0:T(8,128)}, u32[]{:S(2)}) copy-start(f32[1792,128]{1,0:T(8,128)} %shard_map.77) | copy-start | bytes 2752516
  32.5 6.8 %collective-permute-start = (f32[896,128]{1,0:T(8,128)S(1)}, f32[896,128]{1,0:T(8,128)S(1)}, u32[]{:S(2)}, u32[]{:S(2)}) collective-permute-start(f32[896,128]{1,0:T(8,128)S(1)} %constant_dynamic-slice_fusion.1), channel_id=1, source_target_pairs={{0,16},{16,0},{32,48},{48,32},{64,80},{80,64},{96,112},{112,96},{1... | collective-permute-start | bytes 1376264 | tf_op jit(solution)/shard_map/ppermute | solution.py:84
  121.4 21.1 %all-to-all-start.2 = ((f32[16,128,128]{2,1,0:T(8,128)}), f32[16,128,128]{2,1,0:T(8,128)S(1)}, u32[]{:S(2)}, u32[]{:S(2)}) async-start(f32[16,128,128]{2,1,0:T(8,128)} %bitcast.75), calls=%async_computation.2 | async-start | bytes 2097152 | tf_op jit(solution)/shard_map/all_to_all | solution.py:54
  161.8 21.0 %copy-start.2 = (f32[128]{0:T(128)S(1)}, f32[128]{0:T(128)}, u32[]{:S(2)}) copy-start(f32[128]{0:T(128)} %param.11) | copy-start | bytes 1540
  190.2 5.7 %copy-start.1 = (f32[1792,128]{1,0:T(8,128)S(1)}, f32[1792,128]{1,0:T(8,128)}, u32[]{:S(2)}) copy-start(f32[1792,128]{1,0:T(8,128)} %shard_map.79) | copy-start | bytes 2752516
  191.4 4.6 %collective-permute-start.1 = (f32[896,128]{1,0:T(8,128)S(1)}, f32[896,128]{1,0:T(8,128)S(1)}, u32[]{:S(2)}, u32[]{:S(2)}) collective-permute-start(f32[896,128]{1,0:T(8,128)S(1)} %constant_dynamic-slice_fusion), channel_id=1, source_target_pairs={{0,16},{16,0},{32,48},{48,32},{64,80},{80,64},{96,112},{112,96},{1... | collective-permute-start | bytes 1376264 | tf_op jit(solution)/shard_map/ppermute | solution.py:84
  196.7 24.5 %all-to-all-start.5 = ((f32[16,56,128]{2,1,0:T(8,128)}), f32[16,56,128]{2,1,0:T(8,128)S(1)}, u32[]{:S(2)}, u32[]{:S(2)}) async-start(f32[16,56,128]{2,1,0:T(8,128)} %bitcast.17), calls=%async_computation.5 | async-start | bytes 917504 | tf_op jit(solution)/shard_map/all_to_all | solution.py:91
  262.2 10.4 %all-to-all-start.6 = ((f32[16,1,128]{2,1,0:T(1,128)}), f32[16,1,128]{2,1,0:T(1,128)S(1)}, u32[]{:S(2)}, u32[]{:S(2)}) async-start(f32[16,1,128]{2,1,0:T(1,128)} %broadcast_in_dim.27), calls=%async_computation.6 | async-start | bytes 16384 | tf_op jit(solution)/shard_map/all_to_all | solution.py:138
  278.7 18.8 %all-to-all-start.7 = ((f32[16,128,128]{2,1,0:T(8,128)}), f32[16,128,128]{2,1,0:T(8,128)S(1)}, u32[]{:S(2)}, u32[]{:S(2)}) async-start(f32[16,128,128]{2,1,0:T(8,128)} %bitcast.76), calls=%async_computation.7 | async-start | bytes 2097152 | tf_op jit(solution)/shard_map/all_to_all | solution.py:54
  308.5 20.0 %all-to-all-start.9 = ((f32[32,2,128]{2,1,0:T(2,128)}), f32[32,2,128]{2,1,0:T(2,128)S(1)}, u32[]{:S(2)}, u32[]{:S(2)}) async-start(f32[32,2,128]{2,1,0:T(2,128)} %broadcast_in_dim.29), calls=%async_computation.9 | async-start | bytes 65536 | tf_op jit(solution)/shard_map/all_to_all | solution.py:114

commit v7 on v6

--- a/solution.py
+++ b/solution.py
@@ -33,7 +33,7 @@
 
         return carry
 
-    lax.fori_loop(0, values_ref.shape[0], body, 0)
+    lax.fori_loop(0, values_ref.shape[0], body, 0, unroll=True)
 
 
 def block_apply(values, count, out_idx, in_idx, x, out_blocks, transpose):

time: 332 us -> 334 us (level)
  blocking collectives: 166 us -> 172 us
where the time goes in v7:
time: 334 us; the launch traced here: 333 us
  blocking collectives  172 us (51%)
  waiting for transfers between devices  86.3 us (26%)
  starting transfers between devices  38.6 us (12%)
  Pallas kernels  20.8 us (6%)
  other arithmetic  8.18 us (2%)
  local copies, waits for them, and re-layouts  5.72 us (2%)
    all_gather x2, blocking collectives, gather_gradient(): got = lax.all_gather(own, 'comp', axis=0, tiled=False)  80.6 us
    all_to_all x1, blocking collectives, reduce_gradient(): lax.all_to_all(pieces, 'comp', 0, 0, tiled=True, axis_index_groups=same_c...  38 us
    all_to_all x2, waiting for transfers between devices, reduce_over(): return lax.all_to_all(pieces, axis, 0, 0, tiled=True).sum(0)  30.6 us
    all_to_all x1, blocking collectives, comp_total(): return lax.all_to_all(spread, 'comp', 0, 0, tiled=True).sum(0)  22.7 us
    pallas_call x4, Pallas kernels, block_apply(): pl.pallas_call(functools.partial(_block_kernel, transpose), out_shape=jax...  20.8 us
    all_to_all x1, waiting for transfers between devices, reduce_gradient(): lax.all_to_all(pieces, 'comp', 0, 0, tiled=True, axis_index_groups=same_c...  20.6 us
    all_to_all x1, blocking collectives, gather_feat(): return lax.all_to_all(spread, 'feat', 0, 0, tiled=True)  20 us
    all_to_all x1, waiting for transfers between devices, gather_feat(): return lax.all_to_all(spread, 'feat', 0, 0, tiled=True)  13.6 us
  transfers between devices with their start and end apart: 8, of which 8 were waited for; matrix products, arithmetic and copies ran while one was open for 0% of the time, Pallas kernels for 0%

profile of v7, /device:TPU:1, one launch (start us, length us, event | category | flops | bytes accessed | tf_op | source)
XLA Modules:
  0.0 333.0 jit_solution(4081380328674580370)
XLA Ops:
  0.6 1.9 broadcast_in_dim.20
  2.6 7.6 %all-to-all-start = ((f32[16,128,128]{2,1,0:T(8,128)}), f32[16,128,128]{2,1,0:T(8,128)S(1)}, u32[]{:S(2)}, u32[]{:S(2)}) async-start(f32[16,128,128]{2,1,0:T(8,128)} %broadcast_in_dim.20), calls=%async_computation | async-start | bytes 2097152 | tf_op jit(solution)/shard_map/all_to_all | solution.py:110
  10.8 13.6 %all-to-all-done = f32[16,128,128]{2,1,0:T(8,128)S(1)} async-done(((f32[16,128,128]{2,1,0:T(8,128)}), f32[16,128,128]{2,1,0:T(8,128)S(1)}, u32[]{:S(2)}, u32[]{:S(2)}) %all-to-all-start) | async-done | bytes 1048608 | tf_op jit(solution)/shard_map/all_to_all | solution.py:110
  24.4 0.8 bitcast_convert_fusion.x_ref
  25.2 5.6 %shard_map.77 = f32[1792,128]{1,0:T(8,128)} custom-call(s32[1]{0:T(128)} %bitcast.66.count_ref, s32[24]{0:T(128)} %bitcast.81, s32[24]{0:T(128)} %bitcast.85, bf16[24,128,128]{2,1,0:T(8,128)(2,1)} %bitcast.71, bf16[2048,128]{1,0:T(8,128)(2,1)} %bitcast_convert_fusion.x_ref), custom_call_target="tpu_custom_call" | custom-call | tf_op jit(solution)/shard_map/pallas_call | solution.py:43
  30.8 1.1 constant_dynamic-slice_fusion.1
  32.0 4.0 %collective-permute-start = (f32[896,128]{1,0:T(8,128)S(1)}, f32[896,128]{1,0:T(8,128)S(1)}, u32[]{:S(2)}, u32[]{:S(2)}) collective-permute-start(f32[896,128]{1,0:T(8,128)S(1)} %constant_dynamic-slice_fusion.1), channel_id=1, source_target_pairs={{0,16},{16,0},{32,48},{48,32},{64,80},{80,64},{96,112},{112,96},{1... | collective-permute-start | bytes 1376264 | tf_op jit(solution)/shard_map/ppermute | solution.py:84
  35.9 1.4 collective-permute-done
  37.4 0.0 copy-done
  37.4 38.0 %all_to_all.50 = f32[16,56,128]{2,1,0:T(8,128)S(1)} all-to-all(f32[16,56,128]{2,1,0:T(8,128)S(1)} %bitcast.79), channel_id=1, replica_groups={{0,32,64,96,128,160,192,224,256,288,320,352,384,416,448,480},{16,48,80,..., dimensions={0} | all-to-all | bytes 917504 | tf_op jit(solution)/shard_map/all_to_all | solution.py:91
  75.5 40.1 %all-gather = f32[1792,128]{1,0:T(8,128)S(1)} all-gather(f32[56,128]{1,0:T(8,128)S(1)} %reduce_sum.146), channel_id=2, replica_groups=mesh['comp'=32,'feat'=16] {'comp'}, dimensions={0}, use_global_device_ids=true | all-gather | bytes 946176 | tf_op jit(solution)/shard_map/all_gather | solution.py:95
  115.6 0.1 copy.15
  115.7 0.8 bitcast_convert_fusion.1.x_ref
  116.5 4.8 %shard_map.78 = f32[2048,128]{1,0:T(8,128)} custom-call(s32[1]{0:T(128)} %bitcast.67.count_ref, s32[24]{0:T(128)} %bitcast.86, s32[24]{0:T(128)} %bitcast.82, bf16[24,128,128]{2,1,0:T(8,128)(2,1)} %bitcast.72, bf16[1792,128]{1,0:T(8,128)(2,1)} %bitcast_convert_fusion.1.x_ref), custom_call_target="tpu_custom_call" | custom-call | tf_op jit(solution)/shard_map/pallas_call | solution.py:43
  121.3 3.7 %all-to-all-start.2 = ((f32[16,128,128]{2,1,0:T(8,128)}), f32[16,128,128]{2,1,0:T(8,128)S(1)}, u32[]{:S(2)}, u32[]{:S(2)}) async-start(f32[16,128,128]{2,1,0:T(8,128)} %bitcast.75), calls=%async_computation.2 | async-start | bytes 2097152 | tf_op jit(solution)/shard_map/all_to_all | solution.py:54
  125.0 15.7 %all-to-all-done.2 = f32[16,128,128]{2,1,0:T(8,128)S(1)} async-done(((f32[16,128,128]{2,1,0:T(8,128)}), f32[16,128,128]{2,1,0:T(8,128)S(1)}, u32[]{:S(2)}, u32[]{:S(2)}) %all-to-all-start.2) | async-done | bytes 1048608 | tf_op jit(solution)/shard_map/all_to_all | solution.py:54
  140.7 0.1 reduce_sum.147
  140.8 0.1 broadcast_in_dim.23
  140.9 20.0 %all_to_all.51 = f32[16,130,128]{2,1,0:T(8,128)S(1)} all-to-all(f32[16,130,128]{2,1,0:T(8,128)S(1)} %broadcast_in_dim.23), channel_id=1, replica_groups=mesh['comp'=32,'feat'=16] {'feat'}, dimensions={0} | all-to-all | bytes 2129920 | tf_op jit(solution)/shard_map/all_to_all | solution.py:110
  161.0 0.3 fusion.9
  161.3 22.7 %all_to_all.52 = f32[32,3,128]{2,1,0:T(4,128)S(1)} all-to-all(f32[32,3,128]{2,1,0:T(4,128)S(1)} %broadcast_in_dim.25), channel_id=1, replica_groups=mesh['comp'=32,'feat'=16] {'comp'}, dimensions={0} | all-to-all | bytes 98304 | tf_op jit(solution)/shard_map/all_to_all | solution.py:114
  184.0 1.3 fusion.7
  185.3 5.6 %shard_map.79 = f32[1792,128]{1,0:T(8,128)} custom-call(s32[1]{0:T(128)} %bitcast.68.count_ref, s32[24]{0:T(128)} %bitcast.83, s32[24]{0:T(128)} %bitcast.87, bf16[24,128,128]{2,1,0:T(8,128)(2,1)} %bitcast.73, bf16[2048,128]{1,0:T(8,128)(2,1)} %get-tuple-element.6.x_ref), custom_call_target="tpu_custom_call" | custom-call | tf_op jit(solution)/shard_map/pallas_call | solution.py:43
  190.9 1.1 constant_dynamic-slice_fusion
  192.0 1.9 collective-permute-start.1
  193.9 1.8 collective-permute-done.1
  195.7 0.8 dynamic-slice_add_fusion
  196.6 3.6 %all-to-all-start.5 = ((f32[16,56,128]{2,1,0:T(8,128)}), f32[16,56,128]{2,1,0:T(8,128)S(1)}, u32[]{:S(2)}, u32[]{:S(2)}) async-start(f32[16,56,128]{2,1,0:T(8,128)} %bitcast.17), calls=%async_computation.5 | async-start | bytes 917504 | tf_op jit(solution)/shard_map/all_to_all | solution.py:91
  200.1 0.1 broadcast_multiply_fusion
  200.2 20.6 %all-to-all-done.5 = f32[16,56,128]{2,1,0:T(8,128)S(1)} async-done(((f32[16,56,128]{2,1,0:T(8,128)}), f32[16,56,128]{2,1,0:T(8,128)S(1)}, u32[]{:S(2)}, u32[]{:S(2)}) %all-to-all-start.5) | async-done | bytes 458784 | tf_op jit(solution)/shard_map/all_to_all | solution.py:91
  220.9 40.5 %all-gather.2 = f32[32,57,128]{2,1,0:T(8,128)S(1)} all-gather(f32[1,57,128]{2,1,0:T(8,128)S(1)} %maximum_bitcast_fusion), channel_id=3, replica_groups=mesh['comp'=32,'feat'=16] {'comp'}, dimensions={0}, use_global_device_ids=true | all-gather | bytes 963072 | tf_op jit(solution)/shard_map/all_gather | solution.py:95
  261.4 0.1 slice_reduce_fusion
  261.5 0.6 broadcast_in_dim.27
  262.1 5.2 %all-to-all-start.6 = ((f32[16,1,128]{2,1,0:T(1,128)}), f32[16,1,128]{2,1,0:T(1,128)S(1)}, u32[]{:S(2)}, u32[]{:S(2)}) async-start(f32[16,1,128]{2,1,0:T(1,128)} %broadcast_in_dim.27), calls=%async_computation.6 | async-start | bytes 16384 | tf_op jit(solution)/shard_map/all_to_all | solution.py:138
  267.3 0.1 slice.39
  267.4 0.1 copy.18
  267.4 6.2 %all-to-all-done.6 = f32[16,1,128]{2,1,0:T(1,128)S(1)} async-done(((f32[16,1,128]{2,1,0:T(1,128)}), f32[16,1,128]{2,1,0:T(1,128)S(1)}, u32[]{:S(2)}, u32[]{:S(2)}) %all-to-all-start.6) | async-done | bytes 8224 | tf_op jit(solution)/shard_map/all_to_all | solution.py:138
  273.6 0.9 fusion.6
  274.5 4.8 %shard_map.80 = f32[2048,128]{1,0:T(8,128)} custom-call(s32[1]{0:T(128)} %bitcast.69.count_ref, s32[24]{0:T(128)} %bitcast.88, s32[24]{0:T(128)} %bitcast.84, bf16[24,128,128]{2,1,0:T(8,128)(2,1)} %bitcast.74, bf16[1792,128]{1,0:T(8,128)(2,1)} %get-tuple-element.2.x_ref), custom_call_target="tpu_custom_call" | custom-call | tf_op jit(solution)/shard_map/pallas_call | solution.py:43
  279.4 3.7 %all-to-all-start.7 = ((f32[16,128,128]{2,1,0:T(8,128)}), f32[16,128,128]{2,1,0:T(8,128)S(1)}, u32[]{:S(2)}, u32[]{:S(2)}) async-start(f32[16,128,128]{2,1,0:T(8,128)} %bitcast.76), calls=%async_computation.7 | async-start | bytes 2097152 | tf_op jit(solution)/shard_map/all_to_all | solution.py:54
  283.1 14.9 %all-to-all-done.7 = f32[16,128,128]{2,1,0:T(8,128)S(1)} async-done(((f32[16,128,128]{2,1,0:T(8,128)}), f32[16,128,128]{2,1,0:T(8,128)S(1)}, u32[]{:S(2)}, u32[]{:S(2)}) %all-to-all-start.7) | async-done | bytes 1048608 | tf_op jit(solution)/shard_map/all_to_all | solution.py:54
  298.0 0.1 reduce_sum.158
  298.1 10.4 %all_to_all.53 = f32[16,2,128]{2,1,0:T(2,128)S(1)} all-to-all(f32[16,2,128]{2,1,0:T(2,128)S(1)} %broadcast_in_dim.28), channel_id=1, replica_groups=mesh['comp'=32,'feat'=16] {'feat'}, dimensions={0} | all-to-all | bytes 32768 | tf_op jit(solution)/shard_map/all_to_all | solution.py:147
  308.6 0.6 broadcast_in_dim.29
  309.2 9.1 %all-to-all-start.9 = ((f32[32,2,128]{2,1,0:T(2,128)}), f32[32,2,128]{2,1,0:T(2,128)S(1)}, u32[]{:S(2)}, u32[]{:S(2)}) async-start(f32[32,2,128]{2,1,0:T(2,128)} %broadcast_in_dim.29), calls=%async_computation.9 | async-start | bytes 65536 | tf_op jit(solution)/shard_map/all_to_all | solution.py:114
  318.3 12.1 %all-to-all-done.9 = f32[32,2,128]{2,1,0:T(2,128)S(1)} async-done(((f32[32,2,128]{2,1,0:T(2,128)}), f32[32,2,128]{2,1,0:T(2,128)S(1)}, u32[]{:S(2)}, u32[]{:S(2)}) %all-to-all-start.9) | async-done | bytes 32800 | tf_op jit(solution)/shard_map/all_to_all | solution.py:114
  330.5 1.0 multiply_add_fusion
  331.5 1.5 multiply_subtract_fusion
  (27 shorter events, 0.5 us)
Async XLA Ops:
  2.6 21.8 %all-to-all-start = ((f32[16,128,128]{2,1,0:T(8,128)}), f32[16,128,128]{2,1,0:T(8,128)S(1)}, u32[]{:S(2)}, u32[]{:S(2)}) async-start(f32[16,128,128]{2,1,0:T(8,128)} %broadcast_in_dim.20), calls=%async_computation | async-start | bytes 2097152 | tf_op jit(solution)/shard_map/all_to_all | solution.py:110
  30.8 6.5 %copy-start = (f32[1792,128]{1,0:T(8,128)S(1)}, f32[1792,128]{1,0:T(8,128)}, u32[]{:S(2)}) copy-start(f32[1792,128]{1,0:T(8,128)} %shard_map.77) | copy-start | bytes 2752516
  32.0 5.4 %collective-permute-start = (f32[896,128]{1,0:T(8,128)S(1)}, f32[896,128]{1,0:T(8,128)S(1)}, u32[]{:S(2)}, u32[]{:S(2)}) collective-permute-start(f32[896,128]{1,0:T(8,128)S(1)} %constant_dynamic-slice_fusion.1), channel_id=1, source_target_pairs={{0,16},{16,0},{32,48},{48,32},{64,80},{80,64},{96,112},{112,96},{1... | collective-permute-start | bytes 1376264 | tf_op jit(solution)/shard_map/ppermute | solution.py:84
  121.3 19.5 %all-to-all-start.2 = ((f32[16,128,128]{2,1,0:T(8,128)}), f32[16,128,128]{2,1,0:T(8,128)S(1)}, u32[]{:S(2)}, u32[]{:S(2)}) async-start(f32[16,128,128]{2,1,0:T(8,128)} %bitcast.75), calls=%async_computation.2 | async-start | bytes 2097152 | tf_op jit(solution)/shard_map/all_to_all | solution.py:54
  160.9 23.0 %copy-start.2 = (f32[128]{0:T(128)S(1)}, f32[128]{0:T(128)}, u32[]{:S(2)}) copy-start(f32[128]{0:T(128)} %param.11) | copy-start | bytes 1540
  190.9 4.8 %copy-start.1 = (f32[1792,128]{1,0:T(8,128)S(1)}, f32[1792,128]{1,0:T(8,128)}, u32[]{:S(2)}) copy-start(f32[1792,128]{1,0:T(8,128)} %shard_map.79) | copy-start | bytes 2752516
  192.0 3.7 %collective-permute-start.1 = (f32[896,128]{1,0:T(8,128)S(1)}, f32[896,128]{1,0:T(8,128)S(1)}, u32[]{:S(2)}, u32[]{:S(2)}) collective-permute-start(f32[896,128]{1,0:T(8,128)S(1)} %constant_dynamic-slice_fusion), channel_id=1, source_target_pairs={{0,16},{16,0},{32,48},{48,32},{64,80},{80,64},{96,112},{112,96},{1... | collective-permute-start | bytes 1376264 | tf_op jit(solution)/shard_map/ppermute | solution.py:84
  196.6 24.3 %all-to-all-start.5 = ((f32[16,56,128]{2,1,0:T(8,128)}), f32[16,56,128]{2,1,0:T(8,128)S(1)}, u32[]{:S(2)}, u32[]{:S(2)}) async-start(f32[16,56,128]{2,1,0:T(8,128)} %bitcast.17), calls=%async_computation.5 | async-start | bytes 917504 | tf_op jit(solution)/shard_map/all_to_all | solution.py:91
  262.1 11.5 %all-to-all-start.6 = ((f32[16,1,128]{2,1,0:T(1,128)}), f32[16,1,128]{2,1,0:T(1,128)S(1)}, u32[]{:S(2)}, u32[]{:S(2)}) async-start(f32[16,1,128]{2,1,0:T(1,128)} %broadcast_in_dim.27), calls=%async_computation.6 | async-start | bytes 16384 | tf_op jit(solution)/shard_map/all_to_all | solution.py:138
  279.4 18.6 %all-to-all-start.7 = ((f32[16,128,128]{2,1,0:T(8,128)}), f32[16,128,128]{2,1,0:T(8,128)S(1)}, u32[]{:S(2)}, u32[]{:S(2)}) async-start(f32[16,128,128]{2,1,0:T(8,128)} %bitcast.76), calls=%async_computation.7 | async-start | bytes 2097152 | tf_op jit(solution)/shard_map/all_to_all | solution.py:54
  309.2 21.2 %all-to-all-start.9 = ((f32[32,2,128]{2,1,0:T(2,128)}), f32[32,2,128]{2,1,0:T(2,128)S(1)}, u32[]{:S(2)}, u32[]{:S(2)}) async-start(f32[32,2,128]{2,1,0:T(2,128)} %broadcast_in_dim.29), calls=%async_computation.9 | async-start | bytes 65536 | tf_op jit(solution)/shard_map/all_to_all | solution.py:114

commit v8 on v7

--- a/solution.py
+++ b/solution.py
@@ -68,10 +68,17 @@
     def backward(low_slab):
         return block_apply(values, count_of_slots, slot_cols, slot_rows, low_slab, CB_DEV, True)
 
-    def forward(direction):
+    def forward(direction, extra=None):
         low = direction.astype(jnp.bfloat16)
         summed = block_apply(values, count_of_slots, slot_rows, slot_cols, low, RB_DEV, False)
-        return reduce_over(summed, "feat", n_feat)
+        if extra is None:
+            return reduce_over(summed, "feat", n_feat)
+        pieces = summed.reshape(n_feat, -1, summed.shape[1])
+        spread = jnp.broadcast_to(extra[None], (n_feat,) + extra.shape)
+        landed = lax.all_to_all(
+            jnp.concatenate([pieces, spread], axis=1), "feat", 0, 0, tiled=True
+        ).sum(0)
+        return landed[: pieces.shape[1]], landed[pieces.shape[1] :]
 
     core = comp_index % 2
     chip = comp_index // 2
@@ -133,12 +140,14 @@
             gradient, comp_energy = gather_gradient(
                 jnp.concatenate([gradient_own, col_sq(gradient_own)[None]], axis=0)
             )
-            comp_energy = comp_energy[0]
-            spread = jnp.broadcast_to(comp_energy[None, None], (n_feat, 1, responses))
-            next_energy = lax.all_to_all(spread, "feat", 0, 0, tiled=True).sum(0)[0]
-            direction = gradient + next_energy / energy * direction
+            gradient_image, next_energy = forward(gradient, comp_energy)
+            next_energy = next_energy[0]
+            conjugate = next_energy / energy
+            direction = gradient + conjugate * direction
+            image_rows = gradient_image + conjugate * image_rows
             energy = next_energy
-        image_rows = forward(direction)
+        else:
+            image_rows = forward(direction)
         if last:
             sums = [col_sq(image_rows), col_sq(own_part(direction))]
             if energy is None:
@@ -166,6 +175,7 @@
             residual = own_residual - step_size * image_rows
         else:
             residual_slab = residual_slab - step_size * image_slab
+            image_rows = lax.dynamic_slice_in_dim(image_slab, feat_index * own_block, own_block)
     return (solution, residual)
 
 

time: 334 us -> 328 us (0.982)
  waiting for transfers between devices: 86.3 us -> 69.3 us
  blocking collectives: 172 us -> 187 us
  starting transfers between devices: 38.6 us -> 28.7 us
  other arithmetic: 8.18 us -> 14.6 us
    all_to_all x1 -> x2, blocking collectives: 22.7 us -> 40.3 us  [comp_total(): return lax.all_to_all(spread, 'comp', 0, 0, tiled=True).sum(0)]
    all_to_all x2 -> x1, waiting for transfers between devices: 30.6 us -> 16 us  [reduce_over(): return lax.all_to_all(pieces, axis, 0, 0, tiled=True).sum(0)]
    all_to_all x2 -> x1, starting transfers between devices: 14.3 us -> 4.95 us  [forward(): lax.all_to_all(jnp.concatenate([pieces, spread], axis=1), 'feat', 0, 0, t...]
    all_to_all x2 -> x1, starting transfers between devices: 7.31 us -> 4.12 us  [reduce_over(): return lax.all_to_all(pieces, axis, 0, 0, tiled=True).sum(0)]
    all_to_all x2 -> x1, waiting for transfers between devices: 18.3 us -> 17 us  [forward(): lax.all_to_all(jnp.concatenate([pieces, spread], axis=1), 'feat', 0, 0, t...]
  transfers between devices with their start and end apart: 8 -> 6, of which waited for: 8 -> 6; matrix products, arithmetic and copies ran while one was open for 0% -> 0% of each run, Pallas kernels for 0% -> 0%
where the time goes in v8:
time: 328 us; the launch traced here: 327 us
  blocking collectives  187 us (57%)
  waiting for transfers between devices  69.3 us (21%)
  starting transfers between devices  28.7 us (9%)
  Pallas kernels  20.8 us (6%)
  other arithmetic  14.6 us (4%)
  local copies, waits for them, and re-layouts  5.43 us (2%)
    all_gather x2, blocking collectives, gather_gradient(): got = lax.all_gather(own, 'comp', axis=0, tiled=False)  80.3 us
    all_to_all x2, blocking collectives, comp_total(): return lax.all_to_all(spread, 'comp', 0, 0, tiled=True).sum(0)  40.3 us
    all_to_all x1, blocking collectives, reduce_gradient(): lax.all_to_all(pieces, 'comp', 0, 0, tiled=True, axis_index_groups=same_c...  35.7 us
    pallas_call x4, Pallas kernels, block_apply(): pl.pallas_call(functools.partial(_block_kernel, transpose), out_shape=jax...  20.8 us
    all_to_all x1, blocking collectives, gather_feat(): return lax.all_to_all(spread, 'feat', 0, 0, tiled=True)  19.9 us
    all_to_all x1, waiting for transfers between devices, reduce_gradient(): lax.all_to_all(pieces, 'comp', 0, 0, tiled=True, axis_index_groups=same_c...  19.9 us
    all_to_all x1, waiting for transfers between devices, forward(): lax.all_to_all(jnp.concatenate([pieces, spread], axis=1), 'feat', 0, 0, t...  17 us
    all_to_all x1, waiting for transfers between devices, reduce_over(): return lax.all_to_all(pieces, axis, 0, 0, tiled=True).sum(0)  16 us
  transfers between devices with their start and end apart: 6, of which 6 were waited for; matrix products, arithmetic and copies ran while one was open for 0% of the time, Pallas kernels for 0%

profile of v8, /device:TPU:1, one launch (start us, length us, event | category | flops | bytes accessed | tf_op | source)
XLA Modules:
  0.0 327.2 jit_solution(12109671410716947725)
XLA Ops:
  0.6 1.9 broadcast_in_dim.20
  2.6 7.6 %all-to-all-start = ((f32[16,128,128]{2,1,0:T(8,128)}), f32[16,128,128]{2,1,0:T(8,128)S(1)}, u32[]{:S(2)}, u32[]{:S(2)}) async-start(f32[16,128,128]{2,1,0:T(8,128)} %broadcast_in_dim.20), calls=%async_computation | async-start | bytes 2097152 | tf_op jit(solution)/shard_map/all_to_all | solution.py:117
  10.8 13.6 %all-to-all-done = f32[16,128,128]{2,1,0:T(8,128)S(1)} async-done(((f32[16,128,128]{2,1,0:T(8,128)}), f32[16,128,128]{2,1,0:T(8,128)S(1)}, u32[]{:S(2)}, u32[]{:S(2)}) %all-to-all-start) | async-done | bytes 1048608 | tf_op jit(solution)/shard_map/all_to_all | solution.py:117
  24.4 0.8 bitcast_convert_fusion.x_ref
  25.2 5.6 %shard_map.77 = f32[1792,128]{1,0:T(8,128)} custom-call(s32[1]{0:T(128)} %bitcast.60.count_ref, s32[24]{0:T(128)} %bitcast.76, s32[24]{0:T(128)} %bitcast.80, bf16[24,128,128]{2,1,0:T(8,128)(2,1)} %bitcast.65, bf16[2048,128]{1,0:T(8,128)(2,1)} %bitcast_convert_fusion.x_ref), custom_call_target="tpu_custom_call" | custom-call | tf_op jit(solution)/shard_map/pallas_call | solution.py:43
  30.8 1.1 constant_dynamic-slice_fusion.1
  32.0 5.4 %collective-permute-start = (f32[896,128]{1,0:T(8,128)S(1)}, f32[896,128]{1,0:T(8,128)S(1)}, u32[]{:S(2)}, u32[]{:S(2)}) collective-permute-start(f32[896,128]{1,0:T(8,128)S(1)} %constant_dynamic-slice_fusion.1), channel_id=1, source_target_pairs={{0,16},{16,0},{32,48},{48,32},{64,80},{80,64},{96,112},{112,96},{1... | collective-permute-start | bytes 1376264 | tf_op jit(solution)/shard_map/ppermute | solution.py:91
  37.4 1.4 collective-permute-done
  38.8 35.7 %all_to_all.45 = f32[16,56,128]{2,1,0:T(8,128)S(1)} all-to-all(f32[16,56,128]{2,1,0:T(8,128)S(1)} %bitcast.75), channel_id=1, replica_groups={{0,32,64,96,128,160,192,224,256,288,320,352,384,416,448,480},{16,48,80,..., dimensions={0} | all-to-all | bytes 917504 | tf_op jit(solution)/shard_map/all_to_all | solution.py:98
  74.6 40.1 %all-gather = f32[1792,128]{1,0:T(8,128)S(1)} all-gather(f32[56,128]{1,0:T(8,128)S(1)} %reduce_sum.135), channel_id=2, replica_groups=mesh['comp'=32,'feat'=16] {'comp'}, dimensions={0}, use_global_device_ids=true | all-gather | bytes 946176 | tf_op jit(solution)/shard_map/all_gather | solution.py:102
  114.7 0.1 copy.15
  114.8 0.8 bitcast_convert_fusion.2.x_ref
  115.6 4.8 %shard_map.78 = f32[2048,128]{1,0:T(8,128)} custom-call(s32[1]{0:T(128)} %bitcast.61.count_ref, s32[24]{0:T(128)} %bitcast.81, s32[24]{0:T(128)} %bitcast.77, bf16[24,128,128]{2,1,0:T(8,128)(2,1)} %bitcast.66, bf16[1792,128]{1,0:T(8,128)(2,1)} %bitcast_convert_fusion.2.x_ref), custom_call_target="tpu_custom_call" | custom-call | tf_op jit(solution)/shard_map/pallas_call | solution.py:43
  120.4 4.1 %all-to-all-start.2 = ((f32[16,128,128]{2,1,0:T(8,128)}), f32[16,128,128]{2,1,0:T(8,128)S(1)}, u32[]{:S(2)}, u32[]{:S(2)}) async-start(f32[16,128,128]{2,1,0:T(8,128)} %bitcast.71), calls=%async_computation.2 | async-start | bytes 2097152 | tf_op jit(solution)/shard_map/all_to_all | solution.py:54
  124.6 16.0 %all-to-all-done.2 = f32[16,128,128]{2,1,0:T(8,128)S(1)} async-done(((f32[16,128,128]{2,1,0:T(8,128)}), f32[16,128,128]{2,1,0:T(8,128)S(1)}, u32[]{:S(2)}, u32[]{:S(2)}) %all-to-all-start.2) | async-done | bytes 1048608 | tf_op jit(solution)/shard_map/all_to_all | solution.py:54
  140.6 0.1 reduce_sum.136
  140.7 0.1 broadcast_in_dim.23
  140.8 19.9 %all_to_all.46 = f32[16,130,128]{2,1,0:T(8,128)S(1)} all-to-all(f32[16,130,128]{2,1,0:T(8,128)S(1)} %broadcast_in_dim.23), channel_id=1, replica_groups=mesh['comp'=32,'feat'=16] {'feat'}, dimensions={0} | all-to-all | bytes 2129920 | tf_op jit(solution)/shard_map/all_to_all | solution.py:117
  160.7 0.3 fusion.5
  161.1 21.1 %all_to_all.47 = f32[32,3,128]{2,1,0:T(4,128)S(1)} all-to-all(f32[32,3,128]{2,1,0:T(4,128)S(1)} %broadcast_in_dim.25), channel_id=1, replica_groups=mesh['comp'=32,'feat'=16] {'comp'}, dimensions={0} | all-to-all | bytes 98304 | tf_op jit(solution)/shard_map/all_to_all | solution.py:121
  182.2 0.0 copy-done.3
  182.2 1.3 fusion.4
  183.5 5.6 %shard_map.79 = f32[1792,128]{1,0:T(8,128)} custom-call(s32[1]{0:T(128)} %bitcast.62.count_ref, s32[24]{0:T(128)} %bitcast.78, s32[24]{0:T(128)} %bitcast.82, bf16[24,128,128]{2,1,0:T(8,128)(2,1)} %bitcast.67, bf16[2048,128]{1,0:T(8,128)(2,1)} %get-tuple-element.4.x_ref), custom_call_target="tpu_custom_call" | custom-call | tf_op jit(solution)/shard_map/pallas_call | solution.py:43
  189.1 1.1 constant_dynamic-slice_fusion
  190.3 3.1 collective-permute-start.1
  193.4 1.4 collective-permute-done.1
  194.8 0.8 dynamic-slice_add_fusion
  195.7 3.6 %all-to-all-start.5 = ((f32[16,56,128]{2,1,0:T(8,128)}), f32[16,56,128]{2,1,0:T(8,128)S(1)}, u32[]{:S(2)}, u32[]{:S(2)}) async-start(f32[16,56,128]{2,1,0:T(8,128)} %bitcast.17), calls=%async_computation.5 | async-start | bytes 917504 | tf_op jit(solution)/shard_map/all_to_all | solution.py:98
  199.2 1.0 broadcast_multiply_fusion
  200.2 19.9 %all-to-all-done.5 = f32[16,56,128]{2,1,0:T(8,128)S(1)} async-done(((f32[16,56,128]{2,1,0:T(8,128)}), f32[16,56,128]{2,1,0:T(8,128)S(1)}, u32[]{:S(2)}, u32[]{:S(2)}) %all-to-all-start.5) | async-done | bytes 458784 | tf_op jit(solution)/shard_map/all_to_all | solution.py:98
  220.2 0.8 multiply_reduce_fusion.3
  221.0 40.2 %all-gather.2 = f32[32,57,128]{2,1,0:T(8,128)S(1)} all-gather(f32[1,57,128]{2,1,0:T(8,128)S(1)} %maximum_bitcast_fusion), channel_id=3, replica_groups=mesh['comp'=32,'feat'=16] {'comp'}, dimensions={0}, use_global_device_ids=true | all-gather | bytes 963072 | tf_op jit(solution)/shard_map/all_gather | solution.py:102
  261.2 0.1 slice_reduce_fusion
  261.2 0.1 slice.46
  261.3 0.1 copy.17
  261.4 0.8 bitcast_convert_fusion.1.x_ref
  262.2 4.8 %shard_map.80 = f32[2048,128]{1,0:T(8,128)} custom-call(s32[1]{0:T(128)} %bitcast.63.count_ref, s32[24]{0:T(128)} %bitcast.83, s32[24]{0:T(128)} %bitcast.79, bf16[24,128,128]{2,1,0:T(8,128)(2,1)} %bitcast.68, bf16[1792,128]{1,0:T(8,128)(2,1)} %bitcast_convert_fusion.1.x_ref), custom_call_target="tpu_custom_call" | custom-call | tf_op jit(solution)/shard_map/pallas_call | solution.py:43
  267.0 2.3 pad_maximum_fusion
  269.3 4.9 %all-to-all-start.6 = ((f32[16,129,128]{2,1,0:T(8,128)}), f32[16,129,128]{2,1,0:T(8,128)}, u32[]{:S(2)}, u32[]{:S(2)}) async-start(f32[16,129,128]{2,1,0:T(8,128)} %pad_maximum_fusion), calls=%async_computation.6 | async-start | bytes 2228224 | tf_op jit(solution)/shard_map/all_to_all | solution.py:78
  274.3 17.0 %all-to-all-done.6 = f32[16,129,128]{2,1,0:T(8,128)} async-done(((f32[16,129,128]{2,1,0:T(8,128)}), f32[16,129,128]{2,1,0:T(8,128)}, u32[]{:S(2)}, u32[]{:S(2)}) %all-to-all-start.6) | async-done | bytes 1056800 | tf_op jit(solution)/shard_map/all_to_all | solution.py:78
  291.2 1.3 reduce_sum.145
  292.6 0.1 bitcast_add_fusion
  292.7 0.0 copy-start
  292.7 0.9 copy-done
  293.7 10.5 %all_to_all.48 = f32[16,2,128]{2,1,0:T(2,128)S(1)} all-to-all(f32[16,2,128]{2,1,0:T(2,128)S(1)} %broadcast_in_dim.28), channel_id=1, replica_groups=mesh['comp'=32,'feat'=16] {'feat'}, dimensions={0} | all-to-all | bytes 32768 | tf_op jit(solution)/shard_map/all_to_all | solution.py:156
  304.2 19.2 %all_to_all.49 = f32[32,2,128]{2,1,0:T(2,128)S(1)} all-to-all(f32[32,2,128]{2,1,0:T(2,128)S(1)} %broadcast_in_dim.29), channel_id=1, replica_groups=mesh['comp'=32,'feat'=16] {'comp'}, dimensions={0} | all-to-all | bytes 65536 | tf_op jit(solution)/shard_map/all_to_all | solution.py:121
  323.5 2.2 multiply_add_fusion
  325.7 1.5 multiply_subtract_fusion
  (27 shorter events, 0.5 us)
Async XLA Ops:
  2.6 21.8 %all-to-all-start = ((f32[16,128,128]{2,1,0:T(8,128)}), f32[16,128,128]{2,1,0:T(8,128)S(1)}, u32[]{:S(2)}, u32[]{:S(2)}) async-start(f32[16,128,128]{2,1,0:T(8,128)} %broadcast_in_dim.20), calls=%async_computation | async-start | bytes 2097152 | tf_op jit(solution)/shard_map/all_to_all | solution.py:117
  30.8 8.0 %copy-start.1 = (f32[1792,128]{1,0:T(8,128)S(1)}, f32[1792,128]{1,0:T(8,128)}, u32[]{:S(2)}) copy-start(f32[1792,128]{1,0:T(8,128)} %shard_map.77) | copy-start | bytes 2752516
  32.0 6.8 %collective-permute-start = (f32[896,128]{1,0:T(8,128)S(1)}, f32[896,128]{1,0:T(8,128)S(1)}, u32[]{:S(2)}, u32[]{:S(2)}) collective-permute-start(f32[896,128]{1,0:T(8,128)S(1)} %constant_dynamic-slice_fusion.1), channel_id=1, source_target_pairs={{0,16},{16,0},{32,48},{48,32},{64,80},{80,64},{96,112},{112,96},{1... | collective-permute-start | bytes 1376264 | tf_op jit(solution)/shard_map/ppermute | solution.py:91
  120.4 20.2 %all-to-all-start.2 = ((f32[16,128,128]{2,1,0:T(8,128)}), f32[16,128,128]{2,1,0:T(8,128)S(1)}, u32[]{:S(2)}, u32[]{:S(2)}) async-start(f32[16,128,128]{2,1,0:T(8,128)} %bitcast.71), calls=%async_computation.2 | async-start | bytes 2097152 | tf_op jit(solution)/shard_map/all_to_all | solution.py:54
  160.7 21.5 %copy-start.3 = (f32[128]{0:T(128)S(1)}, f32[128]{0:T(128)}, u32[]{:S(2)}) copy-start(f32[128]{0:T(128)} %param.11) | copy-start | bytes 1540
  189.1 5.7 %copy-start.2 = (f32[1792,128]{1,0:T(8,128)S(1)}, f32[1792,128]{1,0:T(8,128)}, u32[]{:S(2)}) copy-start(f32[1792,128]{1,0:T(8,128)} %shard_map.79) | copy-start | bytes 2752516
  190.3 4.6 %collective-permute-start.1 = (f32[896,128]{1,0:T(8,128)S(1)}, f32[896,128]{1,0:T(8,128)S(1)}, u32[]{:S(2)}, u32[]{:S(2)}) collective-permute-start(f32[896,128]{1,0:T(8,128)S(1)} %constant_dynamic-slice_fusion), channel_id=1, source_target_pairs={{0,16},{16,0},{32,48},{48,32},{64,80},{80,64},{96,112},{112,96},{1... | collective-permute-start | bytes 1376264 | tf_op jit(solution)/shard_map/ppermute | solution.py:91
  195.7 24.5 %all-to-all-start.5 = ((f32[16,56,128]{2,1,0:T(8,128)}), f32[16,56,128]{2,1,0:T(8,128)S(1)}, u32[]{:S(2)}, u32[]{:S(2)}) async-start(f32[16,56,128]{2,1,0:T(8,128)} %bitcast.17), calls=%async_computation.5 | async-start | bytes 917504 | tf_op jit(solution)/shard_map/all_to_all | solution.py:98
  269.3 21.9 %all-to-all-start.6 = ((f32[16,129,128]{2,1,0:T(8,128)}), f32[16,129,128]{2,1,0:T(8,128)}, u32[]{:S(2)}, u32[]{:S(2)}) async-start(f32[16,129,128]{2,1,0:T(8,128)} %pad_maximum_fusion), calls=%async_computation.6 | async-start | bytes 2228224 | tf_op jit(solution)/shard_map/all_to_all | solution.py:78
  292.7 0.9 copy-start

commit v9 on v8

--- a/solution.py
+++ b/solution.py
@@ -12,15 +12,20 @@
 ITERS = 2
 
 
-def _block_kernel(transpose, count_ref, out_idx_ref, in_idx_ref, values_ref, x_ref, out_ref):
+def _block_kernel(transpose, pitch, count_ref, out_idx_ref, in_idx_ref, values_ref, x_ref, *rest):
     edge = values_ref.shape[1]
+    out_ref = rest[-1]
     out_ref[...] = jnp.zeros_like(out_ref)
+    if len(rest) == 2:
+        extra_ref = rest[0]
+        for b in range(out_ref.shape[0] // pitch):
+            out_ref[pl.ds(b * pitch + edge, pitch - edge), :] = extra_ref[...]
 
     def body(s, carry):
         @pl.when(s < count_ref[0])
         def _():
             src = pl.multiple_of(in_idx_ref[s] * edge, edge)
-            dst = pl.multiple_of(out_idx_ref[s] * edge, edge)
+            dst = pl.multiple_of(out_idx_ref[s] * pitch, 8)
             block = values_ref[s]
             x = x_ref[pl.ds(src, edge), :]
             if transpose:
@@ -36,16 +41,20 @@
     lax.fori_loop(0, values_ref.shape[0], body, 0, unroll=True)
 
 
-def block_apply(values, count, out_idx, in_idx, x, out_blocks, transpose):
+def block_apply(values, count, out_idx, in_idx, x, out_blocks, transpose, extra=None):
     edge = values.shape[1]
+    pitch = edge if extra is None else edge + extra.shape[0]
     smem = pl.BlockSpec(memory_space=pltpu.SMEM)
     vmem = pl.BlockSpec(memory_space=pltpu.VMEM)
+    operands = [count.reshape(1), out_idx, in_idx, values, x]
+    if extra is not None:
+        operands.append(extra)
     return pl.pallas_call(
-        functools.partial(_block_kernel, transpose),
-        out_shape=jax.ShapeDtypeStruct((out_blocks * edge, x.shape[1]), jnp.float32),
-        in_specs=[smem, smem, smem, vmem, vmem],
+        functools.partial(_block_kernel, transpose, pitch),
+        out_shape=jax.ShapeDtypeStruct((out_blocks * pitch, x.shape[1]), jnp.float32),
+        in_specs=[smem, smem, smem] + [vmem] * (len(operands) - 3),
         out_specs=vmem,
-    )(count.reshape(1), out_idx, in_idx, values, x)
+    )(*operands)
 
 
 def reduce_over(partial, axis, parts):
@@ -70,15 +79,15 @@
 
     def forward(direction, extra=None):
         low = direction.astype(jnp.bfloat16)
-        summed = block_apply(values, count_of_slots, slot_rows, slot_cols, low, RB_DEV, False)
         if extra is None:
+            summed = block_apply(values, count_of_slots, slot_rows, slot_cols, low, RB_DEV, False)
             return reduce_over(summed, "feat", n_feat)
-        pieces = summed.reshape(n_feat, -1, summed.shape[1])
-        spread = jnp.broadcast_to(extra[None], (n_feat,) + extra.shape)
-        landed = lax.all_to_all(
-            jnp.concatenate([pieces, spread], axis=1), "feat", 0, 0, tiled=True
-        ).sum(0)
-        return landed[: pieces.shape[1]], landed[pieces.shape[1] :]
+        padded = jnp.zeros((8, extra.shape[1]), extra.dtype).at[: extra.shape[0]].set(extra)
+        summed = block_apply(
+            values, count_of_slots, slot_rows, slot_cols, low, RB_DEV, False, extra=padded
+        )
+        landed = reduce_over(summed, "feat", n_feat)
+        return landed[:block_edge], landed[block_edge : block_edge + extra.shape[0]]
 
     core = comp_index % 2
     chip = comp_index // 2

time: 328 us -> 327 us (level)
  blocking collectives: 187 us -> 180 us
  waiting for transfers between devices: 69.3 us -> 73.3 us
    all_to_all x1 -> x2, waiting for transfers between devices: 16 us -> 37 us  [reduce_over(): return lax.all_to_all(pieces, axis, 0, 0, tiled=True).sum(0)]
    all_to_all x1 -> x0, waiting for transfers between devices: 17 us -> none  [forward(): lax.all_to_all(jnp.concatenate([pieces, spread], axis=1), 'feat', 0, 0, t...]
    all_to_all x1 -> x0, starting transfers between devices: 4.95 us -> none  [forward(): lax.all_to_all(jnp.concatenate([pieces, spread], axis=1), 'feat', 0, 0, t...]
    all_to_all x1 -> x2, starting transfers between devices: 4.12 us -> 8.2 us  [reduce_over(): return lax.all_to_all(pieces, axis, 0, 0, tiled=True).sum(0)]
    all_to_all x2, blocking collectives: 40.3 us -> 36.7 us  [comp_total(): return lax.all_to_all(spread, 'comp', 0, 0, tiled=True).sum(0)]
where the time goes in v9:
time: 327 us; the launch traced here: 326 us
  blocking collectives  180 us (55%)
  waiting for transfers between devices  73.3 us (22%)
  starting transfers between devices  28.2 us (9%)
  Pallas kernels  24 us (7%)
  other arithmetic  12.3 us (4%)
  local copies, waits for them, and re-layouts  6.02 us (2%)
    all_gather x2, blocking collectives, gather_gradient(): got = lax.all_gather(own, 'comp', axis=0, tiled=False)  80.3 us
    all_to_all x2, waiting for transfers between devices, reduce_over(): return lax.all_to_all(pieces, axis, 0, 0, tiled=True).sum(0)  37 us
    all_to_all x2, blocking collectives, comp_total(): return lax.all_to_all(spread, 'comp', 0, 0, tiled=True).sum(0)  36.7 us
    all_to_all x1, blocking collectives, reduce_gradient(): lax.all_to_all(pieces, 'comp', 0, 0, tiled=True, axis_index_groups=same_c...  34.8 us
    pallas_call x4, Pallas kernels, block_apply(): pl.pallas_call(functools.partial(_block_kernel, transpose, pitch), out_sh...  24 us
    all_to_all x1, waiting for transfers between devices, reduce_gradient(): lax.all_to_all(pieces, 'comp', 0, 0, tiled=True, axis_index_groups=same_c...  19.9 us
    all_to_all x1, blocking collectives, gather_feat(): return lax.all_to_all(spread, 'feat', 0, 0, tiled=True)  19.2 us
    all_to_all x1, waiting for transfers between devices, gather_feat(): return lax.all_to_all(spread, 'feat', 0, 0, tiled=True)  13.6 us
  transfers between devices with their start and end apart: 6, of which 6 were waited for; matrix products, arithmetic and copies ran while one was open for 0% of the time, Pallas kernels for 0%

profile of v9, /device:TPU:1, one launch (start us, length us, event | category | flops | bytes accessed | tf_op | source)
XLA Modules:
  0.0 325.6 jit_solution(10260255303552621198)
XLA Ops:
  0.6 1.9 broadcast_in_dim.18
  2.6 7.6 %all-to-all-start = ((f32[16,128,128]{2,1,0:T(8,128)}), f32[16,128,128]{2,1,0:T(8,128)S(1)}, u32[]{:S(2)}, u32[]{:S(2)}) async-start(f32[16,128,128]{2,1,0:T(8,128)} %broadcast_in_dim.18), calls=%async_computation | async-start | bytes 2097152 | tf_op jit(solution)/shard_map/all_to_all | solution.py:126
  10.8 13.6 %all-to-all-done = f32[16,128,128]{2,1,0:T(8,128)S(1)} async-done(((f32[16,128,128]{2,1,0:T(8,128)}), f32[16,128,128]{2,1,0:T(8,128)S(1)}, u32[]{:S(2)}, u32[]{:S(2)}) %all-to-all-start) | async-done | bytes 1048608 | tf_op jit(solution)/shard_map/all_to_all | solution.py:126
  24.4 0.8 bitcast_convert_fusion.x_ref
  25.2 6.5 %shard_map.77 = f32[1792,128]{1,0:T(8,128)} custom-call(s32[1]{0:T(128)} %bitcast.61.count_ref, s32[24]{0:T(128)} %bitcast.77, s32[24]{0:T(128)} %bitcast.81, bf16[24,128,128]{2,1,0:T(8,128)(2,1)} %bitcast.66, bf16[2048,128]{1,0:T(8,128)(2,1)} %bitcast_convert_fusion.x_ref), custom_call_target="tpu_custom_call" | custom-call | tf_op jit(solution)/shard_map/pallas_call | solution.py:52
  31.7 1.1 constant_dynamic-slice_fusion.1
  32.8 5.6 %collective-permute-start = (f32[896,128]{1,0:T(8,128)S(1)}, f32[896,128]{1,0:T(8,128)S(1)}, u32[]{:S(2)}, u32[]{:S(2)}) collective-permute-start(f32[896,128]{1,0:T(8,128)S(1)} %constant_dynamic-slice_fusion.1), channel_id=1, source_target_pairs={{0,16},{16,0},{32,48},{48,32},{64,80},{80,64},{96,112},{112,96},{1... | collective-permute-start | bytes 1376264 | tf_op jit(solution)/shard_map/ppermute | solution.py:100
  38.4 1.4 collective-permute-done
  39.9 34.8 %all_to_all.45 = f32[16,56,128]{2,1,0:T(8,128)S(1)} all-to-all(f32[16,56,128]{2,1,0:T(8,128)S(1)} %bitcast.76), channel_id=1, replica_groups={{0,32,64,96,128,160,192,224,256,288,320,352,384,416,448,480},{16,48,80,..., dimensions={0} | all-to-all | bytes 917504 | tf_op jit(solution)/shard_map/all_to_all | solution.py:107
  74.7 40.1 %all-gather = f32[1792,128]{1,0:T(8,128)S(1)} all-gather(f32[56,128]{1,0:T(8,128)S(1)} %reduce_sum.135), channel_id=2, replica_groups=mesh['comp'=32,'feat'=16] {'comp'}, dimensions={0}, use_global_device_ids=true | all-gather | bytes 946176 | tf_op jit(solution)/shard_map/all_gather | solution.py:111
  114.8 0.1 copy.15
  114.9 0.8 bitcast_convert_fusion.2.x_ref
  115.7 5.5 %shard_map.78 = f32[2048,128]{1,0:T(8,128)} custom-call(s32[1]{0:T(128)} %bitcast.62.count_ref, s32[24]{0:T(128)} %bitcast.82, s32[24]{0:T(128)} %bitcast.78, bf16[24,128,128]{2,1,0:T(8,128)(2,1)} %bitcast.67, bf16[1792,128]{1,0:T(8,128)(2,1)} %bitcast_convert_fusion.2.x_ref), custom_call_target="tpu_custom_call" | custom-call | tf_op jit(solution)/shard_map/pallas_call | solution.py:52
  121.2 3.8 %all-to-all-start.2 = ((f32[16,128,128]{2,1,0:T(8,128)}), f32[16,128,128]{2,1,0:T(8,128)S(1)}, u32[]{:S(2)}, u32[]{:S(2)}) async-start(f32[16,128,128]{2,1,0:T(8,128)} %bitcast.73), calls=%async_computation.2 | async-start | bytes 2097152 | tf_op jit(solution)/shard_map/all_to_all | solution.py:63
  125.1 18.2 %all-to-all-done.2 = f32[16,128,128]{2,1,0:T(8,128)S(1)} async-done(((f32[16,128,128]{2,1,0:T(8,128)}), f32[16,128,128]{2,1,0:T(8,128)S(1)}, u32[]{:S(2)}, u32[]{:S(2)}) %all-to-all-start.2) | async-done | bytes 1048608 | tf_op jit(solution)/shard_map/all_to_all | solution.py:63
  143.3 0.1 reduce_sum.136
  143.4 0.1 broadcast_in_dim.21
  143.5 19.2 %all_to_all.46 = f32[16,130,128]{2,1,0:T(8,128)S(1)} all-to-all(f32[16,130,128]{2,1,0:T(8,128)S(1)} %broadcast_in_dim.21), channel_id=1, replica_groups=mesh['comp'=32,'feat'=16] {'feat'}, dimensions={0} | all-to-all | bytes 2129920 | tf_op jit(solution)/shard_map/all_to_all | solution.py:126
  162.7 0.3 fusion.5
  163.0 19.0 %all_to_all.47 = f32[32,3,128]{2,1,0:T(4,128)S(1)} all-to-all(f32[32,3,128]{2,1,0:T(4,128)S(1)} %broadcast_in_dim.23), channel_id=1, replica_groups=mesh['comp'=32,'feat'=16] {'comp'}, dimensions={0} | all-to-all | bytes 98304 | tf_op jit(solution)/shard_map/all_to_all | solution.py:130
  182.1 0.0 copy-done.3
  182.1 1.3 fusion.4
  183.4 6.5 %shard_map.79 = f32[1792,128]{1,0:T(8,128)} custom-call(s32[1]{0:T(128)} %bitcast.63.count_ref, s32[24]{0:T(128)} %bitcast.79, s32[24]{0:T(128)} %bitcast.83, bf16[24,128,128]{2,1,0:T(8,128)(2,1)} %bitcast.68, bf16[2048,128]{1,0:T(8,128)(2,1)} %get-tuple-element.16.x_ref), custom_call_target="tpu_custom_call" | custom-call | tf_op jit(solution)/shard_map/pallas_call | solution.py:52
  189.9 1.1 constant_dynamic-slice_fusion
  191.0 3.3 %collective-permute-start.1 = (f32[896,128]{1,0:T(8,128)S(1)}, f32[896,128]{1,0:T(8,128)S(1)}, u32[]{:S(2)}, u32[]{:S(2)}) collective-permute-start(f32[896,128]{1,0:T(8,128)S(1)} %constant_dynamic-slice_fusion), channel_id=1, source_target_pairs={{0,16},{16,0},{32,48},{48,32},{64,80},{80,64},{96,112},{112,96},{1... | collective-permute-start | bytes 1376264 | tf_op jit(solution)/shard_map/ppermute | solution.py:100
  194.3 1.4 collective-permute-done.1
  195.8 0.8 dynamic-slice_add_fusion
  196.6 3.6 %all-to-all-start.5 = ((f32[16,56,128]{2,1,0:T(8,128)}), f32[16,56,128]{2,1,0:T(8,128)S(1)}, u32[]{:S(2)}, u32[]{:S(2)}) async-start(f32[16,56,128]{2,1,0:T(8,128)} %bitcast.17), calls=%async_computation.5 | async-start | bytes 917504 | tf_op jit(solution)/shard_map/all_to_all | solution.py:107
  200.2 1.0 broadcast_multiply_fusion
  201.2 19.9 %all-to-all-done.5 = f32[16,56,128]{2,1,0:T(8,128)S(1)} async-done(((f32[16,56,128]{2,1,0:T(8,128)}), f32[16,56,128]{2,1,0:T(8,128)S(1)}, u32[]{:S(2)}, u32[]{:S(2)}) %all-to-all-start.5) | async-done | bytes 458784 | tf_op jit(solution)/shard_map/all_to_all | solution.py:107
  221.1 0.8 multiply_reduce_fusion.3
  221.9 40.2 %all-gather.2 = f32[32,57,128]{2,1,0:T(8,128)S(1)} all-gather(f32[1,57,128]{2,1,0:T(8,128)S(1)} %maximum_bitcast_fusion), channel_id=3, replica_groups=mesh['comp'=32,'feat'=16] {'comp'}, dimensions={0}, use_global_device_ids=true | all-gather | bytes 963072 | tf_op jit(solution)/shard_map/all_gather | solution.py:111
  262.1 0.1 slice_reduce_fusion
  262.2 0.1 slice.62
  262.3 0.1 copy.17
  262.3 0.6 scatter.4.rest_0_
  262.9 0.8 bitcast_convert_fusion.1.x_ref
  263.7 5.5 %shard_map.80 = f32[2176,128]{1,0:T(8,128)} custom-call(s32[1]{0:T(128)} %bitcast.64.count_ref, s32[24]{0:T(128)} %bitcast.84, s32[24]{0:T(128)} %bitcast.80, bf16[24,128,128]{2,1,0:T(8,128)(2,1)} %bitcast.69, bf16[1792,128]{1,0:T(8,128)(2,1)} %bitcast_convert_fusion.1.x_ref, f32[8,128]{1,0:T(8,128)} %scatter.4.rest_0_), custom_call_target="tpu_custom_call" | custom-call | tf_op jit(solution)/shard_map/pallas_call | solution.py:52
  269.2 4.4 %all-to-all-start.6 = ((f32[16,136,128]{2,1,0:T(8,128)}), f32[16,136,128]{2,1,0:T(8,128)}, u32[]{:S(2)}, u32[]{:S(2)}) async-start(f32[16,136,128]{2,1,0:T(8,128)} %bitcast.72), calls=%async_computation.6 | async-start | bytes 2228224 | tf_op jit(solution)/shard_map/all_to_all | solution.py:63
  273.6 18.7 %all-to-all-done.6 = f32[16,136,128]{2,1,0:T(8,128)} async-done(((f32[16,136,128]{2,1,0:T(8,128)}), f32[16,136,128]{2,1,0:T(8,128)}, u32[]{:S(2)}, u32[]{:S(2)}) %all-to-all-start.6) | async-done | bytes 1114144 | tf_op jit(solution)/shard_map/all_to_all | solution.py:63
  292.4 1.3 reduce_sum.145
  293.7 0.1 bitcast_add_fusion
  293.8 0.0 copy-start
  293.8 0.9 copy-done
  294.8 9.4 %all_to_all.48 = f32[16,2,128]{2,1,0:T(2,128)S(1)} all-to-all(f32[16,2,128]{2,1,0:T(2,128)S(1)} %broadcast_in_dim.25), channel_id=1, replica_groups=mesh['comp'=32,'feat'=16] {'feat'}, dimensions={0} | all-to-all | bytes 32768 | tf_op jit(solution)/shard_map/all_to_all | solution.py:165
  304.2 17.6 %all_to_all.49 = f32[32,2,128]{2,1,0:T(2,128)S(1)} all-to-all(f32[32,2,128]{2,1,0:T(2,128)S(1)} %broadcast_in_dim.26), channel_id=1, replica_groups=mesh['comp'=32,'feat'=16] {'comp'}, dimensions={0} | all-to-all | bytes 65536 | tf_op jit(solution)/shard_map/all_to_all | solution.py:130
  321.9 2.2 multiply_add_fusion
  324.1 1.5 multiply_subtract_fusion
  (26 shorter events, 0.5 us)
Async XLA Ops:
  2.6 21.8 %all-to-all-start = ((f32[16,128,128]{2,1,0:T(8,128)}), f32[16,128,128]{2,1,0:T(8,128)S(1)}, u32[]{:S(2)}, u32[]{:S(2)}) async-start(f32[16,128,128]{2,1,0:T(8,128)} %broadcast_in_dim.18), calls=%async_computation | async-start | bytes 2097152 | tf_op jit(solution)/shard_map/all_to_all | solution.py:126
  31.7 8.1 %copy-start.1 = (f32[1792,128]{1,0:T(8,128)S(1)}, f32[1792,128]{1,0:T(8,128)}, u32[]{:S(2)}) copy-start(f32[1792,128]{1,0:T(8,128)} %shard_map.77) | copy-start | bytes 2752516
  32.8 7.0 %collective-permute-start = (f32[896,128]{1,0:T(8,128)S(1)}, f32[896,128]{1,0:T(8,128)S(1)}, u32[]{:S(2)}, u32[]{:S(2)}) collective-permute-start(f32[896,128]{1,0:T(8,128)S(1)} %constant_dynamic-slice_fusion.1), channel_id=1, source_target_pairs={{0,16},{16,0},{32,48},{48,32},{64,80},{80,64},{96,112},{112,96},{1... | collective-permute-start | bytes 1376264 | tf_op jit(solution)/shard_map/ppermute | solution.py:100
  121.2 22.2 %all-to-all-start.2 = ((f32[16,128,128]{2,1,0:T(8,128)}), f32[16,128,128]{2,1,0:T(8,128)S(1)}, u32[]{:S(2)}, u32[]{:S(2)}) async-start(f32[16,128,128]{2,1,0:T(8,128)} %bitcast.73), calls=%async_computation.2 | async-start | bytes 2097152 | tf_op jit(solution)/shard_map/all_to_all | solution.py:63
  162.7 19.4 %copy-start.3 = (f32[128]{0:T(128)S(1)}, f32[128]{0:T(128)}, u32[]{:S(2)}) copy-start(f32[128]{0:T(128)} %param.13) | copy-start | bytes 1540
  189.9 5.9 %copy-start.2 = (f32[1792,128]{1,0:T(8,128)S(1)}, f32[1792,128]{1,0:T(8,128)}, u32[]{:S(2)}) copy-start(f32[1792,128]{1,0:T(8,128)} %shard_map.79) | copy-start | bytes 2752516
  191.0 4.7 %collective-permute-start.1 = (f32[896,128]{1,0:T(8,128)S(1)}, f32[896,128]{1,0:T(8,128)S(1)}, u32[]{:S(2)}, u32[]{:S(2)}) collective-permute-start(f32[896,128]{1,0:T(8,128)S(1)} %constant_dynamic-slice_fusion), channel_id=1, source_target_pairs={{0,16},{16,0},{32,48},{48,32},{64,80},{80,64},{96,112},{112,96},{1... | collective-permute-start | bytes 1376264 | tf_op jit(solution)/shard_map/ppermute | solution.py:100
  196.6 24.5 %all-to-all-start.5 = ((f32[16,56,128]{2,1,0:T(8,128)}), f32[16,56,128]{2,1,0:T(8,128)S(1)}, u32[]{:S(2)}, u32[]{:S(2)}) async-start(f32[16,56,128]{2,1,0:T(8,128)} %bitcast.17), calls=%async_computation.5 | async-start | bytes 917504 | tf_op jit(solution)/shard_map/all_to_all | solution.py:107
  269.2 23.1 %all-to-all-start.6 = ((f32[16,136,128]{2,1,0:T(8,128)}), f32[16,136,128]{2,1,0:T(8,128)}, u32[]{:S(2)}, u32[]{:S(2)}) async-start(f32[16,136,128]{2,1,0:T(8,128)} %bitcast.72), calls=%async_computation.6 | async-start | bytes 2228224 | tf_op jit(solution)/shard_map/all_to_all | solution.py:63
  293.8 0.9 copy-start

commit v10 on v9

--- a/solution.py
+++ b/solution.py
@@ -91,30 +91,35 @@
 
     core = comp_index % 2
     chip = comp_index // 2
-    n_chips = n_comp // 2
     half_rows = feat_rows // 2
+    quarter_rows = half_rows // 2
+    pair = chip % 2
+    n_groups = n_comp // 4
     siblings = [(i, i ^ 1) for i in range(n_comp)]
-    same_core = [[i for i in range(n_comp) if i % 2 == p] for p in range(2)]
-
-    def swap_with_sibling(x):
-        return lax.ppermute(x, "comp", siblings)
+    neighbours = [(i, i ^ 2) for i in range(n_comp)]
+    same_slot = [[i for i in range(n_comp) if i % 4 == g] for g in range(4)]
+
+    def add_halves(x, keep, exchange, rows):
+        kept = lax.dynamic_slice_in_dim(x, keep * rows, rows, axis=0)
+        sent = lax.dynamic_slice_in_dim(x, (1 - keep) * rows, rows, axis=0)
+        return kept + lax.ppermute(sent, "comp", exchange)
 
     def reduce_gradient(partial):
-        kept = lax.dynamic_slice_in_dim(partial, core * half_rows, half_rows, axis=0)
-        sent = lax.dynamic_slice_in_dim(partial, (1 - core) * half_rows, half_rows, axis=0)
-        chip_sum = kept + swap_with_sibling(sent)
-        pieces = chip_sum.reshape(n_chips, own_rows, chip_sum.shape[1])
-        landed = lax.all_to_all(pieces, "comp", 0, 0, tiled=True, axis_index_groups=same_core)
+        chip_sum = add_halves(partial, core, siblings, half_rows)
+        pair_sum = add_halves(chip_sum, pair, neighbours, quarter_rows)
+        pieces = pair_sum.reshape(n_groups, own_rows, pair_sum.shape[1])
+        landed = lax.all_to_all(pieces, "comp", 0, 0, tiled=True, axis_index_groups=same_slot)
         return landed.sum(0)
 
     def gather_gradient(own):
         got = lax.all_gather(own, "comp", axis=0, tiled=False)
-        by_chip = got[:, :own_rows].reshape(n_chips, 2, own_rows, own.shape[1])
-        rows = by_chip.transpose(1, 0, 2, 3).reshape(feat_rows, own.shape[1])
+        by_slot = got[:, :own_rows].reshape(n_groups, 2, 2, own_rows, own.shape[1])
+        rows = by_slot.transpose(2, 1, 0, 3, 4).reshape(feat_rows, own.shape[1])
         return rows, jnp.sum(got[:, own_rows:], axis=0)
 
     def own_part(full):
-        return lax.dynamic_slice_in_dim(full, core * half_rows + chip * own_rows, own_rows, axis=0)
+        start = core * half_rows + pair * quarter_rows + (chip // 2) * own_rows
+        return lax.dynamic_slice_in_dim(full, start, own_rows, axis=0)
 
     def col_sq(x):
         return jnp.sum(x * x, axis=0)

time: 327 us -> 325 us (level)
  starting transfers between devices: 28.2 us -> 34.8 us
  Pallas kernels: 24 us -> 19.5 us
  blocking collectives: 180 us -> 176 us
    ppermute x2 -> x4, waiting for transfers between devices: 2.83 us -> 15.7 us  [add_halves(): return kept + lax.ppermute(sent, 'comp', exchange)]
    all_gather x2, blocking collectives: 80.3 us -> 69.7 us  [gather_gradient(): got = lax.all_gather(own, 'comp', axis=0, tiled=False)]
    all_to_all x2, blocking collectives: 36.7 us -> 46.1 us  [comp_total(): return lax.all_to_all(spread, 'comp', 0, 0, tiled=True).sum(0)]
    ppermute x2 -> x4, starting transfers between devices: 8.87 us -> 15.8 us  [add_halves(): return kept + lax.ppermute(sent, 'comp', exchange)]
    all_to_all x2, waiting for transfers between devices: 37 us -> 31.6 us  [reduce_over(): return lax.all_to_all(pieces, axis, 0, 0, tiled=True).sum(0)]
    all_to_all x1, waiting for transfers between devices: 19.9 us -> 15.1 us  [reduce_gradient(): lax.all_to_all(pieces, 'comp', 0, 0, tiled=True, axis_index_groups=same_s...]
    pallas_call x4, Pallas kernels: 24 us -> 19.5 us  [block_apply(): pl.pallas_call(functools.partial(_block_kernel, transpose, pitch), out_sh...]
    all_to_all x1, blocking collectives: 34.8 us -> 30.7 us  [reduce_gradient(): lax.all_to_all(pieces, 'comp', 0, 0, tiled=True, axis_index_groups=same_s...]
  transfers between devices with their start and end apart: 6 -> 8, of which waited for: 6 -> 8; matrix products, arithmetic and copies ran while one was open for 0% -> 0% of each run, Pallas kernels for 0% -> 0%
where the time goes in v10:
time: 325 us; the launch traced here: 324 us
  blocking collectives  176 us (54%)
  waiting for transfers between devices  76 us (23%)
  starting transfers between devices  34.8 us (11%)
  Pallas kernels  19.5 us (6%)
  other arithmetic  10.5 us (3%)
  local copies, waits for them, and re-layouts  6.07 us (2%)
    all_gather x2, blocking collectives, gather_gradient(): got = lax.all_gather(own, 'comp', axis=0, tiled=False)  69.7 us
    all_to_all x2, blocking collectives, comp_total(): return lax.all_to_all(spread, 'comp', 0, 0, tiled=True).sum(0)  46.1 us
    all_to_all x2, waiting for transfers between devices, reduce_over(): return lax.all_to_all(pieces, axis, 0, 0, tiled=True).sum(0)  31.6 us
    all_to_all x1, blocking collectives, reduce_gradient(): lax.all_to_all(pieces, 'comp', 0, 0, tiled=True, axis_index_groups=same_s...  30.7 us
    pallas_call x4, Pallas kernels, block_apply(): pl.pallas_call(functools.partial(_block_kernel, transpose, pitch), out_sh...  19.5 us
    all_to_all x1, blocking collectives, gather_feat(): return lax.all_to_all(spread, 'feat', 0, 0, tiled=True)  18.9 us
    ppermute x4, starting transfers between devices, add_halves(): return kept + lax.ppermute(sent, 'comp', exchange)  15.8 us
    ppermute x4, waiting for transfers between devices, add_halves(): return kept + lax.ppermute(sent, 'comp', exchange)  15.7 us
  transfers between devices with their start and end apart: 8, of which 8 were waited for; matrix products, arithmetic and copies ran while one was open for 0% of the time, Pallas kernels for 0%

profile of v10, /device:TPU:1, one launch (start us, length us, event | category | flops | bytes accessed | tf_op | source)
XLA Modules:
  0.0 324.2 jit_solution(4175347544392392267)
XLA Ops:
  0.6 1.9 broadcast_in_dim.18
  2.6 7.6 %all-to-all-start = ((f32[16,128,128]{2,1,0:T(8,128)}), f32[16,128,128]{2,1,0:T(8,128)S(1)}, u32[]{:S(2)}, u32[]{:S(2)}) async-start(f32[16,128,128]{2,1,0:T(8,128)} %broadcast_in_dim.18), calls=%async_computation | async-start | bytes 2097152 | tf_op jit(solution)/shard_map/all_to_all | solution.py:131
  10.8 13.6 %all-to-all-done = f32[16,128,128]{2,1,0:T(8,128)S(1)} async-done(((f32[16,128,128]{2,1,0:T(8,128)}), f32[16,128,128]{2,1,0:T(8,128)S(1)}, u32[]{:S(2)}, u32[]{:S(2)}) %all-to-all-start) | async-done | bytes 1048608 | tf_op jit(solution)/shard_map/all_to_all | solution.py:131
  24.4 0.8 bitcast_convert_fusion.x_ref
  25.2 5.2 %shard_map.77 = f32[1792,128]{1,0:T(8,128)} custom-call(s32[1]{0:T(128)} %bitcast.61.count_ref, s32[24]{0:T(128)} %bitcast.77, s32[24]{0:T(128)} %bitcast.81, bf16[24,128,128]{2,1,0:T(8,128)(2,1)} %bitcast.66, bf16[2048,128]{1,0:T(8,128)(2,1)} %bitcast_convert_fusion.x_ref), custom_call_target="tpu_custom_call" | custom-call | tf_op jit(solution)/shard_map/pallas_call | solution.py:52
  30.5 1.1 constant_dynamic-slice_fusion.3
  31.6 6.8 %collective-permute-start = (f32[896,128]{1,0:T(8,128)S(1)}, f32[896,128]{1,0:T(8,128)S(1)}, u32[]{:S(2)}, u32[]{:S(2)}) collective-permute-start(f32[896,128]{1,0:T(8,128)S(1)} %constant_dynamic-slice_fusion.3), channel_id=1, source_target_pairs={{0,16},{16,0},{32,48},{48,32},{64,80},{80,64},{96,112},{112,96},{1... | collective-permute-start | bytes 1376264 | tf_op jit(solution)/shard_map/ppermute | solution.py:105
  38.5 1.4 collective-permute-done
  39.9 2.5 collective-permute-start.1
  42.5 6.2 %collective-permute-done.1 = f32[448,128]{1,0:T(8,128)S(1)} collective-permute-done((f32[448,128]{1,0:T(8,128)S(1)}, f32[448,128]{1,0:T(8,128)S(1)}, u32[]{:S(2)}, u32[]{:S(2)}) %collective-permute-start.1) | collective-permute-done | bytes 229408 | tf_op jit(solution)/shard_map/ppermute | solution.py:105
  48.7 30.7 %all_to_all.45 = f32[8,56,128]{2,1,0:T(8,128)S(1)} all-to-all(f32[8,56,128]{2,1,0:T(8,128)S(1)} %bitcast.76), channel_id=1, replica_groups={{0,64,128,192,256,320,384,448},{16,80,144,208,272,336,400,464},{32,96,1..., dimensions={0} | all-to-all | bytes 458752 | tf_op jit(solution)/shard_map/all_to_all | solution.py:111
  79.4 34.2 %all-gather = f32[1792,128]{1,0:T(8,128)S(1)} all-gather(f32[56,128]{1,0:T(8,128)S(1)} %reduce_sum.135), channel_id=2, replica_groups=mesh['comp'=32,'feat'=16] {'comp'}, dimensions={0}, use_global_device_ids=true | all-gather | bytes 946176 | tf_op jit(solution)/shard_map/all_gather | solution.py:115
  113.6 0.1 copy.15
  113.7 0.8 bitcast_convert_fusion.2.x_ref
  114.5 4.5 %shard_map.78 = f32[2048,128]{1,0:T(8,128)} custom-call(s32[1]{0:T(128)} %bitcast.62.count_ref, s32[24]{0:T(128)} %bitcast.82, s32[24]{0:T(128)} %bitcast.78, bf16[24,128,128]{2,1,0:T(8,128)(2,1)} %bitcast.67, bf16[1792,128]{1,0:T(8,128)(2,1)} %bitcast_convert_fusion.2.x_ref), custom_call_target="tpu_custom_call" | custom-call | tf_op jit(solution)/shard_map/pallas_call | solution.py:52
  119.0 3.7 %all-to-all-start.2 = ((f32[16,128,128]{2,1,0:T(8,128)}), f32[16,128,128]{2,1,0:T(8,128)S(1)}, u32[]{:S(2)}, u32[]{:S(2)}) async-start(f32[16,128,128]{2,1,0:T(8,128)} %bitcast.73), calls=%async_computation.2 | async-start | bytes 2097152 | tf_op jit(solution)/shard_map/all_to_all | solution.py:63
  122.7 15.4 %all-to-all-done.2 = f32[16,128,128]{2,1,0:T(8,128)S(1)} async-done(((f32[16,128,128]{2,1,0:T(8,128)}), f32[16,128,128]{2,1,0:T(8,128)S(1)}, u32[]{:S(2)}, u32[]{:S(2)}) %all-to-all-start.2) | async-done | bytes 1048608 | tf_op jit(solution)/shard_map/all_to_all | solution.py:63
  138.2 0.1 broadcast_in_dim.21
  138.3 18.9 %all_to_all.46 = f32[16,130,128]{2,1,0:T(8,128)S(1)} all-to-all(f32[16,130,128]{2,1,0:T(8,128)S(1)} %broadcast_in_dim.21), channel_id=1, replica_groups=mesh['comp'=32,'feat'=16] {'feat'}, dimensions={0} | all-to-all | bytes 2129920 | tf_op jit(solution)/shard_map/all_to_all | solution.py:131
  157.2 0.3 fusion.5
  157.5 24.4 %all_to_all.47 = f32[32,3,128]{2,1,0:T(4,128)S(1)} all-to-all(f32[32,3,128]{2,1,0:T(4,128)S(1)} %broadcast_in_dim.23), channel_id=1, replica_groups=mesh['comp'=32,'feat'=16] {'comp'}, dimensions={0} | all-to-all | bytes 98304 | tf_op jit(solution)/shard_map/all_to_all | solution.py:135
  182.0 1.3 fusion.4
  183.3 5.2 %shard_map.79 = f32[1792,128]{1,0:T(8,128)} custom-call(s32[1]{0:T(128)} %bitcast.63.count_ref, s32[24]{0:T(128)} %bitcast.79, s32[24]{0:T(128)} %bitcast.83, bf16[24,128,128]{2,1,0:T(8,128)(2,1)} %bitcast.68, bf16[2048,128]{1,0:T(8,128)(2,1)} %get-tuple-element.16.x_ref), custom_call_target="tpu_custom_call" | custom-call | tf_op jit(solution)/shard_map/pallas_call | solution.py:52
  188.5 1.1 constant_dynamic-slice_fusion.1
  189.6 4.5 %collective-permute-start.2 = (f32[896,128]{1,0:T(8,128)S(1)}, f32[896,128]{1,0:T(8,128)S(1)}, u32[]{:S(2)}, u32[]{:S(2)}) collective-permute-start(f32[896,128]{1,0:T(8,128)S(1)} %constant_dynamic-slice_fusion.1), channel_id=1, source_target_pairs={{0,16},{16,0},{32,48},{48,32},{64,80},{80,64},{96,112},{112,96},{1... | collective-permute-start | bytes 1376264 | tf_op jit(solution)/shard_map/ppermute | solution.py:105
  194.2 1.4 collective-permute-done.2
  195.6 0.1 dynamic-slice_add_fusion
  195.7 1.9 collective-permute-start.3
  197.7 6.8 %collective-permute-done.3 = f32[448,128]{1,0:T(8,128)S(1)} collective-permute-done((f32[448,128]{1,0:T(8,128)S(1)}, f32[448,128]{1,0:T(8,128)S(1)}, u32[]{:S(2)}, u32[]{:S(2)}) %collective-permute-start.3) | collective-permute-done | bytes 229408 | tf_op jit(solution)/shard_map/ppermute | solution.py:105
  204.4 0.7 dynamic-slice_add_fusion.2
  205.2 3.4 %all-to-all-start.5 = ((f32[8,56,128]{2,1,0:T(8,128)}), f32[8,56,128]{2,1,0:T(8,128)S(1)}, u32[]{:S(2)}, u32[]{:S(2)}) async-start(f32[8,56,128]{2,1,0:T(8,128)} %bitcast.17), calls=%async_computation.5 | async-start | bytes 458752 | tf_op jit(solution)/shard_map/all_to_all | solution.py:111
  208.6 0.1 broadcast_multiply_fusion
  208.6 15.1 %all-to-all-done.5 = f32[8,56,128]{2,1,0:T(8,128)S(1)} async-done(((f32[8,56,128]{2,1,0:T(8,128)}), f32[8,56,128]{2,1,0:T(8,128)S(1)}, u32[]{:S(2)}, u32[]{:S(2)}) %all-to-all-start.5) | async-done | bytes 229408 | tf_op jit(solution)/shard_map/all_to_all | solution.py:111
  223.8 35.5 %all-gather.2 = f32[32,57,128]{2,1,0:T(8,128)S(1)} all-gather(f32[1,57,128]{2,1,0:T(8,128)S(1)} %maximum_bitcast_fusion), channel_id=3, replica_groups=mesh['comp'=32,'feat'=16] {'comp'}, dimensions={0}, use_global_device_ids=true | all-gather | bytes 963072 | tf_op jit(solution)/shard_map/all_gather | solution.py:115
  259.3 0.1 slice.62
  259.4 0.1 copy.17
  259.5 0.6 scatter.4.rest_0_
  260.1 0.8 bitcast_convert_fusion.1.x_ref
  260.9 4.5 %shard_map.80 = f32[2176,128]{1,0:T(8,128)} custom-call(s32[1]{0:T(128)} %bitcast.64.count_ref, s32[24]{0:T(128)} %bitcast.84, s32[24]{0:T(128)} %bitcast.80, bf16[24,128,128]{2,1,0:T(8,128)(2,1)} %bitcast.69, bf16[1792,128]{1,0:T(8,128)(2,1)} %bitcast_convert_fusion.1.x_ref, f32[8,128]{1,0:T(8,128)} %scatter.4.rest_0_), custom_call_target="tpu_custom_call" | custom-call | tf_op jit(solution)/shard_map/pallas_call | solution.py:52
  265.4 4.4 %all-to-all-start.6 = ((f32[16,136,128]{2,1,0:T(8,128)}), f32[16,136,128]{2,1,0:T(8,128)}, u32[]{:S(2)}, u32[]{:S(2)}) async-start(f32[16,136,128]{2,1,0:T(8,128)} %bitcast.72), calls=%async_computation.6 | async-start | bytes 2228224 | tf_op jit(solution)/shard_map/all_to_all | solution.py:63
  269.8 16.3 %all-to-all-done.6 = f32[16,136,128]{2,1,0:T(8,128)} async-done(((f32[16,136,128]{2,1,0:T(8,128)}), f32[16,136,128]{2,1,0:T(8,128)}, u32[]{:S(2)}, u32[]{:S(2)}) %all-to-all-start.6) | async-done | bytes 1114144 | tf_op jit(solution)/shard_map/all_to_all | solution.py:63
  286.1 1.3 reduce_sum.145
  287.4 0.1 bitcast_add_fusion
  287.5 0.9 copy-done
  288.5 10.2 %all_to_all.48 = f32[16,2,128]{2,1,0:T(2,128)S(1)} all-to-all(f32[16,2,128]{2,1,0:T(2,128)S(1)} %broadcast_in_dim.25), channel_id=1, replica_groups=mesh['comp'=32,'feat'=16] {'feat'}, dimensions={0} | all-to-all | bytes 32768 | tf_op jit(solution)/shard_map/all_to_all | solution.py:170
  298.7 21.7 %all_to_all.49 = f32[32,2,128]{2,1,0:T(2,128)S(1)} all-to-all(f32[32,2,128]{2,1,0:T(2,128)S(1)} %broadcast_in_dim.26), channel_id=1, replica_groups=mesh['comp'=32,'feat'=16] {'comp'}, dimensions={0} | all-to-all | bytes 65536 | tf_op jit(solution)/shard_map/all_to_all | solution.py:135
  320.5 2.2 multiply_add_fusion
  322.7 1.5 multiply_subtract_fusion
  (34 shorter events, 0.7 us)
Async XLA Ops:
  2.6 21.8 %all-to-all-start = ((f32[16,128,128]{2,1,0:T(8,128)}), f32[16,128,128]{2,1,0:T(8,128)S(1)}, u32[]{:S(2)}, u32[]{:S(2)}) async-start(f32[16,128,128]{2,1,0:T(8,128)} %broadcast_in_dim.18), calls=%async_computation | async-start | bytes 2097152 | tf_op jit(solution)/shard_map/all_to_all | solution.py:131
  30.5 9.4 %copy-start.1 = (f32[1792,128]{1,0:T(8,128)S(1)}, f32[1792,128]{1,0:T(8,128)}, u32[]{:S(2)}) copy-start(f32[1792,128]{1,0:T(8,128)} %shard_map.77) | copy-start | bytes 2752516
  31.6 8.2 %collective-permute-start = (f32[896,128]{1,0:T(8,128)S(1)}, f32[896,128]{1,0:T(8,128)S(1)}, u32[]{:S(2)}, u32[]{:S(2)}) collective-permute-start(f32[896,128]{1,0:T(8,128)S(1)} %constant_dynamic-slice_fusion.3), channel_id=1, source_target_pairs={{0,16},{16,0},{32,48},{48,32},{64,80},{80,64},{96,112},{112,96},{1... | collective-permute-start | bytes 1376264 | tf_op jit(solution)/shard_map/ppermute | solution.py:105
  39.9 8.7 %collective-permute-start.1 = (f32[448,128]{1,0:T(8,128)S(1)}, f32[448,128]{1,0:T(8,128)S(1)}, u32[]{:S(2)}, u32[]{:S(2)}) collective-permute-start(f32[448,128]{1,0:T(8,128)S(1)} %constant_dynamic-slice_fusion.2), channel_id=1, source_target_pairs={{0,32},{16,48},{32,0},{48,16},{64,96},{80,112},{96,64},{112,80},{1... | collective-permute-start | bytes 688136 | tf_op jit(solution)/shard_map/ppermute | solution.py:105
  119.0 19.1 %all-to-all-start.2 = ((f32[16,128,128]{2,1,0:T(8,128)}), f32[16,128,128]{2,1,0:T(8,128)S(1)}, u32[]{:S(2)}, u32[]{:S(2)}) async-start(f32[16,128,128]{2,1,0:T(8,128)} %bitcast.73), calls=%async_computation.2 | async-start | bytes 2097152 | tf_op jit(solution)/shard_map/all_to_all | solution.py:63
  157.2 24.8 %copy-start.3 = (f32[128]{0:T(128)S(1)}, f32[128]{0:T(128)}, u32[]{:S(2)}) copy-start(f32[128]{0:T(128)} %param.13) | copy-start | bytes 1540
  188.5 7.1 %copy-start.2 = (f32[1792,128]{1,0:T(8,128)S(1)}, f32[1792,128]{1,0:T(8,128)}, u32[]{:S(2)}) copy-start(f32[1792,128]{1,0:T(8,128)} %shard_map.79) | copy-start | bytes 2752516
  189.6 6.0 %collective-permute-start.2 = (f32[896,128]{1,0:T(8,128)S(1)}, f32[896,128]{1,0:T(8,128)S(1)}, u32[]{:S(2)}, u32[]{:S(2)}) collective-permute-start(f32[896,128]{1,0:T(8,128)S(1)} %constant_dynamic-slice_fusion.1), channel_id=1, source_target_pairs={{0,16},{16,0},{32,48},{48,32},{64,80},{80,64},{96,112},{112,96},{1... | collective-permute-start | bytes 1376264 | tf_op jit(solution)/shard_map/ppermute | solution.py:105
  195.7 8.7 %collective-permute-start.3 = (f32[448,128]{1,0:T(8,128)S(1)}, f32[448,128]{1,0:T(8,128)S(1)}, u32[]{:S(2)}, u32[]{:S(2)}) collective-permute-start(f32[448,128]{1,0:T(8,128)S(1)} %constant_dynamic-slice_fusion), channel_id=1, source_target_pairs={{0,32},{16,48},{32,0},{48,16},{64,96},{80,112},{96,64},{112,80},{1... | collective-permute-start | bytes 688136 | tf_op jit(solution)/shard_map/ppermute | solution.py:105
  205.2 18.6 %all-to-all-start.5 = ((f32[8,56,128]{2,1,0:T(8,128)}), f32[8,56,128]{2,1,0:T(8,128)S(1)}, u32[]{:S(2)}, u32[]{:S(2)}) async-start(f32[8,56,128]{2,1,0:T(8,128)} %bitcast.17), calls=%async_computation.5 | async-start | bytes 458752 | tf_op jit(solution)/shard_map/all_to_all | solution.py:111
  265.4 20.7 %all-to-all-start.6 = ((f32[16,136,128]{2,1,0:T(8,128)}), f32[16,136,128]{2,1,0:T(8,128)}, u32[]{:S(2)}, u32[]{:S(2)}) async-start(f32[16,136,128]{2,1,0:T(8,128)} %bitcast.72), calls=%async_computation.6 | async-start | bytes 2228224 | tf_op jit(solution)/shard_map/all_to_all | solution.py:63
  287.5 0.9 copy-start

commit v11 on v10

--- a/solution.py
+++ b/solution.py
@@ -27,7 +27,7 @@
             src = pl.multiple_of(in_idx_ref[s] * edge, edge)
             dst = pl.multiple_of(out_idx_ref[s] * pitch, 8)
             block = values_ref[s]
-            x = x_ref[pl.ds(src, edge), :]
+            x = x_ref[pl.ds(src, edge), :].astype(values_ref.dtype)
             if transpose:
                 prod = lax.dot_general(
                     block, x, (((0,), (0,)), ((), ())), preferred_element_type=jnp.float32
@@ -78,7 +78,7 @@
         return block_apply(values, count_of_slots, slot_cols, slot_rows, low_slab, CB_DEV, True)
 
     def forward(direction, extra=None):
-        low = direction.astype(jnp.bfloat16)
+        low = direction
         if extra is None:
             summed = block_apply(values, count_of_slots, slot_rows, slot_cols, low, RB_DEV, False)
             return reduce_over(summed, "feat", n_feat)
@@ -138,7 +138,7 @@
     residual_slab = gather_feat(right_side).reshape(RB_DEV * own_block, responses)
 
     def low_slab(slab):
-        return slab.astype(jnp.bfloat16)
+        return slab
 
     gradient_own = reduce_gradient(backward(low_slab(residual_slab)))
     energy_own = col_sq(gradient_own)

time: 325 us -> 328 us (level)
  Pallas kernels: 19.5 us -> 24.7 us
  blocking collectives: 176 us -> 171 us
  waiting for transfers between devices: 76 us -> 79.9 us
    pallas_call x4, Pallas kernels: 19.5 us -> 24.7 us  [block_apply(): pl.pallas_call(functools.partial(_block_kernel, transpose, pitch), out_sh...]
    all_to_all x2, waiting for transfers between devices: 31.6 us -> 35.7 us  [reduce_over(): return lax.all_to_all(pieces, axis, 0, 0, tiled=True).sum(0)]
    all_to_all x2, blocking collectives: 46.1 us -> 42.1 us  [comp_total(): return lax.all_to_all(spread, 'comp', 0, 0, tiled=True).sum(0)]
    convert_element_type x4 -> x0, other arithmetic: 3.74 us -> none  [the longest x2 2.12 us: low_slab(): return slab.astype(jnp.bfloat16)]
where the time goes in v11:
time: 328 us; the launch traced here: 327 us
  blocking collectives  171 us (52%)
  waiting for transfers between devices  79.9 us (24%)
  starting transfers between devices  33 us (10%)
  Pallas kernels  24.7 us (8%)
  local copies, waits for them, and re-layouts  8.92 us (3%)
  other arithmetic  7.88 us (2%)
    all_gather x2, blocking collectives, gather_gradient(): got = lax.all_gather(own, 'comp', axis=0, tiled=False)  70.6 us
    all_to_all x2, blocking collectives, comp_total(): return lax.all_to_all(spread, 'comp', 0, 0, tiled=True).sum(0)  42.1 us
    all_to_all x2, waiting for transfers between devices, reduce_over(): return lax.all_to_all(pieces, axis, 0, 0, tiled=True).sum(0)  35.7 us
    all_to_all x1, blocking collectives, reduce_gradient(): lax.all_to_all(pieces, 'comp', 0, 0, tiled=True, axis_index_groups=same_s...  29.8 us
    pallas_call x4, Pallas kernels, block_apply(): pl.pallas_call(functools.partial(_block_kernel, transpose, pitch), out_sh...  24.7 us
    all_to_all x1, blocking collectives, gather_feat(): return lax.all_to_all(spread, 'feat', 0, 0, tiled=True)  19.2 us
    ppermute x4, waiting for transfers between devices, add_halves(): return kept + lax.ppermute(sent, 'comp', exchange)  15.5 us
    all_to_all x1, waiting for transfers between devices, reduce_gradient(): lax.all_to_all(pieces, 'comp', 0, 0, tiled=True, axis_index_groups=same_s...  15.1 us
  transfers between devices with their start and end apart: 8, of which 8 were waited for; matrix products, arithmetic and copies ran while one was open for 0% of the time, Pallas kernels for 0%

profile of v11, /device:TPU:1, one launch (start us, length us, event | category | flops | bytes accessed | tf_op | source)
XLA Modules:
  0.0 327.1 jit_solution(3041212672915270822)
XLA Ops:
  0.6 1.9 broadcast_in_dim.18
  2.6 7.6 %all-to-all-start = ((f32[16,128,128]{2,1,0:T(8,128)}), f32[16,128,128]{2,1,0:T(8,128)S(1)}, u32[]{:S(2)}, u32[]{:S(2)}) async-start(f32[16,128,128]{2,1,0:T(8,128)} %broadcast_in_dim.18), calls=%async_computation | async-start | bytes 2097152 | tf_op jit(solution)/shard_map/all_to_all | solution.py:131
  10.8 13.6 %all-to-all-done = f32[16,128,128]{2,1,0:T(8,128)S(1)} async-done(((f32[16,128,128]{2,1,0:T(8,128)}), f32[16,128,128]{2,1,0:T(8,128)S(1)}, u32[]{:S(2)}, u32[]{:S(2)}) %all-to-all-start) | async-done | bytes 1048608 | tf_op jit(solution)/shard_map/all_to_all | solution.py:131
  24.4 1.0 copy-done.1
  25.4 6.7 %shard_map.77 = f32[1792,128]{1,0:T(8,128)} custom-call(s32[1]{0:T(128)} %bitcast.56.count_ref, s32[24]{0:T(128)} %bitcast.79, s32[24]{0:T(128)} %bitcast.75, bf16[24,128,128]{2,1,0:T(8,128)(2,1)} %bitcast.62, f32[2048,128]{1,0:T(8,128)} %bitcast.66), custom_call_target="tpu_custom_call" | custom-call | tf_op jit(solution)/shard_map/pallas_call | solution.py:52
  32.0 1.1 constant_dynamic-slice_fusion.3
  33.2 5.7 %collective-permute-start = (f32[896,128]{1,0:T(8,128)S(1)}, f32[896,128]{1,0:T(8,128)S(1)}, u32[]{:S(2)}, u32[]{:S(2)}) collective-permute-start(f32[896,128]{1,0:T(8,128)S(1)} %constant_dynamic-slice_fusion.3), channel_id=1, source_target_pairs={{0,16},{16,0},{32,48},{48,32},{64,80},{80,64},{96,112},{112,96},{1... | collective-permute-start | bytes 1376264 | tf_op jit(solution)/shard_map/ppermute | solution.py:105
  39.0 1.4 collective-permute-done
  40.4 2.7 collective-permute-start.1
  43.2 6.0 %collective-permute-done.1 = f32[448,128]{1,0:T(8,128)S(1)} collective-permute-done((f32[448,128]{1,0:T(8,128)S(1)}, f32[448,128]{1,0:T(8,128)S(1)}, u32[]{:S(2)}, u32[]{:S(2)}) %collective-permute-start.1) | collective-permute-done | bytes 229408 | tf_op jit(solution)/shard_map/ppermute | solution.py:105
  49.2 29.8 %all_to_all.45 = f32[8,56,128]{2,1,0:T(8,128)S(1)} all-to-all(f32[8,56,128]{2,1,0:T(8,128)S(1)} %bitcast.74), channel_id=1, replica_groups={{0,64,128,192,256,320,384,448},{16,80,144,208,272,336,400,464},{32,96,1..., dimensions={0} | all-to-all | bytes 458752 | tf_op jit(solution)/shard_map/all_to_all | solution.py:111
  79.0 35.1 %all-gather = f32[1792,128]{1,0:T(8,128)S(1)} all-gather(f32[56,128]{1,0:T(8,128)S(1)} %reduce_sum.135), channel_id=2, replica_groups=mesh['comp'=32,'feat'=16] {'comp'}, dimensions={0}, use_global_device_ids=true | all-gather | bytes 946176 | tf_op jit(solution)/shard_map/all_gather | solution.py:115
  114.1 1.0 copy.15
  115.1 5.7 %shard_map.78 = f32[2048,128]{1,0:T(8,128)} custom-call(s32[1]{0:T(128)} %bitcast.57.count_ref, s32[24]{0:T(128)} %bitcast.76, s32[24]{0:T(128)} %bitcast.80, bf16[24,128,128]{2,1,0:T(8,128)(2,1)} %bitcast.63, f32[1792,128]{1,0:T(8,128)} %bitcast.60), custom_call_target="tpu_custom_call" | custom-call | tf_op jit(solution)/shard_map/pallas_call | solution.py:52
  120.8 3.8 %all-to-all-start.2 = ((f32[16,128,128]{2,1,0:T(8,128)}), f32[16,128,128]{2,1,0:T(8,128)S(1)}, u32[]{:S(2)}, u32[]{:S(2)}) async-start(f32[16,128,128]{2,1,0:T(8,128)} %bitcast.71), calls=%async_computation.2 | async-start | bytes 2097152 | tf_op jit(solution)/shard_map/all_to_all | solution.py:63
  124.7 17.3 %all-to-all-done.2 = f32[16,128,128]{2,1,0:T(8,128)S(1)} async-done(((f32[16,128,128]{2,1,0:T(8,128)}), f32[16,128,128]{2,1,0:T(8,128)S(1)}, u32[]{:S(2)}, u32[]{:S(2)}) %all-to-all-start.2) | async-done | bytes 1048608 | tf_op jit(solution)/shard_map/all_to_all | solution.py:63
  142.0 0.1 reduce_sum.136
  142.1 0.1 broadcast_in_dim.21
  142.2 19.2 %all_to_all.46 = f32[16,130,128]{2,1,0:T(8,128)S(1)} all-to-all(f32[16,130,128]{2,1,0:T(8,128)S(1)} %broadcast_in_dim.21), channel_id=1, replica_groups=mesh['comp'=32,'feat'=16] {'feat'}, dimensions={0} | all-to-all | bytes 2129920 | tf_op jit(solution)/shard_map/all_to_all | solution.py:131
  161.3 0.3 fusion.4
  161.7 22.2 %all_to_all.47 = f32[32,3,128]{2,1,0:T(4,128)S(1)} all-to-all(f32[32,3,128]{2,1,0:T(4,128)S(1)} %broadcast_in_dim.23), channel_id=1, replica_groups=mesh['comp'=32,'feat'=16] {'comp'}, dimensions={0} | all-to-all | bytes 98304 | tf_op jit(solution)/shard_map/all_to_all | solution.py:135
  184.0 1.1 multiply_subtract_fusion.x_ref
  185.1 6.7 %shard_map.79 = f32[1792,128]{1,0:T(8,128)} custom-call(s32[1]{0:T(128)} %bitcast.58.count_ref, s32[24]{0:T(128)} %bitcast.81, s32[24]{0:T(128)} %bitcast.77, bf16[24,128,128]{2,1,0:T(8,128)(2,1)} %bitcast.64, f32[2048,128]{1,0:T(8,128)} %multiply_subtract_fusion.x_ref), custom_call_target="tpu_custom_call" | custom-call | tf_op jit(solution)/shard_map/pallas_call | solution.py:52
  191.7 1.1 constant_dynamic-slice_fusion.1
  192.9 3.5 %collective-permute-start.2 = (f32[896,128]{1,0:T(8,128)S(1)}, f32[896,128]{1,0:T(8,128)S(1)}, u32[]{:S(2)}, u32[]{:S(2)}) collective-permute-start(f32[896,128]{1,0:T(8,128)S(1)} %constant_dynamic-slice_fusion.1), channel_id=1, source_target_pairs={{0,16},{16,0},{32,48},{48,32},{64,80},{80,64},{96,112},{112,96},{1... | collective-permute-start | bytes 1376264 | tf_op jit(solution)/shard_map/ppermute | solution.py:105
  196.4 1.4 collective-permute-done.2
  197.9 1.9 collective-permute-start.3
  199.8 6.8 %collective-permute-done.3 = f32[448,128]{1,0:T(8,128)S(1)} collective-permute-done((f32[448,128]{1,0:T(8,128)S(1)}, f32[448,128]{1,0:T(8,128)S(1)}, u32[]{:S(2)}, u32[]{:S(2)}) %collective-permute-start.3) | collective-permute-done | bytes 229408 | tf_op jit(solution)/shard_map/ppermute | solution.py:105
  206.6 0.7 dynamic-slice_add_fusion.2
  207.3 3.4 %all-to-all-start.5 = ((f32[8,56,128]{2,1,0:T(8,128)}), f32[8,56,128]{2,1,0:T(8,128)S(1)}, u32[]{:S(2)}, u32[]{:S(2)}) async-start(f32[8,56,128]{2,1,0:T(8,128)} %bitcast.17), calls=%async_computation.5 | async-start | bytes 458752 | tf_op jit(solution)/shard_map/all_to_all | solution.py:111
  210.7 0.1 broadcast_multiply_fusion
  210.8 15.1 %all-to-all-done.5 = f32[8,56,128]{2,1,0:T(8,128)S(1)} async-done(((f32[8,56,128]{2,1,0:T(8,128)}), f32[8,56,128]{2,1,0:T(8,128)S(1)}, u32[]{:S(2)}, u32[]{:S(2)}) %all-to-all-start.5) | async-done | bytes 229408 | tf_op jit(solution)/shard_map/all_to_all | solution.py:111
  225.9 35.5 %all-gather.2 = f32[32,57,128]{2,1,0:T(8,128)S(1)} all-gather(f32[1,57,128]{2,1,0:T(8,128)S(1)} %maximum_bitcast_fusion), channel_id=3, replica_groups=mesh['comp'=32,'feat'=16] {'comp'}, dimensions={0}, use_global_device_ids=true | all-gather | bytes 963072 | tf_op jit(solution)/shard_map/all_gather | solution.py:115
  261.4 0.1 slice_reduce_fusion
  261.5 0.1 slice.62
  261.5 1.0 copy.17
  262.5 0.6 scatter.4.rest_0_
  263.1 5.7 %shard_map.80 = f32[2176,128]{1,0:T(8,128)} custom-call(s32[1]{0:T(128)} %bitcast.59.count_ref, s32[24]{0:T(128)} %bitcast.78, s32[24]{0:T(128)} %bitcast.82, bf16[24,128,128]{2,1,0:T(8,128)(2,1)} %bitcast.65, f32[1792,128]{1,0:T(8,128)} %bitcast.67, f32[8,128]{1,0:T(8,128)} %scatter.4.rest_0_), custom_call_target="tpu_custom_call" | custom-call | tf_op jit(solution)/shard_map/pallas_call | solution.py:52
  268.8 4.4 %all-to-all-start.6 = ((f32[16,136,128]{2,1,0:T(8,128)}), f32[16,136,128]{2,1,0:T(8,128)}, u32[]{:S(2)}, u32[]{:S(2)}) async-start(f32[16,136,128]{2,1,0:T(8,128)} %bitcast.70), calls=%async_computation.6 | async-start | bytes 2228224 | tf_op jit(solution)/shard_map/all_to_all | solution.py:63
  273.2 0.0 copy-start.3
  273.2 18.4 %all-to-all-done.6 = f32[16,136,128]{2,1,0:T(8,128)} async-done(((f32[16,136,128]{2,1,0:T(8,128)}), f32[16,136,128]{2,1,0:T(8,128)}, u32[]{:S(2)}, u32[]{:S(2)}) %all-to-all-start.6) | async-done | bytes 1114144 | tf_op jit(solution)/shard_map/all_to_all | solution.py:63
  291.5 1.3 reduce_sum.145
  292.9 0.1 multiply_add_fusion.1
  293.0 0.9 copy-done.4
  294.0 9.4 %all_to_all.48 = f32[16,2,128]{2,1,0:T(2,128)S(1)} all-to-all(f32[16,2,128]{2,1,0:T(2,128)S(1)} %broadcast_in_dim.25), channel_id=1, replica_groups=mesh['comp'=32,'feat'=16] {'feat'}, dimensions={0} | all-to-all | bytes 32768 | tf_op jit(solution)/shard_map/all_to_all | solution.py:170
  303.4 19.9 %all_to_all.49 = f32[32,2,128]{2,1,0:T(2,128)S(1)} all-to-all(f32[32,2,128]{2,1,0:T(2,128)S(1)} %broadcast_in_dim.26), channel_id=1, replica_groups=mesh['comp'=32,'feat'=16] {'comp'}, dimensions={0} | all-to-all | bytes 65536 | tf_op jit(solution)/shard_map/all_to_all | solution.py:135
  323.4 1.5 multiply_subtract_fusion.1
  324.9 2.2 multiply_add_fusion
  (39 shorter events, 0.6 us)
Async XLA Ops:
  2.6 21.8 %all-to-all-start = ((f32[16,128,128]{2,1,0:T(8,128)}), f32[16,128,128]{2,1,0:T(8,128)S(1)}, u32[]{:S(2)}, u32[]{:S(2)}) async-start(f32[16,128,128]{2,1,0:T(8,128)} %broadcast_in_dim.18), calls=%async_computation | async-start | bytes 2097152 | tf_op jit(solution)/shard_map/all_to_all | solution.py:131
  24.4 1.0 copy-start.1
  32.0 8.3 %copy-start.5 = (f32[1792,128]{1,0:T(8,128)S(1)}, f32[1792,128]{1,0:T(8,128)}, u32[]{:S(2)}) copy-start(f32[1792,128]{1,0:T(8,128)} %shard_map.77) | copy-start | bytes 2752516
  33.2 7.2 %collective-permute-start = (f32[896,128]{1,0:T(8,128)S(1)}, f32[896,128]{1,0:T(8,128)S(1)}, u32[]{:S(2)}, u32[]{:S(2)}) collective-permute-start(f32[896,128]{1,0:T(8,128)S(1)} %constant_dynamic-slice_fusion.3), channel_id=1, source_target_pairs={{0,16},{16,0},{32,48},{48,32},{64,80},{80,64},{96,112},{112,96},{1... | collective-permute-start | bytes 1376264 | tf_op jit(solution)/shard_map/ppermute | solution.py:105
  40.4 8.7 %collective-permute-start.1 = (f32[448,128]{1,0:T(8,128)S(1)}, f32[448,128]{1,0:T(8,128)S(1)}, u32[]{:S(2)}, u32[]{:S(2)}) collective-permute-start(f32[448,128]{1,0:T(8,128)S(1)} %constant_dynamic-slice_fusion.2), channel_id=1, source_target_pairs={{0,32},{16,48},{32,0},{48,16},{64,96},{80,112},{96,64},{112,80},{1... | collective-permute-start | bytes 688136 | tf_op jit(solution)/shard_map/ppermute | solution.py:105
  120.8 3.8 %copy-start = (f32[2,2,8,56,128]{4,3,2,1,0:T(8,128)S(1)}, f32[2,2,8,56,128]{4,3,2,1,0:T(8,128)}, u32[]{:S(2)}) copy-start(f32[2,2,8,56,128]{4,3,2,1,0:T(8,128)} %copy.15) | copy-start | bytes 2752516
  120.8 21.2 %all-to-all-start.2 = ((f32[16,128,128]{2,1,0:T(8,128)}), f32[16,128,128]{2,1,0:T(8,128)S(1)}, u32[]{:S(2)}, u32[]{:S(2)}) async-start(f32[16,128,128]{2,1,0:T(8,128)} %bitcast.71), calls=%async_computation.2 | async-start | bytes 2097152 | tf_op jit(solution)/shard_map/all_to_all | solution.py:63
  161.3 22.6 %copy-start.7 = (f32[128]{0:T(128)S(1)}, f32[128]{0:T(128)}, u32[]{:S(2)}) copy-start(f32[128]{0:T(128)} %param.13) | copy-start | bytes 1540
  161.3 22.6 %copy-start.2 = (f32[16,128,128]{2,1,0:T(8,128)S(1)}, f32[16,128,128]{2,1,0:T(8,128)}, u32[]{:S(2)}) copy-start(f32[16,128,128]{2,1,0:T(8,128)} %copy-done.1) | copy-start | bytes 3145732
  191.7 6.1 %copy-start.6 = (f32[1792,128]{1,0:T(8,128)S(1)}, f32[1792,128]{1,0:T(8,128)}, u32[]{:S(2)}) copy-start(f32[1792,128]{1,0:T(8,128)} %shard_map.79) | copy-start | bytes 2752516
  192.9 4.9 %collective-permute-start.2 = (f32[896,128]{1,0:T(8,128)S(1)}, f32[896,128]{1,0:T(8,128)S(1)}, u32[]{:S(2)}, u32[]{:S(2)}) collective-permute-start(f32[896,128]{1,0:T(8,128)S(1)} %constant_dynamic-slice_fusion.1), channel_id=1, source_target_pairs={{0,16},{16,0},{32,48},{48,32},{64,80},{80,64},{96,112},{112,96},{1... | collective-permute-start | bytes 1376264 | tf_op jit(solution)/shard_map/ppermute | solution.py:105
  197.9 8.7 %collective-permute-start.3 = (f32[448,128]{1,0:T(8,128)S(1)}, f32[448,128]{1,0:T(8,128)S(1)}, u32[]{:S(2)}, u32[]{:S(2)}) collective-permute-start(f32[448,128]{1,0:T(8,128)S(1)} %constant_dynamic-slice_fusion), channel_id=1, source_target_pairs={{0,32},{16,48},{32,0},{48,16},{64,96},{80,112},{96,64},{112,80},{1... | collective-permute-start | bytes 688136 | tf_op jit(solution)/shard_map/ppermute | solution.py:105
  207.3 18.6 %all-to-all-start.5 = ((f32[8,56,128]{2,1,0:T(8,128)}), f32[8,56,128]{2,1,0:T(8,128)S(1)}, u32[]{:S(2)}, u32[]{:S(2)}) async-start(f32[8,56,128]{2,1,0:T(8,128)} %bitcast.17), calls=%async_computation.5 | async-start | bytes 458752 | tf_op jit(solution)/shard_map/all_to_all | solution.py:111
  268.8 22.8 %all-to-all-start.6 = ((f32[16,136,128]{2,1,0:T(8,128)}), f32[16,136,128]{2,1,0:T(8,128)}, u32[]{:S(2)}, u32[]{:S(2)}) async-start(f32[16,136,128]{2,1,0:T(8,128)} %bitcast.70), calls=%async_computation.6 | async-start | bytes 2228224 | tf_op jit(solution)/shard_map/all_to_all | solution.py:63
  273.2 19.7 %copy-start.3 = (f32[8,2,2,56,128]{4,3,0,1,2:T(8,128)S(1)}, f32[8,2,2,56,128]{4,3,0,1,2:T(8,128)}, u32[]{:S(2)}) copy-start(f32[8,2,2,56,128]{4,3,0,1,2:T(8,128)} %copy.17) | copy-start | bytes 2752516
  293.0 0.9 copy-start.4

commit v12 on v9

--- a/solution.py
+++ b/solution.py
@@ -57,6 +57,49 @@
     )(*operands)
 
 
+def _split_kernel(count_ref, out_idx_ref, in_idx_ref, core_ref, values_ref, x_ref, kept_ref, sent_ref):
+    edge = values_ref.shape[1]
+    half = kept_ref.shape[0] // edge
+    kept_ref[...] = jnp.zeros_like(kept_ref)
+    sent_ref[...] = jnp.zeros_like(sent_ref)
+
+    def body(s, carry):
+        @pl.when(s < count_ref[0])
+        def _():
+            src = pl.multiple_of(in_idx_ref[s] * edge, edge)
+            block_index = out_idx_ref[s]
+            dst = pl.multiple_of((block_index % half) * edge, edge)
+            x = x_ref[pl.ds(src, edge), :].astype(values_ref.dtype)
+            prod = jnp.dot(values_ref[s], x, preferred_element_type=jnp.float32)
+            mine = block_index // half == core_ref[0]
+
+            @pl.when(mine)
+            def _():
+                kept_ref[pl.ds(dst, edge), :] += prod
+
+            @pl.when(jnp.logical_not(mine))
+            def _():
+                sent_ref[pl.ds(dst, edge), :] += prod
+
+        return carry
+
+    lax.fori_loop(0, values_ref.shape[0], body, 0)
+
+
+def split_apply(values, count, out_idx, in_idx, x, core):
+    edge = values.shape[1]
+    rows = CB_DEV * edge // 2
+    smem = pl.BlockSpec(memory_space=pltpu.SMEM)
+    vmem = pl.BlockSpec(memory_space=pltpu.VMEM)
+    half = jax.ShapeDtypeStruct((rows, x.shape[1]), jnp.float32)
+    return pl.pallas_call(
+        _split_kernel,
+        out_shape=(half, half),
+        in_specs=[smem, smem, smem, smem, vmem, vmem],
+        out_specs=(vmem, vmem),
+    )(count.reshape(1), out_idx, in_idx, core.astype(jnp.int32).reshape(1), values, x)
+
+
 def reduce_over(partial, axis, parts):
     rows = partial.shape[0] // parts
     pieces = partial.reshape(parts, rows, *partial.shape[1:])
@@ -73,9 +116,12 @@
     feat_rows = CB_DEV * block_edge
     own_rows = feat_rows // n_comp
     comp_index = lax.axis_index("comp")
+    core = comp_index % 2
+
+    values_t = jnp.swapaxes(values, 1, 2)
 
     def backward(low_slab):
-        return block_apply(values, count_of_slots, slot_cols, slot_rows, low_slab, CB_DEV, True)
+        return split_apply(values_t, count_of_slots, slot_cols, slot_rows, low_slab, core)
 
     def forward(direction, extra=None):
         low = direction.astype(jnp.bfloat16)
@@ -89,7 +135,6 @@
         landed = reduce_over(summed, "feat", n_feat)
         return landed[:block_edge], landed[block_edge : block_edge + extra.shape[0]]
 
-    core = comp_index % 2
     chip = comp_index // 2
     n_chips = n_comp // 2
     half_rows = feat_rows // 2
@@ -99,9 +144,8 @@
     def swap_with_sibling(x):
         return lax.ppermute(x, "comp", siblings)
 
-    def reduce_gradient(partial):
-        kept = lax.dynamic_slice_in_dim(partial, core * half_rows, half_rows, axis=0)
-        sent = lax.dynamic_slice_in_dim(partial, (1 - core) * half_rows, half_rows, axis=0)
+    def reduce_gradient(halves):
+        kept, sent = halves
         chip_sum = kept + swap_with_sibling(sent)
         pieces = chip_sum.reshape(n_chips, own_rows, chip_sum.shape[1])
         landed = lax.all_to_all(pieces, "comp", 0, 0, tiled=True, axis_index_groups=same_core)

time: 327 us -> 326 us (level)
  blocking collectives: 180 us -> 186 us
  waiting for transfers between devices: 73.3 us -> 69.7 us
    pallas_call x4 -> x2, Pallas kernels: 24 us -> 10.4 us  [block_apply(): pl.pallas_call(functools.partial(_block_kernel, transpose, pitch), out_sh...]
    pallas_call x0 -> x2, Pallas kernels: none -> 10.6 us  [split_apply(): pl.pallas_call(_split_kernel, out_shape=(half, half), in_specs=[smem, sme...]
    all_to_all x2, blocking collectives: 36.7 us -> 40.5 us  [comp_total(): return lax.all_to_all(spread, 'comp', 0, 0, tiled=True).sum(0)]
  transfers between devices with their start and end apart: 6 -> 6, of which waited for: 6 -> 6; matrix products, arithmetic and copies ran while one was open for 0% -> 1% of each run, Pallas kernels for 0% -> 0%
where the time goes in v12:
time: 326 us; the launch traced here: 325 us
  blocking collectives  186 us (57%)
  waiting for transfers between devices  69.7 us (21%)
  starting transfers between devices  28.1 us (9%)
  Pallas kernels  21 us (6%)
  other arithmetic  14.3 us (4%)
  local copies, waits for them, and re-layouts  4.92 us (2%)
    all_gather x2, blocking collectives, gather_gradient(): got = lax.all_gather(own, 'comp', axis=0, tiled=False)  80.3 us
    all_to_all x2, blocking collectives, comp_total(): return lax.all_to_all(spread, 'comp', 0, 0, tiled=True).sum(0)  40.5 us
    all_to_all x1, blocking collectives, reduce_gradient(): lax.all_to_all(pieces, 'comp', 0, 0, tiled=True, axis_index_groups=same_c...  35.2 us
    all_to_all x2, waiting for transfers between devices, reduce_over(): return lax.all_to_all(pieces, axis, 0, 0, tiled=True).sum(0)  34.1 us
    all_to_all x1, waiting for transfers between devices, reduce_gradient(): lax.all_to_all(pieces, 'comp', 0, 0, tiled=True, axis_index_groups=same_c...  19.9 us
    all_to_all x1, blocking collectives, gather_feat(): return lax.all_to_all(spread, 'feat', 0, 0, tiled=True)  19.8 us
    all_to_all x1, waiting for transfers between devices, gather_feat(): return lax.all_to_all(spread, 'feat', 0, 0, tiled=True)  12.4 us
    pallas_call x2, Pallas kernels, split_apply(): pl.pallas_call(_split_kernel, out_shape=(half, half), in_specs=[smem, sme...  10.6 us
  transfers between devices with their start and end apart: 6, of which 6 were waited for; matrix products, arithmetic and copies ran while one was open for 1% of the time, Pallas kernels for 0%

profile of v12, /device:TPU:1, one launch (start us, length us, event | category | flops | bytes accessed | tf_op | source)
XLA Modules:
  0.0 325.2 jit_solution(16498899050337358180)
XLA Ops:
  0.6 1.9 broadcast_in_dim.18
  2.6 7.7 %all-to-all-start = ((f32[16,128,128]{2,1,0:T(8,128)}), f32[16,128,128]{2,1,0:T(8,128)S(1)}, u32[]{:S(2)}, u32[]{:S(2)}) async-start(f32[16,128,128]{2,1,0:T(8,128)} %broadcast_in_dim.18), calls=%async_computation | async-start | bytes 2097152 | tf_op jit(solution)/shard_map/all_to_all | solution.py:170
  10.9 0.0 copy-done
  11.0 1.2 copy.23.values_ref
  12.1 12.4 %all-to-all-done = f32[16,128,128]{2,1,0:T(8,128)S(1)} async-done(((f32[16,128,128]{2,1,0:T(8,128)}), f32[16,128,128]{2,1,0:T(8,128)S(1)}, u32[]{:S(2)}, u32[]{:S(2)}) %all-to-all-start) | async-done | bytes 1048608 | tf_op jit(solution)/shard_map/all_to_all | solution.py:170
  24.5 0.8 bitcast_convert_fusion.x_ref
  25.4 5.3 %shard_map.77 = (f32[896,128]{1,0:T(8,128)}, f32[896,128]{1,0:T(8,128)}) custom-call(s32[1]{0:T(128)} %bitcast.64.count_ref, s32[24]{0:T(128)} %bitcast.79, s32[24]{0:T(128)} %bitcast.83, s32[1]{0:T(128)} %bitcast.4.core_ref, bf16[24,128,128]{2,1,0:T(8,128)(2,1)} %copy.23.values_ref, bf16[2048,128]{1,0:T(8,128)(2,1)} %bitcast_convert_fusion.x_ref), custom_call_target="tpu_custom_call" | custom-call | tf_op jit(solution)/shard_map/pallas_call | solution.py:95
  30.6 5.4 %collective-permute-start = (f32[896,128]{1,0:T(8,128)}, f32[896,128]{1,0:T(8,128)S(1)}, u32[]{:S(2)}, u32[]{:S(2)}) collective-permute-start(f32[896,128]{1,0:T(8,128)} %get-tuple-element.19), channel_id=1, source_target_pairs={{0,16},{16,0},{32,48},{48,32},{64,80},{80,64},{96,112},{112,96},{1... | collective-permute-start | bytes 1376264 | tf_op jit(solution)/shard_map/ppermute | solution.py:145
  36.1 1.6 collective-permute-done
  37.7 1.1 add.45
  38.8 35.2 %all_to_all.45 = f32[16,56,128]{2,1,0:T(8,128)S(1)} all-to-all(f32[16,56,128]{2,1,0:T(8,128)S(1)} %bitcast.78), channel_id=1, replica_groups={{0,32,64,96,128,160,192,224,256,288,320,352,384,416,448,480},{16,48,80,..., dimensions={0} | all-to-all | bytes 917504 | tf_op jit(solution)/shard_map/all_to_all | solution.py:151
  74.1 40.1 %all-gather = f32[1792,128]{1,0:T(8,128)S(1)} all-gather(f32[56,128]{1,0:T(8,128)S(1)} %reduce_sum.135), channel_id=2, replica_groups=mesh['comp'=32,'feat'=16] {'comp'}, dimensions={0}, use_global_device_ids=true | all-gather | bytes 946176 | tf_op jit(solution)/shard_map/all_gather | solution.py:155
  114.2 0.1 copy.24
  114.3 0.8 bitcast_convert_fusion.2.x_ref
  115.1 5.2 %shard_map.78 = f32[2048,128]{1,0:T(8,128)} custom-call(s32[1]{0:T(128)} %bitcast.65.count_ref, s32[24]{0:T(128)} %bitcast.84, s32[24]{0:T(128)} %bitcast.80, bf16[24,128,128]{2,1,0:T(8,128)(2,1)} %bitcast.69, bf16[1792,128]{1,0:T(8,128)(2,1)} %bitcast_convert_fusion.2.x_ref), custom_call_target="tpu_custom_call" | custom-call | tf_op jit(solution)/shard_map/pallas_call | solution.py:52
  120.3 3.8 %all-to-all-start.2 = ((f32[16,128,128]{2,1,0:T(8,128)}), f32[16,128,128]{2,1,0:T(8,128)S(1)}, u32[]{:S(2)}, u32[]{:S(2)}) async-start(f32[16,128,128]{2,1,0:T(8,128)} %bitcast.75), calls=%async_computation.2 | async-start | bytes 2097152 | tf_op jit(solution)/shard_map/all_to_all | solution.py:106
  124.2 16.4 %all-to-all-done.2 = f32[16,128,128]{2,1,0:T(8,128)S(1)} async-done(((f32[16,128,128]{2,1,0:T(8,128)}), f32[16,128,128]{2,1,0:T(8,128)S(1)}, u32[]{:S(2)}, u32[]{:S(2)}) %all-to-all-start.2) | async-done | bytes 1048608 | tf_op jit(solution)/shard_map/all_to_all | solution.py:106
  140.6 0.1 reduce_sum.136
  140.7 0.1 broadcast_in_dim.21
  140.7 19.8 %all_to_all.46 = f32[16,130,128]{2,1,0:T(8,128)S(1)} all-to-all(f32[16,130,128]{2,1,0:T(8,128)S(1)} %broadcast_in_dim.21), channel_id=1, replica_groups=mesh['comp'=32,'feat'=16] {'feat'}, dimensions={0} | all-to-all | bytes 2129920 | tf_op jit(solution)/shard_map/all_to_all | solution.py:170
  160.5 0.3 fusion.5
  160.9 20.4 %all_to_all.47 = f32[32,3,128]{2,1,0:T(4,128)S(1)} all-to-all(f32[32,3,128]{2,1,0:T(4,128)S(1)} %broadcast_in_dim.23), channel_id=1, replica_groups=mesh['comp'=32,'feat'=16] {'comp'}, dimensions={0} | all-to-all | bytes 98304 | tf_op jit(solution)/shard_map/all_to_all | solution.py:174
  181.4 1.3 fusion.4
  182.6 5.3 %shard_map.79 = (f32[896,128]{1,0:T(8,128)}, f32[896,128]{1,0:T(8,128)}) custom-call(s32[1]{0:T(128)} %bitcast.66.count_ref, s32[24]{0:T(128)} %bitcast.81, s32[24]{0:T(128)} %bitcast.85, s32[1]{0:T(128)} %bitcast.4.core_ref, bf16[24,128,128]{2,1,0:T(8,128)(2,1)} %copy.23.values_ref, bf16[2048,128]{1,0:T(8,128)(2,1)} %get-tuple-element.24.x_ref), custom_call_target="tpu_custom_call" | custom-call | tf_op jit(solution)/shard_map/pallas_call | solution.py:95
  187.9 3.2 collective-permute-start.1
  191.1 1.6 collective-permute-done.1
  192.7 1.8 add.49
  194.6 3.6 %all-to-all-start.5 = ((f32[16,56,128]{2,1,0:T(8,128)}), f32[16,56,128]{2,1,0:T(8,128)S(1)}, u32[]{:S(2)}, u32[]{:S(2)}) async-start(f32[16,56,128]{2,1,0:T(8,128)} %bitcast.19), calls=%async_computation.5 | async-start | bytes 917504 | tf_op jit(solution)/shard_map/all_to_all | solution.py:151
  198.2 1.0 broadcast_multiply_fusion
  199.1 19.9 %all-to-all-done.5 = f32[16,56,128]{2,1,0:T(8,128)S(1)} async-done(((f32[16,56,128]{2,1,0:T(8,128)}), f32[16,56,128]{2,1,0:T(8,128)S(1)}, u32[]{:S(2)}, u32[]{:S(2)}) %all-to-all-start.5) | async-done | bytes 458784 | tf_op jit(solution)/shard_map/all_to_all | solution.py:151
  219.1 0.8 multiply_reduce_fusion.3
  219.9 40.2 %all-gather.2 = f32[32,57,128]{2,1,0:T(8,128)S(1)} all-gather(f32[1,57,128]{2,1,0:T(8,128)S(1)} %maximum_bitcast_fusion), channel_id=3, replica_groups=mesh['comp'=32,'feat'=16] {'comp'}, dimensions={0}, use_global_device_ids=true | all-gather | bytes 963072 | tf_op jit(solution)/shard_map/all_gather | solution.py:155
  260.1 0.1 slice_reduce_fusion
  260.2 0.1 slice.62
  260.2 0.1 copy.27
  260.3 0.6 scatter.4.rest_0_
  260.9 0.8 bitcast_convert_fusion.1.x_ref
  261.7 5.2 %shard_map.80 = f32[2176,128]{1,0:T(8,128)} custom-call(s32[1]{0:T(128)} %bitcast.67.count_ref, s32[24]{0:T(128)} %bitcast.86, s32[24]{0:T(128)} %bitcast.82, bf16[24,128,128]{2,1,0:T(8,128)(2,1)} %bitcast.70, bf16[1792,128]{1,0:T(8,128)(2,1)} %bitcast_convert_fusion.1.x_ref, f32[8,128]{1,0:T(8,128)} %scatter.4.rest_0_), custom_call_target="tpu_custom_call" | custom-call | tf_op jit(solution)/shard_map/pallas_call | solution.py:52
  267.0 4.4 %all-to-all-start.6 = ((f32[16,136,128]{2,1,0:T(8,128)}), f32[16,136,128]{2,1,0:T(8,128)}, u32[]{:S(2)}, u32[]{:S(2)}) async-start(f32[16,136,128]{2,1,0:T(8,128)} %bitcast.74), calls=%async_computation.6 | async-start | bytes 2228224 | tf_op jit(solution)/shard_map/all_to_all | solution.py:106
  271.3 17.7 %all-to-all-done.6 = f32[16,136,128]{2,1,0:T(8,128)} async-done(((f32[16,136,128]{2,1,0:T(8,128)}), f32[16,136,128]{2,1,0:T(8,128)}, u32[]{:S(2)}, u32[]{:S(2)}) %all-to-all-start.6) | async-done | bytes 1114144 | tf_op jit(solution)/shard_map/all_to_all | solution.py:106
  289.0 1.3 reduce_sum.145
  290.4 0.1 bitcast_add_fusion
  290.5 0.0 copy-start.1
  290.5 0.9 copy-done.1
  291.5 9.9 %all_to_all.48 = f32[16,2,128]{2,1,0:T(2,128)S(1)} all-to-all(f32[16,2,128]{2,1,0:T(2,128)S(1)} %broadcast_in_dim.25), channel_id=1, replica_groups=mesh['comp'=32,'feat'=16] {'feat'}, dimensions={0} | all-to-all | bytes 32768 | tf_op jit(solution)/shard_map/all_to_all | solution.py:209
  301.4 20.1 %all_to_all.49 = f32[32,2,128]{2,1,0:T(2,128)S(1)} all-to-all(f32[32,2,128]{2,1,0:T(2,128)S(1)} %broadcast_in_dim.26), channel_id=1, replica_groups=mesh['comp'=32,'feat'=16] {'comp'}, dimensions={0} | all-to-all | bytes 65536 | tf_op jit(solution)/shard_map/all_to_all | solution.py:174
  321.5 2.2 multiply_add_fusion
  323.7 1.5 multiply_subtract_fusion
  (23 shorter events, 0.4 us)
Async XLA Ops:
  2.6 8.4 %copy-start = (bf16[1,1,24,128,128]{4,3,2,1,0:T(8,128)(2,1)S(1)}, bf16[1,1,24,128,128]{4,3,2,1,0:T(8,128)(2,1)}, u32[]{:S(2)}) copy-start(bf16[1,1,24,128,128]{4,3,2,1,0:T(8,128)(2,1)} %param.8) | copy-start | bytes 2359300
  2.6 22.0 %all-to-all-start = ((f32[16,128,128]{2,1,0:T(8,128)}), f32[16,128,128]{2,1,0:T(8,128)S(1)}, u32[]{:S(2)}, u32[]{:S(2)}) async-start(f32[16,128,128]{2,1,0:T(8,128)} %broadcast_in_dim.18), calls=%async_computation | async-start | bytes 2097152 | tf_op jit(solution)/shard_map/all_to_all | solution.py:170
  30.6 7.1 %collective-permute-start = (f32[896,128]{1,0:T(8,128)}, f32[896,128]{1,0:T(8,128)S(1)}, u32[]{:S(2)}, u32[]{:S(2)}) collective-permute-start(f32[896,128]{1,0:T(8,128)} %get-tuple-element.19), channel_id=1, source_target_pairs={{0,16},{16,0},{32,48},{48,32},{64,80},{80,64},{96,112},{112,96},{1... | collective-permute-start | bytes 1376264 | tf_op jit(solution)/shard_map/ppermute | solution.py:145
  120.3 20.3 %all-to-all-start.2 = ((f32[16,128,128]{2,1,0:T(8,128)}), f32[16,128,128]{2,1,0:T(8,128)S(1)}, u32[]{:S(2)}, u32[]{:S(2)}) async-start(f32[16,128,128]{2,1,0:T(8,128)} %bitcast.75), calls=%async_computation.2 | async-start | bytes 2097152 | tf_op jit(solution)/shard_map/all_to_all | solution.py:106
  160.5 20.8 %copy-start.2 = (f32[128]{0:T(128)S(1)}, f32[128]{0:T(128)}, u32[]{:S(2)}) copy-start(f32[128]{0:T(128)} %param.13) | copy-start | bytes 1540
  187.9 4.8 %collective-permute-start.1 = (f32[896,128]{1,0:T(8,128)}, f32[896,128]{1,0:T(8,128)S(1)}, u32[]{:S(2)}, u32[]{:S(2)}) collective-permute-start(f32[896,128]{1,0:T(8,128)} %get-tuple-element.21), channel_id=1, source_target_pairs={{0,16},{16,0},{32,48},{48,32},{64,80},{80,64},{96,112},{112,96},{1... | collective-permute-start | bytes 1376264 | tf_op jit(solution)/shard_map/ppermute | solution.py:145
  194.6 24.5 %all-to-all-start.5 = ((f32[16,56,128]{2,1,0:T(8,128)}), f32[16,56,128]{2,1,0:T(8,128)S(1)}, u32[]{:S(2)}, u32[]{:S(2)}) async-start(f32[16,56,128]{2,1,0:T(8,128)} %bitcast.19), calls=%async_computation.5 | async-start | bytes 917504 | tf_op jit(solution)/shard_map/all_to_all | solution.py:151
  267.0 22.1 %all-to-all-start.6 = ((f32[16,136,128]{2,1,0:T(8,128)}), f32[16,136,128]{2,1,0:T(8,128)}, u32[]{:S(2)}, u32[]{:S(2)}) async-start(f32[16,136,128]{2,1,0:T(8,128)} %bitcast.74), calls=%async_computation.6 | async-start | bytes 2228224 | tf_op jit(solution)/shard_map/all_to_all | solution.py:106
  290.5 0.9 copy-start.1

commit v13 on v9

--- a/solution.py
+++ b/solution.py
@@ -135,7 +135,8 @@
     def low_slab(slab):
         return slab.astype(jnp.bfloat16)
 
-    gradient_own = reduce_gradient(backward(low_slab(residual_slab)))
+    zero_solution = 0.0 * residual_slab[:feat_rows]
+    gradient_own = reduce_gradient(backward(low_slab(residual_slab))) - ridge * own_part(zero_solution)
     energy_own = col_sq(gradient_own)
     direction, _ = gather_gradient(gradient_own)
     energy = None

time: 327 us -> 327 us (level)
  blocking collectives: 180 us -> 151 us
  starting transfers between devices: 28.2 us -> 45.7 us
  waiting for transfers between devices: 73.3 us -> 88.6 us
  Pallas kernels: 24 us -> 19.5 us
    all_to_all x1 -> x0, blocking collectives: 34.8 us -> none  [reduce_gradient(): lax.all_to_all(pieces, 'comp', 0, 0, tiled=True, axis_index_groups=same_c...]
    all_to_all x1 -> x2, waiting for transfers between devices: 19.9 us -> 40.5 us  [reduce_gradient(): lax.all_to_all(pieces, 'comp', 0, 0, tiled=True, axis_index_groups=same_c...]
    all_to_all x1 -> x2, starting transfers between devices: 3.56 us -> 18.7 us  [reduce_gradient(): lax.all_to_all(pieces, 'comp', 0, 0, tiled=True, axis_index_groups=same_c...]
    all_to_all x2, blocking collectives: 36.7 us -> 42 us  [comp_total(): return lax.all_to_all(spread, 'comp', 0, 0, tiled=True).sum(0)]
    all_to_all x2, waiting for transfers between devices: 37 us -> 31.7 us  [reduce_over(): return lax.all_to_all(pieces, axis, 0, 0, tiled=True).sum(0)]
    pallas_call x4, Pallas kernels: 24 us -> 19.5 us  [block_apply(): pl.pallas_call(functools.partial(_block_kernel, transpose, pitch), out_sh...]
  transfers between devices with their start and end apart: 6 -> 7, of which waited for: 6 -> 7; matrix products, arithmetic and copies ran while one was open for 0% -> 0% of each run, Pallas kernels for 0% -> 0%
where the time goes in v13:
time: 327 us; the launch traced here: 326 us
  blocking collectives  151 us (46%)
  waiting for transfers between devices  88.6 us (27%)
  starting transfers between devices  45.7 us (14%)
  Pallas kernels  19.5 us (6%)
  other arithmetic  13.1 us (4%)
  local copies, waits for them, and re-layouts  6.02 us (2%)
    all_gather x2, blocking collectives, gather_gradient(): got = lax.all_gather(own, 'comp', axis=0, tiled=False)  80.3 us
    all_to_all x2, blocking collectives, comp_total(): return lax.all_to_all(spread, 'comp', 0, 0, tiled=True).sum(0)  42 us
    all_to_all x2, waiting for transfers between devices, reduce_gradient(): lax.all_to_all(pieces, 'comp', 0, 0, tiled=True, axis_index_groups=same_c...  40.5 us
    all_to_all x2, waiting for transfers between devices, reduce_over(): return lax.all_to_all(pieces, axis, 0, 0, tiled=True).sum(0)  31.7 us
    pallas_call x4, Pallas kernels, block_apply(): pl.pallas_call(functools.partial(_block_kernel, transpose, pitch), out_sh...  19.5 us
    all_to_all x1, blocking collectives, gather_feat(): return lax.all_to_all(spread, 'feat', 0, 0, tiled=True)  19 us
    all_to_all x2, starting transfers between devices, reduce_gradient(): lax.all_to_all(pieces, 'comp', 0, 0, tiled=True, axis_index_groups=same_c...  18.7 us
    all_to_all x1, waiting for transfers between devices, gather_feat(): return lax.all_to_all(spread, 'feat', 0, 0, tiled=True)  13.6 us
  transfers between devices with their start and end apart: 7, of which 7 were waited for; matrix products, arithmetic and copies ran while one was open for 0% of the time, Pallas kernels for 0%

profile of v13, /device:TPU:1, one launch (start us, length us, event | category | flops | bytes accessed | tf_op | source)
XLA Modules:
  0.0 326.0 jit_solution(13087020490923630320)
XLA Ops:
  0.6 1.9 broadcast_in_dim.18
  2.6 7.6 %all-to-all-start = ((f32[16,128,128]{2,1,0:T(8,128)}), f32[16,128,128]{2,1,0:T(8,128)S(1)}, u32[]{:S(2)}, u32[]{:S(2)}) async-start(f32[16,128,128]{2,1,0:T(8,128)} %broadcast_in_dim.18), calls=%async_computation | async-start | bytes 2097152 | tf_op jit(solution)/shard_map/all_to_all | solution.py:126
  10.8 13.6 %all-to-all-done = f32[16,128,128]{2,1,0:T(8,128)S(1)} async-done(((f32[16,128,128]{2,1,0:T(8,128)}), f32[16,128,128]{2,1,0:T(8,128)S(1)}, u32[]{:S(2)}, u32[]{:S(2)}) %all-to-all-start) | async-done | bytes 1048608 | tf_op jit(solution)/shard_map/all_to_all | solution.py:126
  24.4 0.8 bitcast_convert_fusion.x_ref
  25.2 5.2 %shard_map.77 = f32[1792,128]{1,0:T(8,128)} custom-call(s32[1]{0:T(128)} %bitcast.62.count_ref, s32[24]{0:T(128)} %bitcast.78, s32[24]{0:T(128)} %bitcast.82, bf16[24,128,128]{2,1,0:T(8,128)(2,1)} %bitcast.67, bf16[2048,128]{1,0:T(8,128)(2,1)} %bitcast_convert_fusion.x_ref), custom_call_target="tpu_custom_call" | custom-call | tf_op jit(solution)/shard_map/pallas_call | solution.py:52
  30.5 1.1 constant_dynamic-slice_fusion.1
  31.6 6.8 %collective-permute-start = (f32[896,128]{1,0:T(8,128)S(1)}, f32[896,128]{1,0:T(8,128)S(1)}, u32[]{:S(2)}, u32[]{:S(2)}) collective-permute-start(f32[896,128]{1,0:T(8,128)S(1)} %constant_dynamic-slice_fusion.1), channel_id=1, source_target_pairs={{0,16},{16,0},{32,48},{48,32},{64,80},{80,64},{96,112},{112,96},{1... | collective-permute-start | bytes 1376264 | tf_op jit(solution)/shard_map/ppermute | solution.py:100
  38.4 1.4 collective-permute-done
  39.8 0.8 dynamic-slice_add_fusion.1
  40.7 15.2 %all-to-all-start.1 = ((f32[16,56,128]{2,1,0:T(8,128)}), f32[16,56,128]{2,1,0:T(8,128)S(1)}, u32[]{:S(2)}, u32[]{:S(2)}) async-start(f32[16,56,128]{2,1,0:T(8,128)} %bitcast.5), calls=%async_computation.1 | async-start | bytes 917504 | tf_op jit(solution)/shard_map/all_to_all | solution.py:107
  55.8 0.1 slice_multiply_fusion
  55.9 20.6 %all-to-all-done.1 = f32[16,56,128]{2,1,0:T(8,128)S(1)} async-done(((f32[16,56,128]{2,1,0:T(8,128)}), f32[16,56,128]{2,1,0:T(8,128)S(1)}, u32[]{:S(2)}, u32[]{:S(2)}) %all-to-all-start.1) | async-done | bytes 458784 | tf_op jit(solution)/shard_map/all_to_all | solution.py:107
  76.6 40.1 %all-gather = f32[1792,128]{1,0:T(8,128)S(1)} all-gather(f32[56,128]{1,0:T(8,128)S(1)} %get-tuple-element.19), channel_id=2, replica_groups=mesh['comp'=32,'feat'=16] {'comp'}, dimensions={0}, use_global_device_ids=true | all-gather | bytes 946176 | tf_op jit(solution)/shard_map/all_gather | solution.py:111
  116.7 0.1 copy.14
  116.8 0.8 bitcast_convert_fusion.2.x_ref
  117.6 4.5 %shard_map.78 = f32[2048,128]{1,0:T(8,128)} custom-call(s32[1]{0:T(128)} %bitcast.63.count_ref, s32[24]{0:T(128)} %bitcast.83, s32[24]{0:T(128)} %bitcast.79, bf16[24,128,128]{2,1,0:T(8,128)(2,1)} %bitcast.68, bf16[1792,128]{1,0:T(8,128)(2,1)} %bitcast_convert_fusion.2.x_ref), custom_call_target="tpu_custom_call" | custom-call | tf_op jit(solution)/shard_map/pallas_call | solution.py:52
  122.1 3.7 %all-to-all-start.2 = ((f32[16,128,128]{2,1,0:T(8,128)}), f32[16,128,128]{2,1,0:T(8,128)S(1)}, u32[]{:S(2)}, u32[]{:S(2)}) async-start(f32[16,128,128]{2,1,0:T(8,128)} %bitcast.74), calls=%async_computation.2 | async-start | bytes 2097152 | tf_op jit(solution)/shard_map/all_to_all | solution.py:63
  125.8 15.5 %all-to-all-done.2 = f32[16,128,128]{2,1,0:T(8,128)S(1)} async-done(((f32[16,128,128]{2,1,0:T(8,128)}), f32[16,128,128]{2,1,0:T(8,128)S(1)}, u32[]{:S(2)}, u32[]{:S(2)}) %all-to-all-start.2) | async-done | bytes 1048608 | tf_op jit(solution)/shard_map/all_to_all | solution.py:63
  141.2 0.1 reduce_sum.136
  141.3 0.1 broadcast_in_dim.21
  141.4 19.0 %all_to_all.45 = f32[16,130,128]{2,1,0:T(8,128)S(1)} all-to-all(f32[16,130,128]{2,1,0:T(8,128)S(1)} %broadcast_in_dim.21), channel_id=1, replica_groups=mesh['comp'=32,'feat'=16] {'feat'}, dimensions={0} | all-to-all | bytes 2129920 | tf_op jit(solution)/shard_map/all_to_all | solution.py:126
  160.4 0.3 fusion.5
  160.7 22.0 %all_to_all.46 = f32[32,3,128]{2,1,0:T(4,128)S(1)} all-to-all(f32[32,3,128]{2,1,0:T(4,128)S(1)} %broadcast_in_dim.23), channel_id=1, replica_groups=mesh['comp'=32,'feat'=16] {'comp'}, dimensions={0} | all-to-all | bytes 98304 | tf_op jit(solution)/shard_map/all_to_all | solution.py:130
  182.7 1.3 fusion.4
  184.0 5.2 %shard_map.79 = f32[1792,128]{1,0:T(8,128)} custom-call(s32[1]{0:T(128)} %bitcast.64.count_ref, s32[24]{0:T(128)} %bitcast.80, s32[24]{0:T(128)} %bitcast.84, bf16[24,128,128]{2,1,0:T(8,128)(2,1)} %bitcast.69, bf16[2048,128]{1,0:T(8,128)(2,1)} %get-tuple-element.16.x_ref), custom_call_target="tpu_custom_call" | custom-call | tf_op jit(solution)/shard_map/pallas_call | solution.py:52
  189.3 1.1 constant_dynamic-slice_fusion
  190.4 4.5 %collective-permute-start.1 = (f32[896,128]{1,0:T(8,128)S(1)}, f32[896,128]{1,0:T(8,128)S(1)}, u32[]{:S(2)}, u32[]{:S(2)}) collective-permute-start(f32[896,128]{1,0:T(8,128)S(1)} %constant_dynamic-slice_fusion), channel_id=1, source_target_pairs={{0,16},{16,0},{32,48},{48,32},{64,80},{80,64},{96,112},{112,96},{1... | collective-permute-start | bytes 1376264 | tf_op jit(solution)/shard_map/ppermute | solution.py:100
  194.9 1.4 collective-permute-done.1
  196.4 0.8 dynamic-slice_add_fusion
  197.2 3.6 %all-to-all-start.5 = ((f32[16,56,128]{2,1,0:T(8,128)}), f32[16,56,128]{2,1,0:T(8,128)S(1)}, u32[]{:S(2)}, u32[]{:S(2)}) async-start(f32[16,56,128]{2,1,0:T(8,128)} %bitcast.18), calls=%async_computation.5 | async-start | bytes 917504 | tf_op jit(solution)/shard_map/all_to_all | solution.py:107
  200.8 1.0 broadcast_multiply_fusion
  201.7 19.9 %all-to-all-done.5 = f32[16,56,128]{2,1,0:T(8,128)S(1)} async-done(((f32[16,56,128]{2,1,0:T(8,128)}), f32[16,56,128]{2,1,0:T(8,128)S(1)}, u32[]{:S(2)}, u32[]{:S(2)}) %all-to-all-start.5) | async-done | bytes 458784 | tf_op jit(solution)/shard_map/all_to_all | solution.py:107
  221.7 0.8 multiply_reduce_fusion.3
  222.5 40.2 %all-gather.2 = f32[32,57,128]{2,1,0:T(8,128)S(1)} all-gather(f32[1,57,128]{2,1,0:T(8,128)S(1)} %maximum_bitcast_fusion), channel_id=3, replica_groups=mesh['comp'=32,'feat'=16] {'comp'}, dimensions={0}, use_global_device_ids=true | all-gather | bytes 963072 | tf_op jit(solution)/shard_map/all_gather | solution.py:111
  262.8 0.1 slice.68
  262.9 0.1 copy.16
  262.9 0.6 scatter.4.rest_0_
  263.5 0.8 bitcast_convert_fusion.1.x_ref
  264.3 4.5 %shard_map.80 = f32[2176,128]{1,0:T(8,128)} custom-call(s32[1]{0:T(128)} %bitcast.65.count_ref, s32[24]{0:T(128)} %bitcast.85, s32[24]{0:T(128)} %bitcast.81, bf16[24,128,128]{2,1,0:T(8,128)(2,1)} %bitcast.70, bf16[1792,128]{1,0:T(8,128)(2,1)} %bitcast_convert_fusion.1.x_ref, f32[8,128]{1,0:T(8,128)} %scatter.4.rest_0_), custom_call_target="tpu_custom_call" | custom-call | tf_op jit(solution)/shard_map/pallas_call | solution.py:52
  268.9 4.4 %all-to-all-start.6 = ((f32[16,136,128]{2,1,0:T(8,128)}), f32[16,136,128]{2,1,0:T(8,128)}, u32[]{:S(2)}, u32[]{:S(2)}) async-start(f32[16,136,128]{2,1,0:T(8,128)} %bitcast.73), calls=%async_computation.6 | async-start | bytes 2228224 | tf_op jit(solution)/shard_map/all_to_all | solution.py:63
  273.3 16.3 %all-to-all-done.6 = f32[16,136,128]{2,1,0:T(8,128)} async-done(((f32[16,136,128]{2,1,0:T(8,128)}), f32[16,136,128]{2,1,0:T(8,128)}, u32[]{:S(2)}, u32[]{:S(2)}) %all-to-all-start.6) | async-done | bytes 1114144 | tf_op jit(solution)/shard_map/all_to_all | solution.py:63
  289.5 1.3 reduce_sum.145
  290.8 0.1 bitcast_add_fusion
  291.0 0.9 copy-done
  292.0 10.2 %all_to_all.47 = f32[16,2,128]{2,1,0:T(2,128)S(1)} all-to-all(f32[16,2,128]{2,1,0:T(2,128)S(1)} %broadcast_in_dim.25), channel_id=1, replica_groups=mesh['comp'=32,'feat'=16] {'feat'}, dimensions={0} | all-to-all | bytes 32768 | tf_op jit(solution)/shard_map/all_to_all | solution.py:166
  302.2 20.0 %all_to_all.48 = f32[32,2,128]{2,1,0:T(2,128)S(1)} all-to-all(f32[32,2,128]{2,1,0:T(2,128)S(1)} %broadcast_in_dim.26), channel_id=1, replica_groups=mesh['comp'=32,'feat'=16] {'comp'}, dimensions={0} | all-to-all | bytes 65536 | tf_op jit(solution)/shard_map/all_to_all | solution.py:130
  322.3 2.2 multiply_add_fusion
  324.5 1.5 multiply_subtract_fusion
  (28 shorter events, 0.5 us)
Async XLA Ops:
  2.6 21.8 %all-to-all-start = ((f32[16,128,128]{2,1,0:T(8,128)}), f32[16,128,128]{2,1,0:T(8,128)S(1)}, u32[]{:S(2)}, u32[]{:S(2)}) async-start(f32[16,128,128]{2,1,0:T(8,128)} %broadcast_in_dim.18), calls=%async_computation | async-start | bytes 2097152 | tf_op jit(solution)/shard_map/all_to_all | solution.py:126
  30.5 9.4 %copy-start.1 = (f32[1792,128]{1,0:T(8,128)S(1)}, f32[1792,128]{1,0:T(8,128)}, u32[]{:S(2)}) copy-start(f32[1792,128]{1,0:T(8,128)} %shard_map.77) | copy-start | bytes 2752516
  31.6 8.2 %collective-permute-start = (f32[896,128]{1,0:T(8,128)S(1)}, f32[896,128]{1,0:T(8,128)S(1)}, u32[]{:S(2)}, u32[]{:S(2)}) collective-permute-start(f32[896,128]{1,0:T(8,128)S(1)} %constant_dynamic-slice_fusion.1), channel_id=1, source_target_pairs={{0,16},{16,0},{32,48},{48,32},{64,80},{80,64},{96,112},{112,96},{1... | collective-permute-start | bytes 1376264 | tf_op jit(solution)/shard_map/ppermute | solution.py:100
  40.7 35.9 %all-to-all-start.1 = ((f32[16,56,128]{2,1,0:T(8,128)}), f32[16,56,128]{2,1,0:T(8,128)S(1)}, u32[]{:S(2)}, u32[]{:S(2)}) async-start(f32[16,56,128]{2,1,0:T(8,128)} %bitcast.5), calls=%async_computation.1 | async-start | bytes 917504 | tf_op jit(solution)/shard_map/all_to_all | solution.py:107
  55.8 20.7 %copy-start.3 = (f32[128]{0:T(128)S(1)}, f32[128]{0:T(128)}, u32[]{:S(2)}) copy-start(f32[128]{0:T(128)} %param.13) | copy-start | bytes 1540
  122.1 19.2 %all-to-all-start.2 = ((f32[16,128,128]{2,1,0:T(8,128)}), f32[16,128,128]{2,1,0:T(8,128)S(1)}, u32[]{:S(2)}, u32[]{:S(2)}) async-start(f32[16,128,128]{2,1,0:T(8,128)} %bitcast.74), calls=%async_computation.2 | async-start | bytes 2097152 | tf_op jit(solution)/shard_map/all_to_all | solution.py:63
  189.3 7.1 %copy-start.2 = (f32[1792,128]{1,0:T(8,128)S(1)}, f32[1792,128]{1,0:T(8,128)}, u32[]{:S(2)}) copy-start(f32[1792,128]{1,0:T(8,128)} %shard_map.79) | copy-start | bytes 2752516
  190.4 6.0 %collective-permute-start.1 = (f32[896,128]{1,0:T(8,128)S(1)}, f32[896,128]{1,0:T(8,128)S(1)}, u32[]{:S(2)}, u32[]{:S(2)}) collective-permute-start(f32[896,128]{1,0:T(8,128)S(1)} %constant_dynamic-slice_fusion), channel_id=1, source_target_pairs={{0,16},{16,0},{32,48},{48,32},{64,80},{80,64},{96,112},{112,96},{1... | collective-permute-start | bytes 1376264 | tf_op jit(solution)/shard_map/ppermute | solution.py:100
  197.2 24.5 %all-to-all-start.5 = ((f32[16,56,128]{2,1,0:T(8,128)}), f32[16,56,128]{2,1,0:T(8,128)S(1)}, u32[]{:S(2)}, u32[]{:S(2)}) async-start(f32[16,56,128]{2,1,0:T(8,128)} %bitcast.18), calls=%async_computation.5 | async-start | bytes 917504 | tf_op jit(solution)/shard_map/all_to_all | solution.py:107
  268.9 20.7 %all-to-all-start.6 = ((f32[16,136,128]{2,1,0:T(8,128)}), f32[16,136,128]{2,1,0:T(8,128)}, u32[]{:S(2)}, u32[]{:S(2)}) async-start(f32[16,136,128]{2,1,0:T(8,128)} %bitcast.73), calls=%async_computation.6 | async-start | bytes 2228224 | tf_op jit(solution)/shard_map/all_to_all | solution.py:63
  290.9 0.9 copy-start

commit v14 on v9

--- a/solution.py
+++ b/solution.py
@@ -126,8 +126,13 @@
         return lax.all_to_all(spread, "feat", 0, 0, tiled=True)
 
     def comp_total(stacked):
-        spread = jnp.broadcast_to(stacked[None], (n_comp,) + stacked.shape)
-        return lax.all_to_all(spread, "comp", 0, 0, tiled=True).sum(0)
+        total = stacked
+        distance = 1
+        while distance < n_comp:
+            partner = [(i, i ^ distance) for i in range(n_comp)]
+            total = total + lax.ppermute(total, "comp", partner)
+            distance *= 2
+        return total
 
     own_block = right_side.shape[0]
     residual_slab = gather_feat(right_side).reshape(RB_DEV * own_block, responses)

time: 327 us -> 367 us (1.12)
  starting transfers between devices: 28.2 us -> 65.4 us
  waiting for transfers between devices: 73.3 us -> 109 us
  blocking collectives: 180 us -> 148 us
    ppermute x0 -> x10, waiting for transfers between devices: none -> 41.1 us  [comp_total(): total = total + lax.ppermute(total, 'comp', partner)]
    all_to_all x2 -> x0, blocking collectives: 36.7 us -> none  [comp_total(): return lax.all_to_all(spread, 'comp', 0, 0, tiled=True).sum(0)]
    ppermute x0 -> x10, starting transfers between devices: none -> 32 us  [comp_total(): total = total + lax.ppermute(total, 'comp', partner)]
    all_to_all x2, waiting for transfers between devices: 37 us -> 32.1 us  [reduce_over(): return lax.all_to_all(pieces, axis, 0, 0, tiled=True).sum(0)]
    ppermute x2, starting transfers between devices: 8.87 us -> 13.7 us  [swap_with_sibling(): return lax.ppermute(x, 'comp', siblings)]
  transfers between devices with their start and end apart: 6 -> 16, of which waited for: 6 -> 16; matrix products, arithmetic and copies ran while one was open for 0% -> 0% of each run, Pallas kernels for 0% -> 0%
where the time goes in v14:
time: 367 us; the launch traced here: 363 us
  blocking collectives  148 us (40%)
  waiting for transfers between devices  109 us (30%)
  starting transfers between devices  65.4 us (18%)
  Pallas kernels  20.8 us (6%)
  other arithmetic  12.2 us (3%)
  local copies, waits for them, and re-layouts  5.99 us (2%)
    all_gather x2, blocking collectives, gather_gradient(): got = lax.all_gather(own, 'comp', axis=0, tiled=False)  80.6 us
    ppermute x10, waiting for transfers between devices, comp_total(): total = total + lax.ppermute(total, 'comp', partner)  41.1 us
    all_to_all x1, blocking collectives, reduce_gradient(): lax.all_to_all(pieces, 'comp', 0, 0, tiled=True, axis_index_groups=same_c...  36.2 us
    all_to_all x2, waiting for transfers between devices, reduce_over(): return lax.all_to_all(pieces, axis, 0, 0, tiled=True).sum(0)  32.1 us
    ppermute x10, starting transfers between devices, comp_total(): total = total + lax.ppermute(total, 'comp', partner)  32 us
    pallas_call x4, Pallas kernels, block_apply(): pl.pallas_call(functools.partial(_block_kernel, transpose, pitch), out_sh...  20.8 us
    all_to_all x1, blocking collectives, gather_feat(): return lax.all_to_all(spread, 'feat', 0, 0, tiled=True)  20.1 us
    all_to_all x1, waiting for transfers between devices, reduce_gradient(): lax.all_to_all(pieces, 'comp', 0, 0, tiled=True, axis_index_groups=same_c...  19.7 us
  transfers between devices with their start and end apart: 16, of which 16 were waited for; matrix products, arithmetic and copies ran while one was open for 0% of the time, Pallas kernels for 0%

profile of v14, /device:TPU:1, one launch (start us, length us, event | category | flops | bytes accessed | tf_op | source)
XLA Modules:
  0.0 362.9 jit_solution(4815741462263485110)
XLA Ops:
  0.6 1.9 broadcast_in_dim.14
  2.6 7.6 %all-to-all-start = ((f32[16,128,128]{2,1,0:T(8,128)}), f32[16,128,128]{2,1,0:T(8,128)S(1)}, u32[]{:S(2)}, u32[]{:S(2)}) async-start(f32[16,128,128]{2,1,0:T(8,128)} %broadcast_in_dim.14), calls=%async_computation | async-start | bytes 2097152 | tf_op jit(solution)/shard_map/all_to_all | solution.py:126
  10.8 13.6 %all-to-all-done = f32[16,128,128]{2,1,0:T(8,128)S(1)} async-done(((f32[16,128,128]{2,1,0:T(8,128)}), f32[16,128,128]{2,1,0:T(8,128)S(1)}, u32[]{:S(2)}, u32[]{:S(2)}) %all-to-all-start) | async-done | bytes 1048608 | tf_op jit(solution)/shard_map/all_to_all | solution.py:126
  25.2 5.6 %shard_map.77 = f32[1792,128]{1,0:T(8,128)} custom-call(s32[1]{0:T(128)} %bitcast.61.count_ref, s32[24]{0:T(128)} %bitcast.77, s32[24]{0:T(128)} %bitcast.81, bf16[24,128,128]{2,1,0:T(8,128)(2,1)} %bitcast.66, bf16[2048,128]{1,0:T(8,128)(2,1)} %bitcast_convert_fusion.x_ref), custom_call_target="tpu_custom_call" | custom-call | tf_op jit(solution)/shard_map/pallas_call | solution.py:52
  30.8 1.1 constant_dynamic-slice_fusion.1
  32.0 6.3 %collective-permute-start = (f32[896,128]{1,0:T(8,128)S(1)}, f32[896,128]{1,0:T(8,128)S(1)}, u32[]{:S(2)}, u32[]{:S(2)}) collective-permute-start(f32[896,128]{1,0:T(8,128)S(1)} %constant_dynamic-slice_fusion.1), channel_id=1, source_target_pairs={{0,16},{16,0},{32,48},{48,32},{64,80},{80,64},{96,112},{112,96},{1... | collective-permute-start | bytes 1376264 | tf_op jit(solution)/shard_map/ppermute | solution.py:100
  38.2 1.4 collective-permute-done
  39.7 36.2 %all_to_all.35 = f32[16,56,128]{2,1,0:T(8,128)S(1)} all-to-all(f32[16,56,128]{2,1,0:T(8,128)S(1)} %bitcast.76), channel_id=1, replica_groups={{0,32,64,96,128,160,192,224,256,288,320,352,384,416,448,480},{16,48,80,..., dimensions={0} | all-to-all | bytes 917504 | tf_op jit(solution)/shard_map/all_to_all | solution.py:107
  75.9 40.1 %all-gather = f32[1792,128]{1,0:T(8,128)S(1)} all-gather(f32[56,128]{1,0:T(8,128)S(1)} %reduce_sum.117), channel_id=2, replica_groups=mesh['comp'=32,'feat'=16] {'comp'}, dimensions={0}, use_global_device_ids=true | all-gather | bytes 946176 | tf_op jit(solution)/shard_map/all_gather | solution.py:111
  116.9 4.8 %shard_map.78 = f32[2048,128]{1,0:T(8,128)} custom-call(s32[1]{0:T(128)} %bitcast.62.count_ref, s32[24]{0:T(128)} %bitcast.82, s32[24]{0:T(128)} %bitcast.78, bf16[24,128,128]{2,1,0:T(8,128)(2,1)} %bitcast.67, bf16[1792,128]{1,0:T(8,128)(2,1)} %bitcast_convert_fusion.2.x_ref), custom_call_target="tpu_custom_call" | custom-call | tf_op jit(solution)/shard_map/pallas_call | solution.py:52
  121.7 3.7 %all-to-all-start.2 = ((f32[16,128,128]{2,1,0:T(8,128)}), f32[16,128,128]{2,1,0:T(8,128)S(1)}, u32[]{:S(2)}, u32[]{:S(2)}) async-start(f32[16,128,128]{2,1,0:T(8,128)} %bitcast.73), calls=%async_computation.2 | async-start | bytes 2097152 | tf_op jit(solution)/shard_map/all_to_all | solution.py:63
  125.4 15.6 %all-to-all-done.2 = f32[16,128,128]{2,1,0:T(8,128)S(1)} async-done(((f32[16,128,128]{2,1,0:T(8,128)}), f32[16,128,128]{2,1,0:T(8,128)S(1)}, u32[]{:S(2)}, u32[]{:S(2)}) %all-to-all-start.2) | async-done | bytes 1048608 | tf_op jit(solution)/shard_map/all_to_all | solution.py:63
  141.2 20.1 %all_to_all.36 = f32[16,130,128]{2,1,0:T(8,128)S(1)} all-to-all(f32[16,130,128]{2,1,0:T(8,128)S(1)} %broadcast_in_dim.17), channel_id=1, replica_groups=mesh['comp'=32,'feat'=16] {'feat'}, dimensions={0} | all-to-all | bytes 2129920 | tf_op jit(solution)/shard_map/all_to_all | solution.py:126
  161.6 5.0 %collective-permute-start.1 = (f32[3,128]{1,0:T(4,128)S(1)}, f32[3,128]{1,0:T(4,128)S(1)}, u32[]{:S(2)}, u32[]{:S(2)}) collective-permute-start(f32[3,128]{1,0:T(4,128)S(1)} %pad_maximum_fusion.1), channel_id=1, source_target_pairs={{0,16},{16,0},{32,48},{48,32},{64,80},{80,64},{96,112},{112,96},{1... | collective-permute-start | bytes 4616 | tf_op jit(solution)/shard_map/ppermute | solution.py:133
  167.4 1.9 collective-permute-start.2
  169.3 2.4 collective-permute-done.2
  171.8 2.4 collective-permute-start.3
  174.2 2.8 collective-permute-done.3
  177.0 3.5 collective-permute-start.4
  180.5 4.7 %collective-permute-done.4 = f32[3,128]{1,0:T(4,128)S(1)} collective-permute-done((f32[3,128]{1,0:T(4,128)S(1)}, f32[3,128]{1,0:T(4,128)S(1)}, u32[]{:S(2)}, u32[]{:S(2)}) %collective-permute-start.4) | collective-permute-done | bytes 1568 | tf_op jit(solution)/shard_map/ppermute | solution.py:133
  185.2 3.5 collective-permute-start.5
  188.7 9.6 %collective-permute-done.5 = f32[3,128]{1,0:T(4,128)S(1)} collective-permute-done((f32[3,128]{1,0:T(4,128)S(1)}, f32[3,128]{1,0:T(4,128)S(1)}, u32[]{:S(2)}, u32[]{:S(2)}) %collective-permute-start.5) | collective-permute-done | bytes 1568 | tf_op jit(solution)/shard_map/ppermute | solution.py:133
  198.2 1.3 fusion.5
  199.5 5.6 %shard_map.79 = f32[1792,128]{1,0:T(8,128)} custom-call(s32[1]{0:T(128)} %bitcast.63.count_ref, s32[24]{0:T(128)} %bitcast.79, s32[24]{0:T(128)} %bitcast.83, bf16[24,128,128]{2,1,0:T(8,128)(2,1)} %bitcast.68, bf16[2048,128]{1,0:T(8,128)(2,1)} %get-tuple-element.16.x_ref), custom_call_target="tpu_custom_call" | custom-call | tf_op jit(solution)/shard_map/pallas_call | solution.py:52
  205.1 1.1 constant_dynamic-slice_fusion
  206.3 7.4 %collective-permute-start.6 = (f32[896,128]{1,0:T(8,128)S(1)}, f32[896,128]{1,0:T(8,128)S(1)}, u32[]{:S(2)}, u32[]{:S(2)}) collective-permute-start(f32[896,128]{1,0:T(8,128)S(1)} %constant_dynamic-slice_fusion), channel_id=1, source_target_pairs={{0,16},{16,0},{32,48},{48,32},{64,80},{80,64},{96,112},{112,96},{1... | collective-permute-start | bytes 1376264 | tf_op jit(solution)/shard_map/ppermute | solution.py:100
  213.7 1.4 collective-permute-done.6
  215.9 4.1 %all-to-all-start.4 = ((f32[16,56,128]{2,1,0:T(8,128)}), f32[16,56,128]{2,1,0:T(8,128)S(1)}, u32[]{:S(2)}, u32[]{:S(2)}) async-start(f32[16,56,128]{2,1,0:T(8,128)} %bitcast.17), calls=%async_computation.4 | async-start | bytes 917504 | tf_op jit(solution)/shard_map/all_to_all | solution.py:107
  220.1 1.0 broadcast_multiply_fusion
  221.1 19.7 %all-to-all-done.4 = f32[16,56,128]{2,1,0:T(8,128)S(1)} async-done(((f32[16,56,128]{2,1,0:T(8,128)}), f32[16,56,128]{2,1,0:T(8,128)S(1)}, u32[]{:S(2)}, u32[]{:S(2)}) %all-to-all-start.4) | async-done | bytes 458784 | tf_op jit(solution)/shard_map/all_to_all | solution.py:107
  241.6 40.5 %all-gather.2 = f32[32,57,128]{2,1,0:T(8,128)S(1)} all-gather(f32[1,57,128]{2,1,0:T(8,128)S(1)} %maximum_bitcast_fusion), channel_id=3, replica_groups=mesh['comp'=32,'feat'=16] {'comp'}, dimensions={0}, use_global_device_ids=true | all-gather | bytes 963072 | tf_op jit(solution)/shard_map/all_gather | solution.py:111
  283.7 4.8 %shard_map.80 = f32[2176,128]{1,0:T(8,128)} custom-call(s32[1]{0:T(128)} %bitcast.64.count_ref, s32[24]{0:T(128)} %bitcast.84, s32[24]{0:T(128)} %bitcast.80, bf16[24,128,128]{2,1,0:T(8,128)(2,1)} %bitcast.69, bf16[1792,128]{1,0:T(8,128)(2,1)} %bitcast_convert_fusion.1.x_ref, f32[8,128]{1,0:T(8,128)} %scatter.4.rest_0_), custom_call_target="tpu_custom_call" | custom-call | tf_op jit(solution)/shard_map/pallas_call | solution.py:52
  288.5 4.4 %all-to-all-start.5 = ((f32[16,136,128]{2,1,0:T(8,128)}), f32[16,136,128]{2,1,0:T(8,128)}, u32[]{:S(2)}, u32[]{:S(2)}) async-start(f32[16,136,128]{2,1,0:T(8,128)} %bitcast.72), calls=%async_computation.5 | async-start | bytes 2228224 | tf_op jit(solution)/shard_map/all_to_all | solution.py:63
  292.9 16.4 %all-to-all-done.5 = f32[16,136,128]{2,1,0:T(8,128)} async-done(((f32[16,136,128]{2,1,0:T(8,128)}), f32[16,136,128]{2,1,0:T(8,128)}, u32[]{:S(2)}, u32[]{:S(2)}) %all-to-all-start.5) | async-done | bytes 1114144 | tf_op jit(solution)/shard_map/all_to_all | solution.py:63
  309.3 1.3 reduce_sum.126
  310.8 0.9 copy-done
  311.8 10.9 %all_to_all.37 = f32[16,2,128]{2,1,0:T(2,128)S(1)} all-to-all(f32[16,2,128]{2,1,0:T(2,128)S(1)} %broadcast_in_dim.20), channel_id=1, replica_groups=mesh['comp'=32,'feat'=16] {'feat'}, dimensions={0} | all-to-all | bytes 32768 | tf_op jit(solution)/shard_map/all_to_all | solution.py:170
  322.7 5.0 %collective-permute-start.7 = (f32[2,128]{1,0:T(2,128)S(1)}, f32[2,128]{1,0:T(2,128)S(1)}, u32[]{:S(2)}, u32[]{:S(2)}) collective-permute-start(f32[2,128]{1,0:T(2,128)S(1)} %reduce_sum.129), channel_id=1, source_target_pairs={{0,16},{16,0},{32,48},{48,32},{64,80},{80,64},{96,112},{112,96},{1... | collective-permute-start | bytes 3080 | tf_op jit(solution)/shard_map/ppermute | solution.py:133
  328.5 1.9 collective-permute-start.8
  330.4 2.4 collective-permute-done.8
  332.8 2.3 collective-permute-start.9
  335.1 2.9 collective-permute-done.9
  338.0 2.6 collective-permute-start.10
  340.6 5.6 %collective-permute-done.10 = f32[2,128]{1,0:T(2,128)S(1)} collective-permute-done((f32[2,128]{1,0:T(2,128)S(1)}, f32[2,128]{1,0:T(2,128)S(1)}, u32[]{:S(2)}, u32[]{:S(2)}) %collective-permute-start.10) | collective-permute-done | bytes 1056 | tf_op jit(solution)/shard_map/ppermute | solution.py:133
  346.2 3.8 %collective-permute-start.11 = (f32[2,128]{1,0:T(2,128)S(1)}, f32[2,128]{1,0:T(2,128)S(1)}, u32[]{:S(2)}, u32[]{:S(2)}) collective-permute-start(f32[2,128]{1,0:T(2,128)S(1)} %add.101), channel_id=1, source_target_pairs={{0,256},{16,272},{32,288},{48,304},{64,320},{80,336},{96,352},{112... | collective-permute-start | bytes 3080 | tf_op jit(solution)/shard_map/ppermute | solution.py:133
  350.1 9.2 %collective-permute-done.11 = f32[2,128]{1,0:T(2,128)S(1)} collective-permute-done((f32[2,128]{1,0:T(2,128)S(1)}, f32[2,128]{1,0:T(2,128)S(1)}, u32[]{:S(2)}, u32[]{:S(2)}) %collective-permute-start.11) | collective-permute-done | bytes 1056 | tf_op jit(solution)/shard_map/ppermute | solution.py:133
  359.3 2.2 multiply_add_fusion
  361.5 1.5 multiply_subtract_fusion
  (50 shorter events, 7.4 us)
Async XLA Ops:
  2.6 21.8 %all-to-all-start = ((f32[16,128,128]{2,1,0:T(8,128)}), f32[16,128,128]{2,1,0:T(8,128)S(1)}, u32[]{:S(2)}, u32[]{:S(2)}) async-start(f32[16,128,128]{2,1,0:T(8,128)} %broadcast_in_dim.14), calls=%async_computation | async-start | bytes 2097152 | tf_op jit(solution)/shard_map/all_to_all | solution.py:126
  30.8 8.8 %copy-start.1 = (f32[1792,128]{1,0:T(8,128)S(1)}, f32[1792,128]{1,0:T(8,128)}, u32[]{:S(2)}) copy-start(f32[1792,128]{1,0:T(8,128)} %shard_map.77) | copy-start | bytes 2752516
  32.0 7.7 %collective-permute-start = (f32[896,128]{1,0:T(8,128)S(1)}, f32[896,128]{1,0:T(8,128)S(1)}, u32[]{:S(2)}, u32[]{:S(2)}) collective-permute-start(f32[896,128]{1,0:T(8,128)S(1)} %constant_dynamic-slice_fusion.1), channel_id=1, source_target_pairs={{0,16},{16,0},{32,48},{48,32},{64,80},{80,64},{96,112},{112,96},{1... | collective-permute-start | bytes 1376264 | tf_op jit(solution)/shard_map/ppermute | solution.py:100
  121.7 19.4 %all-to-all-start.2 = ((f32[16,128,128]{2,1,0:T(8,128)}), f32[16,128,128]{2,1,0:T(8,128)S(1)}, u32[]{:S(2)}, u32[]{:S(2)}) async-start(f32[16,128,128]{2,1,0:T(8,128)} %bitcast.73), calls=%async_computation.2 | async-start | bytes 2097152 | tf_op jit(solution)/shard_map/all_to_all | solution.py:63
  161.3 37.0 %copy-start.3 = (f32[128]{0:T(128)S(1)}, f32[128]{0:T(128)}, u32[]{:S(2)}) copy-start(f32[128]{0:T(128)} %param.13) | copy-start | bytes 1540
  161.6 5.8 %collective-permute-start.1 = (f32[3,128]{1,0:T(4,128)S(1)}, f32[3,128]{1,0:T(4,128)S(1)}, u32[]{:S(2)}, u32[]{:S(2)}) collective-permute-start(f32[3,128]{1,0:T(4,128)S(1)} %pad_maximum_fusion.1), channel_id=1, source_target_pairs={{0,16},{16,0},{32,48},{48,32},{64,80},{80,64},{96,112},{112,96},{1... | collective-permute-start | bytes 4616 | tf_op jit(solution)/shard_map/ppermute | solution.py:133
  167.4 4.3 %collective-permute-start.2 = (f32[3,128]{1,0:T(4,128)S(1)}, f32[3,128]{1,0:T(4,128)S(1)}, u32[]{:S(2)}, u32[]{:S(2)}) collective-permute-start(f32[3,128]{1,0:T(4,128)S(1)} %fusion.4), channel_id=1, source_target_pairs={{0,32},{16,48},{32,0},{48,16},{64,96},{80,112},{96,64},{112,80},{1... | collective-permute-start | bytes 4616 | tf_op jit(solution)/shard_map/ppermute | solution.py:133
  171.8 5.2 %collective-permute-start.3 = (f32[3,128]{1,0:T(4,128)S(1)}, f32[3,128]{1,0:T(4,128)S(1)}, u32[]{:S(2)}, u32[]{:S(2)}) collective-permute-start(f32[3,128]{1,0:T(4,128)S(1)} %add.89), channel_id=1, source_target_pairs={{0,64},{16,80},{32,96},{48,112},{64,0},{80,16},{96,32},{112,48},{1... | collective-permute-start | bytes 4616 | tf_op jit(solution)/shard_map/ppermute | solution.py:133
  177.0 8.2 %collective-permute-start.4 = (f32[3,128]{1,0:T(4,128)S(1)}, f32[3,128]{1,0:T(4,128)S(1)}, u32[]{:S(2)}, u32[]{:S(2)}) collective-permute-start(f32[3,128]{1,0:T(4,128)S(1)} %add.90), channel_id=1, source_target_pairs={{0,128},{16,144},{32,160},{48,176},{64,192},{80,208},{96,224},{112... | collective-permute-start | bytes 4616 | tf_op jit(solution)/shard_map/ppermute | solution.py:133
  185.2 13.0 %collective-permute-start.5 = (f32[3,128]{1,0:T(4,128)S(1)}, f32[3,128]{1,0:T(4,128)S(1)}, u32[]{:S(2)}, u32[]{:S(2)}) collective-permute-start(f32[3,128]{1,0:T(4,128)S(1)} %add.91), channel_id=1, source_target_pairs={{0,256},{16,272},{32,288},{48,304},{64,320},{80,336},{96,352},{112... | collective-permute-start | bytes 4616 | tf_op jit(solution)/shard_map/ppermute | solution.py:133
  205.1 10.0 %copy-start.2 = (f32[1792,128]{1,0:T(8,128)S(1)}, f32[1792,128]{1,0:T(8,128)}, u32[]{:S(2)}) copy-start(f32[1792,128]{1,0:T(8,128)} %shard_map.79) | copy-start | bytes 2752516
  206.3 8.8 %collective-permute-start.6 = (f32[896,128]{1,0:T(8,128)S(1)}, f32[896,128]{1,0:T(8,128)S(1)}, u32[]{:S(2)}, u32[]{:S(2)}) collective-permute-start(f32[896,128]{1,0:T(8,128)S(1)} %constant_dynamic-slice_fusion), channel_id=1, source_target_pairs={{0,16},{16,0},{32,48},{48,32},{64,80},{80,64},{96,112},{112,96},{1... | collective-permute-start | bytes 1376264 | tf_op jit(solution)/shard_map/ppermute | solution.py:100
  215.9 24.8 %all-to-all-start.4 = ((f32[16,56,128]{2,1,0:T(8,128)}), f32[16,56,128]{2,1,0:T(8,128)S(1)}, u32[]{:S(2)}, u32[]{:S(2)}) async-start(f32[16,56,128]{2,1,0:T(8,128)} %bitcast.17), calls=%async_computation.4 | async-start | bytes 917504 | tf_op jit(solution)/shard_map/all_to_all | solution.py:107
  288.5 20.8 %all-to-all-start.5 = ((f32[16,136,128]{2,1,0:T(8,128)}), f32[16,136,128]{2,1,0:T(8,128)}, u32[]{:S(2)}, u32[]{:S(2)}) async-start(f32[16,136,128]{2,1,0:T(8,128)} %bitcast.72), calls=%async_computation.5 | async-start | bytes 2228224 | tf_op jit(solution)/shard_map/all_to_all | solution.py:63
  310.7 0.9 copy-start
  322.7 5.8 %collective-permute-start.7 = (f32[2,128]{1,0:T(2,128)S(1)}, f32[2,128]{1,0:T(2,128)S(1)}, u32[]{:S(2)}, u32[]{:S(2)}) collective-permute-start(f32[2,128]{1,0:T(2,128)S(1)} %reduce_sum.129), channel_id=1, source_target_pairs={{0,16},{16,0},{32,48},{48,32},{64,80},{80,64},{96,112},{112,96},{1... | collective-permute-start | bytes 3080 | tf_op jit(solution)/shard_map/ppermute | solution.py:133
  328.5 4.3 %collective-permute-start.8 = (f32[2,128]{1,0:T(2,128)S(1)}, f32[2,128]{1,0:T(2,128)S(1)}, u32[]{:S(2)}, u32[]{:S(2)}) collective-permute-start(f32[2,128]{1,0:T(2,128)S(1)} %add.98), channel_id=1, source_target_pairs={{0,32},{16,48},{32,0},{48,16},{64,96},{80,112},{96,64},{112,80},{1... | collective-permute-start | bytes 3080 | tf_op jit(solution)/shard_map/ppermute | solution.py:133
  332.8 5.2 %collective-permute-start.9 = (f32[2,128]{1,0:T(2,128)S(1)}, f32[2,128]{1,0:T(2,128)S(1)}, u32[]{:S(2)}, u32[]{:S(2)}) collective-permute-start(f32[2,128]{1,0:T(2,128)S(1)} %add.99), channel_id=1, source_target_pairs={{0,64},{16,80},{32,96},{48,112},{64,0},{80,16},{96,32},{112,48},{1... | collective-permute-start | bytes 3080 | tf_op jit(solution)/shard_map/ppermute | solution.py:133
  338.0 8.2 %collective-permute-start.10 = (f32[2,128]{1,0:T(2,128)S(1)}, f32[2,128]{1,0:T(2,128)S(1)}, u32[]{:S(2)}, u32[]{:S(2)}) collective-permute-start(f32[2,128]{1,0:T(2,128)S(1)} %add.100), channel_id=1, source_target_pairs={{0,128},{16,144},{32,160},{48,176},{64,192},{80,208},{96,224},{112... | collective-permute-start | bytes 3080 | tf_op jit(solution)/shard_map/ppermute | solution.py:133
  346.2 13.0 %collective-permute-start.11 = (f32[2,128]{1,0:T(2,128)S(1)}, f32[2,128]{1,0:T(2,128)S(1)}, u32[]{:S(2)}, u32[]{:S(2)}) collective-permute-start(f32[2,128]{1,0:T(2,128)S(1)} %add.101), channel_id=1, source_target_pairs={{0,256},{16,272},{32,288},{48,304},{64,320},{80,336},{96,352},{112... | collective-permute-start | bytes 3080 | tf_op jit(solution)/shard_map/ppermute | solution.py:133

commit v15 on v9

--- a/solution.py
+++ b/solution.py
@@ -22,20 +22,18 @@
             out_ref[pl.ds(b * pitch + edge, pitch - edge), :] = extra_ref[...]
 
     def body(s, carry):
-        @pl.when(s < count_ref[0])
-        def _():
-            src = pl.multiple_of(in_idx_ref[s] * edge, edge)
-            dst = pl.multiple_of(out_idx_ref[s] * pitch, 8)
-            block = values_ref[s]
-            x = x_ref[pl.ds(src, edge), :]
-            if transpose:
-                prod = lax.dot_general(
-                    block, x, (((0,), (0,)), ((), ())), preferred_element_type=jnp.float32
-                )
-            else:
-                prod = jnp.dot(block, x, preferred_element_type=jnp.float32)
-            out_ref[pl.ds(dst, edge), :] += prod
-
+        src = pl.multiple_of(in_idx_ref[s] * edge, edge)
+        dst = pl.multiple_of(out_idx_ref[s] * pitch, 8)
+        block = values_ref[s]
+        x = x_ref[pl.ds(src, edge), :]
+        if transpose:
+            prod = lax.dot_general(
+                block, x, (((0,), (0,)), ((), ())), preferred_element_type=jnp.float32
+            )
+        else:
+            prod = jnp.dot(block, x, preferred_element_type=jnp.float32)
+        live = s < count_ref[0]
+        out_ref[pl.ds(dst, edge), :] += jnp.where(live, prod, 0.0)
         return carry
 
     lax.fori_loop(0, values_ref.shape[0], body, 0, unroll=True)

time: 327 us -> 316 us (0.966)
  Pallas kernels: 24 us -> 10.6 us
  blocking collectives: 180 us -> 184 us
    pallas_call x4, Pallas kernels: 24 us -> 10.6 us  [block_apply(): pl.pallas_call(functools.partial(_block_kernel, transpose, pitch), out_sh...]
where the time goes in v15:
time: 316 us; the launch traced here: 315 us
  blocking collectives  184 us (58%)
  waiting for transfers between devices  72.1 us (23%)
  starting transfers between devices  28.4 us (9%)
  other arithmetic  12.3 us (4%)
  Pallas kernels  10.6 us (3%)
  local copies, waits for them, and re-layouts  6.02 us (2%)
    all_gather x2, blocking collectives, gather_gradient(): got = lax.all_gather(own, 'comp', axis=0, tiled=False)  80.3 us
    all_to_all x2, blocking collectives, comp_total(): return lax.all_to_all(spread, 'comp', 0, 0, tiled=True).sum(0)  39.2 us
    all_to_all x1, blocking collectives, reduce_gradient(): lax.all_to_all(pieces, 'comp', 0, 0, tiled=True, axis_index_groups=same_c...  36 us
    all_to_all x2, waiting for transfers between devices, reduce_over(): return lax.all_to_all(pieces, axis, 0, 0, tiled=True).sum(0)  35.7 us
    all_to_all x1, waiting for transfers between devices, reduce_gradient(): lax.all_to_all(pieces, 'comp', 0, 0, tiled=True, axis_index_groups=same_c...  19.9 us
    all_to_all x1, blocking collectives, gather_feat(): return lax.all_to_all(spread, 'feat', 0, 0, tiled=True)  19.1 us
    all_to_all x1, waiting for transfers between devices, gather_feat(): return lax.all_to_all(spread, 'feat', 0, 0, tiled=True)  13.6 us
    pallas_call x4, Pallas kernels, block_apply(): pl.pallas_call(functools.partial(_block_kernel, transpose, pitch), out_sh...  10.6 us
  transfers between devices with their start and end apart: 6, of which 6 were waited for; matrix products, arithmetic and copies ran while one was open for 0% of the time, Pallas kernels for 0%

profile of v15, /device:TPU:1, one launch (start us, length us, event | category | flops | bytes accessed | tf_op | source)
XLA Modules:
  0.0 314.9 jit_solution(6175828719587563002)
XLA Ops:
  0.6 1.9 broadcast_in_dim.18
  2.6 7.6 %all-to-all-start = ((f32[16,128,128]{2,1,0:T(8,128)}), f32[16,128,128]{2,1,0:T(8,128)S(1)}, u32[]{:S(2)}, u32[]{:S(2)}) async-start(f32[16,128,128]{2,1,0:T(8,128)} %broadcast_in_dim.18), calls=%async_computation | async-start | bytes 2097152 | tf_op jit(solution)/shard_map/all_to_all | solution.py:124
  10.8 13.6 %all-to-all-done = f32[16,128,128]{2,1,0:T(8,128)S(1)} async-done(((f32[16,128,128]{2,1,0:T(8,128)}), f32[16,128,128]{2,1,0:T(8,128)S(1)}, u32[]{:S(2)}, u32[]{:S(2)}) %all-to-all-start) | async-done | bytes 1048608 | tf_op jit(solution)/shard_map/all_to_all | solution.py:124
  24.4 0.8 bitcast_convert_fusion.x_ref
  25.2 2.7 shard_map.77
  27.9 1.1 constant_dynamic-slice_fusion.1
  29.0 5.7 %collective-permute-start = (f32[896,128]{1,0:T(8,128)S(1)}, f32[896,128]{1,0:T(8,128)S(1)}, u32[]{:S(2)}, u32[]{:S(2)}) collective-permute-start(f32[896,128]{1,0:T(8,128)S(1)} %constant_dynamic-slice_fusion.1), channel_id=1, source_target_pairs={{0,16},{16,0},{32,48},{48,32},{64,80},{80,64},{96,112},{112,96},{1... | collective-permute-start | bytes 1376264 | tf_op jit(solution)/shard_map/ppermute | solution.py:98
  34.8 1.4 collective-permute-done
  36.2 36.0 %all_to_all.45 = f32[16,56,128]{2,1,0:T(8,128)S(1)} all-to-all(f32[16,56,128]{2,1,0:T(8,128)S(1)} %bitcast.76), channel_id=1, replica_groups={{0,32,64,96,128,160,192,224,256,288,320,352,384,416,448,480},{16,48,80,..., dimensions={0} | all-to-all | bytes 917504 | tf_op jit(solution)/shard_map/all_to_all | solution.py:105
  72.3 40.1 %all-gather = f32[1792,128]{1,0:T(8,128)S(1)} all-gather(f32[56,128]{1,0:T(8,128)S(1)} %reduce_sum.135), channel_id=2, replica_groups=mesh['comp'=32,'feat'=16] {'comp'}, dimensions={0}, use_global_device_ids=true | all-gather | bytes 946176 | tf_op jit(solution)/shard_map/all_gather | solution.py:109
  112.4 0.1 copy.15
  112.5 0.8 bitcast_convert_fusion.2.x_ref
  113.3 2.6 shard_map.78
  115.9 3.7 %all-to-all-start.2 = ((f32[16,128,128]{2,1,0:T(8,128)}), f32[16,128,128]{2,1,0:T(8,128)S(1)}, u32[]{:S(2)}, u32[]{:S(2)}) async-start(f32[16,128,128]{2,1,0:T(8,128)} %bitcast.73), calls=%async_computation.2 | async-start | bytes 2097152 | tf_op jit(solution)/shard_map/all_to_all | solution.py:61
  119.7 17.4 %all-to-all-done.2 = f32[16,128,128]{2,1,0:T(8,128)S(1)} async-done(((f32[16,128,128]{2,1,0:T(8,128)}), f32[16,128,128]{2,1,0:T(8,128)S(1)}, u32[]{:S(2)}, u32[]{:S(2)}) %all-to-all-start.2) | async-done | bytes 1048608 | tf_op jit(solution)/shard_map/all_to_all | solution.py:61
  137.0 0.1 reduce_sum.136
  137.1 0.1 broadcast_in_dim.21
  137.2 19.1 %all_to_all.46 = f32[16,130,128]{2,1,0:T(8,128)S(1)} all-to-all(f32[16,130,128]{2,1,0:T(8,128)S(1)} %broadcast_in_dim.21), channel_id=1, replica_groups=mesh['comp'=32,'feat'=16] {'feat'}, dimensions={0} | all-to-all | bytes 2129920 | tf_op jit(solution)/shard_map/all_to_all | solution.py:124
  156.3 0.3 fusion.5
  156.7 20.1 %all_to_all.47 = f32[32,3,128]{2,1,0:T(4,128)S(1)} all-to-all(f32[32,3,128]{2,1,0:T(4,128)S(1)} %broadcast_in_dim.23), channel_id=1, replica_groups=mesh['comp'=32,'feat'=16] {'comp'}, dimensions={0} | all-to-all | bytes 98304 | tf_op jit(solution)/shard_map/all_to_all | solution.py:128
  176.8 0.0 copy-done.3
  176.8 1.3 fusion.4
  178.1 2.6 shard_map.79
  180.7 1.1 constant_dynamic-slice_fusion
  181.9 3.5 %collective-permute-start.1 = (f32[896,128]{1,0:T(8,128)S(1)}, f32[896,128]{1,0:T(8,128)S(1)}, u32[]{:S(2)}, u32[]{:S(2)}) collective-permute-start(f32[896,128]{1,0:T(8,128)S(1)} %constant_dynamic-slice_fusion), channel_id=1, source_target_pairs={{0,16},{16,0},{32,48},{48,32},{64,80},{80,64},{96,112},{112,96},{1... | collective-permute-start | bytes 1376264 | tf_op jit(solution)/shard_map/ppermute | solution.py:98
  185.4 1.4 collective-permute-done.1
  186.8 0.8 dynamic-slice_add_fusion
  187.6 3.6 %all-to-all-start.5 = ((f32[16,56,128]{2,1,0:T(8,128)}), f32[16,56,128]{2,1,0:T(8,128)S(1)}, u32[]{:S(2)}, u32[]{:S(2)}) async-start(f32[16,56,128]{2,1,0:T(8,128)} %bitcast.17), calls=%async_computation.5 | async-start | bytes 917504 | tf_op jit(solution)/shard_map/all_to_all | solution.py:105
  191.2 1.0 broadcast_multiply_fusion
  192.2 19.9 %all-to-all-done.5 = f32[16,56,128]{2,1,0:T(8,128)S(1)} async-done(((f32[16,56,128]{2,1,0:T(8,128)}), f32[16,56,128]{2,1,0:T(8,128)S(1)}, u32[]{:S(2)}, u32[]{:S(2)}) %all-to-all-start.5) | async-done | bytes 458784 | tf_op jit(solution)/shard_map/all_to_all | solution.py:105
  212.2 0.8 multiply_reduce_fusion.3
  212.9 40.2 %all-gather.2 = f32[32,57,128]{2,1,0:T(8,128)S(1)} all-gather(f32[1,57,128]{2,1,0:T(8,128)S(1)} %maximum_bitcast_fusion), channel_id=3, replica_groups=mesh['comp'=32,'feat'=16] {'comp'}, dimensions={0}, use_global_device_ids=true | all-gather | bytes 963072 | tf_op jit(solution)/shard_map/all_gather | solution.py:109
  253.2 0.1 slice_reduce_fusion
  253.2 0.1 slice.62
  253.3 0.1 copy.17
  253.4 0.6 scatter.4.rest_0_
  254.0 0.8 bitcast_convert_fusion.1.x_ref
  254.8 2.7 shard_map.80
  257.4 4.4 %all-to-all-start.6 = ((f32[16,136,128]{2,1,0:T(8,128)}), f32[16,136,128]{2,1,0:T(8,128)}, u32[]{:S(2)}, u32[]{:S(2)}) async-start(f32[16,136,128]{2,1,0:T(8,128)} %bitcast.72), calls=%async_computation.6 | async-start | bytes 2228224 | tf_op jit(solution)/shard_map/all_to_all | solution.py:61
  261.8 18.4 %all-to-all-done.6 = f32[16,136,128]{2,1,0:T(8,128)} async-done(((f32[16,136,128]{2,1,0:T(8,128)}), f32[16,136,128]{2,1,0:T(8,128)}, u32[]{:S(2)}, u32[]{:S(2)}) %all-to-all-start.6) | async-done | bytes 1114144 | tf_op jit(solution)/shard_map/all_to_all | solution.py:61
  280.2 1.3 reduce_sum.145
  281.5 0.1 bitcast_add_fusion
  281.7 0.0 copy-start
  281.7 0.9 copy-done
  282.7 9.4 %all_to_all.48 = f32[16,2,128]{2,1,0:T(2,128)S(1)} all-to-all(f32[16,2,128]{2,1,0:T(2,128)S(1)} %broadcast_in_dim.25), channel_id=1, replica_groups=mesh['comp'=32,'feat'=16] {'feat'}, dimensions={0} | all-to-all | bytes 32768 | tf_op jit(solution)/shard_map/all_to_all | solution.py:163
  292.1 19.1 %all_to_all.49 = f32[32,2,128]{2,1,0:T(2,128)S(1)} all-to-all(f32[32,2,128]{2,1,0:T(2,128)S(1)} %broadcast_in_dim.26), channel_id=1, replica_groups=mesh['comp'=32,'feat'=16] {'comp'}, dimensions={0} | all-to-all | bytes 65536 | tf_op jit(solution)/shard_map/all_to_all | solution.py:128
  311.2 2.2 multiply_add_fusion
  313.4 1.5 multiply_subtract_fusion
  (26 shorter events, 0.5 us)
Async XLA Ops:
  2.6 21.8 %all-to-all-start = ((f32[16,128,128]{2,1,0:T(8,128)}), f32[16,128,128]{2,1,0:T(8,128)S(1)}, u32[]{:S(2)}, u32[]{:S(2)}) async-start(f32[16,128,128]{2,1,0:T(8,128)} %broadcast_in_dim.18), calls=%async_computation | async-start | bytes 2097152 | tf_op jit(solution)/shard_map/all_to_all | solution.py:124
  27.9 8.3 %copy-start.1 = (f32[1792,128]{1,0:T(8,128)S(1)}, f32[1792,128]{1,0:T(8,128)}, u32[]{:S(2)}) copy-start(f32[1792,128]{1,0:T(8,128)} %shard_map.77) | copy-start | bytes 2752516
  29.0 7.2 %collective-permute-start = (f32[896,128]{1,0:T(8,128)S(1)}, f32[896,128]{1,0:T(8,128)S(1)}, u32[]{:S(2)}, u32[]{:S(2)}) collective-permute-start(f32[896,128]{1,0:T(8,128)S(1)} %constant_dynamic-slice_fusion.1), channel_id=1, source_target_pairs={{0,16},{16,0},{32,48},{48,32},{64,80},{80,64},{96,112},{112,96},{1... | collective-permute-start | bytes 1376264 | tf_op jit(solution)/shard_map/ppermute | solution.py:98
  115.9 21.1 %all-to-all-start.2 = ((f32[16,128,128]{2,1,0:T(8,128)}), f32[16,128,128]{2,1,0:T(8,128)S(1)}, u32[]{:S(2)}, u32[]{:S(2)}) async-start(f32[16,128,128]{2,1,0:T(8,128)} %bitcast.73), calls=%async_computation.2 | async-start | bytes 2097152 | tf_op jit(solution)/shard_map/all_to_all | solution.py:61
  156.3 20.5 %copy-start.3 = (f32[128]{0:T(128)S(1)}, f32[128]{0:T(128)}, u32[]{:S(2)}) copy-start(f32[128]{0:T(128)} %param.13) | copy-start | bytes 1540
  180.7 6.1 %copy-start.2 = (f32[1792,128]{1,0:T(8,128)S(1)}, f32[1792,128]{1,0:T(8,128)}, u32[]{:S(2)}) copy-start(f32[1792,128]{1,0:T(8,128)} %shard_map.79) | copy-start | bytes 2752516
  181.9 4.9 %collective-permute-start.1 = (f32[896,128]{1,0:T(8,128)S(1)}, f32[896,128]{1,0:T(8,128)S(1)}, u32[]{:S(2)}, u32[]{:S(2)}) collective-permute-start(f32[896,128]{1,0:T(8,128)S(1)} %constant_dynamic-slice_fusion), channel_id=1, source_target_pairs={{0,16},{16,0},{32,48},{48,32},{64,80},{80,64},{96,112},{112,96},{1... | collective-permute-start | bytes 1376264 | tf_op jit(solution)/shard_map/ppermute | solution.py:98
  187.6 24.5 %all-to-all-start.5 = ((f32[16,56,128]{2,1,0:T(8,128)}), f32[16,56,128]{2,1,0:T(8,128)S(1)}, u32[]{:S(2)}, u32[]{:S(2)}) async-start(f32[16,56,128]{2,1,0:T(8,128)} %bitcast.17), calls=%async_computation.5 | async-start | bytes 917504 | tf_op jit(solution)/shard_map/all_to_all | solution.py:105
  257.4 22.8 %all-to-all-start.6 = ((f32[16,136,128]{2,1,0:T(8,128)}), f32[16,136,128]{2,1,0:T(8,128)}, u32[]{:S(2)}, u32[]{:S(2)}) async-start(f32[16,136,128]{2,1,0:T(8,128)} %bitcast.72), calls=%async_computation.6 | async-start | bytes 2228224 | tf_op jit(solution)/shard_map/all_to_all | solution.py:61
  281.7 0.9 copy-start

commit v16 on v15

--- a/solution.py
+++ b/solution.py
@@ -12,7 +12,7 @@
 ITERS = 2
 
 
-def _block_kernel(transpose, pitch, count_ref, out_idx_ref, in_idx_ref, values_ref, x_ref, *rest):
+def _block_kernel(transpose, pitch, keep_first, count_ref, out_idx_ref, in_idx_ref, core_ref, values_ref, x_ref, *rest):
     edge = values_ref.shape[1]
     out_ref = rest[-1]
     out_ref[...] = jnp.zeros_like(out_ref)
@@ -23,7 +23,12 @@
 
     def body(s, carry):
         src = pl.multiple_of(in_idx_ref[s] * edge, edge)
-        dst = pl.multiple_of(out_idx_ref[s] * pitch, 8)
+        block_index = out_idx_ref[s]
+        if keep_first:
+            half = out_ref.shape[0] // pitch // 2
+            other = (block_index // half != core_ref[0]).astype(jnp.int32)
+            block_index = block_index % half + other * half
+        dst = pl.multiple_of(block_index * pitch, 8)
         block = values_ref[s]
         x = x_ref[pl.ds(src, edge), :]
         if transpose:
@@ -39,18 +44,20 @@
     lax.fori_loop(0, values_ref.shape[0], body, 0, unroll=True)
 
 
-def block_apply(values, count, out_idx, in_idx, x, out_blocks, transpose, extra=None):
+def block_apply(values, count, out_idx, in_idx, x, out_blocks, transpose, extra=None, core=None):
     edge = values.shape[1]
     pitch = edge if extra is None else edge + extra.shape[0]
     smem = pl.BlockSpec(memory_space=pltpu.SMEM)
     vmem = pl.BlockSpec(memory_space=pltpu.VMEM)
-    operands = [count.reshape(1), out_idx, in_idx, values, x]
+    keep_first = core is not None
+    core = jnp.zeros((1,), jnp.int32) if core is None else core.astype(jnp.int32).reshape(1)
+    operands = [count.reshape(1), out_idx, in_idx, core, values, x]
     if extra is not None:
         operands.append(extra)
     return pl.pallas_call(
-        functools.partial(_block_kernel, transpose, pitch),
+        functools.partial(_block_kernel, transpose, pitch, keep_first),
         out_shape=jax.ShapeDtypeStruct((out_blocks * pitch, x.shape[1]), jnp.float32),
-        in_specs=[smem, smem, smem] + [vmem] * (len(operands) - 3),
+        in_specs=[smem, smem, smem, smem] + [vmem] * (len(operands) - 4),
         out_specs=vmem,
     )(*operands)
 
@@ -71,9 +78,12 @@
     feat_rows = CB_DEV * block_edge
     own_rows = feat_rows // n_comp
     comp_index = lax.axis_index("comp")
+    core = comp_index % 2
 
     def backward(low_slab):
-        return block_apply(values, count_of_slots, slot_cols, slot_rows, low_slab, CB_DEV, True)
+        return block_apply(
+            values, count_of_slots, slot_cols, slot_rows, low_slab, CB_DEV, True, core=core
+        )
 
     def forward(direction, extra=None):
         low = direction.astype(jnp.bfloat16)
@@ -87,7 +97,6 @@
         landed = reduce_over(summed, "feat", n_feat)
         return landed[:block_edge], landed[block_edge : block_edge + extra.shape[0]]
 
-    core = comp_index % 2
     chip = comp_index // 2
     n_chips = n_comp // 2
     half_rows = feat_rows // 2
@@ -98,8 +107,7 @@
         return lax.ppermute(x, "comp", siblings)
 
     def reduce_gradient(partial):
-        kept = lax.dynamic_slice_in_dim(partial, core * half_rows, half_rows, axis=0)
-        sent = lax.dynamic_slice_in_dim(partial, (1 - core) * half_rows, half_rows, axis=0)
+        kept, sent = partial[:half_rows], partial[half_rows:]
         chip_sum = kept + swap_with_sibling(sent)
         pieces = chip_sum.reshape(n_chips, own_rows, chip_sum.shape[1])
         landed = lax.all_to_all(pieces, "comp", 0, 0, tiled=True, axis_index_groups=same_core)

time: 316 us -> 316 us (level)
  no operation moved by 1% of the time
where the time goes in v16:
time: 316 us; the launch traced here: 315 us
  blocking collectives  184 us (58%)
  waiting for transfers between devices  71.9 us (23%)
  starting transfers between devices  28.4 us (9%)
  other arithmetic  12.3 us (4%)
  Pallas kernels  10.6 us (3%)
  local copies, waits for them, and re-layouts  6.02 us (2%)
    all_gather x2, blocking collectives, gather_gradient(): got = lax.all_gather(own, 'comp', axis=0, tiled=False)  80.3 us
    all_to_all x2, blocking collectives, comp_total(): return lax.all_to_all(spread, 'comp', 0, 0, tiled=True).sum(0)  39.3 us
    all_to_all x1, blocking collectives, reduce_gradient(): lax.all_to_all(pieces, 'comp', 0, 0, tiled=True, axis_index_groups=same_c...  36 us
    all_to_all x2, waiting for transfers between devices, reduce_over(): return lax.all_to_all(pieces, axis, 0, 0, tiled=True).sum(0)  35.6 us
    all_to_all x1, waiting for transfers between devices, reduce_gradient(): lax.all_to_all(pieces, 'comp', 0, 0, tiled=True, axis_index_groups=same_c...  19.9 us
    all_to_all x1, blocking collectives, gather_feat(): return lax.all_to_all(spread, 'feat', 0, 0, tiled=True)  19.2 us
    all_to_all x1, waiting for transfers between devices, gather_feat(): return lax.all_to_all(spread, 'feat', 0, 0, tiled=True)  13.6 us
    pallas_call x4, Pallas kernels, block_apply(): pl.pallas_call(functools.partial(_block_kernel, transpose, pitch, keep_fi...  10.6 us
  transfers between devices with their start and end apart: 6, of which 6 were waited for; matrix products, arithmetic and copies ran while one was open for 0% of the time, Pallas kernels for 0%

profile of v16, /device:TPU:1, one launch (start us, length us, event | category | flops | bytes accessed | tf_op | source)
XLA Modules:
  0.0 315.0 jit_solution(14074694894038983670)
XLA Ops:
  0.6 1.9 broadcast_in_dim.18
  2.6 7.6 %all-to-all-start = ((f32[16,128,128]{2,1,0:T(8,128)}), f32[16,128,128]{2,1,0:T(8,128)S(1)}, u32[]{:S(2)}, u32[]{:S(2)}) async-start(f32[16,128,128]{2,1,0:T(8,128)} %broadcast_in_dim.18), calls=%async_computation | async-start | bytes 2097152 | tf_op jit(solution)/shard_map/all_to_all | solution.py:132
  10.8 13.6 %all-to-all-done = f32[16,128,128]{2,1,0:T(8,128)S(1)} async-done(((f32[16,128,128]{2,1,0:T(8,128)}), f32[16,128,128]{2,1,0:T(8,128)S(1)}, u32[]{:S(2)}, u32[]{:S(2)}) %all-to-all-start) | async-done | bytes 1048608 | tf_op jit(solution)/shard_map/all_to_all | solution.py:132
  24.4 0.8 bitcast_convert_fusion.x_ref
  25.2 2.7 shard_map.77
  27.9 1.1 slice.77
  29.0 5.7 %collective-permute-start = (f32[896,128]{1,0:T(8,128)S(1)}, f32[896,128]{1,0:T(8,128)S(1)}, u32[]{:S(2)}, u32[]{:S(2)}) collective-permute-start(f32[896,128]{1,0:T(8,128)S(1)} %slice.77), channel_id=1, source_target_pairs={{0,16},{16,0},{32,48},{48,32},{64,80},{80,64},{96,112},{112,96},{1... | collective-permute-start | bytes 1376264 | tf_op jit(solution)/shard_map/ppermute | solution.py:107
  34.8 1.4 collective-permute-done
  36.2 0.1 slice_add_fusion.1
  36.3 36.0 %all_to_all.45 = f32[16,56,128]{2,1,0:T(8,128)S(1)} all-to-all(f32[16,56,128]{2,1,0:T(8,128)S(1)} %bitcast.77), channel_id=1, replica_groups={{0,32,64,96,128,160,192,224,256,288,320,352,384,416,448,480},{16,48,80,..., dimensions={0} | all-to-all | bytes 917504 | tf_op jit(solution)/shard_map/all_to_all | solution.py:113
  72.3 40.1 %all-gather = f32[1792,128]{1,0:T(8,128)S(1)} all-gather(f32[56,128]{1,0:T(8,128)S(1)} %reduce_sum.135), channel_id=2, replica_groups=mesh['comp'=32,'feat'=16] {'comp'}, dimensions={0}, use_global_device_ids=true | all-gather | bytes 946176 | tf_op jit(solution)/shard_map/all_gather | solution.py:117
  112.4 0.1 copy.15
  112.5 0.8 bitcast_convert_fusion.2.x_ref
  113.3 2.6 shard_map.78
  115.9 3.7 %all-to-all-start.2 = ((f32[16,128,128]{2,1,0:T(8,128)}), f32[16,128,128]{2,1,0:T(8,128)S(1)}, u32[]{:S(2)}, u32[]{:S(2)}) async-start(f32[16,128,128]{2,1,0:T(8,128)} %bitcast.74), calls=%async_computation.2 | async-start | bytes 2097152 | tf_op jit(solution)/shard_map/all_to_all | solution.py:68
  119.7 17.3 %all-to-all-done.2 = f32[16,128,128]{2,1,0:T(8,128)S(1)} async-done(((f32[16,128,128]{2,1,0:T(8,128)}), f32[16,128,128]{2,1,0:T(8,128)S(1)}, u32[]{:S(2)}, u32[]{:S(2)}) %all-to-all-start.2) | async-done | bytes 1048608 | tf_op jit(solution)/shard_map/all_to_all | solution.py:68
  137.0 0.1 reduce_sum.136
  137.0 0.1 broadcast_in_dim.21
  137.1 19.2 %all_to_all.46 = f32[16,130,128]{2,1,0:T(8,128)S(1)} all-to-all(f32[16,130,128]{2,1,0:T(8,128)S(1)} %broadcast_in_dim.21), channel_id=1, replica_groups=mesh['comp'=32,'feat'=16] {'feat'}, dimensions={0} | all-to-all | bytes 2129920 | tf_op jit(solution)/shard_map/all_to_all | solution.py:132
  156.3 0.3 fusion.5
  156.6 20.2 %all_to_all.47 = f32[32,3,128]{2,1,0:T(4,128)S(1)} all-to-all(f32[32,3,128]{2,1,0:T(4,128)S(1)} %broadcast_in_dim.23), channel_id=1, replica_groups=mesh['comp'=32,'feat'=16] {'comp'}, dimensions={0} | all-to-all | bytes 98304 | tf_op jit(solution)/shard_map/all_to_all | solution.py:136
  176.9 1.3 fusion.4
  178.1 2.7 shard_map.79
  180.8 1.1 slice.81
  181.9 3.5 %collective-permute-start.1 = (f32[896,128]{1,0:T(8,128)S(1)}, f32[896,128]{1,0:T(8,128)S(1)}, u32[]{:S(2)}, u32[]{:S(2)}) collective-permute-start(f32[896,128]{1,0:T(8,128)S(1)} %slice.81), channel_id=1, source_target_pairs={{0,16},{16,0},{32,48},{48,32},{64,80},{80,64},{96,112},{112,96},{1... | collective-permute-start | bytes 1376264 | tf_op jit(solution)/shard_map/ppermute | solution.py:107
  185.4 1.4 collective-permute-done.1
  186.9 0.8 slice_add_fusion
  187.7 3.6 %all-to-all-start.5 = ((f32[16,56,128]{2,1,0:T(8,128)}), f32[16,56,128]{2,1,0:T(8,128)S(1)}, u32[]{:S(2)}, u32[]{:S(2)}) async-start(f32[16,56,128]{2,1,0:T(8,128)} %bitcast.18), calls=%async_computation.5 | async-start | bytes 917504 | tf_op jit(solution)/shard_map/all_to_all | solution.py:113
  191.2 1.0 broadcast_multiply_fusion
  192.2 19.9 %all-to-all-done.5 = f32[16,56,128]{2,1,0:T(8,128)S(1)} async-done(((f32[16,56,128]{2,1,0:T(8,128)}), f32[16,56,128]{2,1,0:T(8,128)S(1)}, u32[]{:S(2)}, u32[]{:S(2)}) %all-to-all-start.5) | async-done | bytes 458784 | tf_op jit(solution)/shard_map/all_to_all | solution.py:113
  212.2 0.8 multiply_reduce_fusion.3
  213.0 40.2 %all-gather.2 = f32[32,57,128]{2,1,0:T(8,128)S(1)} all-gather(f32[1,57,128]{2,1,0:T(8,128)S(1)} %maximum_bitcast_fusion), channel_id=3, replica_groups=mesh['comp'=32,'feat'=16] {'comp'}, dimensions={0}, use_global_device_ids=true | all-gather | bytes 963072 | tf_op jit(solution)/shard_map/all_gather | solution.py:117
  253.2 0.1 slice_reduce_fusion
  253.3 0.1 slice.82
  253.3 0.1 copy.17
  253.4 0.6 scatter.4.rest_0_
  254.0 0.8 bitcast_convert_fusion.1.x_ref
  254.8 2.7 shard_map.80
  257.5 4.4 %all-to-all-start.6 = ((f32[16,136,128]{2,1,0:T(8,128)}), f32[16,136,128]{2,1,0:T(8,128)}, u32[]{:S(2)}, u32[]{:S(2)}) async-start(f32[16,136,128]{2,1,0:T(8,128)} %bitcast.73), calls=%async_computation.6 | async-start | bytes 2228224 | tf_op jit(solution)/shard_map/all_to_all | solution.py:68
  261.9 18.3 %all-to-all-done.6 = f32[16,136,128]{2,1,0:T(8,128)} async-done(((f32[16,136,128]{2,1,0:T(8,128)}), f32[16,136,128]{2,1,0:T(8,128)}, u32[]{:S(2)}, u32[]{:S(2)}) %all-to-all-start.6) | async-done | bytes 1114144 | tf_op jit(solution)/shard_map/all_to_all | solution.py:68
  280.2 1.3 reduce_sum.145
  281.5 0.1 bitcast_add_fusion
  281.6 0.0 copy-start
  281.6 0.9 copy-done
  282.6 9.4 %all_to_all.48 = f32[16,2,128]{2,1,0:T(2,128)S(1)} all-to-all(f32[16,2,128]{2,1,0:T(2,128)S(1)} %broadcast_in_dim.25), channel_id=1, replica_groups=mesh['comp'=32,'feat'=16] {'feat'}, dimensions={0} | all-to-all | bytes 32768 | tf_op jit(solution)/shard_map/all_to_all | solution.py:171
  292.1 19.1 %all_to_all.49 = f32[32,2,128]{2,1,0:T(2,128)S(1)} all-to-all(f32[32,2,128]{2,1,0:T(2,128)S(1)} %broadcast_in_dim.26), channel_id=1, replica_groups=mesh['comp'=32,'feat'=16] {'comp'}, dimensions={0} | all-to-all | bytes 65536 | tf_op jit(solution)/shard_map/all_to_all | solution.py:136
  311.3 2.2 multiply_add_fusion
  313.5 1.5 multiply_subtract_fusion
  (26 shorter events, 0.4 us)
Async XLA Ops:
  2.6 21.8 %all-to-all-start = ((f32[16,128,128]{2,1,0:T(8,128)}), f32[16,128,128]{2,1,0:T(8,128)S(1)}, u32[]{:S(2)}, u32[]{:S(2)}) async-start(f32[16,128,128]{2,1,0:T(8,128)} %broadcast_in_dim.18), calls=%async_computation | async-start | bytes 2097152 | tf_op jit(solution)/shard_map/all_to_all | solution.py:132
  27.9 8.3 %copy-start.2 = (f32[1792,128]{1,0:T(8,128)S(1)}, f32[1792,128]{1,0:T(8,128)}, u32[]{:S(2)}) copy-start(f32[1792,128]{1,0:T(8,128)} %shard_map.77) | copy-start | bytes 2752516
  29.0 7.2 %collective-permute-start = (f32[896,128]{1,0:T(8,128)S(1)}, f32[896,128]{1,0:T(8,128)S(1)}, u32[]{:S(2)}, u32[]{:S(2)}) collective-permute-start(f32[896,128]{1,0:T(8,128)S(1)} %slice.77), channel_id=1, source_target_pairs={{0,16},{16,0},{32,48},{48,32},{64,80},{80,64},{96,112},{112,96},{1... | collective-permute-start | bytes 1376264 | tf_op jit(solution)/shard_map/ppermute | solution.py:107
  115.9 21.0 %all-to-all-start.2 = ((f32[16,128,128]{2,1,0:T(8,128)}), f32[16,128,128]{2,1,0:T(8,128)S(1)}, u32[]{:S(2)}, u32[]{:S(2)}) async-start(f32[16,128,128]{2,1,0:T(8,128)} %bitcast.74), calls=%async_computation.2 | async-start | bytes 2097152 | tf_op jit(solution)/shard_map/all_to_all | solution.py:68
  156.3 20.5 %copy-start.3 = (f32[128]{0:T(128)S(1)}, f32[128]{0:T(128)}, u32[]{:S(2)}) copy-start(f32[128]{0:T(128)} %param.13) | copy-start | bytes 1540
  180.8 6.0 %copy-start.1 = (f32[1792,128]{1,0:T(8,128)S(1)}, f32[1792,128]{1,0:T(8,128)}, u32[]{:S(2)}) copy-start(f32[1792,128]{1,0:T(8,128)} %shard_map.79) | copy-start | bytes 2752516
  181.9 4.9 %collective-permute-start.1 = (f32[896,128]{1,0:T(8,128)S(1)}, f32[896,128]{1,0:T(8,128)S(1)}, u32[]{:S(2)}, u32[]{:S(2)}) collective-permute-start(f32[896,128]{1,0:T(8,128)S(1)} %slice.81), channel_id=1, source_target_pairs={{0,16},{16,0},{32,48},{48,32},{64,80},{80,64},{96,112},{112,96},{1... | collective-permute-start | bytes 1376264 | tf_op jit(solution)/shard_map/ppermute | solution.py:107
  187.7 24.5 %all-to-all-start.5 = ((f32[16,56,128]{2,1,0:T(8,128)}), f32[16,56,128]{2,1,0:T(8,128)S(1)}, u32[]{:S(2)}, u32[]{:S(2)}) async-start(f32[16,56,128]{2,1,0:T(8,128)} %bitcast.18), calls=%async_computation.5 | async-start | bytes 917504 | tf_op jit(solution)/shard_map/all_to_all | solution.py:113
  257.5 22.7 %all-to-all-start.6 = ((f32[16,136,128]{2,1,0:T(8,128)}), f32[16,136,128]{2,1,0:T(8,128)}, u32[]{:S(2)}, u32[]{:S(2)}) async-start(f32[16,136,128]{2,1,0:T(8,128)} %bitcast.73), calls=%async_computation.6 | async-start | bytes 2228224 | tf_op jit(solution)/shard_map/all_to_all | solution.py:68
  281.6 0.9 copy-start

commit v17 on v15

--- a/solution.py
+++ b/solution.py
@@ -138,6 +138,7 @@
     direction, _ = gather_gradient(gradient_own)
     energy = None
     solution = None
+    own_residual = right_side
     for step_index in range(ITERS):
         last = step_index + 1 == ITERS
         if step_index > 0:
@@ -178,11 +179,10 @@
         step_size = energy / (image_energy + ridge * direction_energy)
         solution = step_size * direction if solution is None else solution + step_size * direction
         if last:
-            own_residual = lax.dynamic_slice_in_dim(residual_slab, feat_index * own_block, own_block)
             residual = own_residual - step_size * image_rows
         else:
+            own_residual = own_residual - step_size * image_rows
             residual_slab = residual_slab - step_size * image_slab
-            image_rows = lax.dynamic_slice_in_dim(image_slab, feat_index * own_block, own_block)
     return (solution, residual)
 
 

time: 316 us -> 309 us (0.978)
  blocking collectives: 184 us -> 205 us
  waiting for transfers between devices: 72.1 us -> 54.6 us
  other arithmetic: 12.3 us -> 6.98 us
  starting transfers between devices: 28.4 us -> 24 us
    all_to_all x0 -> x1, blocking collectives: none -> 21.2 us  [reduce_over(): return lax.all_to_all(pieces, axis, 0, 0, tiled=True).sum(0)]
    all_to_all x2 -> x1, waiting for transfers between devices: 35.7 us -> 17.3 us  [reduce_over(): return lax.all_to_all(pieces, axis, 0, 0, tiled=True).sum(0)]
    all_to_all x2 -> x1, starting transfers between devices: 8.03 us -> 3.65 us  [reduce_over(): return lax.all_to_all(pieces, axis, 0, 0, tiled=True).sum(0)]
  transfers between devices with their start and end apart: 6 -> 5, of which waited for: 6 -> 5; matrix products, arithmetic and copies ran while one was open for 0% -> 0% of each run, Pallas kernels for 0% -> 0%
where the time goes in v17:
time: 309 us; the launch traced here: 308 us
  blocking collectives  205 us (66%)
  waiting for transfers between devices  54.6 us (18%)
  starting transfers between devices  24 us (8%)
  Pallas kernels  10.6 us (3%)
  other arithmetic  6.98 us (2%)
  local copies, waits for them, and re-layouts  5.11 us (2%)
    all_gather x2, blocking collectives, gather_gradient(): got = lax.all_gather(own, 'comp', axis=0, tiled=False)  80.3 us
    all_to_all x2, blocking collectives, comp_total(): return lax.all_to_all(spread, 'comp', 0, 0, tiled=True).sum(0)  38.9 us
    all_to_all x1, blocking collectives, reduce_gradient(): lax.all_to_all(pieces, 'comp', 0, 0, tiled=True, axis_index_groups=same_c...  36 us
    all_to_all x1, blocking collectives, reduce_over(): return lax.all_to_all(pieces, axis, 0, 0, tiled=True).sum(0)  21.2 us
    all_to_all x1, waiting for transfers between devices, reduce_gradient(): lax.all_to_all(pieces, 'comp', 0, 0, tiled=True, axis_index_groups=same_c...  20.8 us
    all_to_all x1, blocking collectives, gather_feat(): return lax.all_to_all(spread, 'feat', 0, 0, tiled=True)  19.2 us
    all_to_all x1, waiting for transfers between devices, reduce_over(): return lax.all_to_all(pieces, axis, 0, 0, tiled=True).sum(0)  17.3 us
    all_to_all x1, waiting for transfers between devices, gather_feat(): return lax.all_to_all(spread, 'feat', 0, 0, tiled=True)  13.6 us
  transfers between devices with their start and end apart: 5, of which 5 were waited for; matrix products, arithmetic and copies ran while one was open for 0% of the time, Pallas kernels for 0%

profile of v17, /device:TPU:1, one launch (start us, length us, event | category | flops | bytes accessed | tf_op | source)
XLA Modules:
  0.0 308.0 jit_solution(17378328366634330466)
XLA Ops:
  0.6 1.9 broadcast_in_dim.18
  2.6 7.6 %all-to-all-start = ((f32[16,128,128]{2,1,0:T(8,128)}), f32[16,128,128]{2,1,0:T(8,128)S(1)}, u32[]{:S(2)}, u32[]{:S(2)}) async-start(f32[16,128,128]{2,1,0:T(8,128)} %broadcast_in_dim.18), calls=%async_computation | async-start | bytes 2097152 | tf_op jit(solution)/shard_map/all_to_all | solution.py:124
  10.8 13.6 %all-to-all-done = f32[16,128,128]{2,1,0:T(8,128)S(1)} async-done(((f32[16,128,128]{2,1,0:T(8,128)}), f32[16,128,128]{2,1,0:T(8,128)S(1)}, u32[]{:S(2)}, u32[]{:S(2)}) %all-to-all-start) | async-done | bytes 1048608 | tf_op jit(solution)/shard_map/all_to_all | solution.py:124
  24.4 0.8 bitcast_convert_fusion.x_ref
  25.2 2.7 shard_map.77
  27.9 0.0 copy-start
  27.9 1.1 constant_dynamic-slice_fusion.1
  29.0 5.7 %collective-permute-start = (f32[896,128]{1,0:T(8,128)S(1)}, f32[896,128]{1,0:T(8,128)S(1)}, u32[]{:S(2)}, u32[]{:S(2)}) collective-permute-start(f32[896,128]{1,0:T(8,128)S(1)} %constant_dynamic-slice_fusion.1), channel_id=1, source_target_pairs={{0,16},{16,0},{32,48},{48,32},{64,80},{80,64},{96,112},{112,96},{1... | collective-permute-start | bytes 1376264 | tf_op jit(solution)/shard_map/ppermute | solution.py:98
  34.8 1.4 collective-permute-done
  36.2 0.0 copy-done
  36.2 36.0 %all_to_all.45 = f32[16,56,128]{2,1,0:T(8,128)S(1)} all-to-all(f32[16,56,128]{2,1,0:T(8,128)S(1)} %bitcast.76), channel_id=1, replica_groups={{0,32,64,96,128,160,192,224,256,288,320,352,384,416,448,480},{16,48,80,..., dimensions={0} | all-to-all | bytes 917504 | tf_op jit(solution)/shard_map/all_to_all | solution.py:105
  72.3 40.1 %all-gather = f32[1792,128]{1,0:T(8,128)S(1)} all-gather(f32[56,128]{1,0:T(8,128)S(1)} %reduce_sum.135), channel_id=2, replica_groups=mesh['comp'=32,'feat'=16] {'comp'}, dimensions={0}, use_global_device_ids=true | all-gather | bytes 946176 | tf_op jit(solution)/shard_map/all_gather | solution.py:109
  112.4 0.1 copy.15
  112.5 0.8 bitcast_convert_fusion.2.x_ref
  113.3 2.7 shard_map.78
  115.9 3.7 %all-to-all-start.2 = ((f32[16,128,128]{2,1,0:T(8,128)}), f32[16,128,128]{2,1,0:T(8,128)S(1)}, u32[]{:S(2)}, u32[]{:S(2)}) async-start(f32[16,128,128]{2,1,0:T(8,128)} %bitcast.73), calls=%async_computation.2 | async-start | bytes 2097152 | tf_op jit(solution)/shard_map/all_to_all | solution.py:61
  119.7 17.3 %all-to-all-done.2 = f32[16,128,128]{2,1,0:T(8,128)S(1)} async-done(((f32[16,128,128]{2,1,0:T(8,128)}), f32[16,128,128]{2,1,0:T(8,128)S(1)}, u32[]{:S(2)}, u32[]{:S(2)}) %all-to-all-start.2) | async-done | bytes 1048608 | tf_op jit(solution)/shard_map/all_to_all | solution.py:61
  137.0 0.1 reduce_sum.136
  137.1 0.1 broadcast_in_dim.21
  137.1 19.2 %all_to_all.46 = f32[16,130,128]{2,1,0:T(8,128)S(1)} all-to-all(f32[16,130,128]{2,1,0:T(8,128)S(1)} %broadcast_in_dim.21), channel_id=1, replica_groups=mesh['comp'=32,'feat'=16] {'feat'}, dimensions={0} | all-to-all | bytes 2129920 | tf_op jit(solution)/shard_map/all_to_all | solution.py:124
  156.3 0.3 fusion.6
  156.7 20.1 %all_to_all.47 = f32[32,3,128]{2,1,0:T(4,128)S(1)} all-to-all(f32[32,3,128]{2,1,0:T(4,128)S(1)} %broadcast_in_dim.23), channel_id=1, replica_groups=mesh['comp'=32,'feat'=16] {'comp'}, dimensions={0} | all-to-all | bytes 98304 | tf_op jit(solution)/shard_map/all_to_all | solution.py:128
  176.8 0.0 copy-done.3
  176.8 0.9 fusion.1.x_ref
  177.7 2.7 shard_map.79
  180.4 1.1 constant_dynamic-slice_fusion
  181.5 3.5 %collective-permute-start.1 = (f32[896,128]{1,0:T(8,128)S(1)}, f32[896,128]{1,0:T(8,128)S(1)}, u32[]{:S(2)}, u32[]{:S(2)}) collective-permute-start(f32[896,128]{1,0:T(8,128)S(1)} %constant_dynamic-slice_fusion), channel_id=1, source_target_pairs={{0,16},{16,0},{32,48},{48,32},{64,80},{80,64},{96,112},{112,96},{1... | collective-permute-start | bytes 1376264 | tf_op jit(solution)/shard_map/ppermute | solution.py:98
  185.0 1.4 collective-permute-done.1
  186.4 0.0 copy-done.1
  186.4 0.8 dynamic-slice_add_fusion
  187.3 3.6 %all-to-all-start.5 = ((f32[16,56,128]{2,1,0:T(8,128)}), f32[16,56,128]{2,1,0:T(8,128)S(1)}, u32[]{:S(2)}, u32[]{:S(2)}) async-start(f32[16,56,128]{2,1,0:T(8,128)} %bitcast.17), calls=%async_computation.5 | async-start | bytes 917504 | tf_op jit(solution)/shard_map/all_to_all | solution.py:105
  190.8 0.1 broadcast_multiply_fusion
  190.9 20.8 %all-to-all-done.5 = f32[16,56,128]{2,1,0:T(8,128)S(1)} async-done(((f32[16,56,128]{2,1,0:T(8,128)}), f32[16,56,128]{2,1,0:T(8,128)S(1)}, u32[]{:S(2)}, u32[]{:S(2)}) %all-to-all-start.5) | async-done | bytes 458784 | tf_op jit(solution)/shard_map/all_to_all | solution.py:105
  211.8 40.2 %all-gather.2 = f32[32,57,128]{2,1,0:T(8,128)S(1)} all-gather(f32[1,57,128]{2,1,0:T(8,128)S(1)} %maximum_bitcast_fusion), channel_id=3, replica_groups=mesh['comp'=32,'feat'=16] {'comp'}, dimensions={0}, use_global_device_ids=true | all-gather | bytes 963072 | tf_op jit(solution)/shard_map/all_gather | solution.py:109
  252.0 0.1 slice_reduce_fusion
  252.1 0.1 slice.62
  252.2 0.1 copy.17
  252.2 0.6 scatter.4.rest_0_
  252.8 0.8 bitcast_convert_fusion.1.x_ref
  253.7 2.7 shard_map.80
  256.3 21.2 %all_to_all.48 = f32[16,136,128]{2,1,0:T(8,128)S(1)} all-to-all(f32[16,136,128]{2,1,0:T(8,128)} %bitcast.72), channel_id=1, replica_groups=mesh['comp'=32,'feat'=16] {'feat'}, dimensions={0} | all-to-all | bytes 2228224 | tf_op jit(solution)/shard_map/all_to_all | solution.py:61
  277.6 0.1 reduce_sum.145
  277.6 0.1 bitcast_add_fusion
  277.8 9.6 %all_to_all.49 = f32[16,2,128]{2,1,0:T(2,128)S(1)} all-to-all(f32[16,2,128]{2,1,0:T(2,128)S(1)} %broadcast_in_dim.25), channel_id=1, replica_groups=mesh['comp'=32,'feat'=16] {'feat'}, dimensions={0} | all-to-all | bytes 32768 | tf_op jit(solution)/shard_map/all_to_all | solution.py:164
  287.5 18.8 %all_to_all.50 = f32[32,2,128]{2,1,0:T(2,128)S(1)} all-to-all(f32[32,2,128]{2,1,0:T(2,128)S(1)} %broadcast_in_dim.26), channel_id=1, replica_groups=mesh['comp'=32,'feat'=16] {'comp'}, dimensions={0} | all-to-all | bytes 65536 | tf_op jit(solution)/shard_map/all_to_all | solution.py:128
  306.3 1.0 multiply_add_fusion
  307.4 0.0 copy-done.2
  307.4 0.6 multiply_subtract_fusion
  (25 shorter events, 0.5 us)
Async XLA Ops:
  2.6 21.8 %all-to-all-start = ((f32[16,128,128]{2,1,0:T(8,128)}), f32[16,128,128]{2,1,0:T(8,128)S(1)}, u32[]{:S(2)}, u32[]{:S(2)}) async-start(f32[16,128,128]{2,1,0:T(8,128)} %broadcast_in_dim.18), calls=%async_computation | async-start | bytes 2097152 | tf_op jit(solution)/shard_map/all_to_all | solution.py:124
  27.9 8.3 %copy-start = (f32[1792,128]{1,0:T(8,128)S(1)}, f32[1792,128]{1,0:T(8,128)}, u32[]{:S(2)}) copy-start(f32[1792,128]{1,0:T(8,128)} %shard_map.77) | copy-start | bytes 2752516
  29.0 7.2 %collective-permute-start = (f32[896,128]{1,0:T(8,128)S(1)}, f32[896,128]{1,0:T(8,128)S(1)}, u32[]{:S(2)}, u32[]{:S(2)}) collective-permute-start(f32[896,128]{1,0:T(8,128)S(1)} %constant_dynamic-slice_fusion.1), channel_id=1, source_target_pairs={{0,16},{16,0},{32,48},{48,32},{64,80},{80,64},{96,112},{112,96},{1... | collective-permute-start | bytes 1376264 | tf_op jit(solution)/shard_map/ppermute | solution.py:98
  115.9 21.1 %all-to-all-start.2 = ((f32[16,128,128]{2,1,0:T(8,128)}), f32[16,128,128]{2,1,0:T(8,128)S(1)}, u32[]{:S(2)}, u32[]{:S(2)}) async-start(f32[16,128,128]{2,1,0:T(8,128)} %bitcast.73), calls=%async_computation.2 | async-start | bytes 2097152 | tf_op jit(solution)/shard_map/all_to_all | solution.py:61
  156.3 20.5 %copy-start.3 = (f32[128]{0:T(128)S(1)}, f32[128]{0:T(128)}, u32[]{:S(2)}) copy-start(f32[128]{0:T(128)} %param.13) | copy-start | bytes 1540
  180.4 6.0 %copy-start.1 = (f32[1792,128]{1,0:T(8,128)S(1)}, f32[1792,128]{1,0:T(8,128)}, u32[]{:S(2)}) copy-start(f32[1792,128]{1,0:T(8,128)} %shard_map.79) | copy-start | bytes 2752516
  181.5 4.9 %collective-permute-start.1 = (f32[896,128]{1,0:T(8,128)S(1)}, f32[896,128]{1,0:T(8,128)S(1)}, u32[]{:S(2)}, u32[]{:S(2)}) collective-permute-start(f32[896,128]{1,0:T(8,128)S(1)} %constant_dynamic-slice_fusion), channel_id=1, source_target_pairs={{0,16},{16,0},{32,48},{48,32},{64,80},{80,64},{96,112},{112,96},{1... | collective-permute-start | bytes 1376264 | tf_op jit(solution)/shard_map/ppermute | solution.py:98
  187.3 24.5 %all-to-all-start.5 = ((f32[16,56,128]{2,1,0:T(8,128)}), f32[16,56,128]{2,1,0:T(8,128)S(1)}, u32[]{:S(2)}, u32[]{:S(2)}) async-start(f32[16,56,128]{2,1,0:T(8,128)} %bitcast.17), calls=%async_computation.5 | async-start | bytes 917504 | tf_op jit(solution)/shard_map/all_to_all | solution.py:105
  306.3 1.0 copy-start.2

commit v18 on v17

--- a/solution.py
+++ b/solution.py
@@ -166,15 +166,13 @@
                 energy = totals[2]
             image_energy, direction_energy = totals[0], totals[1]
         else:
-            parts = [image_rows, col_sq(own_part(direction))[None]]
-            if energy is None:
-                parts.append(energy_own[None])
-            gathered = gather_feat(jnp.concatenate(parts, axis=0))
+            own_energy = energy_own if energy is None else col_sq(own_part(direction))
+            gathered = gather_feat(jnp.concatenate([image_rows, own_energy[None]], axis=0))
             image_slab = gathered[:, :own_block].reshape(RB_DEV * own_block, responses)
             feat_sums = jnp.sum(gathered[:, own_block:], axis=0)
             totals = comp_total(jnp.concatenate([col_sq(image_slab)[None], feat_sums], axis=0))
             if energy is None:
-                energy = totals[2]
+                energy = totals[1]
             image_energy, direction_energy = totals[0], totals[1]
         step_size = energy / (image_energy + ridge * direction_energy)
         solution = step_size * direction if solution is None else solution + step_size * direction

time: 309 us -> 308 us (level)
  no operation moved by 1% of the time
where the time goes in v18:
time: 308 us; the launch traced here: 307 us
  blocking collectives  204 us (66%)
  waiting for transfers between devices  54.6 us (18%)
  starting transfers between devices  23.6 us (8%)
  Pallas kernels  10.6 us (3%)
  other arithmetic  6.94 us (2%)
  local copies, waits for them, and re-layouts  5.11 us (2%)
    all_gather x2, blocking collectives, gather_gradient(): got = lax.all_gather(own, 'comp', axis=0, tiled=False)  80.3 us
    all_to_all x2, blocking collectives, comp_total(): return lax.all_to_all(spread, 'comp', 0, 0, tiled=True).sum(0)  37.9 us
    all_to_all x1, blocking collectives, reduce_gradient(): lax.all_to_all(pieces, 'comp', 0, 0, tiled=True, axis_index_groups=same_c...  36 us
    all_to_all x1, blocking collectives, reduce_over(): return lax.all_to_all(pieces, axis, 0, 0, tiled=True).sum(0)  21.3 us
    all_to_all x1, waiting for transfers between devices, reduce_gradient(): lax.all_to_all(pieces, 'comp', 0, 0, tiled=True, axis_index_groups=same_c...  20.8 us
    all_to_all x1, blocking collectives, gather_feat(): return lax.all_to_all(spread, 'feat', 0, 0, tiled=True)  19.1 us
    all_to_all x1, waiting for transfers between devices, reduce_over(): return lax.all_to_all(pieces, axis, 0, 0, tiled=True).sum(0)  17.4 us
    all_to_all x1, waiting for transfers between devices, gather_feat(): return lax.all_to_all(spread, 'feat', 0, 0, tiled=True)  13.6 us
  transfers between devices with their start and end apart: 5, of which 5 were waited for; matrix products, arithmetic and copies ran while one was open for 0% of the time, Pallas kernels for 0%

profile of v18, /device:TPU:1, one launch (start us, length us, event | category | flops | bytes accessed | tf_op | source)
XLA Modules:
  0.0 306.6 jit_solution(2432280973075401370)
XLA Ops:
  0.6 1.9 broadcast_in_dim.16
  2.6 7.6 %all-to-all-start = ((f32[16,128,128]{2,1,0:T(8,128)}), f32[16,128,128]{2,1,0:T(8,128)S(1)}, u32[]{:S(2)}, u32[]{:S(2)}) async-start(f32[16,128,128]{2,1,0:T(8,128)} %broadcast_in_dim.16), calls=%async_computation | async-start | bytes 2097152 | tf_op jit(solution)/shard_map/all_to_all | solution.py:124
  10.8 13.6 %all-to-all-done = f32[16,128,128]{2,1,0:T(8,128)S(1)} async-done(((f32[16,128,128]{2,1,0:T(8,128)}), f32[16,128,128]{2,1,0:T(8,128)S(1)}, u32[]{:S(2)}, u32[]{:S(2)}) %all-to-all-start) | async-done | bytes 1048608 | tf_op jit(solution)/shard_map/all_to_all | solution.py:124
  24.4 0.8 bitcast_convert_fusion.x_ref
  25.2 2.7 shard_map.77
  27.9 0.0 copy-start
  27.9 1.1 constant_dynamic-slice_fusion.1
  29.0 5.7 %collective-permute-start = (f32[896,128]{1,0:T(8,128)S(1)}, f32[896,128]{1,0:T(8,128)S(1)}, u32[]{:S(2)}, u32[]{:S(2)}) collective-permute-start(f32[896,128]{1,0:T(8,128)S(1)} %constant_dynamic-slice_fusion.1), channel_id=1, source_target_pairs={{0,16},{16,0},{32,48},{48,32},{64,80},{80,64},{96,112},{112,96},{1... | collective-permute-start | bytes 1376264 | tf_op jit(solution)/shard_map/ppermute | solution.py:98
  34.8 1.4 collective-permute-done
  36.2 0.0 copy-done
  36.2 36.0 %all_to_all.45 = f32[16,56,128]{2,1,0:T(8,128)S(1)} all-to-all(f32[16,56,128]{2,1,0:T(8,128)S(1)} %bitcast.76), channel_id=1, replica_groups={{0,32,64,96,128,160,192,224,256,288,320,352,384,416,448,480},{16,48,80,..., dimensions={0} | all-to-all | bytes 917504 | tf_op jit(solution)/shard_map/all_to_all | solution.py:105
  72.3 40.1 %all-gather = f32[1792,128]{1,0:T(8,128)S(1)} all-gather(f32[56,128]{1,0:T(8,128)S(1)} %reduce_sum.128), channel_id=2, replica_groups=mesh['comp'=32,'feat'=16] {'comp'}, dimensions={0}, use_global_device_ids=true | all-gather | bytes 946176 | tf_op jit(solution)/shard_map/all_gather | solution.py:109
  112.4 0.1 copy.15
  112.5 0.8 bitcast_convert_fusion.2.x_ref
  113.3 2.6 shard_map.78
  115.9 3.7 %all-to-all-start.2 = ((f32[16,128,128]{2,1,0:T(8,128)}), f32[16,128,128]{2,1,0:T(8,128)S(1)}, u32[]{:S(2)}, u32[]{:S(2)}) async-start(f32[16,128,128]{2,1,0:T(8,128)} %bitcast.73), calls=%async_computation.2 | async-start | bytes 2097152 | tf_op jit(solution)/shard_map/all_to_all | solution.py:61
  119.6 17.4 %all-to-all-done.2 = f32[16,128,128]{2,1,0:T(8,128)S(1)} async-done(((f32[16,128,128]{2,1,0:T(8,128)}), f32[16,128,128]{2,1,0:T(8,128)S(1)}, u32[]{:S(2)}, u32[]{:S(2)}) %all-to-all-start.2) | async-done | bytes 1048608 | tf_op jit(solution)/shard_map/all_to_all | solution.py:61
  137.0 0.1 reduce_sum.129
  137.1 0.1 broadcast_in_dim.18
  137.2 19.1 %all_to_all.46 = f32[16,129,128]{2,1,0:T(8,128)S(1)} all-to-all(f32[16,129,128]{2,1,0:T(8,128)S(1)} %broadcast_in_dim.18), channel_id=1, replica_groups=mesh['comp'=32,'feat'=16] {'feat'}, dimensions={0} | all-to-all | bytes 2113536 | tf_op jit(solution)/shard_map/all_to_all | solution.py:124
  156.4 0.3 fusion.5
  156.7 19.1 %all_to_all.47 = f32[32,2,128]{2,1,0:T(2,128)S(1)} all-to-all(f32[32,2,128]{2,1,0:T(2,128)S(1)} %broadcast_in_dim.20), channel_id=1, replica_groups=mesh['comp'=32,'feat'=16] {'comp'}, dimensions={0} | all-to-all | bytes 65536 | tf_op jit(solution)/shard_map/all_to_all | solution.py:128
  175.8 0.0 copy-done.3
  175.9 0.9 fusion.1.x_ref
  176.8 2.7 shard_map.79
  179.4 1.1 constant_dynamic-slice_fusion
  180.6 3.0 collective-permute-start.1
  183.6 1.4 collective-permute-done.1
  185.0 0.0 copy-done.1
  185.0 0.8 dynamic-slice_add_fusion
  185.8 3.6 %all-to-all-start.5 = ((f32[16,56,128]{2,1,0:T(8,128)}), f32[16,56,128]{2,1,0:T(8,128)S(1)}, u32[]{:S(2)}, u32[]{:S(2)}) async-start(f32[16,56,128]{2,1,0:T(8,128)} %bitcast.16), calls=%async_computation.5 | async-start | bytes 917504 | tf_op jit(solution)/shard_map/all_to_all | solution.py:105
  189.4 0.1 bitcast_multiply_fusion.2
  189.5 20.8 %all-to-all-done.5 = f32[16,56,128]{2,1,0:T(8,128)S(1)} async-done(((f32[16,56,128]{2,1,0:T(8,128)}), f32[16,56,128]{2,1,0:T(8,128)S(1)}, u32[]{:S(2)}, u32[]{:S(2)}) %all-to-all-start.5) | async-done | bytes 458784 | tf_op jit(solution)/shard_map/all_to_all | solution.py:105
  210.4 40.2 %all-gather.2 = f32[32,57,128]{2,1,0:T(8,128)S(1)} all-gather(f32[1,57,128]{2,1,0:T(8,128)S(1)} %maximum_bitcast_fusion), channel_id=3, replica_groups=mesh['comp'=32,'feat'=16] {'comp'}, dimensions={0}, use_global_device_ids=true | all-gather | bytes 963072 | tf_op jit(solution)/shard_map/all_gather | solution.py:109
  250.6 0.1 slice_reduce_fusion
  250.7 0.1 slice.59
  250.8 0.1 copy.17
  250.8 0.6 scatter.4.rest_0_
  251.4 0.8 bitcast_convert_fusion.1.x_ref
  252.2 2.7 shard_map.80
  254.9 21.3 %all_to_all.48 = f32[16,136,128]{2,1,0:T(8,128)S(1)} all-to-all(f32[16,136,128]{2,1,0:T(8,128)} %bitcast.72), channel_id=1, replica_groups=mesh['comp'=32,'feat'=16] {'feat'}, dimensions={0} | all-to-all | bytes 2228224 | tf_op jit(solution)/shard_map/all_to_all | solution.py:61
  276.2 0.1 reduce_sum.138
  276.3 0.1 bitcast_add_fusion
  276.4 9.6 %all_to_all.49 = f32[16,2,128]{2,1,0:T(2,128)S(1)} all-to-all(f32[16,2,128]{2,1,0:T(2,128)S(1)} %broadcast_in_dim.22), channel_id=1, replica_groups=mesh['comp'=32,'feat'=16] {'feat'}, dimensions={0} | all-to-all | bytes 32768 | tf_op jit(solution)/shard_map/all_to_all | solution.py:164
  286.1 18.8 %all_to_all.50 = f32[32,2,128]{2,1,0:T(2,128)S(1)} all-to-all(f32[32,2,128]{2,1,0:T(2,128)S(1)} %broadcast_in_dim.23), channel_id=1, replica_groups=mesh['comp'=32,'feat'=16] {'comp'}, dimensions={0} | all-to-all | bytes 65536 | tf_op jit(solution)/shard_map/all_to_all | solution.py:128
  304.9 1.0 multiply_add_fusion
  306.0 0.0 copy-done.2
  306.0 0.6 multiply_subtract_fusion
  (24 shorter events, 0.5 us)
Async XLA Ops:
  2.6 21.8 %all-to-all-start = ((f32[16,128,128]{2,1,0:T(8,128)}), f32[16,128,128]{2,1,0:T(8,128)S(1)}, u32[]{:S(2)}, u32[]{:S(2)}) async-start(f32[16,128,128]{2,1,0:T(8,128)} %broadcast_in_dim.16), calls=%async_computation | async-start | bytes 2097152 | tf_op jit(solution)/shard_map/all_to_all | solution.py:124
  27.9 8.3 %copy-start = (f32[1792,128]{1,0:T(8,128)S(1)}, f32[1792,128]{1,0:T(8,128)}, u32[]{:S(2)}) copy-start(f32[1792,128]{1,0:T(8,128)} %shard_map.77) | copy-start | bytes 2752516
  29.0 7.2 %collective-permute-start = (f32[896,128]{1,0:T(8,128)S(1)}, f32[896,128]{1,0:T(8,128)S(1)}, u32[]{:S(2)}, u32[]{:S(2)}) collective-permute-start(f32[896,128]{1,0:T(8,128)S(1)} %constant_dynamic-slice_fusion.1), channel_id=1, source_target_pairs={{0,16},{16,0},{32,48},{48,32},{64,80},{80,64},{96,112},{112,96},{1... | collective-permute-start | bytes 1376264 | tf_op jit(solution)/shard_map/ppermute | solution.py:98
  115.9 21.1 %all-to-all-start.2 = ((f32[16,128,128]{2,1,0:T(8,128)}), f32[16,128,128]{2,1,0:T(8,128)S(1)}, u32[]{:S(2)}, u32[]{:S(2)}) async-start(f32[16,128,128]{2,1,0:T(8,128)} %bitcast.73), calls=%async_computation.2 | async-start | bytes 2097152 | tf_op jit(solution)/shard_map/all_to_all | solution.py:61
  156.4 19.5 %copy-start.3 = (f32[128]{0:T(128)S(1)}, f32[128]{0:T(128)}, u32[]{:S(2)}) copy-start(f32[128]{0:T(128)} %param.13) | copy-start | bytes 1540
  179.4 5.6 %copy-start.1 = (f32[1792,128]{1,0:T(8,128)S(1)}, f32[1792,128]{1,0:T(8,128)}, u32[]{:S(2)}) copy-start(f32[1792,128]{1,0:T(8,128)} %shard_map.79) | copy-start | bytes 2752516
  180.6 4.5 %collective-permute-start.1 = (f32[896,128]{1,0:T(8,128)S(1)}, f32[896,128]{1,0:T(8,128)S(1)}, u32[]{:S(2)}, u32[]{:S(2)}) collective-permute-start(f32[896,128]{1,0:T(8,128)S(1)} %constant_dynamic-slice_fusion), channel_id=1, source_target_pairs={{0,16},{16,0},{32,48},{48,32},{64,80},{80,64},{96,112},{112,96},{1... | collective-permute-start | bytes 1376264 | tf_op jit(solution)/shard_map/ppermute | solution.py:98
  185.8 24.5 %all-to-all-start.5 = ((f32[16,56,128]{2,1,0:T(8,128)}), f32[16,56,128]{2,1,0:T(8,128)S(1)}, u32[]{:S(2)}, u32[]{:S(2)}) async-start(f32[16,56,128]{2,1,0:T(8,128)} %bitcast.16), calls=%async_computation.5 | async-start | bytes 917504 | tf_op jit(solution)/shard_map/all_to_all | solution.py:105
  304.9 1.0 copy-start.2

commit v19 on v18

--- a/solution.py
+++ b/solution.py
@@ -145,9 +145,11 @@
             gradient_own = reduce_gradient(backward(low_slab(residual_slab))) - ridge * own_part(
                 solution
             )
+            energy_rows = jnp.zeros((8, responses), jnp.float32).at[0].set(col_sq(gradient_own))
             gradient, comp_energy = gather_gradient(
-                jnp.concatenate([gradient_own, col_sq(gradient_own)[None]], axis=0)
+                jnp.concatenate([gradient_own, energy_rows], axis=0)
             )
+            comp_energy = comp_energy[:1]
             gradient_image, next_energy = forward(gradient, comp_energy)
             next_energy = next_energy[0]
             conjugate = next_energy / energy

time: 308 us -> 359 us (1.17)
  waiting for transfers between devices: 54.6 us -> 123 us
  blocking collectives: 204 us -> 171 us
  between operations: 1.48 us -> 14.9 us
    all_gather x0 -> x1, waiting for transfers between devices: none -> 68.7 us  [gather_gradient(): got = lax.all_gather(own, 'comp', axis=0, tiled=False)]
    all_gather x2 -> x1, blocking collectives: 80.3 us -> 40.1 us  [gather_gradient(): got = lax.all_gather(own, 'comp', axis=0, tiled=False)]
    all_to_all x2, blocking collectives: 37.9 us -> 42 us  [comp_total(): return lax.all_to_all(spread, 'comp', 0, 0, tiled=True).sum(0)]
  transfers between devices with their start and end apart: 5 -> 6, of which waited for: 5 -> 6; matrix products, arithmetic and copies ran while one was open for 0% -> 0% of each run, Pallas kernels for 0% -> 0%
where the time goes in v19:
time: 359 us; the launch traced here: 358 us
  blocking collectives  171 us (48%)
  waiting for transfers between devices  123 us (34%)
  starting transfers between devices  23.6 us (7%)
  between operations  14.9 us (4%)
  Pallas kernels  10.6 us (3%)
  other arithmetic  9.11 us (3%)
  local copies, waits for them, and re-layouts  5.68 us (2%)
    all_gather x1, waiting for transfers between devices, gather_gradient(): got = lax.all_gather(own, 'comp', axis=0, tiled=False)  68.7 us
    all_to_all x2, blocking collectives, comp_total(): return lax.all_to_all(spread, 'comp', 0, 0, tiled=True).sum(0)  42 us
    all_gather x1, blocking collectives, gather_gradient(): got = lax.all_gather(own, 'comp', axis=0, tiled=False)  40.1 us
    all_to_all x1, blocking collectives, reduce_gradient(): lax.all_to_all(pieces, 'comp', 0, 0, tiled=True, axis_index_groups=same_c...  36 us
    all_to_all x1, blocking collectives, reduce_over(): return lax.all_to_all(pieces, axis, 0, 0, tiled=True).sum(0)  23.7 us
    all_to_all x1, waiting for transfers between devices, reduce_gradient(): lax.all_to_all(pieces, 'comp', 0, 0, tiled=True, axis_index_groups=same_c...  20.8 us
    all_to_all x1, blocking collectives, gather_feat(): return lax.all_to_all(spread, 'feat', 0, 0, tiled=True)  19.1 us
    all_to_all x1, waiting for transfers between devices, reduce_over(): return lax.all_to_all(pieces, axis, 0, 0, tiled=True).sum(0)  17.4 us
  transfers between devices with their start and end apart: 6, of which 6 were waited for; matrix products, arithmetic and copies ran while one was open for 0% of the time, Pallas kernels for 0%

profile of v19, /device:TPU:1, one launch (start us, length us, event | category | flops | bytes accessed | tf_op | source)
XLA Modules:
  0.0 357.8 jit_solution(18168630882113469096)
XLA Ops:
  7.2 1.9 broadcast_in_dim.14
  9.1 7.6 %all-to-all-start = ((f32[16,128,128]{2,1,0:T(8,128)}), f32[16,128,128]{2,1,0:T(8,128)S(1)}, u32[]{:S(2)}, u32[]{:S(2)}) async-start(f32[16,128,128]{2,1,0:T(8,128)} %broadcast_in_dim.14), calls=%async_computation | async-start | bytes 2097152 | tf_op jit(solution)/shard_map/all_to_all | solution.py:124
  17.4 13.6 %all-to-all-done = f32[16,128,128]{2,1,0:T(8,128)S(1)} async-done(((f32[16,128,128]{2,1,0:T(8,128)}), f32[16,128,128]{2,1,0:T(8,128)S(1)}, u32[]{:S(2)}, u32[]{:S(2)}) %all-to-all-start) | async-done | bytes 1048608 | tf_op jit(solution)/shard_map/all_to_all | solution.py:124
  30.9 0.8 bitcast_convert_fusion.x_ref
  31.8 2.7 shard_map.77
  34.4 1.1 constant_dynamic-slice_fusion.1
  35.6 5.7 %collective-permute-start = (f32[896,128]{1,0:T(8,128)S(1)}, f32[896,128]{1,0:T(8,128)S(1)}, u32[]{:S(2)}, u32[]{:S(2)}) collective-permute-start(f32[896,128]{1,0:T(8,128)S(1)} %constant_dynamic-slice_fusion.1), channel_id=1, source_target_pairs={{0,16},{16,0},{32,48},{48,32},{64,80},{80,64},{96,112},{112,96},{1... | collective-permute-start | bytes 1376264 | tf_op jit(solution)/shard_map/ppermute | solution.py:98
  41.3 1.4 collective-permute-done
  42.7 0.0 copy-done
  42.8 36.0 %all_to_all.45 = f32[16,56,128]{2,1,0:T(8,128)S(1)} all-to-all(f32[16,56,128]{2,1,0:T(8,128)S(1)} %bitcast.74), channel_id=1, replica_groups={{0,32,64,96,128,160,192,224,256,288,320,352,384,416,448,480},{16,48,80,..., dimensions={0} | all-to-all | bytes 917504 | tf_op jit(solution)/shard_map/all_to_all | solution.py:105
  78.8 40.1 %all-gather = f32[1792,128]{1,0:T(8,128)S(1)} all-gather(f32[56,128]{1,0:T(8,128)S(1)} %reduce_sum.128), channel_id=2, replica_groups=mesh['comp'=32,'feat'=16] {'comp'}, dimensions={0}, use_global_device_ids=true | all-gather | bytes 946176 | tf_op jit(solution)/shard_map/all_gather | solution.py:109
  118.9 0.1 copy.12
  119.0 0.8 bitcast_convert_fusion.2.x_ref
  119.8 2.6 shard_map.78
  122.5 3.7 %all-to-all-start.2 = ((f32[16,128,128]{2,1,0:T(8,128)}), f32[16,128,128]{2,1,0:T(8,128)S(1)}, u32[]{:S(2)}, u32[]{:S(2)}) async-start(f32[16,128,128]{2,1,0:T(8,128)} %bitcast.71), calls=%async_computation.2 | async-start | bytes 2097152 | tf_op jit(solution)/shard_map/all_to_all | solution.py:61
  126.1 17.4 %all-to-all-done.2 = f32[16,128,128]{2,1,0:T(8,128)S(1)} async-done(((f32[16,128,128]{2,1,0:T(8,128)}), f32[16,128,128]{2,1,0:T(8,128)S(1)}, u32[]{:S(2)}, u32[]{:S(2)}) %all-to-all-start.2) | async-done | bytes 1048608 | tf_op jit(solution)/shard_map/all_to_all | solution.py:61
  143.6 0.1 reduce_sum.129
  143.6 0.1 broadcast_in_dim.16
  143.7 19.1 %all_to_all.46 = f32[16,129,128]{2,1,0:T(8,128)S(1)} all-to-all(f32[16,129,128]{2,1,0:T(8,128)S(1)} %broadcast_in_dim.16), channel_id=1, replica_groups=mesh['comp'=32,'feat'=16] {'feat'}, dimensions={0} | all-to-all | bytes 2113536 | tf_op jit(solution)/shard_map/all_to_all | solution.py:124
  162.9 0.3 fusion.5
  163.2 19.1 %all_to_all.47 = f32[32,2,128]{2,1,0:T(2,128)S(1)} all-to-all(f32[32,2,128]{2,1,0:T(2,128)S(1)} %broadcast_in_dim.18), channel_id=1, replica_groups=mesh['comp'=32,'feat'=16] {'comp'}, dimensions={0} | all-to-all | bytes 65536 | tf_op jit(solution)/shard_map/all_to_all | solution.py:128
  182.4 0.9 fusion.1.x_ref
  183.3 2.7 shard_map.79
  186.0 1.1 constant_dynamic-slice_fusion
  187.1 3.0 collective-permute-start.1
  190.1 1.4 collective-permute-done.1
  191.6 0.8 dynamic-slice_add_fusion
  192.4 3.6 all-to-all-start.5
  196.0 0.0 all-gather.4.cloned.1.call-start
  196.0 0.1 bitcast_multiply_fusion.2
  196.1 20.8 %all-to-all-done.5 = f32[16,56,128]{2,1,0:T(8,128)S(1)} async-done(((f32[16,56,128]{2,1,0:T(8,128)}), f32[16,56,128]{2,1,0:T(8,128)S(1)}, u32[]{:S(2)}, u32[]{:S(2)}) %all-to-all-start.5) | async-done | bytes 458784 | tf_op jit(solution)/shard_map/all_to_all | solution.py:105
  216.9 0.6 select_maximum_fusion
  217.6 0.0 all-gather.4.cloned.1.call-update
  217.6 68.7 %all-gather.4.cloned.1.call-done = f32[2048,128]{1,0:T(8,128)} async-done(((f32[64,128]{1,0:T(8,128)}), f32[2048,128]{1,0:T(8,128)}) %all-gather.4.cloned.1.call-update) | async-done | bytes 1048592 | tf_op jit(solution)/shard_map/all_gather | solution.py:109
  286.3 0.9 slice_reduce_fusion
  287.3 1.2 slice.75
  288.5 0.1 copy.14
  288.6 0.0 copy-start.4
  288.6 0.8 bitcast_convert_fusion.1.x_ref
  289.4 0.7 broadcast_select_fusion.rest_0_
  290.1 2.7 shard_map.80
  292.7 23.7 %all_to_all.48 = f32[16,136,128]{2,1,0:T(8,128)S(1)} all-to-all(f32[16,136,128]{2,1,0:T(8,128)} %bitcast.70), channel_id=1, replica_groups=mesh['comp'=32,'feat'=16] {'feat'}, dimensions={0} | all-to-all | bytes 2228224 | tf_op jit(solution)/shard_map/all_to_all | solution.py:61
  316.5 0.1 reduce_sum.138
  316.5 0.1 bitcast_add_fusion
  316.7 9.6 %all_to_all.49 = f32[16,2,128]{2,1,0:T(2,128)S(1)} all-to-all(f32[16,2,128]{2,1,0:T(2,128)S(1)} %broadcast_in_dim.19), channel_id=1, replica_groups=mesh['comp'=32,'feat'=16] {'feat'}, dimensions={0} | all-to-all | bytes 32768 | tf_op jit(solution)/shard_map/all_to_all | solution.py:166
  326.4 22.9 %all_to_all.50 = f32[32,2,128]{2,1,0:T(2,128)S(1)} all-to-all(f32[32,2,128]{2,1,0:T(2,128)S(1)} %broadcast_in_dim.20), channel_id=1, replica_groups=mesh['comp'=32,'feat'=16] {'comp'}, dimensions={0} | all-to-all | bytes 65536 | tf_op jit(solution)/shard_map/all_to_all | solution.py:128
  349.3 1.0 multiply_add_fusion
  350.3 0.6 multiply_subtract_fusion
  (28 shorter events, 0.5 us)
Async XLA Ops:
  9.1 21.8 %all-to-all-start = ((f32[16,128,128]{2,1,0:T(8,128)}), f32[16,128,128]{2,1,0:T(8,128)S(1)}, u32[]{:S(2)}, u32[]{:S(2)}) async-start(f32[16,128,128]{2,1,0:T(8,128)} %broadcast_in_dim.14), calls=%async_computation | async-start | bytes 2097152 | tf_op jit(solution)/shard_map/all_to_all | solution.py:124
  34.4 8.3 %copy-start = (f32[1792,128]{1,0:T(8,128)S(1)}, f32[1792,128]{1,0:T(8,128)}, u32[]{:S(2)}) copy-start(f32[1792,128]{1,0:T(8,128)} %shard_map.77) | copy-start | bytes 2752516
  35.6 7.2 %collective-permute-start = (f32[896,128]{1,0:T(8,128)S(1)}, f32[896,128]{1,0:T(8,128)S(1)}, u32[]{:S(2)}, u32[]{:S(2)}) collective-permute-start(f32[896,128]{1,0:T(8,128)S(1)} %constant_dynamic-slice_fusion.1), channel_id=1, source_target_pairs={{0,16},{16,0},{32,48},{48,32},{64,80},{80,64},{96,112},{112,96},{1... | collective-permute-start | bytes 1376264 | tf_op jit(solution)/shard_map/ppermute | solution.py:98
  122.5 21.1 %all-to-all-start.2 = ((f32[16,128,128]{2,1,0:T(8,128)}), f32[16,128,128]{2,1,0:T(8,128)S(1)}, u32[]{:S(2)}, u32[]{:S(2)}) async-start(f32[16,128,128]{2,1,0:T(8,128)} %bitcast.71), calls=%async_computation.2 | async-start | bytes 2097152 | tf_op jit(solution)/shard_map/all_to_all | solution.py:61
  162.9 19.5 %copy-start.3 = (f32[128]{0:T(128)S(1)}, f32[128]{0:T(128)}, u32[]{:S(2)}) copy-start(f32[128]{0:T(128)} %param.15) | copy-start | bytes 1540
  186.0 5.6 %copy-start.1 = (f32[1792,128]{1,0:T(8,128)S(1)}, f32[1792,128]{1,0:T(8,128)}, u32[]{:S(2)}) copy-start(f32[1792,128]{1,0:T(8,128)} %shard_map.79) | copy-start | bytes 2752516
  187.1 4.5 %collective-permute-start.1 = (f32[896,128]{1,0:T(8,128)S(1)}, f32[896,128]{1,0:T(8,128)S(1)}, u32[]{:S(2)}, u32[]{:S(2)}) collective-permute-start(f32[896,128]{1,0:T(8,128)S(1)} %constant_dynamic-slice_fusion), channel_id=1, source_target_pairs={{0,16},{16,0},{32,48},{48,32},{64,80},{80,64},{96,112},{112,96},{1... | collective-permute-start | bytes 1376264 | tf_op jit(solution)/shard_map/ppermute | solution.py:98
  192.4 24.5 %all-to-all-start.5 = ((f32[16,56,128]{2,1,0:T(8,128)}), f32[16,56,128]{2,1,0:T(8,128)S(1)}, u32[]{:S(2)}, u32[]{:S(2)}) async-start(f32[16,56,128]{2,1,0:T(8,128)} %bitcast.16), calls=%async_computation.5 | async-start | bytes 917504 | tf_op jit(solution)/shard_map/all_to_all | solution.py:105
  196.0 90.4 %all-gather.4.cloned.1.call-start = ((), (), s32[]{:S(2)}) async-start(), calls=%async_computation.9 | async-start | bytes 1081344 | tf_op jit(solution)/shard_map/all_gather | solution.py:109
  288.6 0.8 copy-start.4
  349.3 1.0 copy-start.2
Sparse Core Ops, SparseCore 0:
  217.7 68.5 all-gather.3
